TPU v7x, 32 devices: a whole 2x2x4 slice. The times are simulated.
32 devices in a mesh: groups: 2 (over y), area: 4 (over z), neuron: 4 (over x, core).
Axes of the slice: x: 2, y: 2, z: 4, core: 2. Of those that a mesh axis runs over, the one named last changes fastest.
Arguments:
- window: bfloat16 [32, 16, 32768], P(None, 'groups', ('area', 'neuron')), parts along dimension 1, may hold values from -6 to 6
- err_grad: float32 [16, 16, 32768], P(None, 'groups', ('area', 'neuron')), parts along dimension 1, may hold values from -6 to 6
- surrogate: float32 [16, 16, 32768], P(None, 'groups', ('area', 'neuron')), parts along dimension 1, may hold values from 0 to 0.5
- lv_end: float32 [16, 32768], P('groups', ('area', 'neuron')), parts along dimension 0, may hold values from -6 to 6
- la_end: float32 [16, 32768], P('groups', ('area', 'neuron')), parts along dimension 0, may hold values from -6 to 6
- alpha: float32 [32768], P(('area', 'neuron')), may hold values from 0.8 to 0.99
- rho: float32 [32768], P(('area', 'neuron')), may hold values from 0.9 to 0.999
- beta: float32 [32768], P(('area', 'neuron')), may hold values from 0.3 to 2
- weights: bfloat16 [4, 4, 64, 4, 128, 128], P(None, 'area', 'neuron'), may hold values from -0.25 to 0.25
- block_index: int32 [4, 4, 64, 4], P(None, 'area', 'neuron'), may hold values from 0 to 63, as said below
- delays: int32 [4, 4], replicated, may hold values from 16 to 31, as said below
Outputs:
- cur_adjoint: bfloat16 [16, 16, 32768], P(None, 'groups', ('area', 'neuron')), parts along dimension 1
- lv_start: float32 [16, 32768], P('groups', ('area', 'neuron')), parts along dimension 0
- la_start: float32 [16, 32768], P('groups', ('area', 'neuron')), parts along dimension 0
There are 2 independent parts, one for each index of `groups`. A program takes and returns all parts, laid end to end along the dimension named above; an argument that names none is the same for every part. Nothing has to cross between parts.
Inputs may be any that keep to these rules, and one draw needn't show every extreme that they name: `delays`: every entry lies in 16 to 31 and both ends occur. `block_index`: both ends occur.
All inputs are finite; a program needn't handle non-finite values.
Results may differ from a plain program's by a relative error of at most 0.001.
Values may be sent and summed in bfloat16 or wider, within the bound.
No kernel may reach another device: no remote copies, remote signals or barrier semaphores. Data moves between devices by JAX's collectives and lax.ppermute only.
A program may use at most 64 MiB of HBM per device.

v0:
```python
import jax
import jax.numpy as jnp
from jax import lax
from jax.sharding import PartitionSpec as P


def partner(value, axis, bit):
    mask = 2**bit
    pairs = [(source, source ^ mask) for source in range(lax.axis_size(axis))]
    return lax.ppermute(value, axis, pairs)


def adjoint_scan(err_grad, surrogate, rec, lv_end, la_end, alpha, rho, beta):

    def step(carry, inputs):
        lv_now, la_now = carry
        error_t, surr_t, rec_t = inputs
        total = error_t + rec_t - lv_now + la_now
        lv_next = alpha * lv_now + surr_t * total
        la_next = rho * la_now - beta * surr_t * total
        return ((lv_next, la_next), lv_now.astype(jnp.bfloat16))

    (lv_start, la_start), currents = lax.scan(
        step, (lv_end, la_end), (err_grad, surrogate, rec), reverse=True
    )
    return (currents, lv_start, la_start)


def per_device(
    window, err_grad, surrogate, lv_end, la_end, alpha, rho, beta, weights, block_index, delays
):
    steps = err_grad.shape[0]
    batch = err_grad.shape[1]
    local_neurons = err_grad.shape[2]
    block_side = weights.shape[-1]
    rounds = weights.shape[0]
    levels = lax.axis_size("area").bit_length() - 1
    me_area = lax.axis_index("area")
    rec = jnp.zeros((steps * batch, local_neurons), jnp.float32)
    for rnd in range(rounds):
        bit = rnd % levels
        arrived = partner(window, "area", bit)
        start = delays[rnd, me_area] - steps
        used = lax.dynamic_slice_in_dim(arrived, start, steps, 0)
        panel = lax.all_gather(used, "neuron", axis=2, tiled=True)
        flat = panel.reshape(steps * batch, panel.shape[2] // block_side, block_side)
        picked = jnp.take(flat, block_index[rnd, 0], axis=1)
        contrib = jnp.einsum(
            "rjkc,jkcd->rjd", picked, weights[rnd, 0], preferred_element_type=jnp.float32
        )
        rec = rec + contrib.reshape(steps * batch, local_neurons)
    rec = rec.reshape(steps, batch, local_neurons)
    return adjoint_scan(err_grad, surrogate, rec, lv_end, la_end, alpha, rho, beta)


def solution(mesh):
    placed = (
        P(None, "groups", ("area", "neuron")),
        P(None, "groups", ("area", "neuron")),
        P(None, "groups", ("area", "neuron")),
        P("groups", ("area", "neuron")),
        P("groups", ("area", "neuron")),
        P(("area", "neuron")),
        P(("area", "neuron")),
        P(("area", "neuron")),
        P(None, "area", "neuron", None, None, None),
        P(None, "area", "neuron", None),
        P(),
    )
    return jax.shard_map(
        per_device,
        mesh=mesh,
        in_specs=placed,
        out_specs=(
            P(None, "groups", ("area", "neuron")),
            P("groups", ("area", "neuron")),
            P("groups", ("area", "neuron")),
        ),
        check_vma=False,
    )
```

profile of v0, /device:TPU:0, one launch (start us, length us, event | category | flops | bytes accessed | tf_op | source)
XLA Modules:
  0.0 206.2 jit_solution(3993261804340114842)
XLA Ops:
  7.2 3.1 %collective-permute-start = (bf16[32,8,2048]{2,1,0:T(8,128)(2,1)}, bf16[32,8,2048]{2,1,0:T(8,128)(2,1)S(1)}, u32[]{:S(2)}, u32[]{:S(2)}) collective-permute-start(bf16[32,8,2048]{2,1,0:T(8,128)(2,1)} %param.15), channel_id=1, source_target_pairs={{0,4},{4,0},{8,12},{12,8},{1,5},{5,1},{9,13},{13,9},{2,6},{6,2},{1... | collective-permute-start | bytes 3145736 | tf_op jit(solution)/shard_map/ppermute | solution.py:10
  10.3 1.5 constant_dynamic-slice_fusion.5
  14.4 19.3 %collective-permute-done = bf16[32,8,2048]{2,1,0:T(8,128)(2,1)S(1)} collective-permute-done((bf16[32,8,2048]{2,1,0:T(8,128)(2,1)}, bf16[32,8,2048]{2,1,0:T(8,128)(2,1)S(1)}, u32[]{:S(2)}, u32[]{:S(2)}) %collective-permute-start) | collective-permute-done | bytes 1048608 | tf_op jit(solution)/shard_map/ppermute | solution.py:10
  33.7 1.1 constant_dynamic-slice_fusion.1
  34.8 0.0 all-gather.7.cloned.1.call-start
  34.9 2.8 %collective-permute-start.1 = (bf16[32,8,2048]{2,1,0:T(8,128)(2,1)S(1)}, bf16[32,8,2048]{2,1,0:T(8,128)(2,1)S(1)}, u32[]{:S(2)}, u32[]{:S(2)}) collective-permute-start(bf16[32,8,2048]{2,1,0:T(8,128)(2,1)S(1)} %copy-done.12), channel_id=1, source_target_pairs={{0,8},{4,12},{8,0},{12,4},{1,9},{5,13},{9,1},{13,5},{2,10},{6,14},... | collective-permute-start | bytes 3145736 | tf_op jit(solution)/shard_map/ppermute | solution.py:10
  40.1 42.5 %collective-permute-done.1 = bf16[32,8,2048]{2,1,0:T(8,128)(2,1)S(1)} collective-permute-done((bf16[32,8,2048]{2,1,0:T(8,128)(2,1)S(1)}, bf16[32,8,2048]{2,1,0:T(8,128)(2,1)S(1)}, u32[]{:S(2)}, u32[]{:S(2)}) %collective-permute-start.1) | collective-permute-done | bytes 1048608 | tf_op jit(solution)/shard_map/ppermute | solution.py:10
  82.6 1.0 constant_dynamic-slice_fusion
  83.7 0.0 all-gather.9.cloned.1.call-start
  83.7 0.7 all-gather.9.cloned.1.call-update
  84.4 0.0 all-gather.11.cloned.1.call-start
  84.5 0.5 all-gather.11.cloned.1.call-update
  85.0 0.1 copy.36
  85.1 0.1 reshape.99
  85.2 0.1 copy.35
  85.3 0.1 copy.39
  85.4 0.1 reshape.103
  85.5 0.1 copy.38
  85.6 0.1 copy.42
  85.7 0.1 reshape.107
  85.8 0.1 copy.41
  85.9 0.1 copy.45
  86.0 0.1 reshape.111
  86.0 0.1 copy.44
  86.2 2.2 %copy.52 = bf16[16,8,64,128]{3,2,1,0:T(8,128)(2,1)S(1)} copy(bf16[16,8,64,128]{3,1,2,0:T(8,128)(2,1)} %bitcast.147) | data formatting | bytes 4194304
  88.4 1.4 copy.37
  89.8 17.6 %all-gather.7.cloned.1.call-done = bf16[16,8,8192]{2,1,0:T(8,128)(2,1)} async-done(((bf16[16,8,2048]{2,1,0:T(8,128)(2,1)}), bf16[16,8,8192]{2,1,0:T(8,128)(2,1)}) %all-gather.7.cloned.1.call-update) | async-done | bytes 2097168 | tf_op jit(solution)/shard_map/all_gather | solution.py:45
  107.4 2.2 %copy.53 = bf16[16,8,64,128]{3,2,1,0:T(8,128)(2,1)S(1)} copy(bf16[16,8,64,128]{3,1,2,0:T(8,128)(2,1)} %bitcast.148) | data formatting | bytes 4194304
  109.6 2.7 %copy.40 = bf16[128,64,128]{2,0,1:T(8,128)(2,1)} copy(bf16[128,64,128]{2,1,0:T(8,128)(2,1)S(1)} %bitcast.144) | data formatting | bytes 4194304 | tf_op jit(solution)/shard_map/reshape | solution.py:46
  112.3 19.9 %all-gather.9.cloned.1.call-done = bf16[16,8,8192]{2,1,0:T(8,128)(2,1)} async-done(((bf16[16,8,2048]{2,1,0:T(8,128)(2,1)}), bf16[16,8,8192]{2,1,0:T(8,128)(2,1)}) %all-gather.9.cloned.1.call-update) | async-done | bytes 2097168 | tf_op jit(solution)/shard_map/all_gather | solution.py:45
  132.2 2.2 %copy.54 = bf16[16,8,64,128]{3,2,1,0:T(8,128)(2,1)S(1)} copy(bf16[16,8,64,128]{3,1,2,0:T(8,128)(2,1)} %bitcast.149) | data formatting | bytes 4194304
  134.4 2.7 %copy.43 = bf16[128,64,128]{2,0,1:T(8,128)(2,1)} copy(bf16[128,64,128]{2,1,0:T(8,128)(2,1)S(1)} %bitcast.145) | data formatting | bytes 4194304 | tf_op jit(solution)/shard_map/reshape | solution.py:46
  137.1 19.1 %all-gather.11.cloned.1.call-done = bf16[16,8,8192]{2,1,0:T(8,128)(2,1)} async-done(((bf16[16,8,2048]{2,1,0:T(8,128)(2,1)}), bf16[16,8,8192]{2,1,0:T(8,128)(2,1)}) %all-gather.11.cloned.1.call-update) | async-done | bytes 2097168 | tf_op jit(solution)/shard_map/all_gather | solution.py:45
  156.2 2.2 %copy.55 = bf16[16,8,64,128]{3,2,1,0:T(8,128)(2,1)S(1)} copy(bf16[16,8,64,128]{3,1,2,0:T(8,128)(2,1)} %bitcast.150) | data formatting | bytes 4194304
  158.4 2.7 %copy.46 = bf16[128,64,128]{2,0,1:T(8,128)(2,1)} copy(bf16[128,64,128]{2,1,0:T(8,128)(2,1)S(1)} %bitcast.146) | data formatting | bytes 4194304 | tf_op jit(solution)/shard_map/reshape | solution.py:46
  161.1 2.1 %gather_fusion = bf16[64,128,128]{2,1,0:T(8,128)(2,1)} fusion(bf16[128,64,128]{2,0,1:T(8,128)(2,1)S(1)} %copy.37, s32[1024]{0:T(1024)S(1)} %pad_clamp_fusion.3), kind=kCustom, calls=%fused_computation.clone | custom fusion | bytes 4194560 | tf_op jit(solution)/shard_map/jit(_take)/gather | solution.py:47
  163.3 4.0 %gather_fusion.1 = bf16[64,128,128]{2,1,0:T(8,128)(2,1)} fusion(bf16[128,64,128]{2,0,1:T(8,128)(2,1)} %copy.40, s32[1024]{0:T(1024)S(1)} %pad_clamp_fusion.2), kind=kCustom, calls=%fused_computation.1.clone | custom fusion | bytes 4194560 | tf_op jit(solution)/shard_map/jit(_take)/gather | solution.py:47
  167.2 2.2 %gather_fusion.2 = bf16[64,128,128]{2,1,0:T(8,128)(2,1)} fusion(bf16[128,64,128]{2,0,1:T(8,128)(2,1)S(1)} %copy-done, s32[1024]{0:T(1024)S(1)} %pad_clamp_fusion.1), kind=kCustom, calls=%fused_computation.2.clone | custom fusion | bytes 4194560 | tf_op jit(solution)/shard_map/jit(_take)/gather | solution.py:47
  169.4 2.5 %gather_fusion.3 = bf16[64,128,128]{2,1,0:T(8,128)(2,1)S(1)} fusion(bf16[128,64,128]{2,0,1:T(8,128)(2,1)} %copy.46, s32[1024]{0:T(1024)S(1)} %pad_clamp_fusion), kind=kCustom, calls=%fused_computation.3.clone | custom fusion | bytes 4194560 | tf_op jit(solution)/shard_map/jit(_take)/gather | solution.py:47
  172.0 3.1 %fusion.28 = f32[16,128,128]{2,1,0:T(8,128)S(1)} fusion(bf16[4,1,16,4,128,128]{5,4,3,2,1,0:T(8,128)(2,1)} %param.23, bf16[16,4,128,128]{3,2,1,0:T(8,128)(2,1)} %bitcast.153, pred[16,4]{1,0:T(8,128)(4,1)S(1)} %copy.35), kind=kOutput, calls=%fused_computation.36 | convolution fusion | flops 269484032 | bytes 5242944 | tf_op jit(solution)/shard_map/rjkc,jkcd->rjd/dot_general | solution.py:48
  175.1 2.5 %fusion.63 = f32[16,128,128]{2,1,0:T(8,128)S(1)} fusion(f32[16,128,128]{2,1,0:T(8,128)S(1)} %fusion.28, bf16[4,1,16,4,128,128]{5,4,3,2,1,0:T(8,128)(2,1)} %param.23, bf16[16,4,128,128]{3,2,1,0:T(8,128)(2,1)S(1)} %bitcast.154, pred[16,4]{1,0:T(8,128)(4,1)S(1)} %copy.38), kind=kOutput, calls=%fused_computation.43 | convolution fusion | flops 269746176 | bytes 6291520 | tf_op jit(solution)/shard_map/rjkc,jkcd->rjd/dot_general | solution.py:48
  177.6 2.4 %fusion.58 = f32[16,128,128]{2,1,0:T(8,128)S(1)} fusion(f32[16,128,128]{2,1,0:T(8,128)S(1)} %fusion.63, bf16[4,1,16,4,128,128]{5,4,3,2,1,0:T(8,128)(2,1)} %param.23, bf16[16,4,128,128]{3,2,1,0:T(8,128)(2,1)S(1)} %bitcast.152, pred[16,4]{1,0:T(8,128)(4,1)S(1)} %copy.41), kind=kOutput, calls=%fused_computation.42 | convolution fusion | flops 269746176 | bytes 6291520 | tf_op jit(solution)/shard_map/rjkc,jkcd->rjd/dot_general | solution.py:48
  180.0 2.4 %fusion.53 = f32[128,16,128]{2,0,1:T(8,128)S(1)} fusion(f32[16,128,128]{2,1,0:T(8,128)S(1)} %fusion.58, bf16[4,1,16,4,128,128]{5,4,3,2,1,0:T(8,128)(2,1)} %param.23, bf16[16,4,128,128]{3,2,1,0:T(8,128)(2,1)S(1)} %bitcast.151, pred[16,4]{1,0:T(8,128)(4,1)S(1)} %copy.44), kind=kOutput, calls=%fused_computation.41 | convolution fusion | flops 269746176 | bytes 6291520 | tf_op jit(solution)/shard_map/rjkc,jkcd->rjd/dot_general | solution.py:48
  182.5 0.6 copy.47
  183.1 0.2 add.133
  183.4 15.5 %while.18 = (s32[]{:T(128)}, f32[8,2048]{1,0:T(8,128)S(1)}, f32[8,2048]{1,0:T(8,128)S(1)}, bf16[16,8,2048]{2,1,0:T(8,128)(2,1)S(1)}, f32[2048]{0:T(1024)S(1)}, /...) while((s32[]{:T(128)}, f32[8,2048]{1,0:T(8,128)S(1)}, ...), condition=%wide.region_1.3_spmd, body=%wide.region_0.0_spmd.sunk | while | flops 180227 | bytes 581769 | solution.py:23
  183.4 0.9 fusion.77
  184.4 0.9 fusion.77
  185.3 0.9 fusion.77
  186.3 0.9 fusion.77
  187.3 0.9 fusion.77
  188.2 0.9 fusion.77
  189.2 0.9 fusion.77
  190.2 0.9 fusion.77
  191.1 0.9 fusion.77
  192.1 0.9 fusion.77
  193.1 0.9 fusion.77
  194.0 0.9 fusion.77
  195.0 0.9 fusion.77
  196.0 0.9 fusion.77
  196.9 0.9 fusion.77
  197.9 0.9 fusion.77
  198.9 0.6 copy-done.1
  199.5 0.2 copy-done.7
  (51 shorter events, 0.4 us)
Async XLA Ops:
  7.2 27.7 %copy-start.12 = (bf16[32,8,2048]{2,1,0:T(8,128)(2,1)S(1)}, bf16[32,8,2048]{2,1,0:T(8,128)(2,1)}, u32[]{:S(2)}) copy-start(bf16[32,8,2048]{2,1,0:T(8,128)(2,1)} %param.15) | copy-start | bytes 3145732
  7.2 79.0 %all-gather.5.cloned.1.call-start = ((), (), s32[]{:S(2)}) async-start(), calls=%async_computation | async-start | bytes 2621440 | tf_op jit(solution)/shard_map/all_gather | solution.py:45
  7.2 26.5 %collective-permute-start = (bf16[32,8,2048]{2,1,0:T(8,128)(2,1)}, bf16[32,8,2048]{2,1,0:T(8,128)(2,1)S(1)}, u32[]{:S(2)}, u32[]{:S(2)}) collective-permute-start(bf16[32,8,2048]{2,1,0:T(8,128)(2,1)} %param.15), channel_id=1, source_target_pairs={{0,4},{4,0},{8,12},{12,8},{1,5},{5,1},{9,13},{13,9},{2,6},{6,2},{1... | collective-permute-start | bytes 3145736 | tf_op jit(solution)/shard_map/ppermute | solution.py:10
  34.8 50.2 %copy-start.11 = (s32[4,1,16,4]{2,3,1,0:T(4,128)S(1)}, s32[4,1,16,4]{2,3,1,0:T(4,128)}, u32[]{:S(2)}) copy-start(s32[4,1,16,4]{2,3,1,0:T(4,128)} %param.24) | copy-start | bytes 3076
  34.8 72.6 %all-gather.7.cloned.1.call-start = ((), (), s32[]{:S(2)}) async-start(), calls=%async_computation.1 | async-start | bytes 2621440 | tf_op jit(solution)/shard_map/all_gather | solution.py:45
  34.9 47.8 %collective-permute-start.1 = (bf16[32,8,2048]{2,1,0:T(8,128)(2,1)S(1)}, bf16[32,8,2048]{2,1,0:T(8,128)(2,1)S(1)}, u32[]{:S(2)}, u32[]{:S(2)}) collective-permute-start(bf16[32,8,2048]{2,1,0:T(8,128)(2,1)S(1)} %copy-done.12), channel_id=1, source_target_pairs={{0,8},{4,12},{8,0},{12,4},{1,9},{5,13},{9,1},{13,5},{2,10},{6,14},... | collective-permute-start | bytes 3145736 | tf_op jit(solution)/shard_map/ppermute | solution.py:10
  83.7 48.5 %all-gather.9.cloned.1.call-start = ((), (), s32[]{:S(2)}) async-start(), calls=%async_computation.2 | async-start | bytes 2621440 | tf_op jit(solution)/shard_map/all_gather | solution.py:45
  84.4 71.8 %all-gather.11.cloned.1.call-start = ((), (), s32[]{:S(2)}) async-start(), calls=%async_computation.3 | async-start | bytes 2621440 | tf_op jit(solution)/shard_map/all_gather | solution.py:45
  163.3 4.0 %copy-start = (bf16[128,64,128]{2,0,1:T(8,128)(2,1)S(1)}, bf16[128,64,128]{2,0,1:T(8,128)(2,1)}, u32[]{:S(2)}) copy-start(bf16[128,64,128]{2,0,1:T(8,128)(2,1)} %copy.43) | copy-start | bytes 6291460
  171.9 3.1 %copy-start.6 = (bf16[64,128,128]{2,1,0:T(8,128)(2,1)S(1)}, bf16[64,128,128]{2,1,0:T(8,128)(2,1)}, u32[]{:S(2)}) copy-start(bf16[64,128,128]{2,1,0:T(8,128)(2,1)} %gather_fusion.1) | copy-start | bytes 6291460
  175.1 2.6 %copy-start.5 = (bf16[64,128,128]{2,1,0:T(8,128)(2,1)S(1)}, bf16[64,128,128]{2,1,0:T(8,128)(2,1)}, u32[]{:S(2)}) copy-start(bf16[64,128,128]{2,1,0:T(8,128)(2,1)} %gather_fusion.2) | copy-start | bytes 6291460
  182.4 0.9 copy-start.2
  182.5 0.9 copy-start.4
  182.5 0.9 copy-start.8
  182.5 0.9 copy-start.9
  182.5 0.9 copy-start.10
  198.8 0.6 copy-start.1
  198.9 0.6 copy-start.3
  198.9 0.8 copy-start.7
Sparse Core Ops, SparseCore 0:
  34.9 23.9 all-gather.4
  83.8 23.5 all-gather.6
  109.6 22.5 all-gather.8
  133.6 22.5 all-gather.10
where the time goes:
time: 207 us; the launch traced here: 206 us
  waiting for transfers between devices  120 us (58%)
  local copies, waits for them, and re-layouts  35.4 us (17%)
  between operations  19.1 us (9%)
  other arithmetic  15.2 us (7%)
  matrix products  10.4 us (5%)
  starting transfers between devices  6.07 us (3%)
    ppermute x2, waiting for transfers between devices, partner(): return lax.ppermute(value, axis, pairs)  61.8 us
    all_gather x4, waiting for transfers between devices, per_device(): panel = lax.all_gather(used, 'neuron', axis=2, tiled=True)  56.6 us
    sub x16, other arithmetic, step(): la_next = rho * la_now - beta * surr_t * total  15 us
    gather x4, local copies, waits for them, and re-layouts, per_device(): picked = jnp.take(flat, block_index[rnd, 0], axis=1)  10.8 us
    dot_general x4, matrix products, per_device(): jnp.einsum('rjkc,jkcd->rjd', picked, weights[rnd, 0], preferred_element_t...  10.4 us
    unnamed x30, local copies, waits for them, and re-layouts  9.6 us
    reshape x4, local copies, waits for them, and re-layouts, per_device(): panel.reshape(steps * batch, panel.shape[2] // block_side, block_side)  9.53 us
    ppermute x2, starting transfers between devices, partner(): return lax.ppermute(value, axis, pairs)  5.91 us
  transfers between devices with their start and end apart: 6, of which 5 were waited for; matrix products, arithmetic and copies ran while one was open for 8% of the time, Pallas kernels for 0%

commit v1 on v0

--- a/solution.py
+++ b/solution.py
@@ -4,26 +4,40 @@
 from jax.sharding import PartitionSpec as P
 
 
-def partner(value, axis, bit):
-    mask = 2**bit
+def swap(value, axis, mask):
     pairs = [(source, source ^ mask) for source in range(lax.axis_size(axis))]
     return lax.ppermute(value, axis, pairs)
 
 
+def gather_neuron(piece):
+    size = lax.axis_size("neuron")
+    bits = size.bit_length() - 1
+    held = piece[None]
+    for bit in reversed(range(bits)):
+        other = swap(held, "neuron", 1 << bit)
+        held = jnp.concatenate([held, other], axis=0)
+    return held
+
+
+def relative_position(n, me, bits):
+    d = n ^ me
+    pos = jnp.zeros_like(d)
+    for s, bit in enumerate(reversed(range(bits))):
+        pos = pos | (((d >> bit) & 1) << s)
+    return pos
+
+
 def adjoint_scan(err_grad, surrogate, rec, lv_end, la_end, alpha, rho, beta):
-
-    def step(carry, inputs):
-        lv_now, la_now = carry
-        error_t, surr_t, rec_t = inputs
-        total = error_t + rec_t - lv_now + la_now
-        lv_next = alpha * lv_now + surr_t * total
-        la_next = rho * la_now - beta * surr_t * total
-        return ((lv_next, la_next), lv_now.astype(jnp.bfloat16))
-
-    (lv_start, la_start), currents = lax.scan(
-        step, (lv_end, la_end), (err_grad, surrogate, rec), reverse=True
-    )
-    return (currents, lv_start, la_start)
+    steps = err_grad.shape[0]
+    lv_now, la_now = lv_end, la_end
+    currents = [None] * steps
+    for t in reversed(range(steps)):
+        total = err_grad[t] + rec[t] - lv_now + la_now
+        currents[t] = lv_now.astype(jnp.bfloat16)
+        lv_next = alpha * lv_now + surrogate[t] * total
+        la_next = rho * la_now - beta * surrogate[t] * total
+        lv_now, la_now = lv_next, la_next
+    return (jnp.stack(currents), lv_now, la_now)
 
 
 def per_device(
@@ -33,18 +47,25 @@
     batch = err_grad.shape[1]
     local_neurons = err_grad.shape[2]
     block_side = weights.shape[-1]
+    local_blocks = local_neurons // block_side
     rounds = weights.shape[0]
     levels = lax.axis_size("area").bit_length() - 1
+    nbits = lax.axis_size("neuron").bit_length() - 1
     me_area = lax.axis_index("area")
+    me_neuron = lax.axis_index("neuron")
     rec = jnp.zeros((steps * batch, local_neurons), jnp.float32)
     for rnd in range(rounds):
-        bit = rnd % levels
-        arrived = partner(window, "area", bit)
-        start = delays[rnd, me_area] - steps
-        used = lax.dynamic_slice_in_dim(arrived, start, steps, 0)
-        panel = lax.all_gather(used, "neuron", axis=2, tiled=True)
-        flat = panel.reshape(steps * batch, panel.shape[2] // block_side, block_side)
-        picked = jnp.take(flat, block_index[rnd, 0], axis=1)
+        mask = 1 << (rnd % levels)
+        start = delays[rnd, me_area ^ mask] - steps
+        piece = lax.dynamic_slice_in_dim(window, start, steps, 0)
+        arrived = swap(piece, "area", mask)
+        panel = gather_neuron(arrived)
+        flat = panel.reshape(panel.shape[0], steps * batch, local_blocks, block_side)
+        flat = jnp.moveaxis(flat, 1, 0).reshape(steps * batch, -1, block_side)
+        idx = block_index[rnd, 0]
+        owner = idx // local_blocks
+        pos = relative_position(owner, me_neuron, nbits) * local_blocks + idx % local_blocks
+        picked = jnp.take(flat, pos, axis=1)
         contrib = jnp.einsum(
             "rjkc,jkcd->rjd", picked, weights[rnd, 0], preferred_element_type=jnp.float32
         )

time: 207 us -> 132 us (0.64)
  waiting for transfers between devices: 120 us -> 55 us
  between operations: 19.1 us -> 6.41 us
  starting transfers between devices: 6.07 us -> 13.3 us
  other arithmetic: 15.2 us -> 10.4 us
    all_gather x4 -> x0, waiting for transfers between devices: 56.6 us -> none  [per_device(): panel = lax.all_gather(used, 'neuron', axis=2, tiled=True)]
    sub x16 -> x1, other arithmetic: 15 us -> 0.72 us  [adjoint_scan(): la_next = rho * la_now - beta * surrogate[t] * total]
    concatenate x0 -> x8, other arithmetic: none -> 8.42 us  [gather_neuron(): held = jnp.concatenate([held, other], axis=0)]
    ppermute x2 -> x12, starting transfers between devices: 5.91 us -> 13.3 us  [swap(): return lax.ppermute(value, axis, pairs)]
    ppermute x2 -> x12, waiting for transfers between devices: 61.8 us -> 55 us  [swap(): return lax.ppermute(value, axis, pairs)]
    dynamic_slice x3 -> x2, local copies, waits for them, and re-layouts: 3.61 us -> 4.29 us  [the longest x1 2.8 us: per_device(): piece = lax.dynamic_slice_in_dim(window, start, steps, 0)]
    unnamed x30 -> x48, local copies, waits for them, and re-layouts: 9.6 us -> 8.94 us
  transfers between devices with their start and end apart: 6 -> 12, of which waited for: 5 -> 6; matrix products, arithmetic and copies ran while one was open for 8% -> 18% of each run, Pallas kernels for 0% -> 0%
where the time goes in v1:
time: 132 us; the launch traced here: 131 us
  waiting for transfers between devices  55 us (42%)
  local copies, waits for them, and re-layouts  36.1 us (27%)
  starting transfers between devices  13.3 us (10%)
  other arithmetic  10.4 us (8%)
  matrix products  10.3 us (8%)
  between operations  6.41 us (5%)
    ppermute x12, waiting for transfers between devices, swap(): return lax.ppermute(value, axis, pairs)  55 us
    ppermute x12, starting transfers between devices, swap(): return lax.ppermute(value, axis, pairs)  13.3 us
    gather x4, local copies, waits for them, and re-layouts, per_device(): picked = jnp.take(flat, pos, axis=1)  12.2 us
    dot_general x4, matrix products, per_device(): jnp.einsum('rjkc,jkcd->rjd', picked, weights[rnd, 0], preferred_element_t...  10.3 us
    reshape x4, local copies, waits for them, and re-layouts, per_device(): flat = jnp.moveaxis(flat, 1, 0).reshape(steps * batch, -1, block_side)  9.55 us
    unnamed x48, local copies, waits for them, and re-layouts  8.94 us
    concatenate x8, other arithmetic, gather_neuron(): held = jnp.concatenate([held, other], axis=0)  8.42 us
    dynamic_slice x1, local copies, waits for them, and re-layouts, per_device(): piece = lax.dynamic_slice_in_dim(window, start, steps, 0)  2.8 us
  transfers between devices with their start and end apart: 12, of which 6 were waited for; matrix products, arithmetic and copies ran while one was open for 18% of the time, Pallas kernels for 0%

profile of v1, /device:TPU:0, one launch (start us, length us, event | category | flops | bytes accessed | tf_op | source)
XLA Modules:
  0.0 131.5 jit_solution(2570425894087307594)
XLA Ops:
  0.6 1.5 %constant_dynamic-slice_fusion.5 = (s32[1,1]{1,0:T(1,128)}, s32[1,1]{1,0:T(1,128)}, s32[1,1]{1,0:T(1,128)}, s32[1,1]{1,0:T(1,128)}) fusion(s32[4,4]{1,0:T(4,128)} %param.23, s32[]{:T(128)S(6)} %select_n.63, s32[]{:T(128)S(6)} %select_n.59), kind=kLoop, calls=%fused_computation.273 | loop fusion | bytes 40 | tf_op jit(solution)/shard_map/dynamic_slice | solution.py:59
  7.4 2.8 %constant_dynamic-slice_fusion = (bf16[16,8,2048]{2,1,0:T(8,128)(2,1)}, bf16[16,8,2048]{2,1,0:T(8,128)(2,1)S(1)}, bf16[16,8,2048]{2,1,0:T(8,128)(2,1)S(1)}, bf16[16,8,2048]{2,1,0:T(8,128)(2,1)}) fusion(bf16[32,8,2048]{2,1,0:T(8,128)(2,1)} %param.13, s32[]{:T(128)S(6)} %select_n.70, s32[]{:T(128)S(6)} %select_n.64, s32[]{:T(128)S(6)} %select_n.60, ...), kind=kLoop, calls=%fused_computation.268 | loop fusion | bytes 4194320 | tf_op jit(solution)/shard_map/dynamic_slice | solution.py:60
  10.2 3.0 %collective-permute-start = (bf16[16,8,2048]{2,1,0:T(8,128)(2,1)S(1)}, bf16[16,8,2048]{2,1,0:T(8,128)(2,1)S(1)}, u32[]{:S(2)}, u32[]{:S(2)}) collective-permute-start(bf16[16,8,2048]{2,1,0:T(8,128)(2,1)S(1)} %get-tuple-element.44), channel_id=1, source_target_pairs={{0,4},{4,0},{8,12},{12,8},{1,5},{5,1},{9,13},{13,9},{2,6},{6,2},{1... | collective-permute-start | bytes 1572872 | tf_op jit(solution)/shard_map/ppermute | solution.py:9
  13.2 2.6 %collective-permute-start.3 = (bf16[16,8,2048]{2,1,0:T(8,128)(2,1)S(1)}, bf16[16,8,2048]{2,1,0:T(8,128)(2,1)S(1)}, u32[]{:S(2)}, u32[]{:S(2)}) collective-permute-start(bf16[16,8,2048]{2,1,0:T(8,128)(2,1)S(1)} %get-tuple-element.43), channel_id=1, source_target_pairs={{0,8},{4,12},{8,0},{12,4},{1,9},{5,13},{9,1},{13,5},{2,10},{6,14},... | collective-permute-start | bytes 1572872 | tf_op jit(solution)/shard_map/ppermute | solution.py:9
  15.8 0.5 collective-permute-start.6
  16.2 20.8 %collective-permute-done = bf16[16,8,2048]{2,1,0:T(8,128)(2,1)S(1)} collective-permute-done((bf16[16,8,2048]{2,1,0:T(8,128)(2,1)S(1)}, bf16[16,8,2048]{2,1,0:T(8,128)(2,1)S(1)}, u32[]{:S(2)}, u32[]{:S(2)}) %collective-permute-start) | collective-permute-done | bytes 524320 | tf_op jit(solution)/shard_map/ppermute | solution.py:9
  37.0 2.1 %collective-permute-start.1 = (bf16[1,16,8,2048]{3,2,1,0:T(8,128)(2,1)S(1)}, bf16[1,16,8,2048]{3,2,1,0:T(8,128)(2,1)S(1)}, u32[]{:S(2)}, u32[]{:S(2)}) collective-permute-start(bf16[1,16,8,2048]{3,2,1,0:T(8,128)(2,1)S(1)} %bitcast.804), channel_id=1, source_target_pairs={{0,2},{1,3},{2,0},{3,1},{4,6},{5,7},{6,4},{7,5},{8,10},{9,11},{10,... | collective-permute-start | bytes 1572872 | tf_op jit(solution)/shard_map/ppermute | solution.py:9
  39.1 1.2 collective-permute-done.3
  40.3 1.5 %collective-permute-start.4 = (bf16[1,16,8,2048]{3,2,1,0:T(8,128)(2,1)S(1)}, bf16[1,16,8,2048]{3,2,1,0:T(8,128)(2,1)S(1)}, u32[]{:S(2)}, u32[]{:S(2)}) collective-permute-start(bf16[1,16,8,2048]{3,2,1,0:T(8,128)(2,1)S(1)} %bitcast.807), channel_id=1, source_target_pairs={{0,2},{1,3},{2,0},{3,1},{4,6},{5,7},{6,4},{7,5},{8,10},{9,11},{10,... | collective-permute-start | bytes 1572872 | tf_op jit(solution)/shard_map/ppermute | solution.py:9
  41.7 16.9 %collective-permute-done.6 = bf16[16,8,2048]{2,1,0:T(8,128)(2,1)S(1)} collective-permute-done((bf16[16,8,2048]{2,1,0:T(8,128)(2,1)}, bf16[16,8,2048]{2,1,0:T(8,128)(2,1)S(1)}, u32[]{:S(2)}, u32[]{:S(2)}) %collective-permute-start.6) | collective-permute-done | bytes 524320 | tf_op jit(solution)/shard_map/ppermute | solution.py:9
  58.7 1.7 %collective-permute-start.7 = (bf16[1,16,8,2048]{3,2,1,0:T(8,128)(2,1)S(1)}, bf16[1,16,8,2048]{3,2,1,0:T(8,128)(2,1)}, u32[]{:S(2)}, u32[]{:S(2)}) collective-permute-start(bf16[1,16,8,2048]{3,2,1,0:T(8,128)(2,1)S(1)} %bitcast.810), channel_id=1, source_target_pairs={{0,2},{1,3},{2,0},{3,1},{4,6},{5,7},{6,4},{7,5},{8,10},{9,11},{10,... | collective-permute-start | bytes 1572872 | tf_op jit(solution)/shard_map/ppermute | solution.py:9
  60.4 0.9 collective-permute-done.9
  61.2 1.5 %collective-permute-start.10 = (bf16[1,16,8,2048]{3,2,1,0:T(8,128)(2,1)S(1)}, bf16[1,16,8,2048]{3,2,1,0:T(8,128)(2,1)}, u32[]{:S(2)}, u32[]{:S(2)}) collective-permute-start(bf16[1,16,8,2048]{3,2,1,0:T(8,128)(2,1)S(1)} %bitcast.813), channel_id=1, source_target_pairs={{0,2},{1,3},{2,0},{3,1},{4,6},{5,7},{6,4},{7,5},{8,10},{9,11},{10,... | collective-permute-start | bytes 1572872 | tf_op jit(solution)/shard_map/ppermute | solution.py:9
  62.7 1.1 pad_maximum_fusion.4
  63.8 1.0 pad_maximum_fusion.5
  64.9 0.5 collective-permute-start.5
  65.4 0.1 copy.28
  65.5 0.1 reshape.166
  65.6 0.1 copy.24
  65.7 0.1 reshape.162
  65.8 7.9 %collective-permute-done.7 = bf16[1,16,8,2048]{3,2,1,0:T(8,128)(2,1)} collective-permute-done((bf16[1,16,8,2048]{3,2,1,0:T(8,128)(2,1)S(1)}, bf16[1,16,8,2048]{3,2,1,0:T(8,128)(2,1)}, u32[]{:S(2)}, u32[]{:S(2)}) %collective-permute-start.7) | collective-permute-done | bytes 524320 | tf_op jit(solution)/shard_map/ppermute | solution.py:9
  73.7 2.2 %pad_maximum_fusion.6 = bf16[2,16,8,2048]{3,2,1,0:T(8,128)(2,1)} fusion(bf16[1,16,8,2048]{3,2,1,0:T(8,128)(2,1)} %collective-permute-done.7, bf16[1,16,8,2048]{3,2,1,0:T(8,128)(2,1)S(1)} %bitcast.811), kind=kLoop, calls=%fused_computation.42 | loop fusion | flops 524288 | bytes 2097152 | tf_op jit(solution)/shard_map/concatenate | solution.py:18
  75.8 7.3 %collective-permute-done.10 = bf16[1,16,8,2048]{3,2,1,0:T(8,128)(2,1)} collective-permute-done((bf16[1,16,8,2048]{3,2,1,0:T(8,128)(2,1)S(1)}, bf16[1,16,8,2048]{3,2,1,0:T(8,128)(2,1)}, u32[]{:S(2)}, u32[]{:S(2)}) %collective-permute-start.10) | collective-permute-done | bytes 524320 | tf_op jit(solution)/shard_map/ppermute | solution.py:9
  83.1 2.1 %pad_maximum_fusion.7 = bf16[2,16,8,2048]{3,2,1,0:T(8,128)(2,1)} fusion(bf16[1,16,8,2048]{3,2,1,0:T(8,128)(2,1)} %collective-permute-done.10, bf16[1,16,8,2048]{3,2,1,0:T(8,128)(2,1)S(1)} %bitcast.814), kind=kLoop, calls=%fused_computation.43 | loop fusion | flops 524288 | bytes 2097152 | tf_op jit(solution)/shard_map/concatenate | solution.py:18
  85.3 0.1 copy.22
  85.4 0.1 copy.26
  85.5 0.1 copy.36
  85.6 0.1 reshape.174
  85.7 0.1 copy.32
  85.7 0.1 reshape.170
  85.8 0.1 copy.30
  85.9 0.1 copy.34
  86.0 0.1 copy.46
  86.2 0.1 copy.49
  86.3 0.1 copy.52
  86.4 0.1 copy.55
  86.5 0.1 copy.47
  86.7 0.1 copy.50
  86.8 1.1 copy.53
  87.9 1.1 copy.56
  89.1 1.4 %copy.48 = bf16[32,8,16,128]{3,2,1,0:T(8,128)(2,1)S(1)} copy(bf16[32,8,16,128]{3,1,2,0:T(8,128)(2,1)} %bitcast.126) | data formatting | bytes 2097152
  90.6 0.5 pad_maximum_fusion
  91.1 1.4 %copy.25 = bf16[128,64,128]{2,0,1:T(8,128)(2,1)S(1)} copy(bf16[128,64,128]{2,1,0:T(8,128)(2,1)S(1)} %bitcast.792) | data formatting | bytes 4194304 | tf_op jit(solution)/shard_map/reshape | solution.py:64
  92.4 1.4 %copy.51 = bf16[32,8,16,128]{3,2,1,0:T(8,128)(2,1)S(1)} copy(bf16[32,8,16,128]{3,1,2,0:T(8,128)(2,1)} %bitcast.142) | data formatting | bytes 2097152
  93.9 0.5 pad_maximum_fusion.1
  94.4 2.7 %copy.29 = bf16[128,64,128]{2,0,1:T(8,128)(2,1)} copy(bf16[128,64,128]{2,1,0:T(8,128)(2,1)S(1)} %bitcast.793) | data formatting | bytes 4194304 | tf_op jit(solution)/shard_map/reshape | solution.py:64
  97.1 1.4 %copy.54 = bf16[32,8,16,128]{3,2,1,0:T(8,128)(2,1)S(1)} copy(bf16[32,8,16,128]{3,1,2,0:T(8,128)(2,1)} %bitcast.158) | data formatting | bytes 2097152
  98.6 0.5 pad_maximum_fusion.2
  99.1 2.8 %copy.33 = bf16[128,64,128]{2,0,1:T(8,128)(2,1)} copy(bf16[128,64,128]{2,1,0:T(8,128)(2,1)S(1)} %bitcast.794) | data formatting | bytes 4194304 | tf_op jit(solution)/shard_map/reshape | solution.py:64
  101.8 1.4 %copy.57 = bf16[32,8,16,128]{3,2,1,0:T(8,128)(2,1)S(1)} copy(bf16[32,8,16,128]{3,1,2,0:T(8,128)(2,1)} %bitcast.174) | data formatting | bytes 2097152
  103.3 0.5 pad_maximum_fusion.3
  103.8 2.7 %copy.37 = bf16[128,64,128]{2,0,1:T(8,128)(2,1)} copy(bf16[128,64,128]{2,1,0:T(8,128)(2,1)S(1)} %bitcast.795) | data formatting | bytes 4194304 | tf_op jit(solution)/shard_map/reshape | solution.py:64
  106.5 2.1 %gather_fusion = bf16[64,128,128]{2,1,0:T(8,128)(2,1)} fusion(bf16[128,64,128]{2,0,1:T(8,128)(2,1)S(1)} %copy.25, s32[1024]{0:T(1024)S(1)} %get-tuple-element.59), kind=kCustom, calls=%fused_computation.clone | custom fusion | bytes 4194560 | tf_op jit(solution)/shard_map/jit(_take)/gather | solution.py:68
  108.7 3.9 %gather_fusion.1 = bf16[64,128,128]{2,1,0:T(8,128)(2,1)} fusion(bf16[128,64,128]{2,0,1:T(8,128)(2,1)} %copy.29, s32[1024]{0:T(1024)S(1)} %get-tuple-element.58), kind=kCustom, calls=%fused_computation.1.clone | custom fusion | bytes 4194560 | tf_op jit(solution)/shard_map/jit(_take)/gather | solution.py:68
  112.6 2.2 %gather_fusion.2 = bf16[64,128,128]{2,1,0:T(8,128)(2,1)} fusion(bf16[128,64,128]{2,0,1:T(8,128)(2,1)S(1)} %copy-done, s32[1024]{0:T(1024)S(1)} %get-tuple-element.57), kind=kCustom, calls=%fused_computation.2.clone | custom fusion | bytes 4194560 | tf_op jit(solution)/shard_map/jit(_take)/gather | solution.py:68
  114.8 4.0 %gather_fusion.3 = bf16[64,128,128]{2,1,0:T(8,128)(2,1)} fusion(bf16[128,64,128]{2,0,1:T(8,128)(2,1)} %copy.37, s32[1024]{0:T(1024)S(1)} %get-tuple-element.56), kind=kCustom, calls=%fused_computation.3.clone | custom fusion | bytes 4194560 | tf_op jit(solution)/shard_map/jit(_take)/gather | solution.py:68
  118.8 2.7 %fusion.24 = f32[16,128,128]{2,1,0:T(8,128)S(1)} fusion(bf16[4,1,16,4,128,128]{5,4,3,2,1,0:T(8,128)(2,1)} %param.21, bf16[16,4,128,128]{3,2,1,0:T(8,128)(2,1)S(1)} %bitcast.800, pred[16,4]{1,0:T(8,128)(4,1)S(1)} %copy.22), kind=kOutput, calls=%fused_computation.32 | convolution fusion | flops 269484032 | bytes 5242944 | tf_op jit(solution)/shard_map/rjkc,jkcd->rjd/dot_general | solution.py:69
  121.5 2.5 %fusion.59 = f32[16,128,128]{2,1,0:T(8,128)S(1)} fusion(f32[16,128,128]{2,1,0:T(8,128)S(1)} %fusion.24, bf16[4,1,16,4,128,128]{5,4,3,2,1,0:T(8,128)(2,1)} %param.21, bf16[16,4,128,128]{3,2,1,0:T(8,128)(2,1)S(1)} %bitcast.803, pred[16,4]{1,0:T(8,128)(4,1)S(1)} %copy.26), kind=kOutput, calls=%fused_computation.39 | convolution fusion | flops 269746176 | bytes 6291520 | tf_op jit(solution)/shard_map/rjkc,jkcd->rjd/dot_general | solution.py:69
  124.1 2.5 %fusion.54 = f32[16,128,128]{2,1,0:T(8,128)S(1)} fusion(f32[16,128,128]{2,1,0:T(8,128)S(1)} %fusion.59, bf16[4,1,16,4,128,128]{5,4,3,2,1,0:T(8,128)(2,1)} %param.21, bf16[16,4,128,128]{3,2,1,0:T(8,128)(2,1)S(1)} %bitcast.801, pred[16,4]{1,0:T(8,128)(4,1)S(1)} %copy.30), kind=kOutput, calls=%fused_computation.38 | convolution fusion | flops 269746176 | bytes 6291520 | tf_op jit(solution)/shard_map/rjkc,jkcd->rjd/dot_general | solution.py:69
  126.7 2.5 %fusion.49 = f32[128,16,128]{2,0,1:T(8,128)S(1)} fusion(f32[16,128,128]{2,1,0:T(8,128)S(1)} %fusion.54, bf16[4,1,16,4,128,128]{5,4,3,2,1,0:T(8,128)(2,1)} %param.21, bf16[16,4,128,128]{3,2,1,0:T(8,128)(2,1)S(1)} %bitcast.802, pred[16,4]{1,0:T(8,128)(4,1)S(1)} %copy.34), kind=kOutput, calls=%fused_computation.37 | convolution fusion | flops 269746176 | bytes 6291520 | tf_op jit(solution)/shard_map/rjkc,jkcd->rjd/dot_general | solution.py:69
  129.3 0.1 fusion.109
  129.4 0.1 fusion.103
  129.7 0.7 fusion.118
  130.7 0.7 fusion.116
  (61 shorter events, 0.5 us)
Async XLA Ops:
  10.2 26.9 %collective-permute-start = (bf16[16,8,2048]{2,1,0:T(8,128)(2,1)S(1)}, bf16[16,8,2048]{2,1,0:T(8,128)(2,1)S(1)}, u32[]{:S(2)}, u32[]{:S(2)}) collective-permute-start(bf16[16,8,2048]{2,1,0:T(8,128)(2,1)S(1)} %get-tuple-element.44), channel_id=1, source_target_pairs={{0,4},{4,0},{8,12},{12,8},{1,5},{5,1},{9,13},{13,9},{2,6},{6,2},{1... | collective-permute-start | bytes 1572872 | tf_op jit(solution)/shard_map/ppermute | solution.py:9
  13.2 27.1 %collective-permute-start.3 = (bf16[16,8,2048]{2,1,0:T(8,128)(2,1)S(1)}, bf16[16,8,2048]{2,1,0:T(8,128)(2,1)S(1)}, u32[]{:S(2)}, u32[]{:S(2)}) collective-permute-start(bf16[16,8,2048]{2,1,0:T(8,128)(2,1)S(1)} %get-tuple-element.43), channel_id=1, source_target_pairs={{0,8},{4,12},{8,0},{12,4},{1,9},{5,13},{9,1},{13,5},{2,10},{6,14},... | collective-permute-start | bytes 1572872 | tf_op jit(solution)/shard_map/ppermute | solution.py:9
  15.8 42.9 %collective-permute-start.6 = (bf16[16,8,2048]{2,1,0:T(8,128)(2,1)}, bf16[16,8,2048]{2,1,0:T(8,128)(2,1)S(1)}, u32[]{:S(2)}, u32[]{:S(2)}) collective-permute-start(bf16[16,8,2048]{2,1,0:T(8,128)(2,1)} %get-tuple-element.45), channel_id=1, source_target_pairs={{0,4},{4,0},{8,12},{12,8},{1,5},{5,1},{9,13},{13,9},{2,6},{6,2},{1... | collective-permute-start | bytes 1572872 | tf_op jit(solution)/shard_map/ppermute | solution.py:9
  16.2 45.0 %collective-permute-start.9 = (bf16[16,8,2048]{2,1,0:T(8,128)(2,1)}, bf16[16,8,2048]{2,1,0:T(8,128)(2,1)S(1)}, u32[]{:S(2)}, u32[]{:S(2)}) collective-permute-start(bf16[16,8,2048]{2,1,0:T(8,128)(2,1)} %get-tuple-element.42), channel_id=1, source_target_pairs={{0,8},{4,12},{8,0},{12,4},{1,9},{5,13},{9,1},{13,5},{2,10},{6,14},... | collective-permute-start | bytes 1572872 | tf_op jit(solution)/shard_map/ppermute | solution.py:9
  37.0 25.7 %collective-permute-start.1 = (bf16[1,16,8,2048]{3,2,1,0:T(8,128)(2,1)S(1)}, bf16[1,16,8,2048]{3,2,1,0:T(8,128)(2,1)S(1)}, u32[]{:S(2)}, u32[]{:S(2)}) collective-permute-start(bf16[1,16,8,2048]{3,2,1,0:T(8,128)(2,1)S(1)} %bitcast.804), channel_id=1, source_target_pairs={{0,2},{1,3},{2,0},{3,1},{4,6},{5,7},{6,4},{7,5},{8,10},{9,11},{10,... | collective-permute-start | bytes 1572872 | tf_op jit(solution)/shard_map/ppermute | solution.py:9
  40.3 23.6 %collective-permute-start.4 = (bf16[1,16,8,2048]{3,2,1,0:T(8,128)(2,1)S(1)}, bf16[1,16,8,2048]{3,2,1,0:T(8,128)(2,1)S(1)}, u32[]{:S(2)}, u32[]{:S(2)}) collective-permute-start(bf16[1,16,8,2048]{3,2,1,0:T(8,128)(2,1)S(1)} %bitcast.807), channel_id=1, source_target_pairs={{0,2},{1,3},{2,0},{3,1},{4,6},{5,7},{6,4},{7,5},{8,10},{9,11},{10,... | collective-permute-start | bytes 1572872 | tf_op jit(solution)/shard_map/ppermute | solution.py:9
  58.7 15.0 %collective-permute-start.7 = (bf16[1,16,8,2048]{3,2,1,0:T(8,128)(2,1)S(1)}, bf16[1,16,8,2048]{3,2,1,0:T(8,128)(2,1)}, u32[]{:S(2)}, u32[]{:S(2)}) collective-permute-start(bf16[1,16,8,2048]{3,2,1,0:T(8,128)(2,1)S(1)} %bitcast.810), channel_id=1, source_target_pairs={{0,2},{1,3},{2,0},{3,1},{4,6},{5,7},{6,4},{7,5},{8,10},{9,11},{10,... | collective-permute-start | bytes 1572872 | tf_op jit(solution)/shard_map/ppermute | solution.py:9
  61.2 4.1 %copy-start.12 = (s32[4,1,16,4]{2,3,1,0:T(4,128)S(1)}, s32[4,1,16,4]{2,3,1,0:T(4,128)}, u32[]{:S(2)}) copy-start(s32[4,1,16,4]{2,3,1,0:T(4,128)} %param.22) | copy-start | bytes 3076
  61.2 21.9 %collective-permute-start.10 = (bf16[1,16,8,2048]{3,2,1,0:T(8,128)(2,1)S(1)}, bf16[1,16,8,2048]{3,2,1,0:T(8,128)(2,1)}, u32[]{:S(2)}, u32[]{:S(2)}) collective-permute-start(bf16[1,16,8,2048]{3,2,1,0:T(8,128)(2,1)S(1)} %bitcast.813), channel_id=1, source_target_pairs={{0,2},{1,3},{2,0},{3,1},{4,6},{5,7},{6,4},{7,5},{8,10},{9,11},{10,... | collective-permute-start | bytes 1572872 | tf_op jit(solution)/shard_map/ppermute | solution.py:9
  63.8 25.3 %collective-permute-start.2 = (bf16[2,16,8,2048]{3,2,1,0:T(8,128)(2,1)}, bf16[2,16,8,2048]{3,2,1,0:T(8,128)(2,1)}, u32[]{:S(2)}, u32[]{:S(2)}) collective-permute-start(bf16[2,16,8,2048]{3,2,1,0:T(8,128)(2,1)} %pad_maximum_fusion.4), channel_id=1, source_target_pairs={{0,1},{1,0},{2,3},{3,2},{4,5},{5,4},{6,7},{7,6},{8,9},{9,8},{10,11... | collective-permute-start | bytes 3145736 | tf_op jit(solution)/shard_map/ppermute | solution.py:9
  64.9 27.6 %collective-permute-start.5 = (bf16[2,16,8,2048]{3,2,1,0:T(8,128)(2,1)}, bf16[2,16,8,2048]{3,2,1,0:T(8,128)(2,1)}, u32[]{:S(2)}, u32[]{:S(2)}) collective-permute-start(bf16[2,16,8,2048]{3,2,1,0:T(8,128)(2,1)} %pad_maximum_fusion.5), channel_id=1, source_target_pairs={{0,1},{1,0},{2,3},{3,2},{4,5},{5,4},{6,7},{7,6},{8,9},{9,8},{10,11... | collective-permute-start | bytes 3145736 | tf_op jit(solution)/shard_map/ppermute | solution.py:9
  75.8 21.3 %collective-permute-start.8 = (bf16[2,16,8,2048]{3,2,1,0:T(8,128)(2,1)}, bf16[2,16,8,2048]{3,2,1,0:T(8,128)(2,1)}, u32[]{:S(2)}, u32[]{:S(2)}) collective-permute-start(bf16[2,16,8,2048]{3,2,1,0:T(8,128)(2,1)} %pad_maximum_fusion.6), channel_id=1, source_target_pairs={{0,1},{1,0},{2,3},{3,2},{4,5},{5,4},{6,7},{7,6},{8,9},{9,8},{10,11... | collective-permute-start | bytes 3145736 | tf_op jit(solution)/shard_map/ppermute | solution.py:9
  85.3 16.6 %collective-permute-start.11 = (bf16[2,16,8,2048]{3,2,1,0:T(8,128)(2,1)}, bf16[2,16,8,2048]{3,2,1,0:T(8,128)(2,1)}, u32[]{:S(2)}, u32[]{:S(2)}) collective-permute-start(bf16[2,16,8,2048]{3,2,1,0:T(8,128)(2,1)} %pad_maximum_fusion.7), channel_id=1, source_target_pairs={{0,1},{1,0},{2,3},{3,2},{4,5},{5,4},{6,7},{7,6},{8,9},{9,8},{10,11... | collective-permute-start | bytes 3145736 | tf_op jit(solution)/shard_map/ppermute | solution.py:9
  108.7 3.9 %copy-start = (bf16[128,64,128]{2,0,1:T(8,128)(2,1)S(1)}, bf16[128,64,128]{2,0,1:T(8,128)(2,1)}, u32[]{:S(2)}) copy-start(bf16[128,64,128]{2,0,1:T(8,128)(2,1)} %copy.33) | copy-start | bytes 6291460
  114.8 4.0 %copy-start.1 = (bf16[64,128,128]{2,1,0:T(8,128)(2,1)S(1)}, bf16[64,128,128]{2,1,0:T(8,128)(2,1)}, u32[]{:S(2)}) copy-start(bf16[64,128,128]{2,1,0:T(8,128)(2,1)} %gather_fusion) | copy-start | bytes 6291460
  118.8 2.7 %copy-start.4 = (bf16[64,128,128]{2,1,0:T(8,128)(2,1)S(1)}, bf16[64,128,128]{2,1,0:T(8,128)(2,1)}, u32[]{:S(2)}) copy-start(bf16[64,128,128]{2,1,0:T(8,128)(2,1)} %gather_fusion.1) | copy-start | bytes 6291460
  121.5 2.6 %copy-start.2 = (bf16[64,128,128]{2,1,0:T(8,128)(2,1)S(1)}, bf16[64,128,128]{2,1,0:T(8,128)(2,1)}, u32[]{:S(2)}) copy-start(bf16[64,128,128]{2,1,0:T(8,128)(2,1)} %gather_fusion.2) | copy-start | bytes 6291460
  124.1 2.6 %copy-start.3 = (bf16[64,128,128]{2,1,0:T(8,128)(2,1)S(1)}, bf16[64,128,128]{2,1,0:T(8,128)(2,1)}, u32[]{:S(2)}) copy-start(bf16[64,128,128]{2,1,0:T(8,128)(2,1)} %gather_fusion.3) | copy-start | bytes 6291460
  126.6 2.6 %copy-start.5 = (f32[16,8,2048]{2,1,0:T(8,128)S(1)}, f32[16,8,2048]{2,1,0:T(8,128)}, u32[]{:S(2)}) copy-start(f32[16,8,2048]{2,1,0:T(8,128)} %param.15) | copy-start | bytes 3145732
  126.6 2.6 %copy-start.6 = (f32[16,8,2048]{2,1,0:T(8,128)S(1)}, f32[16,8,2048]{2,1,0:T(8,128)}, u32[]{:S(2)}) copy-start(f32[16,8,2048]{2,1,0:T(8,128)} %param.14) | copy-start | bytes 3145732
  126.6 2.6 %copy-start.7 = (f32[2048]{0:T(1024)S(1)}, f32[2048]{0:T(1024)}, u32[]{:S(2)}) copy-start(f32[2048]{0:T(1024)} %param.20) | copy-start | bytes 24580
  126.7 2.6 %copy-start.8 = (f32[2048]{0:T(1024)S(1)}, f32[2048]{0:T(1024)}, u32[]{:S(2)}) copy-start(f32[2048]{0:T(1024)} %param.19) | copy-start | bytes 24580
  126.7 2.6 %copy-start.9 = (f32[2048]{0:T(1024)S(1)}, f32[2048]{0:T(1024)}, u32[]{:S(2)}) copy-start(f32[2048]{0:T(1024)} %param.18) | copy-start | bytes 24580
  126.7 2.6 %copy-start.10 = (f32[8,2048]{1,0:T(8,128)S(1)}, f32[8,2048]{1,0:T(8,128)}, u32[]{:S(2)}) copy-start(f32[8,2048]{1,0:T(8,128)} %param.16) | copy-start | bytes 196612
  126.7 2.6 %copy-start.11 = (f32[8,2048]{1,0:T(8,128)S(1)}, f32[8,2048]{1,0:T(8,128)}, u32[]{:S(2)}) copy-start(f32[8,2048]{1,0:T(8,128)} %param.17) | copy-start | bytes 196612
  130.6 0.8 copy-start.13

commit v2 on v1

--- a/solution.py
+++ b/solution.py
@@ -1,6 +1,10 @@
+import functools
+
 import jax
 import jax.numpy as jnp
 from jax import lax
+from jax.experimental import pallas as pl
+from jax.experimental.pallas import tpu as pltpu
 from jax.sharding import PartitionSpec as P
 
 
@@ -12,10 +16,9 @@
 def gather_neuron(piece):
     size = lax.axis_size("neuron")
     bits = size.bit_length() - 1
-    held = piece[None]
+    held = [piece]
     for bit in reversed(range(bits)):
-        other = swap(held, "neuron", 1 << bit)
-        held = jnp.concatenate([held, other], axis=0)
+        held = held + [swap(chunk, "neuron", 1 << bit) for chunk in held]
     return held
 
 
@@ -25,6 +28,61 @@
     for s, bit in enumerate(reversed(range(bits))):
         pos = pos | (((d >> bit) & 1) << s)
     return pos
+
+
+def round_kernel(pos_ref, *refs, n_chunks, local_blocks, nnz, first):
+    chunk_refs = refs[:n_chunks]
+    w_ref = refs[n_chunks]
+    if first:
+        out_ref, blocks = refs[n_chunks + 1:]
+        rec_ref = None
+    else:
+        rec_ref, out_ref, blocks = refs[n_chunks + 1:]
+    steps, batch, _ = chunk_refs[0].shape
+    side = w_ref.shape[-1]
+    rows = steps * batch
+    for c in range(n_chunks):
+        for i in range(local_blocks):
+            x = chunk_refs[c][:, :, i * side:(i + 1) * side].astype(jnp.float32)
+            blocks[c * local_blocks + i] = x.reshape(rows, side).astype(jnp.bfloat16)
+    for j in range(local_blocks):
+        if first:
+            acc = jnp.zeros((rows, side), jnp.float32)
+        else:
+            acc = rec_ref[:, :, j * side:(j + 1) * side].reshape(rows, side)
+        for k in range(nnz):
+            x = blocks[pos_ref[j * nnz + k]]
+            acc = acc + jnp.dot(x, w_ref[j, k], preferred_element_type=jnp.float32)
+        out_ref[:, :, j * side:(j + 1) * side] = acc.reshape(steps, batch, side)
+
+
+def round_contrib(pos, chunks, weights, rnd, rec):
+    steps, batch, local = chunks[0].shape
+    rounds, _, local_blocks, nnz, side, _ = weights.shape
+    n_chunks = len(chunks)
+    first = rec is None
+    chunk_spec = pl.BlockSpec((steps, batch, local), lambda g, p: (0, 0, 0))
+    w_spec = pl.BlockSpec(
+        (None, None, local_blocks, nnz, side, side), lambda g, p: (rnd, 0, 0, 0, 0, 0)
+    )
+    rec_spec = pl.BlockSpec((steps, batch, local), lambda g, p: (0, 0, 0))
+    in_specs = [chunk_spec] * n_chunks + [w_spec] + ([] if first else [rec_spec])
+    operands = list(chunks) + [weights] + ([] if first else [rec])
+    kernel = functools.partial(
+        round_kernel, n_chunks=n_chunks, local_blocks=local_blocks, nnz=nnz, first=first
+    )
+    return pl.pallas_call(
+        kernel,
+        grid_spec=pltpu.PrefetchScalarGridSpec(
+            num_scalar_prefetch=1,
+            grid=(1,),
+            in_specs=in_specs,
+            out_specs=rec_spec,
+            scratch_shapes=[pltpu.VMEM((n_chunks * local_blocks, steps * batch, side), jnp.bfloat16)],
+        ),
+        out_shape=jax.ShapeDtypeStruct((steps, batch, local), jnp.float32),
+        input_output_aliases={} if first else {1 + n_chunks + 1: 0},
+    )(pos, *operands)
 
 
 def adjoint_scan(err_grad, surrogate, rec, lv_end, la_end, alpha, rho, beta):
@@ -44,7 +102,6 @@
     window, err_grad, surrogate, lv_end, la_end, alpha, rho, beta, weights, block_index, delays
 ):
     steps = err_grad.shape[0]
-    batch = err_grad.shape[1]
     local_neurons = err_grad.shape[2]
     block_side = weights.shape[-1]
     local_blocks = local_neurons // block_side
@@ -53,24 +110,29 @@
     nbits = lax.axis_size("neuron").bit_length() - 1
     me_area = lax.axis_index("area")
     me_neuron = lax.axis_index("neuron")
-    rec = jnp.zeros((steps * batch, local_neurons), jnp.float32)
+    uses = {}
     for rnd in range(rounds):
-        mask = 1 << (rnd % levels)
-        start = delays[rnd, me_area ^ mask] - steps
-        piece = lax.dynamic_slice_in_dim(window, start, steps, 0)
-        arrived = swap(piece, "area", mask)
-        panel = gather_neuron(arrived)
-        flat = panel.reshape(panel.shape[0], steps * batch, local_blocks, block_side)
-        flat = jnp.moveaxis(flat, 1, 0).reshape(steps * batch, -1, block_side)
+        uses.setdefault(rnd % levels, []).append(rnd)
+    whole = {}
+    for bit, rnds in uses.items():
+        if len(rnds) > 1:
+            whole[bit] = swap(window, "area", 1 << bit)
+    rec = None
+    for rnd in range(rounds):
+        bit = rnd % levels
+        mask = 1 << bit
+        if bit in whole:
+            start = delays[rnd, me_area] - steps
+            arrived = lax.dynamic_slice_in_dim(whole[bit], start, steps, 0)
+        else:
+            start = delays[rnd, me_area ^ mask] - steps
+            piece = lax.dynamic_slice_in_dim(window, start, steps, 0)
+            arrived = swap(piece, "area", mask)
+        chunks = gather_neuron(arrived)
         idx = block_index[rnd, 0]
         owner = idx // local_blocks
         pos = relative_position(owner, me_neuron, nbits) * local_blocks + idx % local_blocks
-        picked = jnp.take(flat, pos, axis=1)
-        contrib = jnp.einsum(
-            "rjkc,jkcd->rjd", picked, weights[rnd, 0], preferred_element_type=jnp.float32
-        )
-        rec = rec + contrib.reshape(steps * batch, local_neurons)
-    rec = rec.reshape(steps, batch, local_neurons)
+        rec = round_contrib(pos.reshape(-1).astype(jnp.int32), chunks, weights, rnd, rec)
     return adjoint_scan(err_grad, surrogate, rec, lv_end, la_end, alpha, rho, beta)
 
 

time: 132 us -> 130 us (0.985)
  local copies, waits for them, and re-layouts: 36.1 us -> 3.15 us
  Pallas kernels: 0 us -> 20.6 us
  waiting for transfers between devices: 55 us -> 75.5 us
  matrix products: 10.3 us -> 0 us
    pallas_call x0 -> x4, Pallas kernels: none -> 20.6 us  [round_contrib(): pl.pallas_call(kernel, grid_spec=pltpu.PrefetchScalarGridSpec(num_scalar_...]
    ppermute x12 -> x14, waiting for transfers between devices: 55 us -> 75.5 us  [swap(): return lax.ppermute(value, axis, pairs)]
    gather x4 -> x0, local copies, waits for them, and re-layouts: 12.2 us -> none  [per_device(): picked = jnp.take(flat, pos, axis=1)]
    dot_general x4 -> x0, matrix products: 10.3 us -> none  [per_device(): jnp.einsum('rjkc,jkcd->rjd', picked, weights[rnd, 0], preferred_element_t...]
    reshape x4 -> x0, local copies, waits for them, and re-layouts: 9.55 us -> none  [per_device(): flat = jnp.moveaxis(flat, 1, 0).reshape(steps * batch, -1, block_side)]
    unnamed x48 -> x36, local copies, waits for them, and re-layouts: 8.94 us -> 0.11 us
    concatenate x8 -> x0, other arithmetic: 8.42 us -> none  [gather_neuron(): held = jnp.concatenate([held, other], axis=0)]
    add x6, other arithmetic: 0.38 us -> 5.64 us  [adjoint_scan(): total = err_grad[t] + rec[t] - lv_now + la_now]
  transfers between devices with their start and end apart: 12 -> 14, of which waited for: 6 -> 5; matrix products, arithmetic and copies ran while one was open for 18% -> 4% of each run, Pallas kernels for 0% -> 12%
where the time goes in v2:
time: 130 us; the launch traced here: 129 us
  waiting for transfers between devices  75.5 us (58%)
  Pallas kernels  20.6 us (16%)
  starting transfers between devices  12.4 us (10%)
  other arithmetic  11.2 us (9%)
  between operations  6 us (5%)
  local copies, waits for them, and re-layouts  3.15 us (2%)
    ppermute x14, waiting for transfers between devices, swap(): return lax.ppermute(value, axis, pairs)  75.5 us
    pallas_call x4, Pallas kernels, round_contrib(): pl.pallas_call(kernel, grid_spec=pltpu.PrefetchScalarGridSpec(num_scalar_...  20.6 us
    ppermute x14, starting transfers between devices, swap(): return lax.ppermute(value, axis, pairs)  12.4 us
    add x6, other arithmetic, adjoint_scan(): total = err_grad[t] + rec[t] - lv_now + la_now  5.64 us
  transfers between devices with their start and end apart: 14, of which 5 were waited for; matrix products, arithmetic and copies ran while one was open for 4% of the time, Pallas kernels for 12%

profile of v2, /device:TPU:0, one launch (start us, length us, event | category | flops | bytes accessed | tf_op | source)
XLA Modules:
  0.0 128.8 jit_solution(7824016368188020038)
XLA Ops:
  0.6 3.1 %collective-permute-start.4 = (bf16[32,8,2048]{2,1,0:T(8,128)(2,1)}, bf16[32,8,2048]{2,1,0:T(8,128)(2,1)S(1)}, u32[]{:S(2)}, u32[]{:S(2)}) collective-permute-start(bf16[32,8,2048]{2,1,0:T(8,128)(2,1)} %param.11), channel_id=1, source_target_pairs={{0,4},{4,0},{8,12},{12,8},{1,5},{5,1},{9,13},{13,9},{2,6},{6,2},{1... | collective-permute-start | bytes 3145736 | tf_op jit(solution)/shard_map/ppermute | solution.py:13
  3.7 2.6 %collective-permute-start = (bf16[32,8,2048]{2,1,0:T(8,128)(2,1)}, bf16[32,8,2048]{2,1,0:T(8,128)(2,1)S(1)}, u32[]{:S(2)}, u32[]{:S(2)}) collective-permute-start(bf16[32,8,2048]{2,1,0:T(8,128)(2,1)} %param.11), channel_id=1, source_target_pairs={{0,8},{4,12},{8,0},{12,4},{1,9},{5,13},{9,1},{13,5},{2,10},{6,14},... | collective-permute-start | bytes 3145736 | tf_op jit(solution)/shard_map/ppermute | solution.py:13
  6.3 1.4 %constant_dynamic-slice_fusion.1 = (s32[1,1]{1,0:T(1,128)}, s32[1,1]{1,0:T(1,128)}, s32[1,1]{1,0:T(1,128)}, s32[1,1]{1,0:T(1,128)}) fusion(s32[4,4]{1,0:T(4,128)} %param.21, s32[]{:T(128)S(6)} %select_n.61), kind=kLoop, calls=%fused_computation.169 | loop fusion | bytes 36 | tf_op jit(solution)/shard_map/dynamic_slice | solution.py:125
  10.3 39.1 %collective-permute-done.4 = bf16[32,8,2048]{2,1,0:T(8,128)(2,1)S(1)} collective-permute-done((bf16[32,8,2048]{2,1,0:T(8,128)(2,1)}, bf16[32,8,2048]{2,1,0:T(8,128)(2,1)S(1)}, u32[]{:S(2)}, u32[]{:S(2)}) %collective-permute-start.4) | collective-permute-done | bytes 1048608 | tf_op jit(solution)/shard_map/ppermute | solution.py:13
  49.4 0.1 constant_dynamic-slice_fusion
  49.6 1.7 %collective-permute-start.11 = (bf16[16,8,2048]{2,1,0:T(8,128)(2,1)S(1)}, bf16[16,8,2048]{2,1,0:T(8,128)(2,1)}, u32[]{:S(2)}, u32[]{:S(2)}) collective-permute-start(bf16[16,8,2048]{2,1,0:T(8,128)(2,1)S(1)} %get-tuple-element.33.refs_0_), channel_id=1, source_target_pairs={{0,2},{1,3},{2,0},{3,1},{4,6},{5,7},{6,4},{7,5},{8,10},{9,11},{10,... | collective-permute-start | bytes 1572872 | tf_op jit(solution)/shard_map/ppermute | solution.py:13
  51.3 0.0 collective-permute-start.12
  53.7 0.0 collective-permute-done
  53.7 0.1 constant_dynamic-slice_fusion.2
  53.8 0.0 copy-start.3
  53.8 0.0 copy-start.2
  53.9 0.4 collective-permute-start.8
  54.3 0.2 collective-permute-start.9
  54.5 1.7 %collective-permute-start.5 = (bf16[16,8,2048]{2,1,0:T(8,128)(2,1)S(1)}, bf16[16,8,2048]{2,1,0:T(8,128)(2,1)S(1)}, u32[]{:S(2)}, u32[]{:S(2)}) collective-permute-start(bf16[16,8,2048]{2,1,0:T(8,128)(2,1)S(1)} %get-tuple-element.34.refs_0_), channel_id=1, source_target_pairs={{0,2},{1,3},{2,0},{3,1},{4,6},{5,7},{6,4},{7,5},{8,10},{9,11},{10,... | collective-permute-start | bytes 1572872 | tf_op jit(solution)/shard_map/ppermute | solution.py:13
  56.2 8.4 %collective-permute-done.11.refs_1_ = bf16[16,8,2048]{2,1,0:T(8,128)(2,1)} collective-permute-done((bf16[16,8,2048]{2,1,0:T(8,128)(2,1)S(1)}, bf16[16,8,2048]{2,1,0:T(8,128)(2,1)}, u32[]{:S(2)}, u32[]{:S(2)}) %collective-permute-start.11) | collective-permute-done | bytes 524320 | tf_op jit(solution)/shard_map/ppermute | solution.py:13
  64.6 1.7 %collective-permute-start.1 = (bf16[16,8,2048]{2,1,0:T(8,128)(2,1)S(1)}, bf16[16,8,2048]{2,1,0:T(8,128)(2,1)S(1)}, u32[]{:S(2)}, u32[]{:S(2)}) collective-permute-start(bf16[16,8,2048]{2,1,0:T(8,128)(2,1)S(1)} %get-tuple-element.36.refs_0_), channel_id=1, source_target_pairs={{0,2},{1,3},{2,0},{3,1},{4,6},{5,7},{6,4},{7,5},{8,10},{9,11},{10,... | collective-permute-start | bytes 1572872 | tf_op jit(solution)/shard_map/ppermute | solution.py:13
  66.2 0.0 collective-permute-done.12.refs_2_
  66.2 0.0 collective-permute-start.13
  66.2 0.7 fusion.123
  67.0 0.1 copy.24
  67.1 0.1 squeeze.44
  67.2 0.1 copy.23
  67.2 0.1 squeeze.43
  67.3 0.6 fusion.99.pos_ref
  67.9 7.9 %collective-permute-done.8.refs_1_ = bf16[16,8,2048]{2,1,0:T(8,128)(2,1)} collective-permute-done((bf16[16,8,2048]{2,1,0:T(8,128)(2,1)S(1)}, bf16[16,8,2048]{2,1,0:T(8,128)(2,1)}, u32[]{:S(2)}, u32[]{:S(2)}) %collective-permute-start.8) | collective-permute-done | bytes 524320 | tf_op jit(solution)/shard_map/ppermute | solution.py:13
  75.8 0.0 collective-permute-start.6
  75.8 0.0 collective-permute-done.9.refs_2_
  75.8 0.5 collective-permute-start.2
  76.3 10.6 %collective-permute-done.5.refs_1_ = bf16[16,8,2048]{2,1,0:T(8,128)(2,1)S(1)} collective-permute-done((bf16[16,8,2048]{2,1,0:T(8,128)(2,1)S(1)}, bf16[16,8,2048]{2,1,0:T(8,128)(2,1)S(1)}, u32[]{:S(2)}, u32[]{:S(2)}) %collective-permute-start.5) | collective-permute-done | bytes 524320 | tf_op jit(solution)/shard_map/ppermute | solution.py:13
  87.0 0.0 collective-permute-start.10
  87.0 9.5 %collective-permute-done.1.refs_1_ = bf16[16,8,2048]{2,1,0:T(8,128)(2,1)S(1)} collective-permute-done((bf16[16,8,2048]{2,1,0:T(8,128)(2,1)S(1)}, bf16[16,8,2048]{2,1,0:T(8,128)(2,1)S(1)}, u32[]{:S(2)}, u32[]{:S(2)}) %collective-permute-start.1) | collective-permute-done | bytes 524320 | tf_op jit(solution)/shard_map/ppermute | solution.py:13
  96.4 0.0 collective-permute-start.7
  96.4 0.0 collective-permute-done.13.refs_3_
  96.4 0.5 collective-permute-start.3
  97.0 0.6 fusion.98.pos_ref
  97.6 0.1 copy.22
  97.6 0.1 squeeze.42
  97.7 0.1 copy.21
  97.8 0.1 squeeze.41
  97.9 0.5 fusion.97.pos_ref
  98.4 0.5 fusion.96.pos_ref
  99.0 4.9 %shard_map.130.refs_5_ = f32[16,8,2048]{2,1,0:T(8,128)} custom-call(s32[64]{0:T(128)} %fusion.99.pos_ref, bf16[16,8,2048]{2,1,0:T(8,128)(2,1)} %copy-done.1, bf16[16,8,2048]{2,1,0:T(8,128)(2,1)} %collective-permute-done.11.refs_1_, bf16[16,8,2048]{2,1,0:T(8,128)(2,1)} %collective-permute-done.12.refs_2_, ...), custom_call_target="tpu_custom_call" | custom-call | tf_op jit(solution)/shard_map/pallas_call | solution.py:74
  103.9 0.0 collective-permute-done.10.refs_3_
  103.9 0.0 copy-done.3
  103.9 5.2 %shard_map.131.refs_5_ = f32[16,8,2048]{2,1,0:T(8,128)} custom-call(s32[64]{0:T(128)} %fusion.98.pos_ref, bf16[16,8,2048]{2,1,0:T(8,128)(2,1)} %copy-done.3, bf16[16,8,2048]{2,1,0:T(8,128)(2,1)} %collective-permute-done.8.refs_1_, bf16[16,8,2048]{2,1,0:T(8,128)(2,1)} %collective-permute-done.9.refs_2_, ...), custom_call_target="tpu_custom_call", output_to_operand_aliasing={{}: (6, {})} | custom-call | tf_op jit(solution)/shard_map/pallas_call | solution.py:74
  109.1 0.0 collective-permute-done.6.refs_2_
  109.1 0.0 collective-permute-done.7.refs_3_
  109.1 5.2 %shard_map.132.refs_5_ = f32[16,8,2048]{2,1,0:T(8,128)} custom-call(s32[64]{0:T(128)} %fusion.97.pos_ref, bf16[16,8,2048]{2,1,0:T(8,128)(2,1)} %copy-done, bf16[16,8,2048]{2,1,0:T(8,128)(2,1)} %copy-done.10, bf16[16,8,2048]{2,1,0:T(8,128)(2,1)} %collective-permute-done.6.refs_2_, ...), custom_call_target="tpu_custom_call", output_to_operand_aliasing={{}: (6, {})} | custom-call | tf_op jit(solution)/shard_map/pallas_call | solution.py:74
  114.3 0.0 copy-start.7
  114.3 0.0 copy-start.8
  114.3 0.0 copy-start.11
  114.3 0.0 copy-start.12
  114.4 0.0 collective-permute-done.2.refs_2_
  114.4 0.0 collective-permute-done.3.refs_3_
  114.4 5.3 %shard_map.133 = f32[16,8,2048]{2,1,0:T(8,128)} custom-call(s32[64]{0:T(128)} %fusion.96.pos_ref, bf16[16,8,2048]{2,1,0:T(8,128)(2,1)} %copy-done.2, bf16[16,8,2048]{2,1,0:T(8,128)(2,1)} %copy-done.9, bf16[16,8,2048]{2,1,0:T(8,128)(2,1)} %collective-permute-done.2.refs_2_, ...), custom_call_target="tpu_custom_call", output_to_operand_aliasing={{}: (6, {})} | custom-call | tf_op jit(solution)/shard_map/pallas_call | solution.py:74
  119.7 1.0 fusion.41
  120.7 0.9 fusion.35
  121.7 0.9 fusion.29
  122.6 0.9 fusion.23
  123.5 0.9 fusion.17
  124.5 0.9 fusion.11
  125.4 1.6 %fusion.50 = (f32[8,2048]{1,0:T(8,128)}, f32[8,2048]{1,0:T(8,128)S(1)}, f32[8,2048]{1,0:T(8,128)S(1)}, bf16[8,2048]{1,0:T(8,128)(2,1)S(1)}, f32[8,2048]{1,0:T(8,128)S(1)}, /*index=5*/bf16[8,2048]{1,0:T(8,128)(2,1)S(1)}) fusion(f32[16,8,2048]{2,1,0:T(8,128)S(1)} %copy-done.4, f32[2048]{0:T(1024)S(1)} %copy-done.6, f32[2048]{0:T(1024)S(1)} %copy-done.7, ...), kind=kLoop, calls=%fused_computation.68 | loop fusion | flops 589824 | bytes 1204224 | tf_op jit(solution)/shard_map/sub | solution.py:96
  127.2 0.0 copy-start.13
  127.2 1.6 %fusion.48 = f32[8,2048]{1,0:T(8,128)} fusion(f32[8,2048]{1,0:T(8,128)S(1)} %get-tuple-element.4, f32[16,8,2048]{2,1,0:T(8,128)S(1)} %copy-done.4, f32[2048]{0:T(1024)S(1)} %copy-done.8, f32[8,2048]{1,0:T(8,128)S(1)} %get-tuple-element.5, f32[2048]{0:T(1024)S(1)} %copy-done.6, f32[8,2048]{1,0:T(8,128)S(1)} %get-tuple-element.7, f32[2048]{0:T(1024)S(1)} %copy-done.7, ...), kind=kLoop, calls=%fused_computation.66 | loop fusion | flops 163840 | bytes 548864 | tf_op jit(solution)/shard_map/add | solution.py:95
  (36 shorter events, 0.1 us)
Async XLA Ops:
  0.6 48.8 %collective-permute-start.4 = (bf16[32,8,2048]{2,1,0:T(8,128)(2,1)}, bf16[32,8,2048]{2,1,0:T(8,128)(2,1)S(1)}, u32[]{:S(2)}, u32[]{:S(2)}) collective-permute-start(bf16[32,8,2048]{2,1,0:T(8,128)(2,1)} %param.11), channel_id=1, source_target_pairs={{0,4},{4,0},{8,12},{12,8},{1,5},{5,1},{9,13},{13,9},{2,6},{6,2},{1... | collective-permute-start | bytes 3145736 | tf_op jit(solution)/shard_map/ppermute | solution.py:13
  3.7 50.0 %collective-permute-start = (bf16[32,8,2048]{2,1,0:T(8,128)(2,1)}, bf16[32,8,2048]{2,1,0:T(8,128)(2,1)S(1)}, u32[]{:S(2)}, u32[]{:S(2)}) collective-permute-start(bf16[32,8,2048]{2,1,0:T(8,128)(2,1)} %param.11), channel_id=1, source_target_pairs={{0,8},{4,12},{8,0},{12,4},{1,9},{5,13},{9,1},{13,5},{2,10},{6,14},... | collective-permute-start | bytes 3145736 | tf_op jit(solution)/shard_map/ppermute | solution.py:13
  49.5 49.4 %copy-start.1 = (bf16[16,8,2048]{2,1,0:T(8,128)(2,1)}, bf16[16,8,2048]{2,1,0:T(8,128)(2,1)S(1)}, u32[]{:S(2)}) copy-start(bf16[16,8,2048]{2,1,0:T(8,128)(2,1)S(1)} %get-tuple-element.33.refs_0_) | copy-start | bytes 1572868
  49.5 59.5 %copy-start = (bf16[16,8,2048]{2,1,0:T(8,128)(2,1)}, bf16[16,8,2048]{2,1,0:T(8,128)(2,1)S(1)}, u32[]{:S(2)}) copy-start(bf16[16,8,2048]{2,1,0:T(8,128)(2,1)S(1)} %get-tuple-element.34.refs_0_) | copy-start | bytes 1572868
  49.6 15.0 %collective-permute-start.11 = (bf16[16,8,2048]{2,1,0:T(8,128)(2,1)S(1)}, bf16[16,8,2048]{2,1,0:T(8,128)(2,1)}, u32[]{:S(2)}, u32[]{:S(2)}) collective-permute-start(bf16[16,8,2048]{2,1,0:T(8,128)(2,1)S(1)} %get-tuple-element.33.refs_0_), channel_id=1, source_target_pairs={{0,2},{1,3},{2,0},{3,1},{4,6},{5,7},{6,4},{7,5},{8,10},{9,11},{10,... | collective-permute-start | bytes 1572872 | tf_op jit(solution)/shard_map/ppermute | solution.py:13
  51.3 15.0 %collective-permute-start.12 = (bf16[16,8,2048]{2,1,0:T(8,128)(2,1)S(1)}, bf16[16,8,2048]{2,1,0:T(8,128)(2,1)}, u32[]{:S(2)}, u32[]{:S(2)}) collective-permute-start(bf16[16,8,2048]{2,1,0:T(8,128)(2,1)S(1)} %get-tuple-element.33.refs_0_), channel_id=1, source_target_pairs={{0,1},{1,0},{2,3},{3,2},{4,5},{5,4},{6,7},{7,6},{8,9},{9,8},{10,11... | collective-permute-start | bytes 1572872 | tf_op jit(solution)/shard_map/ppermute | solution.py:13
  53.8 50.1 %copy-start.3 = (bf16[16,8,2048]{2,1,0:T(8,128)(2,1)}, bf16[16,8,2048]{2,1,0:T(8,128)(2,1)S(1)}, u32[]{:S(2)}) copy-start(bf16[16,8,2048]{2,1,0:T(8,128)(2,1)S(1)} %get-tuple-element.35.refs_0_) | copy-start | bytes 1572868
  53.8 55.2 %copy-start.2 = (bf16[16,8,2048]{2,1,0:T(8,128)(2,1)}, bf16[16,8,2048]{2,1,0:T(8,128)(2,1)S(1)}, u32[]{:S(2)}) copy-start(bf16[16,8,2048]{2,1,0:T(8,128)(2,1)S(1)} %get-tuple-element.36.refs_0_) | copy-start | bytes 1572868
  53.9 22.0 %collective-permute-start.8 = (bf16[16,8,2048]{2,1,0:T(8,128)(2,1)S(1)}, bf16[16,8,2048]{2,1,0:T(8,128)(2,1)}, u32[]{:S(2)}, u32[]{:S(2)}) collective-permute-start(bf16[16,8,2048]{2,1,0:T(8,128)(2,1)S(1)} %get-tuple-element.35.refs_0_), channel_id=1, source_target_pairs={{0,2},{1,3},{2,0},{3,1},{4,6},{5,7},{6,4},{7,5},{8,10},{9,11},{10,... | collective-permute-start | bytes 1572872 | tf_op jit(solution)/shard_map/ppermute | solution.py:13
  54.3 21.5 %collective-permute-start.9 = (bf16[16,8,2048]{2,1,0:T(8,128)(2,1)S(1)}, bf16[16,8,2048]{2,1,0:T(8,128)(2,1)}, u32[]{:S(2)}, u32[]{:S(2)}) collective-permute-start(bf16[16,8,2048]{2,1,0:T(8,128)(2,1)S(1)} %get-tuple-element.35.refs_0_), channel_id=1, source_target_pairs={{0,1},{1,0},{2,3},{3,2},{4,5},{5,4},{6,7},{7,6},{8,9},{9,8},{10,11... | collective-permute-start | bytes 1572872 | tf_op jit(solution)/shard_map/ppermute | solution.py:13
  54.5 32.4 %collective-permute-start.5 = (bf16[16,8,2048]{2,1,0:T(8,128)(2,1)S(1)}, bf16[16,8,2048]{2,1,0:T(8,128)(2,1)S(1)}, u32[]{:S(2)}, u32[]{:S(2)}) collective-permute-start(bf16[16,8,2048]{2,1,0:T(8,128)(2,1)S(1)} %get-tuple-element.34.refs_0_), channel_id=1, source_target_pairs={{0,2},{1,3},{2,0},{3,1},{4,6},{5,7},{6,4},{7,5},{8,10},{9,11},{10,... | collective-permute-start | bytes 1572872 | tf_op jit(solution)/shard_map/ppermute | solution.py:13
  64.6 31.9 %collective-permute-start.1 = (bf16[16,8,2048]{2,1,0:T(8,128)(2,1)S(1)}, bf16[16,8,2048]{2,1,0:T(8,128)(2,1)S(1)}, u32[]{:S(2)}, u32[]{:S(2)}) collective-permute-start(bf16[16,8,2048]{2,1,0:T(8,128)(2,1)S(1)} %get-tuple-element.36.refs_0_), channel_id=1, source_target_pairs={{0,2},{1,3},{2,0},{3,1},{4,6},{5,7},{6,4},{7,5},{8,10},{9,11},{10,... | collective-permute-start | bytes 1572872 | tf_op jit(solution)/shard_map/ppermute | solution.py:13
  66.2 30.2 %collective-permute-start.13 = (bf16[16,8,2048]{2,1,0:T(8,128)(2,1)}, bf16[16,8,2048]{2,1,0:T(8,128)(2,1)}, u32[]{:S(2)}, u32[]{:S(2)}) collective-permute-start(bf16[16,8,2048]{2,1,0:T(8,128)(2,1)} %collective-permute-done.11.refs_1_), channel_id=1, source_target_pairs={{0,1},{1,0},{2,3},{3,2},{4,5},{5,4},{6,7},{7,6},{8,9},{9,8},{10,11... | collective-permute-start | bytes 1572872 | tf_op jit(solution)/shard_map/ppermute | solution.py:13
  75.8 33.3 %collective-permute-start.6 = (bf16[16,8,2048]{2,1,0:T(8,128)(2,1)S(1)}, bf16[16,8,2048]{2,1,0:T(8,128)(2,1)}, u32[]{:S(2)}, u32[]{:S(2)}) collective-permute-start(bf16[16,8,2048]{2,1,0:T(8,128)(2,1)S(1)} %get-tuple-element.34.refs_0_), channel_id=1, source_target_pairs={{0,1},{1,0},{2,3},{3,2},{4,5},{5,4},{6,7},{7,6},{8,9},{9,8},{10,11... | collective-permute-start | bytes 1572872 | tf_op jit(solution)/shard_map/ppermute | solution.py:13
  75.8 38.5 %collective-permute-start.2 = (bf16[16,8,2048]{2,1,0:T(8,128)(2,1)S(1)}, bf16[16,8,2048]{2,1,0:T(8,128)(2,1)}, u32[]{:S(2)}, u32[]{:S(2)}) collective-permute-start(bf16[16,8,2048]{2,1,0:T(8,128)(2,1)S(1)} %get-tuple-element.36.refs_0_), channel_id=1, source_target_pairs={{0,1},{1,0},{2,3},{3,2},{4,5},{5,4},{6,7},{7,6},{8,9},{9,8},{10,11... | collective-permute-start | bytes 1572872 | tf_op jit(solution)/shard_map/ppermute | solution.py:13
  87.0 22.1 %copy-start.10 = (bf16[16,8,2048]{2,1,0:T(8,128)(2,1)}, bf16[16,8,2048]{2,1,0:T(8,128)(2,1)S(1)}, u32[]{:S(2)}) copy-start(bf16[16,8,2048]{2,1,0:T(8,128)(2,1)S(1)} %collective-permute-done.5.refs_1_) | copy-start | bytes 1572868
  87.0 16.9 %collective-permute-start.10 = (bf16[16,8,2048]{2,1,0:T(8,128)(2,1)}, bf16[16,8,2048]{2,1,0:T(8,128)(2,1)}, u32[]{:S(2)}, u32[]{:S(2)}) collective-permute-start(bf16[16,8,2048]{2,1,0:T(8,128)(2,1)} %collective-permute-done.8.refs_1_), channel_id=1, source_target_pairs={{0,1},{1,0},{2,3},{3,2},{4,5},{5,4},{6,7},{7,6},{8,9},{9,8},{10,11... | collective-permute-start | bytes 1572872 | tf_op jit(solution)/shard_map/ppermute | solution.py:13
  96.4 12.7 %copy-start.9 = (bf16[16,8,2048]{2,1,0:T(8,128)(2,1)}, bf16[16,8,2048]{2,1,0:T(8,128)(2,1)S(1)}, u32[]{:S(2)}) copy-start(bf16[16,8,2048]{2,1,0:T(8,128)(2,1)S(1)} %collective-permute-done.1.refs_1_) | copy-start | bytes 1572868
  96.4 12.7 %collective-permute-start.7 = (bf16[16,8,2048]{2,1,0:T(8,128)(2,1)S(1)}, bf16[16,8,2048]{2,1,0:T(8,128)(2,1)}, u32[]{:S(2)}, u32[]{:S(2)}) collective-permute-start(bf16[16,8,2048]{2,1,0:T(8,128)(2,1)S(1)} %collective-permute-done.5.refs_1_), channel_id=1, source_target_pairs={{0,1},{1,0},{2,3},{3,2},{4,5},{5,4},{6,7},{7,6},{8,9},{9,8},{10,11... | collective-permute-start | bytes 1572872 | tf_op jit(solution)/shard_map/ppermute | solution.py:13
  96.4 17.9 %collective-permute-start.3 = (bf16[16,8,2048]{2,1,0:T(8,128)(2,1)S(1)}, bf16[16,8,2048]{2,1,0:T(8,128)(2,1)}, u32[]{:S(2)}, u32[]{:S(2)}) collective-permute-start(bf16[16,8,2048]{2,1,0:T(8,128)(2,1)S(1)} %collective-permute-done.1.refs_1_), channel_id=1, source_target_pairs={{0,1},{1,0},{2,3},{3,2},{4,5},{5,4},{6,7},{7,6},{8,9},{9,8},{10,11... | collective-permute-start | bytes 1572872 | tf_op jit(solution)/shard_map/ppermute | solution.py:13
  114.3 5.4 %copy-start.4 = (f32[16,8,2048]{2,1,0:T(8,128)S(1)}, f32[16,8,2048]{2,1,0:T(8,128)}, u32[]{:S(2)}) copy-start(f32[16,8,2048]{2,1,0:T(8,128)} %param.13) | copy-start | bytes 3145732
  114.3 5.4 %copy-start.5 = (f32[16,8,2048]{2,1,0:T(8,128)S(1)}, f32[16,8,2048]{2,1,0:T(8,128)}, u32[]{:S(2)}) copy-start(f32[16,8,2048]{2,1,0:T(8,128)} %param.12) | copy-start | bytes 3145732
  114.3 5.4 %copy-start.6 = (f32[2048]{0:T(1024)S(1)}, f32[2048]{0:T(1024)}, u32[]{:S(2)}) copy-start(f32[2048]{0:T(1024)} %param.18) | copy-start | bytes 24580
  114.3 5.4 %copy-start.7 = (f32[2048]{0:T(1024)S(1)}, f32[2048]{0:T(1024)}, u32[]{:S(2)}) copy-start(f32[2048]{0:T(1024)} %param.17) | copy-start | bytes 24580
  114.3 5.4 %copy-start.8 = (f32[2048]{0:T(1024)S(1)}, f32[2048]{0:T(1024)}, u32[]{:S(2)}) copy-start(f32[2048]{0:T(1024)} %param.16) | copy-start | bytes 24580
  114.3 5.4 %copy-start.11 = (f32[8,2048]{1,0:T(8,128)S(1)}, f32[8,2048]{1,0:T(8,128)}, u32[]{:S(2)}) copy-start(f32[8,2048]{1,0:T(8,128)} %param.14) | copy-start | bytes 196612
  114.3 5.4 %copy-start.12 = (f32[8,2048]{1,0:T(8,128)S(1)}, f32[8,2048]{1,0:T(8,128)}, u32[]{:S(2)}) copy-start(f32[8,2048]{1,0:T(8,128)} %param.15) | copy-start | bytes 196612
  127.2 1.6 %copy-start.13 = (bf16[16,8,2048]{2,1,0:T(8,128)(2,1)}, bf16[16,8,2048]{2,1,0:T(8,128)(2,1)S(1)}, u32[]{:S(2)}) copy-start(bf16[16,8,2048]{2,1,0:T(8,128)(2,1)S(1)} %constant_dynamic-update-slice_fusion) | copy-start | bytes 1572868

commit v3 on v2

v3 whole, which is shorter than its diff:
```python
import functools

import jax
import jax.numpy as jnp
from jax import lax
from jax.experimental import pallas as pl
from jax.experimental.pallas import tpu as pltpu
from jax.sharding import PartitionSpec as P


def swap(value, axis, mask):
    pairs = [(source, source ^ mask) for source in range(lax.axis_size(axis))]
    return lax.ppermute(value, axis, pairs)


def gather_neuron(piece):
    size = lax.axis_size("neuron")
    bits = size.bit_length() - 1
    held = [piece]
    for bit in reversed(range(bits)):
        held = held + [swap(chunk, "neuron", 1 << bit) for chunk in held]
    return held


def relative_position(n, me, bits):
    d = n ^ me
    pos = jnp.zeros_like(d)
    for s, bit in enumerate(reversed(range(bits))):
        pos = pos | (((d >> bit) & 1) << s)
    return pos


def round_kernel(pos_ref, *refs, n_chunks, local_blocks, nnz, mode):
    chunk_refs = refs[:n_chunks]
    w_ref = refs[n_chunks]
    rest = refs[n_chunks + 1:]
    if mode == "first":
        (out_ref, blocks) = rest
    elif mode == "middle":
        (rec_ref, out_ref, blocks) = rest
    else:
        (rec_ref, err_ref, surr_ref, lv_ref, la_ref, alpha_ref, rho_ref, beta_ref,
         cur_ref, lv_out, la_out, blocks) = rest
    steps, batch, _ = chunk_refs[0].shape
    side = w_ref.shape[-1]
    rows = steps * batch
    for c in range(n_chunks):
        for i in range(local_blocks):
            x = chunk_refs[c][:, :, i * side:(i + 1) * side].astype(jnp.float32)
            blocks[c * local_blocks + i] = x.reshape(rows, side).astype(jnp.bfloat16)
    for j in range(local_blocks):
        cols = slice(j * side, (j + 1) * side)
        if mode == "first":
            acc = jnp.zeros((rows, side), jnp.float32)
        else:
            acc = rec_ref[:, :, cols].reshape(rows, side)
        for k in range(nnz):
            x = blocks[pos_ref[j * nnz + k]]
            acc = acc + jnp.dot(x, w_ref[j, k], preferred_element_type=jnp.float32)
        rec = acc.reshape(steps, batch, side)
        if mode != "final":
            out_ref[:, :, cols] = rec
            continue
        alpha = alpha_ref[:, cols]
        rho = rho_ref[:, cols]
        beta = beta_ref[:, cols]
        lv_now = lv_ref[:, cols]
        la_now = la_ref[:, cols]
        for t in reversed(range(steps)):
            surr = surr_ref[t, :, cols]
            total = err_ref[t, :, cols] + rec[t] - lv_now + la_now
            cur_ref[t, :, cols] = lv_now.astype(cur_ref.dtype)
            lv_next = alpha * lv_now + surr * total
            la_next = rho * la_now - beta * surr * total
            lv_now, la_now = lv_next, la_next
        lv_out[:, cols] = lv_now
        la_out[:, cols] = la_now


def round_contrib(pos, chunks, weights, rnd, rec, scan_args=None):
    steps, batch, local = chunks[0].shape
    rounds, _, local_blocks, nnz, side, _ = weights.shape
    n_chunks = len(chunks)
    mode = "first" if rec is None else ("middle" if scan_args is None else "final")
    full3 = pl.BlockSpec((steps, batch, local), lambda g, p: (0, 0, 0))
    full2 = pl.BlockSpec((batch, local), lambda g, p: (0, 0))
    row = pl.BlockSpec((1, local), lambda g, p: (0, 0))
    w_spec = pl.BlockSpec(
        (None, None, local_blocks, nnz, side, side), lambda g, p: (rnd, 0, 0, 0, 0, 0)
    )
    in_specs = [full3] * n_chunks + [w_spec]
    operands = list(chunks) + [weights]
    aliases = {}
    if mode != "first":
        in_specs.append(full3)
        operands.append(rec)
    if mode == "middle":
        aliases = {1 + n_chunks + 1: 0}
    if mode == "final":
        err_grad, surrogate, lv_end, la_end, alpha, rho, beta = scan_args
        in_specs += [full3, full3, full2, full2, row, row, row]
        operands += [err_grad, surrogate, lv_end, la_end,
                     alpha.reshape(1, local), rho.reshape(1, local), beta.reshape(1, local)]
        out_specs = (full3, full2, full2)
        out_shape = (
            jax.ShapeDtypeStruct((steps, batch, local), jnp.bfloat16),
            jax.ShapeDtypeStruct((batch, local), jnp.float32),
            jax.ShapeDtypeStruct((batch, local), jnp.float32),
        )
    else:
        out_specs = full3
        out_shape = jax.ShapeDtypeStruct((steps, batch, local), jnp.float32)
    kernel = functools.partial(
        round_kernel, n_chunks=n_chunks, local_blocks=local_blocks, nnz=nnz, mode=mode
    )
    return pl.pallas_call(
        kernel,
        grid_spec=pltpu.PrefetchScalarGridSpec(
            num_scalar_prefetch=1,
            grid=(1,),
            in_specs=in_specs,
            out_specs=out_specs,
            scratch_shapes=[pltpu.VMEM((n_chunks * local_blocks, steps * batch, side), jnp.bfloat16)],
        ),
        out_shape=out_shape,
        input_output_aliases=aliases,
    )(pos, *operands)


def per_device(
    window, err_grad, surrogate, lv_end, la_end, alpha, rho, beta, weights, block_index, delays
):
    steps = err_grad.shape[0]
    local_neurons = err_grad.shape[2]
    block_side = weights.shape[-1]
    local_blocks = local_neurons // block_side
    rounds = weights.shape[0]
    levels = lax.axis_size("area").bit_length() - 1
    nbits = lax.axis_size("neuron").bit_length() - 1
    me_area = lax.axis_index("area")
    me_neuron = lax.axis_index("neuron")
    arrived = []
    gate = None
    for first in range(0, rounds, 2):
        stage = list(range(first, min(first + 2, rounds)))
        pieces = []
        for rnd in stage:
            mask = 1 << (rnd % levels)
            start = delays[rnd, me_area ^ mask] - steps
            pieces.append(lax.dynamic_slice_in_dim(window, start, steps, 0))
        if gate is not None:
            pieces, _ = lax.optimization_barrier((pieces, gate))
        got = [swap(piece, "area", 1 << (rnd % levels)) for piece, rnd in zip(pieces, stage)]
        arrived += got
        gate = got
    rec = None
    for rnd in range(rounds):
        chunks = gather_neuron(arrived[rnd])
        idx = block_index[rnd, 0]
        owner = idx // local_blocks
        pos = relative_position(owner, me_neuron, nbits) * local_blocks + idx % local_blocks
        scan_args = None
        if rnd == rounds - 1:
            scan_args = (err_grad, surrogate, lv_end, la_end, alpha, rho, beta)
        rec = round_contrib(pos.reshape(-1).astype(jnp.int32), chunks, weights, rnd, rec, scan_args)
    return rec


def solution(mesh):
    placed = (
        P(None, "groups", ("area", "neuron")),
        P(None, "groups", ("area", "neuron")),
        P(None, "groups", ("area", "neuron")),
        P("groups", ("area", "neuron")),
        P("groups", ("area", "neuron")),
        P(("area", "neuron")),
        P(("area", "neuron")),
        P(("area", "neuron")),
        P(None, "area", "neuron", None, None, None),
        P(None, "area", "neuron", None),
        P(),
    )
    return jax.shard_map(
        per_device,
        mesh=mesh,
        in_specs=placed,
        out_specs=(
            P(None, "groups", ("area", "neuron")),
            P("groups", ("area", "neuron")),
            P("groups", ("area", "neuron")),
        ),
        check_vma=False,
    )
```

time: 130 us -> 112 us (0.86)
  waiting for transfers between devices: 75.5 us -> 62 us
  other arithmetic: 11.2 us -> 1.67 us
  starting transfers between devices: 12.4 us -> 15.9 us
  local copies, waits for them, and re-layouts: 3.15 us -> 4.62 us
    ppermute x14 -> x16, waiting for transfers between devices: 75.5 us -> 62 us  [swap(): return lax.ppermute(value, axis, pairs)]
    add x7 -> x0, other arithmetic: 7.23 us -> none  [the longest x6 5.64 us: adjoint_scan(): total = err_grad[t] + rec[t] - lv_now + la_now]
    ppermute x14 -> x16, starting transfers between devices: 12.4 us -> 15.9 us  [swap(): return lax.ppermute(value, axis, pairs)]
    sub x1 -> x0, other arithmetic: 1.63 us -> none  [adjoint_scan(): la_next = rho * la_now - beta * surrogate[t] * total]
    dynamic_slice x3 -> x2, local copies, waits for them, and re-layouts: 1.63 us -> 3.18 us  [the longest x1 1.69 us: per_device(): pieces.append(lax.dynamic_slice_in_dim(window, start, steps, 0))]
  transfers between devices with their start and end apart: 14 -> 16, of which waited for: 5 -> 6; matrix products, arithmetic and copies ran while one was open for 4% -> 3% of each run, Pallas kernels for 12% -> 14%
where the time goes in v3:
time: 112 us; the launch traced here: 111 us
  waiting for transfers between devices  62 us (55%)
  Pallas kernels  21.2 us (19%)
  starting transfers between devices  15.9 us (14%)
  between operations  5.99 us (5%)
  local copies, waits for them, and re-layouts  4.62 us (4%)
  other arithmetic  1.67 us (1%)
    ppermute x16, waiting for transfers between devices, swap(): return lax.ppermute(value, axis, pairs)  62 us
    pallas_call x4, Pallas kernels, round_contrib(): pl.pallas_call(kernel, grid_spec=pltpu.PrefetchScalarGridSpec(num_scalar_...  21.2 us
    ppermute x16, starting transfers between devices, swap(): return lax.ppermute(value, axis, pairs)  15.9 us
  transfers between devices with their start and end apart: 16, of which 6 were waited for; matrix products, arithmetic and copies ran while one was open for 3% of the time, Pallas kernels for 14%

profile of v3, /device:TPU:0, one launch (start us, length us, event | category | flops | bytes accessed | tf_op | source)
XLA Modules:
  0.0 111.4 jit_solution(5557471561219274487)
XLA Ops:
  0.6 1.5 %constant_dynamic-slice_fusion.7 = (s32[1,1]{1,0:T(1,128)}, s32[1,1]{1,0:T(1,128)}, s32[1,1]{1,0:T(1,128)}, s32[1,1]{1,0:T(1,128)}) fusion(s32[4,4]{1,0:T(4,128)} %param.21, s32[]{:T(128)S(6)} %select_n.65, s32[]{:T(128)S(6)} %select_n.63), kind=kLoop, calls=%fused_computation.31 | loop fusion | bytes 40 | tf_op jit(solution)/shard_map/dynamic_slice | solution.py:149
  7.4 1.7 %constant_dynamic-slice_fusion = (bf16[16,8,2048]{2,1,0:T(8,128)(2,1)S(1)}, bf16[16,8,2048]{2,1,0:T(8,128)(2,1)S(1)}, bf16[16,8,2048]{2,1,0:T(8,128)(2,1)S(1)}, bf16[16,8,2048]{2,1,0:T(8,128)(2,1)S(1)}) fusion(bf16[32,8,2048]{2,1,0:T(8,128)(2,1)} %param.11, s32[]{:T(128)S(6)} %select_n.68, s32[]{:T(128)S(6)} %select_n.66, s32[]{:T(128)S(6)} %select_n.64, ...), kind=kLoop, calls=%fused_computation.8 | loop fusion | bytes 4194320 | tf_op jit(solution)/shard_map/dynamic_slice | solution.py:150
  9.1 3.1 %collective-permute-start = (bf16[16,8,2048]{2,1,0:T(8,128)(2,1)S(1)}, bf16[16,8,2048]{2,1,0:T(8,128)(2,1)S(1)}, u32[]{:S(2)}, u32[]{:S(2)}) collective-permute-start(bf16[16,8,2048]{2,1,0:T(8,128)(2,1)S(1)} %get-tuple-element.10), channel_id=1, source_target_pairs={{0,4},{4,0},{8,12},{12,8},{1,5},{5,1},{9,13},{13,9},{2,6},{6,2},{1... | collective-permute-start | bytes 1572872 | tf_op jit(solution)/shard_map/ppermute | solution.py:13
  12.2 2.6 %collective-permute-start.1 = (bf16[16,8,2048]{2,1,0:T(8,128)(2,1)S(1)}, bf16[16,8,2048]{2,1,0:T(8,128)(2,1)S(1)}, u32[]{:S(2)}, u32[]{:S(2)}) collective-permute-start(bf16[16,8,2048]{2,1,0:T(8,128)(2,1)S(1)} %get-tuple-element.7), channel_id=1, source_target_pairs={{0,8},{4,12},{8,0},{12,4},{1,9},{5,13},{9,1},{13,5},{2,10},{6,14},... | collective-permute-start | bytes 1572872 | tf_op jit(solution)/shard_map/ppermute | solution.py:13
  14.8 20.4 %collective-permute-done.refs_0_ = bf16[16,8,2048]{2,1,0:T(8,128)(2,1)S(1)} collective-permute-done((bf16[16,8,2048]{2,1,0:T(8,128)(2,1)S(1)}, bf16[16,8,2048]{2,1,0:T(8,128)(2,1)S(1)}, u32[]{:S(2)}, u32[]{:S(2)}) %collective-permute-start) | collective-permute-done | bytes 524320 | tf_op jit(solution)/shard_map/ppermute | solution.py:13
  35.2 0.0 copy-start.2
  35.2 1.6 %collective-permute-start.13 = (bf16[16,8,2048]{2,1,0:T(8,128)(2,1)S(1)}, bf16[16,8,2048]{2,1,0:T(8,128)(2,1)S(1)}, u32[]{:S(2)}, u32[]{:S(2)}) collective-permute-start(bf16[16,8,2048]{2,1,0:T(8,128)(2,1)S(1)} %collective-permute-done.refs_0_), channel_id=1, source_target_pairs={{0,2},{1,3},{2,0},{3,1},{4,6},{5,7},{6,4},{7,5},{8,10},{9,11},{10,... | collective-permute-start | bytes 1572872 | tf_op jit(solution)/shard_map/ppermute | solution.py:13
  36.9 0.9 collective-permute-done.1.refs_0_
  37.8 0.0 copy-start.1
  37.8 0.0 collective-permute-start.14
  37.8 0.5 collective-permute-start.6
  38.2 2.6 %collective-permute-start.2 = (bf16[16,8,2048]{2,1,0:T(8,128)(2,1)S(1)}, bf16[16,8,2048]{2,1,0:T(8,128)(2,1)S(1)}, u32[]{:S(2)}, u32[]{:S(2)}) collective-permute-start(bf16[16,8,2048]{2,1,0:T(8,128)(2,1)S(1)} %get-tuple-element.5), channel_id=1, source_target_pairs={{0,8},{4,12},{8,0},{12,4},{1,9},{5,13},{9,1},{13,5},{2,10},{6,14},... | collective-permute-start | bytes 1572872 | tf_op jit(solution)/shard_map/ppermute | solution.py:13
  40.8 1.5 %collective-permute-start.10 = (bf16[16,8,2048]{2,1,0:T(8,128)(2,1)S(1)}, bf16[16,8,2048]{2,1,0:T(8,128)(2,1)}, u32[]{:S(2)}, u32[]{:S(2)}) collective-permute-start(bf16[16,8,2048]{2,1,0:T(8,128)(2,1)S(1)} %collective-permute-done.1.refs_0_), channel_id=1, source_target_pairs={{0,2},{1,3},{2,0},{3,1},{4,6},{5,7},{6,4},{7,5},{8,10},{9,11},{10,... | collective-permute-start | bytes 1572872 | tf_op jit(solution)/shard_map/ppermute | solution.py:13
  42.3 7.8 %collective-permute-done.13.refs_1_ = bf16[16,8,2048]{2,1,0:T(8,128)(2,1)S(1)} collective-permute-done((bf16[16,8,2048]{2,1,0:T(8,128)(2,1)S(1)}, bf16[16,8,2048]{2,1,0:T(8,128)(2,1)S(1)}, u32[]{:S(2)}, u32[]{:S(2)}) %collective-permute-start.13) | collective-permute-done | bytes 524320 | tf_op jit(solution)/shard_map/ppermute | solution.py:13
  50.1 0.0 copy-start.4
  50.1 0.0 collective-permute-start.11
  50.1 0.0 collective-permute-done.14.refs_2_
  50.1 0.0 copy-start.5
  50.1 0.5 collective-permute-start.15
  50.6 12.4 %collective-permute-done.6.refs_0_ = bf16[16,8,2048]{2,1,0:T(8,128)(2,1)S(1)} collective-permute-done((bf16[16,8,2048]{2,1,0:T(8,128)(2,1)S(1)}, bf16[16,8,2048]{2,1,0:T(8,128)(2,1)S(1)}, u32[]{:S(2)}, u32[]{:S(2)}) %collective-permute-start.6) | collective-permute-done | bytes 524320 | tf_op jit(solution)/shard_map/ppermute | solution.py:13
  63.1 0.0 copy-start.3
  63.1 1.5 %collective-permute-start.7 = (bf16[16,8,2048]{2,1,0:T(8,128)(2,1)S(1)}, bf16[16,8,2048]{2,1,0:T(8,128)(2,1)}, u32[]{:S(2)}, u32[]{:S(2)}) collective-permute-start(bf16[16,8,2048]{2,1,0:T(8,128)(2,1)S(1)} %collective-permute-done.6.refs_0_), channel_id=1, source_target_pairs={{0,2},{1,3},{2,0},{3,1},{4,6},{5,7},{6,4},{7,5},{8,10},{9,11},{10,... | collective-permute-start | bytes 1572872 | tf_op jit(solution)/shard_map/ppermute | solution.py:13
  64.6 0.0 collective-permute-done.2.refs_0_
  64.6 0.0 copy-start
  64.6 1.4 %collective-permute-start.3 = (bf16[16,8,2048]{2,1,0:T(8,128)(2,1)S(1)}, bf16[16,8,2048]{2,1,0:T(8,128)(2,1)}, u32[]{:S(2)}, u32[]{:S(2)}) collective-permute-start(bf16[16,8,2048]{2,1,0:T(8,128)(2,1)S(1)} %collective-permute-done.2.refs_0_), channel_id=1, source_target_pairs={{0,2},{1,3},{2,0},{3,1},{4,6},{5,7},{6,4},{7,5},{8,10},{9,11},{10,... | collective-permute-start | bytes 1572872 | tf_op jit(solution)/shard_map/ppermute | solution.py:13
  65.9 0.7 fusion.4
  66.7 0.1 copy.23
  66.8 0.1 squeeze.19
  66.9 0.0 collective-permute-done.10.refs_1_
  66.9 0.1 collective-permute-start.8
  66.9 0.0 collective-permute-done.11.refs_2_
  67.0 0.5 collective-permute-start.4
  67.4 0.0 collective-permute-done.15.refs_3_
  67.4 0.1 collective-permute-start.12
  67.5 10.5 %collective-permute-done.7.refs_1_ = bf16[16,8,2048]{2,1,0:T(8,128)(2,1)} collective-permute-done((bf16[16,8,2048]{2,1,0:T(8,128)(2,1)S(1)}, bf16[16,8,2048]{2,1,0:T(8,128)(2,1)}, u32[]{:S(2)}, u32[]{:S(2)}) %collective-permute-start.7) | collective-permute-done | bytes 524320 | tf_op jit(solution)/shard_map/ppermute | solution.py:13
  78.0 0.0 collective-permute-start.9
  78.0 10.0 %collective-permute-done.3.refs_1_ = bf16[16,8,2048]{2,1,0:T(8,128)(2,1)} collective-permute-done((bf16[16,8,2048]{2,1,0:T(8,128)(2,1)S(1)}, bf16[16,8,2048]{2,1,0:T(8,128)(2,1)}, u32[]{:S(2)}, u32[]{:S(2)}) %collective-permute-start.3) | collective-permute-done | bytes 524320 | tf_op jit(solution)/shard_map/ppermute | solution.py:13
  88.0 0.0 collective-permute-start.5
  88.0 0.6 fusion.3.pos_ref
  88.6 0.1 copy.22
  88.6 0.1 squeeze.18
  88.7 0.1 copy.20
  88.8 0.1 squeeze.16
  88.9 0.1 copy.21
  89.0 0.1 squeeze.17
  89.1 0.5 fusion.2.pos_ref
  89.6 0.5 fusion
  90.2 0.0 copy-done.2
  90.2 0.0 copy-done.4
  90.2 0.0 copy-done.5
  90.2 5.0 %shard_map.130.refs_5_ = f32[16,8,2048]{2,1,0:T(8,128)} custom-call(s32[64]{0:T(128)} %fusion.3.pos_ref, bf16[16,8,2048]{2,1,0:T(8,128)(2,1)} %copy-done.2, bf16[16,8,2048]{2,1,0:T(8,128)(2,1)} %copy-done.4, bf16[16,8,2048]{2,1,0:T(8,128)(2,1)} %copy-done.5, bf16[16,8,2048]{2,1,0:T(8,128)(2,1)} %collective-permute-done.15.refs_3_, ...), custom_call_target="tpu_custom_call" | custom-call | tf_op jit(solution)/shard_map/pallas_call | solution.py:116
  95.1 0.0 collective-permute-done.12.refs_3_
  95.1 0.0 copy-done.1
  95.1 5.2 %shard_map.131.refs_5_ = f32[16,8,2048]{2,1,0:T(8,128)} custom-call(s32[64]{0:T(128)} %fusion.2.pos_ref, bf16[16,8,2048]{2,1,0:T(8,128)(2,1)} %copy-done.1, bf16[16,8,2048]{2,1,0:T(8,128)(2,1)} %collective-permute-done.10.refs_1_, bf16[16,8,2048]{2,1,0:T(8,128)(2,1)} %collective-permute-done.11.refs_2_, ...), custom_call_target="tpu_custom_call", output_to_operand_aliasing={{}: (6, {})} | custom-call | tf_op jit(solution)/shard_map/pallas_call | solution.py:116
  100.3 0.0 copy-done.3
  100.4 0.0 copy-done
  100.4 0.0 collective-permute-done.8.refs_2_
  100.4 0.0 collective-permute-done.9.refs_3_
  100.4 5.2 %shard_map.132.refs_5_ = f32[16,8,2048]{2,1,0:T(8,128)} custom-call(s32[64]{0:T(128)} %get-tuple-element.20.pos_ref, bf16[16,8,2048]{2,1,0:T(8,128)(2,1)} %copy-done.3, bf16[16,8,2048]{2,1,0:T(8,128)(2,1)} %collective-permute-done.7.refs_1_, bf16[16,8,2048]{2,1,0:T(8,128)(2,1)} %collective-permute-done.8.refs_2_, ...), custom_call_target="tpu_custom_call", output_to_operand_aliasing={{}: (6, {})} | custom-call | tf_op jit(solution)/shard_map/pallas_call | solution.py:116
  105.6 0.0 collective-permute-done.4.refs_2_
  105.6 0.0 collective-permute-done.5.refs_3_
  105.6 5.8 %shard_map.133 = (bf16[16,8,2048]{2,1,0:T(8,128)(2,1)}, f32[8,2048]{1,0:T(8,128)}, f32[8,2048]{1,0:T(8,128)}) custom-call(s32[64]{0:T(128)} %get-tuple-element.19.pos_ref, bf16[16,8,2048]{2,1,0:T(8,128)(2,1)} %copy-done, bf16[16,8,2048]{2,1,0:T(8,128)(2,1)} %collective-permute-done.3.refs_1_, bf16[16,8,2048]{2,1,0:T(8,128)(2,1)} %collective-permute-done.4.refs_2_, ...), custom_call_target="tpu_custom_call" | custom-call | tf_op jit(solution)/shard_map/pallas_call | solution.py:116
Async XLA Ops:
  9.1 26.2 %collective-permute-start = (bf16[16,8,2048]{2,1,0:T(8,128)(2,1)S(1)}, bf16[16,8,2048]{2,1,0:T(8,128)(2,1)S(1)}, u32[]{:S(2)}, u32[]{:S(2)}) collective-permute-start(bf16[16,8,2048]{2,1,0:T(8,128)(2,1)S(1)} %get-tuple-element.10), channel_id=1, source_target_pairs={{0,4},{4,0},{8,12},{12,8},{1,5},{5,1},{9,13},{13,9},{2,6},{6,2},{1... | collective-permute-start | bytes 1572872 | tf_op jit(solution)/shard_map/ppermute | solution.py:13
  12.2 25.6 %collective-permute-start.1 = (bf16[16,8,2048]{2,1,0:T(8,128)(2,1)S(1)}, bf16[16,8,2048]{2,1,0:T(8,128)(2,1)S(1)}, u32[]{:S(2)}, u32[]{:S(2)}) collective-permute-start(bf16[16,8,2048]{2,1,0:T(8,128)(2,1)S(1)} %get-tuple-element.7), channel_id=1, source_target_pairs={{0,8},{4,12},{8,0},{12,4},{1,9},{5,13},{9,1},{13,5},{2,10},{6,14},... | collective-permute-start | bytes 1572872 | tf_op jit(solution)/shard_map/ppermute | solution.py:13
  35.2 54.9 %copy-start.2 = (bf16[16,8,2048]{2,1,0:T(8,128)(2,1)}, bf16[16,8,2048]{2,1,0:T(8,128)(2,1)S(1)}, u32[]{:S(2)}) copy-start(bf16[16,8,2048]{2,1,0:T(8,128)(2,1)S(1)} %collective-permute-done.refs_0_) | copy-start | bytes 1572868
  35.2 14.9 %collective-permute-start.13 = (bf16[16,8,2048]{2,1,0:T(8,128)(2,1)S(1)}, bf16[16,8,2048]{2,1,0:T(8,128)(2,1)S(1)}, u32[]{:S(2)}, u32[]{:S(2)}) collective-permute-start(bf16[16,8,2048]{2,1,0:T(8,128)(2,1)S(1)} %collective-permute-done.refs_0_), channel_id=1, source_target_pairs={{0,2},{1,3},{2,0},{3,1},{4,6},{5,7},{6,4},{7,5},{8,10},{9,11},{10,... | collective-permute-start | bytes 1572872 | tf_op jit(solution)/shard_map/ppermute | solution.py:13
  37.8 57.4 %copy-start.1 = (bf16[16,8,2048]{2,1,0:T(8,128)(2,1)}, bf16[16,8,2048]{2,1,0:T(8,128)(2,1)S(1)}, u32[]{:S(2)}) copy-start(bf16[16,8,2048]{2,1,0:T(8,128)(2,1)S(1)} %collective-permute-done.1.refs_0_) | copy-start | bytes 1572868
  37.8 12.4 %collective-permute-start.14 = (bf16[16,8,2048]{2,1,0:T(8,128)(2,1)S(1)}, bf16[16,8,2048]{2,1,0:T(8,128)(2,1)S(1)}, u32[]{:S(2)}, u32[]{:S(2)}) collective-permute-start(bf16[16,8,2048]{2,1,0:T(8,128)(2,1)S(1)} %collective-permute-done.refs_0_), channel_id=1, source_target_pairs={{0,1},{1,0},{2,3},{3,2},{4,5},{5,4},{6,7},{7,6},{8,9},{9,8},{10,11... | collective-permute-start | bytes 1572872 | tf_op jit(solution)/shard_map/ppermute | solution.py:13
  37.8 25.3 %collective-permute-start.6 = (bf16[16,8,2048]{2,1,0:T(8,128)(2,1)S(1)}, bf16[16,8,2048]{2,1,0:T(8,128)(2,1)S(1)}, u32[]{:S(2)}, u32[]{:S(2)}) collective-permute-start(bf16[16,8,2048]{2,1,0:T(8,128)(2,1)S(1)} %get-tuple-element.6), channel_id=1, source_target_pairs={{0,4},{4,0},{8,12},{12,8},{1,5},{5,1},{9,13},{13,9},{2,6},{6,2},{1... | collective-permute-start | bytes 1572872 | tf_op jit(solution)/shard_map/ppermute | solution.py:13
  38.2 26.3 %collective-permute-start.2 = (bf16[16,8,2048]{2,1,0:T(8,128)(2,1)S(1)}, bf16[16,8,2048]{2,1,0:T(8,128)(2,1)S(1)}, u32[]{:S(2)}, u32[]{:S(2)}) collective-permute-start(bf16[16,8,2048]{2,1,0:T(8,128)(2,1)S(1)} %get-tuple-element.5), channel_id=1, source_target_pairs={{0,8},{4,12},{8,0},{12,4},{1,9},{5,13},{9,1},{13,5},{2,10},{6,14},... | collective-permute-start | bytes 1572872 | tf_op jit(solution)/shard_map/ppermute | solution.py:13
  40.8 26.0 %collective-permute-start.10 = (bf16[16,8,2048]{2,1,0:T(8,128)(2,1)S(1)}, bf16[16,8,2048]{2,1,0:T(8,128)(2,1)}, u32[]{:S(2)}, u32[]{:S(2)}) collective-permute-start(bf16[16,8,2048]{2,1,0:T(8,128)(2,1)S(1)} %collective-permute-done.1.refs_0_), channel_id=1, source_target_pairs={{0,2},{1,3},{2,0},{3,1},{4,6},{5,7},{6,4},{7,5},{8,10},{9,11},{10,... | collective-permute-start | bytes 1572872 | tf_op jit(solution)/shard_map/ppermute | solution.py:13
  50.1 40.1 %copy-start.4 = (bf16[16,8,2048]{2,1,0:T(8,128)(2,1)}, bf16[16,8,2048]{2,1,0:T(8,128)(2,1)S(1)}, u32[]{:S(2)}) copy-start(bf16[16,8,2048]{2,1,0:T(8,128)(2,1)S(1)} %collective-permute-done.13.refs_1_) | copy-start | bytes 1572868
  50.1 16.8 %collective-permute-start.11 = (bf16[16,8,2048]{2,1,0:T(8,128)(2,1)S(1)}, bf16[16,8,2048]{2,1,0:T(8,128)(2,1)}, u32[]{:S(2)}, u32[]{:S(2)}) collective-permute-start(bf16[16,8,2048]{2,1,0:T(8,128)(2,1)S(1)} %collective-permute-done.1.refs_0_), channel_id=1, source_target_pairs={{0,1},{1,0},{2,3},{3,2},{4,5},{5,4},{6,7},{7,6},{8,9},{9,8},{10,11... | collective-permute-start | bytes 1572872 | tf_op jit(solution)/shard_map/ppermute | solution.py:13
  50.1 40.0 %copy-start.5 = (bf16[16,8,2048]{2,1,0:T(8,128)(2,1)}, bf16[16,8,2048]{2,1,0:T(8,128)(2,1)S(1)}, u32[]{:S(2)}) copy-start(bf16[16,8,2048]{2,1,0:T(8,128)(2,1)S(1)} %collective-permute-done.14.refs_2_) | copy-start | bytes 1572868
  50.1 17.3 %collective-permute-start.15 = (bf16[16,8,2048]{2,1,0:T(8,128)(2,1)S(1)}, bf16[16,8,2048]{2,1,0:T(8,128)(2,1)}, u32[]{:S(2)}, u32[]{:S(2)}) collective-permute-start(bf16[16,8,2048]{2,1,0:T(8,128)(2,1)S(1)} %collective-permute-done.13.refs_1_), channel_id=1, source_target_pairs={{0,1},{1,0},{2,3},{3,2},{4,5},{5,4},{6,7},{7,6},{8,9},{9,8},{10,11... | collective-permute-start | bytes 1572872 | tf_op jit(solution)/shard_map/ppermute | solution.py:13
  63.1 37.3 %copy-start.3 = (bf16[16,8,2048]{2,1,0:T(8,128)(2,1)}, bf16[16,8,2048]{2,1,0:T(8,128)(2,1)S(1)}, u32[]{:S(2)}) copy-start(bf16[16,8,2048]{2,1,0:T(8,128)(2,1)S(1)} %collective-permute-done.6.refs_0_) | copy-start | bytes 1572868
  63.1 14.9 %collective-permute-start.7 = (bf16[16,8,2048]{2,1,0:T(8,128)(2,1)S(1)}, bf16[16,8,2048]{2,1,0:T(8,128)(2,1)}, u32[]{:S(2)}, u32[]{:S(2)}) collective-permute-start(bf16[16,8,2048]{2,1,0:T(8,128)(2,1)S(1)} %collective-permute-done.6.refs_0_), channel_id=1, source_target_pairs={{0,2},{1,3},{2,0},{3,1},{4,6},{5,7},{6,4},{7,5},{8,10},{9,11},{10,... | collective-permute-start | bytes 1572872 | tf_op jit(solution)/shard_map/ppermute | solution.py:13
  64.6 35.8 %copy-start = (bf16[16,8,2048]{2,1,0:T(8,128)(2,1)}, bf16[16,8,2048]{2,1,0:T(8,128)(2,1)S(1)}, u32[]{:S(2)}) copy-start(bf16[16,8,2048]{2,1,0:T(8,128)(2,1)S(1)} %collective-permute-done.2.refs_0_) | copy-start | bytes 1572868
  64.6 23.4 %collective-permute-start.3 = (bf16[16,8,2048]{2,1,0:T(8,128)(2,1)S(1)}, bf16[16,8,2048]{2,1,0:T(8,128)(2,1)}, u32[]{:S(2)}, u32[]{:S(2)}) collective-permute-start(bf16[16,8,2048]{2,1,0:T(8,128)(2,1)S(1)} %collective-permute-done.2.refs_0_), channel_id=1, source_target_pairs={{0,2},{1,3},{2,0},{3,1},{4,6},{5,7},{6,4},{7,5},{8,10},{9,11},{10,... | collective-permute-start | bytes 1572872 | tf_op jit(solution)/shard_map/ppermute | solution.py:13
  66.9 33.5 %collective-permute-start.8 = (bf16[16,8,2048]{2,1,0:T(8,128)(2,1)S(1)}, bf16[16,8,2048]{2,1,0:T(8,128)(2,1)}, u32[]{:S(2)}, u32[]{:S(2)}) collective-permute-start(bf16[16,8,2048]{2,1,0:T(8,128)(2,1)S(1)} %collective-permute-done.6.refs_0_), channel_id=1, source_target_pairs={{0,1},{1,0},{2,3},{3,2},{4,5},{5,4},{6,7},{7,6},{8,9},{9,8},{10,11... | collective-permute-start | bytes 1572872 | tf_op jit(solution)/shard_map/ppermute | solution.py:13
  67.0 38.6 %collective-permute-start.4 = (bf16[16,8,2048]{2,1,0:T(8,128)(2,1)S(1)}, bf16[16,8,2048]{2,1,0:T(8,128)(2,1)}, u32[]{:S(2)}, u32[]{:S(2)}) collective-permute-start(bf16[16,8,2048]{2,1,0:T(8,128)(2,1)S(1)} %collective-permute-done.2.refs_0_), channel_id=1, source_target_pairs={{0,1},{1,0},{2,3},{3,2},{4,5},{5,4},{6,7},{7,6},{8,9},{9,8},{10,11... | collective-permute-start | bytes 1572872 | tf_op jit(solution)/shard_map/ppermute | solution.py:13
  67.4 27.7 %collective-permute-start.12 = (bf16[16,8,2048]{2,1,0:T(8,128)(2,1)}, bf16[16,8,2048]{2,1,0:T(8,128)(2,1)}, u32[]{:S(2)}, u32[]{:S(2)}) collective-permute-start(bf16[16,8,2048]{2,1,0:T(8,128)(2,1)} %collective-permute-done.10.refs_1_), channel_id=1, source_target_pairs={{0,1},{1,0},{2,3},{3,2},{4,5},{5,4},{6,7},{7,6},{8,9},{9,8},{10,11... | collective-permute-start | bytes 1572872 | tf_op jit(solution)/shard_map/ppermute | solution.py:13
  78.0 22.4 %collective-permute-start.9 = (bf16[16,8,2048]{2,1,0:T(8,128)(2,1)}, bf16[16,8,2048]{2,1,0:T(8,128)(2,1)}, u32[]{:S(2)}, u32[]{:S(2)}) collective-permute-start(bf16[16,8,2048]{2,1,0:T(8,128)(2,1)} %collective-permute-done.7.refs_1_), channel_id=1, source_target_pairs={{0,1},{1,0},{2,3},{3,2},{4,5},{5,4},{6,7},{7,6},{8,9},{9,8},{10,11... | collective-permute-start | bytes 1572872 | tf_op jit(solution)/shard_map/ppermute | solution.py:13
  88.0 17.6 %collective-permute-start.5 = (bf16[16,8,2048]{2,1,0:T(8,128)(2,1)}, bf16[16,8,2048]{2,1,0:T(8,128)(2,1)}, u32[]{:S(2)}, u32[]{:S(2)}) collective-permute-start(bf16[16,8,2048]{2,1,0:T(8,128)(2,1)} %collective-permute-done.3.refs_1_), channel_id=1, source_target_pairs={{0,1},{1,0},{2,3},{3,2},{4,5},{5,4},{6,7},{7,6},{8,9},{9,8},{10,11... | collective-permute-start | bytes 1572872 | tf_op jit(solution)/shard_map/ppermute | solution.py:13

commit v4 on v3

--- a/solution.py
+++ b/solution.py
@@ -30,10 +30,11 @@
     return pos
 
 
-def round_kernel(pos_ref, *refs, n_chunks, local_blocks, nnz, mode):
-    chunk_refs = refs[:n_chunks]
-    w_ref = refs[n_chunks]
-    rest = refs[n_chunks + 1:]
+def round_kernel(pos_ref, *refs, n_chunks, n_halves, local_blocks, nnz, mode):
+    n_in = n_chunks * n_halves
+    chunk_refs = refs[:n_in]
+    w_ref = refs[n_in]
+    rest = refs[n_in + 1:]
     if mode == "first":
         (out_ref, blocks) = rest
     elif mode == "middle":
@@ -44,9 +45,12 @@
     steps, batch, _ = chunk_refs[0].shape
     side = w_ref.shape[-1]
     rows = steps * batch
+    per_half = local_blocks // n_halves
     for c in range(n_chunks):
         for i in range(local_blocks):
-            x = chunk_refs[c][:, :, i * side:(i + 1) * side].astype(jnp.float32)
+            src = chunk_refs[c * n_halves + i // per_half]
+            off = (i % per_half) * side
+            x = src[:, :, off:off + side].astype(jnp.float32)
             blocks[c * local_blocks + i] = x.reshape(rows, side).astype(jnp.bfloat16)
     for j in range(local_blocks):
         cols = slice(j * side, (j + 1) * side)
@@ -77,51 +81,41 @@
         la_out[:, cols] = la_now
 
 
-def round_contrib(pos, chunks, weights, rnd, rec, scan_args=None):
-    steps, batch, local = chunks[0].shape
-    rounds, _, local_blocks, nnz, side, _ = weights.shape
-    n_chunks = len(chunks)
+def round_contrib(pos, chunks, n_halves, w_round, rec, scan_args=None):
+    steps, batch, _ = chunks[0].shape
+    local_blocks, nnz, side, _ = w_round.shape
+    local = local_blocks * side
+    n_chunks = len(chunks) // n_halves
     mode = "first" if rec is None else ("middle" if scan_args is None else "final")
-    full3 = pl.BlockSpec((steps, batch, local), lambda g, p: (0, 0, 0))
-    full2 = pl.BlockSpec((batch, local), lambda g, p: (0, 0))
-    row = pl.BlockSpec((1, local), lambda g, p: (0, 0))
-    w_spec = pl.BlockSpec(
-        (None, None, local_blocks, nnz, side, side), lambda g, p: (rnd, 0, 0, 0, 0, 0)
-    )
-    in_specs = [full3] * n_chunks + [w_spec]
-    operands = list(chunks) + [weights]
+    vmem = pl.BlockSpec(memory_space=pltpu.VMEM)
+    operands = list(chunks) + [w_round]
+    if mode != "first":
+        operands.append(rec)
     aliases = {}
-    if mode != "first":
-        in_specs.append(full3)
-        operands.append(rec)
     if mode == "middle":
-        aliases = {1 + n_chunks + 1: 0}
+        aliases = {len(operands): 0}
     if mode == "final":
         err_grad, surrogate, lv_end, la_end, alpha, rho, beta = scan_args
-        in_specs += [full3, full3, full2, full2, row, row, row]
         operands += [err_grad, surrogate, lv_end, la_end,
                      alpha.reshape(1, local), rho.reshape(1, local), beta.reshape(1, local)]
-        out_specs = (full3, full2, full2)
+        out_specs = (vmem, vmem, vmem)
         out_shape = (
             jax.ShapeDtypeStruct((steps, batch, local), jnp.bfloat16),
             jax.ShapeDtypeStruct((batch, local), jnp.float32),
             jax.ShapeDtypeStruct((batch, local), jnp.float32),
         )
     else:
-        out_specs = full3
+        out_specs = vmem
         out_shape = jax.ShapeDtypeStruct((steps, batch, local), jnp.float32)
     kernel = functools.partial(
-        round_kernel, n_chunks=n_chunks, local_blocks=local_blocks, nnz=nnz, mode=mode
+        round_kernel, n_chunks=n_chunks, n_halves=n_halves, local_blocks=local_blocks,
+        nnz=nnz, mode=mode,
     )
     return pl.pallas_call(
         kernel,
-        grid_spec=pltpu.PrefetchScalarGridSpec(
-            num_scalar_prefetch=1,
-            grid=(1,),
-            in_specs=in_specs,
-            out_specs=out_specs,
-            scratch_shapes=[pltpu.VMEM((n_chunks * local_blocks, steps * batch, side), jnp.bfloat16)],
-        ),
+        in_specs=[pl.BlockSpec(memory_space=pltpu.SMEM)] + [vmem] * len(operands),
+        out_specs=out_specs,
+        scratch_shapes=[pltpu.VMEM((n_chunks * local_blocks, steps * batch, side), jnp.bfloat16)],
         out_shape=out_shape,
         input_output_aliases=aliases,
     )(pos, *operands)
@@ -139,30 +133,38 @@
     nbits = lax.axis_size("neuron").bit_length() - 1
     me_area = lax.axis_index("area")
     me_neuron = lax.axis_index("neuron")
-    arrived = []
+    n_halves = 2 if local_blocks % 2 == 0 else 1
+    width = local_neurons // n_halves
+    arrived = {}
     gate = None
     for first in range(0, rounds, 2):
-        stage = list(range(first, min(first + 2, rounds)))
-        pieces = []
-        for rnd in stage:
-            mask = 1 << (rnd % levels)
-            start = delays[rnd, me_area ^ mask] - steps
-            pieces.append(lax.dynamic_slice_in_dim(window, start, steps, 0))
-        if gate is not None:
-            pieces, _ = lax.optimization_barrier((pieces, gate))
-        got = [swap(piece, "area", 1 << (rnd % levels)) for piece, rnd in zip(pieces, stage)]
-        arrived += got
-        gate = got
+        pair = list(range(first, min(first + 2, rounds)))
+        for h in range(n_halves):
+            pieces = []
+            for rnd in pair:
+                mask = 1 << (rnd % levels)
+                start = delays[rnd, me_area ^ mask] - steps
+                piece = lax.dynamic_slice_in_dim(window, start, steps, 0)
+                pieces.append(piece[:, :, h * width:(h + 1) * width])
+            if gate is not None:
+                pieces, _ = lax.optimization_barrier((pieces, gate))
+            got = [swap(piece, "area", 1 << (rnd % levels)) for piece, rnd in zip(pieces, pair)]
+            for rnd, g in zip(pair, got):
+                arrived[(rnd, h)] = g
+            gate = got
     rec = None
     for rnd in range(rounds):
-        chunks = gather_neuron(arrived[rnd])
+        halves = [gather_neuron(arrived[(rnd, h)]) for h in range(n_halves)]
+        chunks = [halves[h][c] for c in range(len(halves[0])) for h in range(n_halves)]
         idx = block_index[rnd, 0]
         owner = idx // local_blocks
         pos = relative_position(owner, me_neuron, nbits) * local_blocks + idx % local_blocks
         scan_args = None
         if rnd == rounds - 1:
             scan_args = (err_grad, surrogate, lv_end, la_end, alpha, rho, beta)
-        rec = round_contrib(pos.reshape(-1).astype(jnp.int32), chunks, weights, rnd, rec, scan_args)
+        rec = round_contrib(
+            pos.reshape(-1).astype(jnp.int32), chunks, n_halves, weights[rnd, 0], rec, scan_args
+        )
     return rec
 
 

time: 112 us -> 108 us (0.964)
  waiting for transfers between devices: 62 us -> 47.2 us
  local copies, waits for them, and re-layouts: 4.62 us -> 12.2 us
  starting transfers between devices: 15.9 us -> 22.5 us
  Pallas kernels: 21.2 us -> 18.4 us
    ppermute x16 -> x32, waiting for transfers between devices: 62 us -> 47.2 us  [swap(): return lax.ppermute(value, axis, pairs)]
    ppermute x16 -> x32, starting transfers between devices: 15.9 us -> 22.5 us  [swap(): return lax.ppermute(value, axis, pairs)]
    squeeze x0 -> x1, local copies, waits for them, and re-layouts: none -> 6.02 us  [per_device(): weights[rnd, 0]]
    pallas_call x4, Pallas kernels: 21.2 us -> 18.4 us  [round_contrib(): pl.pallas_call(kernel, in_specs=[pl.BlockSpec(memory_space=pltpu.SMEM)] +...]
    unnamed x12 -> x62, local copies, waits for them, and re-layouts: 0.02 us -> 2.03 us
    slice x0 -> x1, local copies, waits for them, and re-layouts: none -> 1.92 us  [per_device(): pieces.append(piece[:, :, h * width:(h + 1) * width])]
    dynamic_slice x1 -> x0, local copies, waits for them, and re-layouts: 1.69 us -> none  [per_device(): pieces.append(lax.dynamic_slice_in_dim(window, start, steps, 0))]
  transfers between devices with their start and end apart: 16 -> 32, of which waited for: 6 -> 13; matrix products, arithmetic and copies ran while one was open for 3% -> 8% of each run, Pallas kernels for 14% -> 12%
where the time goes in v4:
time: 108 us
  waiting for transfers between devices  47.2 us (44%)
  starting transfers between devices  22.5 us (21%)
  Pallas kernels  18.4 us (17%)
  local copies, waits for them, and re-layouts  12.2 us (11%)
  between operations  6.18 us (6%)
  other arithmetic  1.69 us (2%)
    ppermute x32, waiting for transfers between devices, swap(): return lax.ppermute(value, axis, pairs)  47.2 us
    ppermute x32, starting transfers between devices, swap(): return lax.ppermute(value, axis, pairs)  22.5 us
    pallas_call x4, Pallas kernels, round_contrib(): pl.pallas_call(kernel, in_specs=[pl.BlockSpec(memory_space=pltpu.SMEM)] +...  18.4 us
    squeeze x1, local copies, waits for them, and re-layouts, per_device(): weights[rnd, 0]  6.02 us
  transfers between devices with their start and end apart: 32, of which 13 were waited for; matrix products, arithmetic and copies ran while one was open for 8% of the time, Pallas kernels for 12%

profile of v4, /device:TPU:0, one launch (start us, length us, event | category | flops | bytes accessed | tf_op | source)
XLA Modules:
  0.0 108.2 jit_solution(6699857245254601222)
XLA Ops:
  0.6 1.5 %constant_dynamic-slice_fusion.11 = (s32[1,1]{1,0:T(1,128)}, s32[1,1]{1,0:T(1,128)}, s32[1,1]{1,0:T(1,128)}, s32[1,1]{1,0:T(1,128)}) fusion(s32[4,4]{1,0:T(4,128)} %param.21, s32[]{:T(128)S(6)} %select_n.73, s32[]{:T(128)S(6)} %select_n.71), kind=kLoop, calls=%fused_computation.39 | loop fusion | bytes 40 | tf_op jit(solution)/shard_map/dynamic_slice | solution.py:146
  7.3 1.9 %constant_dynamic-slice_fusion.7 = (bf16[16,8,1024]{2,1,0:T(8,128)(2,1)S(1)}, bf16[16,8,1024]{2,1,0:T(8,128)(2,1)S(1)}, bf16[16,8,1024]{2,1,0:T(8,128)(2,1)S(1)}...) fusion(bf16[32,8,2048]{2,1,0:T(8,128)(2,1)} %param.11, ...), kind=kLoop, calls=%fused_computation.11 | loop fusion | bytes 4194324 | tf_op jit(solution)/shard_map/slice | solution.py:148
  9.2 3.1 %collective-permute-start = (bf16[16,8,1024]{2,1,0:T(8,128)(2,1)S(1)}, bf16[16,8,1024]{2,1,0:T(8,128)(2,1)S(1)}, u32[]{:S(2)}, u32[]{:S(2)}) collective-permute-start(bf16[16,8,1024]{2,1,0:T(8,128)(2,1)S(1)} %get-tuple-element.26), channel_id=1, source_target_pairs={{0,4},{4,0},{8,12},{12,8},{1,5},{5,1},{9,13},{13,9},{2,6},{6,2},{1... | collective-permute-start | bytes 786440 | tf_op jit(solution)/shard_map/ppermute | solution.py:13
  12.3 2.6 %collective-permute-start.1 = (bf16[16,8,1024]{2,1,0:T(8,128)(2,1)S(1)}, bf16[16,8,1024]{2,1,0:T(8,128)(2,1)S(1)}, u32[]{:S(2)}, u32[]{:S(2)}) collective-permute-start(bf16[16,8,1024]{2,1,0:T(8,128)(2,1)S(1)} %get-tuple-element.25), channel_id=1, source_target_pairs={{0,8},{4,12},{8,0},{12,4},{1,9},{5,13},{9,1},{13,5},{2,10},{6,14},... | collective-permute-start | bytes 786440 | tf_op jit(solution)/shard_map/ppermute | solution.py:13
  14.9 9.3 %collective-permute-done.refs_0_ = bf16[16,8,1024]{2,1,0:T(8,128)(2,1)S(1)} collective-permute-done((bf16[16,8,1024]{2,1,0:T(8,128)(2,1)S(1)}, bf16[16,8,1024]{2,1,0:T(8,128)(2,1)S(1)}, u32[]{:S(2)}, u32[]{:S(2)}) %collective-permute-start) | collective-permute-done | bytes 262176 | tf_op jit(solution)/shard_map/ppermute | solution.py:13
  24.2 2.4 %collective-permute-done.1.refs_0_ = bf16[16,8,1024]{2,1,0:T(8,128)(2,1)S(1)} collective-permute-done((bf16[16,8,1024]{2,1,0:T(8,128)(2,1)S(1)}, bf16[16,8,1024]{2,1,0:T(8,128)(2,1)S(1)}, u32[]{:S(2)}, u32[]{:S(2)}) %collective-permute-start.1) | collective-permute-done | bytes 262176 | tf_op jit(solution)/shard_map/ppermute | solution.py:13
  26.6 0.5 collective-permute-start.2
  27.2 2.7 %collective-permute-start.3 = (bf16[16,8,1024]{2,1,0:T(8,128)(2,1)S(1)}, bf16[16,8,1024]{2,1,0:T(8,128)(2,1)S(1)}, u32[]{:S(2)}, u32[]{:S(2)}) collective-permute-start(bf16[16,8,1024]{2,1,0:T(8,128)(2,1)S(1)} %get-tuple-element.10), channel_id=1, source_target_pairs={{0,8},{4,12},{8,0},{12,4},{1,9},{5,13},{9,1},{13,5},{2,10},{6,14},... | collective-permute-start | bytes 786440 | tf_op jit(solution)/shard_map/ppermute | solution.py:13
  29.9 1.5 %collective-permute-start.26 = (bf16[16,8,1024]{2,1,0:T(8,128)(2,1)S(1)}, bf16[16,8,1024]{2,1,0:T(8,128)(2,1)S(1)}, u32[]{:S(2)}, u32[]{:S(2)}) collective-permute-start(bf16[16,8,1024]{2,1,0:T(8,128)(2,1)S(1)} %collective-permute-done.refs_0_), channel_id=1, source_target_pairs={{0,2},{1,3},{2,0},{3,1},{4,6},{5,7},{6,4},{7,5},{8,10},{9,11},{10,... | collective-permute-start | bytes 786440 | tf_op jit(solution)/shard_map/ppermute | solution.py:13
  31.4 0.0 collective-permute-start.28
  31.4 0.5 collective-permute-start.20
  31.9 4.9 %collective-permute-done.2.refs_1_ = bf16[16,8,1024]{2,1,0:T(8,128)(2,1)S(1)} collective-permute-done((bf16[16,8,1024]{2,1,0:T(8,128)(2,1)S(1)}, bf16[16,8,1024]{2,1,0:T(8,128)(2,1)S(1)}, u32[]{:S(2)}, u32[]{:S(2)}) %collective-permute-start.2) | collective-permute-done | bytes 262176 | tf_op jit(solution)/shard_map/ppermute | solution.py:13
  36.8 3.8 %collective-permute-done.3.refs_1_ = bf16[16,8,1024]{2,1,0:T(8,128)(2,1)S(1)} collective-permute-done((bf16[16,8,1024]{2,1,0:T(8,128)(2,1)S(1)}, bf16[16,8,1024]{2,1,0:T(8,128)(2,1)S(1)}, u32[]{:S(2)}, u32[]{:S(2)}) %collective-permute-start.3) | collective-permute-done | bytes 262176 | tf_op jit(solution)/shard_map/ppermute | solution.py:13
  40.6 1.5 %collective-permute-start.27 = (bf16[16,8,1024]{2,1,0:T(8,128)(2,1)S(1)}, bf16[16,8,1024]{2,1,0:T(8,128)(2,1)S(1)}, u32[]{:S(2)}, u32[]{:S(2)}) collective-permute-start(bf16[16,8,1024]{2,1,0:T(8,128)(2,1)S(1)} %collective-permute-done.2.refs_1_), channel_id=1, source_target_pairs={{0,2},{1,3},{2,0},{3,1},{4,6},{5,7},{6,4},{7,5},{8,10},{9,11},{10,... | collective-permute-start | bytes 786440 | tf_op jit(solution)/shard_map/ppermute | solution.py:13
  42.1 0.0 collective-permute-done.26.refs_2_
  42.1 0.0 collective-permute-done.28.refs_4_
  42.1 0.4 collective-permute-start.4
  42.5 0.4 copy-done.25
  42.9 0.8 collective-permute-done.20.refs_2_
  43.6 0.8 collective-permute-start.5
  44.4 3.0 %collective-permute-done.27.refs_3_ = bf16[16,8,1024]{2,1,0:T(8,128)(2,1)S(1)} collective-permute-done((bf16[16,8,1024]{2,1,0:T(8,128)(2,1)S(1)}, bf16[16,8,1024]{2,1,0:T(8,128)(2,1)S(1)}, u32[]{:S(2)}, u32[]{:S(2)}) %collective-permute-start.27) | collective-permute-done | bytes 262176 | tf_op jit(solution)/shard_map/ppermute | solution.py:13
  47.5 1.5 %collective-permute-start.21 = (bf16[16,8,1024]{2,1,0:T(8,128)(2,1)S(1)}, bf16[16,8,1024]{2,1,0:T(8,128)(2,1)S(1)}, u32[]{:S(2)}, u32[]{:S(2)}) collective-permute-start(bf16[16,8,1024]{2,1,0:T(8,128)(2,1)S(1)} %collective-permute-done.3.refs_1_), channel_id=1, source_target_pairs={{0,2},{1,3},{2,0},{3,1},{4,6},{5,7},{6,4},{7,5},{8,10},{9,11},{10,... | collective-permute-start | bytes 786440 | tf_op jit(solution)/shard_map/ppermute | solution.py:13
  49.0 7.4 %collective-permute-done.4.refs_0_ = bf16[16,8,1024]{2,1,0:T(8,128)(2,1)S(1)} collective-permute-done((bf16[16,8,1024]{2,1,0:T(8,128)(2,1)S(1)}, bf16[16,8,1024]{2,1,0:T(8,128)(2,1)S(1)}, u32[]{:S(2)}, u32[]{:S(2)}) %collective-permute-start.4) | collective-permute-done | bytes 262176 | tf_op jit(solution)/shard_map/ppermute | solution.py:13
  56.4 0.0 collective-permute-start.24
  56.4 0.7 collective-permute-done.5.refs_0_
  57.2 0.1 collective-permute-start.13
  57.3 0.0 collective-permute-done.21.refs_3_
  57.3 2.5 %collective-permute-start.6 = (bf16[16,8,1024]{2,1,0:T(8,128)(2,1)S(1)}, bf16[16,8,1024]{2,1,0:T(8,128)(2,1)S(1)}, u32[]{:S(2)}, u32[]{:S(2)}) collective-permute-start(bf16[16,8,1024]{2,1,0:T(8,128)(2,1)S(1)} %get-tuple-element.13), channel_id=1, source_target_pairs={{0,8},{4,12},{8,0},{12,4},{1,9},{5,13},{9,1},{13,5},{2,10},{6,14},... | collective-permute-start | bytes 786440 | tf_op jit(solution)/shard_map/ppermute | solution.py:13
  59.8 0.5 collective-permute-start.14
  60.3 0.0 collective-permute-done.24.refs_6_
  60.3 0.0 collective-permute-start.16
  60.4 0.7 copy-done.29
  61.1 0.4 collective-permute-start.25
  61.6 6.0 %slice_bitcast_fusion = (bf16[16,4,128,128]{3,2,1,0:T(8,128)(2,1)}, bf16[16,4,128,128]{3,2,1,0:T(8,128)(2,1)}, bf16[16,4,128,128]{3,2,1,0:T(8,128)(2,1)}, bf16[16,4,128,128]{3,2,1,0:T(8,128)(2,1)}) fusion(bf16[4,1,16,4,128,128]{5,4,3,2,1,0:T(8,128)(2,1)} %param.19), kind=kLoop, calls=%fused_computation | loop fusion | bytes 16777216 | tf_op jit(solution)/shard_map/squeeze | solution.py:166
  67.7 0.0 collective-permute-done.25.refs_7_
  67.7 1.6 %collective-permute-start.7 = (bf16[16,8,1024]{2,1,0:T(8,128)(2,1)S(1)}, bf16[16,8,1024]{2,1,0:T(8,128)(2,1)S(1)}, u32[]{:S(2)}, u32[]{:S(2)}) collective-permute-start(bf16[16,8,1024]{2,1,0:T(8,128)(2,1)S(1)} %collective-permute-done.4.refs_0_), channel_id=1, source_target_pairs={{0,2},{1,3},{2,0},{3,1},{4,6},{5,7},{6,4},{7,5},{8,10},{9,11},{10,... | collective-permute-start | bytes 786440 | tf_op jit(solution)/shard_map/ppermute | solution.py:13
  69.3 1.3 %collective-permute-done.13.refs_1_ = bf16[16,8,1024]{2,1,0:T(8,128)(2,1)S(1)} collective-permute-done((bf16[16,8,1024]{2,1,0:T(8,128)(2,1)S(1)}, bf16[16,8,1024]{2,1,0:T(8,128)(2,1)S(1)}, u32[]{:S(2)}, u32[]{:S(2)}) %collective-permute-start.13) | collective-permute-done | bytes 262176 | tf_op jit(solution)/shard_map/ppermute | solution.py:13
  70.6 0.5 collective-permute-start.15
  71.1 0.5 collective-permute-start.18
  71.6 0.9 collective-permute-done.6.refs_1_
  72.6 0.6 collective-permute-start.8
  73.2 0.1 copy.23
  73.3 0.1 squeeze.38
  73.4 0.1 copy.22
  73.5 0.1 squeeze.36
  73.5 0.5 fusion.3.pos_ref
  74.1 2.8 %collective-permute-done.7.refs_2_ = bf16[16,8,1024]{2,1,0:T(8,128)(2,1)S(1)} collective-permute-done((bf16[16,8,1024]{2,1,0:T(8,128)(2,1)S(1)}, bf16[16,8,1024]{2,1,0:T(8,128)(2,1)S(1)}, u32[]{:S(2)}, u32[]{:S(2)}) %collective-permute-start.7) | collective-permute-done | bytes 262176 | tf_op jit(solution)/shard_map/ppermute | solution.py:13
  76.9 5.6 %collective-permute-done.15.refs_3_ = bf16[16,8,1024]{2,1,0:T(8,128)(2,1)S(1)} collective-permute-done((bf16[16,8,1024]{2,1,0:T(8,128)(2,1)S(1)}, bf16[16,8,1024]{2,1,0:T(8,128)(2,1)S(1)}, u32[]{:S(2)}, u32[]{:S(2)}) %collective-permute-start.15) | collective-permute-done | bytes 262176 | tf_op jit(solution)/shard_map/ppermute | solution.py:13
  82.6 0.5 collective-permute-start.11
  83.1 0.1 collective-permute-start.19
  83.1 4.1 %collective-permute-done.8.refs_3_ = bf16[16,8,1024]{2,1,0:T(8,128)(2,1)S(1)} collective-permute-done((bf16[16,8,1024]{2,1,0:T(8,128)(2,1)S(1)}, bf16[16,8,1024]{2,1,0:T(8,128)(2,1)S(1)}, u32[]{:S(2)}, u32[]{:S(2)}) %collective-permute-start.8) | collective-permute-done | bytes 262176 | tf_op jit(solution)/shard_map/ppermute | solution.py:13
  87.3 0.6 fusion.2.pos_ref
  87.9 0.1 copy.20
  87.9 0.1 squeeze.32
  88.0 0.1 copy.21
  88.1 0.1 squeeze.34
  88.2 0.6 fusion
  88.8 4.3 %shard_map.130.refs_9_ = f32[16,8,2048]{2,1,0:T(8,128)} custom-call(s32[64]{0:T(128)} %fusion.3.pos_ref, bf16[16,8,1024]{2,1,0:T(8,128)(2,1)} %copy-done.22, bf16[16,8,1024]{2,1,0:T(8,128)(2,1)} %copy-done.23, bf16[16,8,1024]{2,1,0:T(8,128)(2,1)} %copy-done.24, bf16[16,8,1024]{2,1,0:T(8,128)(2,1)} %copy-done.26, bf16[16,8,1024]{2,1,0:T(8,128)(2,1)} %copy-done.25, ...), custom_call_target="tpu_custom_call" | custom-call | tf_op jit(solution)/shard_map/pallas_call | solution.py:114
  93.1 4.5 %shard_map.131.refs_9_ = f32[16,8,2048]{2,1,0:T(8,128)} custom-call(s32[64]{0:T(128)} %fusion.2.pos_ref, bf16[16,8,1024]{2,1,0:T(8,128)(2,1)} %copy-done, bf16[16,8,1024]{2,1,0:T(8,128)(2,1)} %copy-done.2, bf16[16,8,1024]{2,1,0:T(8,128)(2,1)} %copy-done.3, bf16[16,8,1024]{2,1,0:T(8,128)(2,1)} %copy-done.7, ...), custom_call_target="tpu_custom_call", output_to_operand_aliasing={{}: (10, {})} | custom-call | tf_op jit(solution)/shard_map/pallas_call | solution.py:114
  97.7 4.5 %shard_map.132.refs_9_ = f32[16,8,2048]{2,1,0:T(8,128)} custom-call(s32[64]{0:T(128)} %get-tuple-element.36.pos_ref, bf16[16,8,1024]{2,1,0:T(8,128)(2,1)} %copy-done.5, bf16[16,8,1024]{2,1,0:T(8,128)(2,1)} %copy-done.10, bf16[16,8,1024]{2,1,0:T(8,128)(2,1)} %copy-done.12, bf16[16,8,1024]{2,1,0:T(8,128)(2,1)} %copy-done.16, ...), custom_call_target="tpu_custom_call", output_to_operand_aliasing={{}: (10, {})} | custom-call | tf_op jit(solution)/shard_map/pallas_call | solution.py:114
  102.2 0.6 copy-done.19
  102.9 0.1 copy-done.20
  103.0 0.1 copy-done.21
  103.1 5.1 %shard_map.133 = (bf16[16,8,2048]{2,1,0:T(8,128)(2,1)}, f32[8,2048]{1,0:T(8,128)}, f32[8,2048]{1,0:T(8,128)}) custom-call(s32[64]{0:T(128)} %get-tuple-element.35.pos_ref, bf16[16,8,1024]{2,1,0:T(8,128)(2,1)} %copy-done.1, bf16[16,8,1024]{2,1,0:T(8,128)(2,1)} %copy-done.6, bf16[16,8,1024]{2,1,0:T(8,128)(2,1)} %copy-done.11, bf16[16,8,1024]{2,1,0:T(8,128)(2,1)} %copy-done.15, ...), custom_call_target="tpu_custom_call" | custom-call | tf_op jit(solution)/shard_map/pallas_call | solution.py:114
  (81 shorter events, 0.2 us)
Async XLA Ops:
  9.2 15.0 %collective-permute-start = (bf16[16,8,1024]{2,1,0:T(8,128)(2,1)S(1)}, bf16[16,8,1024]{2,1,0:T(8,128)(2,1)S(1)}, u32[]{:S(2)}, u32[]{:S(2)}) collective-permute-start(bf16[16,8,1024]{2,1,0:T(8,128)(2,1)S(1)} %get-tuple-element.26), channel_id=1, source_target_pairs={{0,4},{4,0},{8,12},{12,8},{1,5},{5,1},{9,13},{13,9},{2,6},{6,2},{1... | collective-permute-start | bytes 786440 | tf_op jit(solution)/shard_map/ppermute | solution.py:13
  12.3 14.3 %collective-permute-start.1 = (bf16[16,8,1024]{2,1,0:T(8,128)(2,1)S(1)}, bf16[16,8,1024]{2,1,0:T(8,128)(2,1)S(1)}, u32[]{:S(2)}, u32[]{:S(2)}) collective-permute-start(bf16[16,8,1024]{2,1,0:T(8,128)(2,1)S(1)} %get-tuple-element.25), channel_id=1, source_target_pairs={{0,8},{4,12},{8,0},{12,4},{1,9},{5,13},{9,1},{13,5},{2,10},{6,14},... | collective-permute-start | bytes 786440 | tf_op jit(solution)/shard_map/ppermute | solution.py:13
  24.2 36.1 %copy-start.22 = (bf16[16,8,1024]{2,1,0:T(8,128)(2,1)}, bf16[16,8,1024]{2,1,0:T(8,128)(2,1)S(1)}, u32[]{:S(2)}) copy-start(bf16[16,8,1024]{2,1,0:T(8,128)(2,1)S(1)} %collective-permute-done.refs_0_) | copy-start | bytes 786436
  26.6 41.0 %copy-start = (bf16[16,8,1024]{2,1,0:T(8,128)(2,1)}, bf16[16,8,1024]{2,1,0:T(8,128)(2,1)S(1)}, u32[]{:S(2)}) copy-start(bf16[16,8,1024]{2,1,0:T(8,128)(2,1)S(1)} %collective-permute-done.1.refs_0_) | copy-start | bytes 786436
  26.6 10.1 %collective-permute-start.2 = (bf16[16,8,1024]{2,1,0:T(8,128)(2,1)S(1)}, bf16[16,8,1024]{2,1,0:T(8,128)(2,1)S(1)}, u32[]{:S(2)}, u32[]{:S(2)}) collective-permute-start(bf16[16,8,1024]{2,1,0:T(8,128)(2,1)S(1)} %get-tuple-element.9), channel_id=1, source_target_pairs={{0,4},{4,0},{8,12},{12,8},{1,5},{5,1},{9,13},{13,9},{2,6},{6,2},{1... | collective-permute-start | bytes 786440 | tf_op jit(solution)/shard_map/ppermute | solution.py:13
  27.2 13.4 %collective-permute-start.3 = (bf16[16,8,1024]{2,1,0:T(8,128)(2,1)S(1)}, bf16[16,8,1024]{2,1,0:T(8,128)(2,1)S(1)}, u32[]{:S(2)}, u32[]{:S(2)}) collective-permute-start(bf16[16,8,1024]{2,1,0:T(8,128)(2,1)S(1)} %get-tuple-element.10), channel_id=1, source_target_pairs={{0,8},{4,12},{8,0},{12,4},{1,9},{5,13},{9,1},{13,5},{2,10},{6,14},... | collective-permute-start | bytes 786440 | tf_op jit(solution)/shard_map/ppermute | solution.py:13
  29.9 12.2 %collective-permute-start.26 = (bf16[16,8,1024]{2,1,0:T(8,128)(2,1)S(1)}, bf16[16,8,1024]{2,1,0:T(8,128)(2,1)S(1)}, u32[]{:S(2)}, u32[]{:S(2)}) collective-permute-start(bf16[16,8,1024]{2,1,0:T(8,128)(2,1)S(1)} %collective-permute-done.refs_0_), channel_id=1, source_target_pairs={{0,2},{1,3},{2,0},{3,1},{4,6},{5,7},{6,4},{7,5},{8,10},{9,11},{10,... | collective-permute-start | bytes 786440 | tf_op jit(solution)/shard_map/ppermute | solution.py:13
  31.4 10.7 %collective-permute-start.28 = (bf16[16,8,1024]{2,1,0:T(8,128)(2,1)S(1)}, bf16[16,8,1024]{2,1,0:T(8,128)(2,1)S(1)}, u32[]{:S(2)}, u32[]{:S(2)}) collective-permute-start(bf16[16,8,1024]{2,1,0:T(8,128)(2,1)S(1)} %collective-permute-done.refs_0_), channel_id=1, source_target_pairs={{0,1},{1,0},{2,3},{3,2},{4,5},{5,4},{6,7},{7,6},{8,9},{9,8},{10,11... | collective-permute-start | bytes 786440 | tf_op jit(solution)/shard_map/ppermute | solution.py:13
  31.4 12.3 %collective-permute-start.20 = (bf16[16,8,1024]{2,1,0:T(8,128)(2,1)S(1)}, bf16[16,8,1024]{2,1,0:T(8,128)(2,1)S(1)}, u32[]{:S(2)}, u32[]{:S(2)}) collective-permute-start(bf16[16,8,1024]{2,1,0:T(8,128)(2,1)S(1)} %collective-permute-done.1.refs_0_), channel_id=1, source_target_pairs={{0,2},{1,3},{2,0},{3,1},{4,6},{5,7},{6,4},{7,5},{8,10},{9,11},{10,... | collective-permute-start | bytes 786440 | tf_op jit(solution)/shard_map/ppermute | solution.py:13
  36.7 23.6 %copy-start.23 = (bf16[16,8,1024]{2,1,0:T(8,128)(2,1)}, bf16[16,8,1024]{2,1,0:T(8,128)(2,1)S(1)}, u32[]{:S(2)}) copy-start(bf16[16,8,1024]{2,1,0:T(8,128)(2,1)S(1)} %collective-permute-done.2.refs_1_) | copy-start | bytes 786436
  36.7 7.7 %collective-permute-start.22 = (bf16[16,8,1024]{2,1,0:T(8,128)(2,1)S(1)}, bf16[16,8,1024]{2,1,0:T(8,128)(2,1)S(1)}, u32[]{:S(2)}, u32[]{:S(2)}) collective-permute-start(bf16[16,8,1024]{2,1,0:T(8,128)(2,1)S(1)} %collective-permute-done.1.refs_0_), channel_id=1, source_target_pairs={{0,1},{1,0},{2,3},{3,2},{4,5},{5,4},{6,7},{7,6},{8,9},{9,8},{10,11... | collective-permute-start | bytes 786440 | tf_op jit(solution)/shard_map/ppermute | solution.py:13
  40.6 27.0 %copy-start.2 = (bf16[16,8,1024]{2,1,0:T(8,128)(2,1)}, bf16[16,8,1024]{2,1,0:T(8,128)(2,1)S(1)}, u32[]{:S(2)}) copy-start(bf16[16,8,1024]{2,1,0:T(8,128)(2,1)S(1)} %collective-permute-done.3.refs_1_) | copy-start | bytes 786436
  40.6 6.9 %collective-permute-start.27 = (bf16[16,8,1024]{2,1,0:T(8,128)(2,1)S(1)}, bf16[16,8,1024]{2,1,0:T(8,128)(2,1)S(1)}, u32[]{:S(2)}, u32[]{:S(2)}) collective-permute-start(bf16[16,8,1024]{2,1,0:T(8,128)(2,1)S(1)} %collective-permute-done.2.refs_1_), channel_id=1, source_target_pairs={{0,2},{1,3},{2,0},{3,1},{4,6},{5,7},{6,4},{7,5},{8,10},{9,11},{10,... | collective-permute-start | bytes 786440 | tf_op jit(solution)/shard_map/ppermute | solution.py:13
  42.1 18.3 %copy-start.24 = (bf16[16,8,1024]{2,1,0:T(8,128)(2,1)}, bf16[16,8,1024]{2,1,0:T(8,128)(2,1)S(1)}, u32[]{:S(2)}) copy-start(bf16[16,8,1024]{2,1,0:T(8,128)(2,1)S(1)} %collective-permute-done.26.refs_2_) | copy-start | bytes 786436
  42.1 6.9 %collective-permute-start.29 = (bf16[16,8,1024]{2,1,0:T(8,128)(2,1)S(1)}, bf16[16,8,1024]{2,1,0:T(8,128)(2,1)S(1)}, u32[]{:S(2)}, u32[]{:S(2)}) collective-permute-start(bf16[16,8,1024]{2,1,0:T(8,128)(2,1)S(1)} %collective-permute-done.2.refs_1_), channel_id=1, source_target_pairs={{0,1},{1,0},{2,3},{3,2},{4,5},{5,4},{6,7},{7,6},{8,9},{9,8},{10,11... | collective-permute-start | bytes 786440 | tf_op jit(solution)/shard_map/ppermute | solution.py:13
  42.1 0.8 copy-start.25
  42.1 14.3 %collective-permute-start.4 = (bf16[16,8,1024]{2,1,0:T(8,128)(2,1)S(1)}, bf16[16,8,1024]{2,1,0:T(8,128)(2,1)S(1)}, u32[]{:S(2)}, u32[]{:S(2)}) collective-permute-start(bf16[16,8,1024]{2,1,0:T(8,128)(2,1)S(1)} %get-tuple-element.11), channel_id=1, source_target_pairs={{0,8},{4,12},{8,0},{12,4},{1,9},{5,13},{9,1},{13,5},{2,10},{6,14},... | collective-permute-start | bytes 786440 | tf_op jit(solution)/shard_map/ppermute | solution.py:13
  43.6 24.0 %copy-start.3 = (bf16[16,8,1024]{2,1,0:T(8,128)(2,1)}, bf16[16,8,1024]{2,1,0:T(8,128)(2,1)S(1)}, u32[]{:S(2)}) copy-start(bf16[16,8,1024]{2,1,0:T(8,128)(2,1)S(1)} %collective-permute-done.20.refs_2_) | copy-start | bytes 786436
  43.6 13.5 %collective-permute-start.5 = (bf16[16,8,1024]{2,1,0:T(8,128)(2,1)S(1)}, bf16[16,8,1024]{2,1,0:T(8,128)(2,1)S(1)}, u32[]{:S(2)}, u32[]{:S(2)}) collective-permute-start(bf16[16,8,1024]{2,1,0:T(8,128)(2,1)S(1)} %get-tuple-element.12), channel_id=1, source_target_pairs={{0,4},{4,0},{8,12},{12,8},{1,5},{5,1},{9,13},{13,9},{2,6},{6,2},{1... | collective-permute-start | bytes 786440 | tf_op jit(solution)/shard_map/ppermute | solution.py:13
  44.4 23.2 %copy-start.4 = (bf16[16,8,1024]{2,1,0:T(8,128)(2,1)}, bf16[16,8,1024]{2,1,0:T(8,128)(2,1)S(1)}, u32[]{:S(2)}) copy-start(bf16[16,8,1024]{2,1,0:T(8,128)(2,1)S(1)} %collective-permute-done.22.refs_4_) | copy-start | bytes 786436
  44.4 12.7 %collective-permute-start.30 = (bf16[16,8,1024]{2,1,0:T(8,128)(2,1)S(1)}, bf16[16,8,1024]{2,1,0:T(8,128)(2,1)S(1)}, u32[]{:S(2)}, u32[]{:S(2)}) collective-permute-start(bf16[16,8,1024]{2,1,0:T(8,128)(2,1)S(1)} %collective-permute-done.26.refs_2_), channel_id=1, source_target_pairs={{0,1},{1,0},{2,3},{3,2},{4,5},{5,4},{6,7},{7,6},{8,9},{9,8},{10,11... | collective-permute-start | bytes 786440 | tf_op jit(solution)/shard_map/ppermute | solution.py:13
  47.5 12.9 %copy-start.26 = (bf16[16,8,1024]{2,1,0:T(8,128)(2,1)}, bf16[16,8,1024]{2,1,0:T(8,128)(2,1)S(1)}, u32[]{:S(2)}) copy-start(bf16[16,8,1024]{2,1,0:T(8,128)(2,1)S(1)} %collective-permute-done.27.refs_3_) | copy-start | bytes 786436
  47.5 9.8 %collective-permute-start.21 = (bf16[16,8,1024]{2,1,0:T(8,128)(2,1)S(1)}, bf16[16,8,1024]{2,1,0:T(8,128)(2,1)S(1)}, u32[]{:S(2)}, u32[]{:S(2)}) collective-permute-start(bf16[16,8,1024]{2,1,0:T(8,128)(2,1)S(1)} %collective-permute-done.3.refs_1_), channel_id=1, source_target_pairs={{0,2},{1,3},{2,0},{3,1},{4,6},{5,7},{6,4},{7,5},{8,10},{9,11},{10,... | collective-permute-start | bytes 786440 | tf_op jit(solution)/shard_map/ppermute | solution.py:13
  49.0 11.4 %copy-start.27 = (bf16[16,8,1024]{2,1,0:T(8,128)(2,1)}, bf16[16,8,1024]{2,1,0:T(8,128)(2,1)S(1)}, u32[]{:S(2)}) copy-start(bf16[16,8,1024]{2,1,0:T(8,128)(2,1)S(1)} %collective-permute-done.29.refs_5_) | copy-start | bytes 786436
  49.0 10.8 %collective-permute-start.23 = (bf16[16,8,1024]{2,1,0:T(8,128)(2,1)S(1)}, bf16[16,8,1024]{2,1,0:T(8,128)(2,1)S(1)}, u32[]{:S(2)}, u32[]{:S(2)}) collective-permute-start(bf16[16,8,1024]{2,1,0:T(8,128)(2,1)S(1)} %collective-permute-done.3.refs_1_), channel_id=1, source_target_pairs={{0,1},{1,0},{2,3},{3,2},{4,5},{5,4},{6,7},{7,6},{8,9},{9,8},{10,11... | collective-permute-start | bytes 786440 | tf_op jit(solution)/shard_map/ppermute | solution.py:13
  56.4 20.5 %copy-start.1 = (bf16[16,8,1024]{2,1,0:T(8,128)(2,1)}, bf16[16,8,1024]{2,1,0:T(8,128)(2,1)S(1)}, u32[]{:S(2)}) copy-start(bf16[16,8,1024]{2,1,0:T(8,128)(2,1)S(1)} %collective-permute-done.4.refs_0_) | copy-start | bytes 786436
  56.4 3.9 %collective-permute-start.24 = (bf16[16,8,1024]{2,1,0:T(8,128)(2,1)S(1)}, bf16[16,8,1024]{2,1,0:T(8,128)(2,1)S(1)}, u32[]{:S(2)}, u32[]{:S(2)}) collective-permute-start(bf16[16,8,1024]{2,1,0:T(8,128)(2,1)S(1)} %collective-permute-done.20.refs_2_), channel_id=1, source_target_pairs={{0,1},{1,0},{2,3},{3,2},{4,5},{5,4},{6,7},{7,6},{8,9},{9,8},{10,11... | collective-permute-start | bytes 786440 | tf_op jit(solution)/shard_map/ppermute | solution.py:13
  57.2 10.5 %copy-start.5 = (bf16[16,8,1024]{2,1,0:T(8,128)(2,1)}, bf16[16,8,1024]{2,1,0:T(8,128)(2,1)S(1)}, u32[]{:S(2)}) copy-start(bf16[16,8,1024]{2,1,0:T(8,128)(2,1)S(1)} %collective-permute-done.5.refs_0_) | copy-start | bytes 786436
  57.2 3.2 %collective-permute-start.31 = (bf16[16,8,1024]{2,1,0:T(8,128)(2,1)S(1)}, bf16[16,8,1024]{2,1,0:T(8,128)(2,1)S(1)}, u32[]{:S(2)}, u32[]{:S(2)}) collective-permute-start(bf16[16,8,1024]{2,1,0:T(8,128)(2,1)S(1)} %collective-permute-done.27.refs_3_), channel_id=1, source_target_pairs={{0,1},{1,0},{2,3},{3,2},{4,5},{5,4},{6,7},{7,6},{8,9},{9,8},{10,11... | collective-permute-start | bytes 786440 | tf_op jit(solution)/shard_map/ppermute | solution.py:13
  57.2 16.0 %copy-start.30 = (s32[4,1,16,4]{2,3,1,0:T(4,128)S(1)}, s32[4,1,16,4]{2,3,1,0:T(4,128)}, u32[]{:S(2)}) copy-start(s32[4,1,16,4]{2,3,1,0:T(4,128)} %param.20) | copy-start | bytes 3076
  57.2 3.2 %copy-start.28 = (bf16[16,8,1024]{2,1,0:T(8,128)(2,1)}, bf16[16,8,1024]{2,1,0:T(8,128)(2,1)S(1)}, u32[]{:S(2)}) copy-start(bf16[16,8,1024]{2,1,0:T(8,128)(2,1)S(1)} %collective-permute-done.30.refs_6_) | copy-start | bytes 786436
  57.2 13.4 %collective-permute-start.13 = (bf16[16,8,1024]{2,1,0:T(8,128)(2,1)S(1)}, bf16[16,8,1024]{2,1,0:T(8,128)(2,1)S(1)}, u32[]{:S(2)}, u32[]{:S(2)}) collective-permute-start(bf16[16,8,1024]{2,1,0:T(8,128)(2,1)S(1)} %get-tuple-element.14), channel_id=1, source_target_pairs={{0,4},{4,0},{8,12},{12,8},{1,5},{5,1},{9,13},{13,9},{2,6},{6,2},{1... | collective-permute-start | bytes 786440 | tf_op jit(solution)/shard_map/ppermute | solution.py:13
  57.3 10.4 %copy-start.7 = (bf16[16,8,1024]{2,1,0:T(8,128)(2,1)}, bf16[16,8,1024]{2,1,0:T(8,128)(2,1)S(1)}, u32[]{:S(2)}) copy-start(bf16[16,8,1024]{2,1,0:T(8,128)(2,1)S(1)} %collective-permute-done.21.refs_3_) | copy-start | bytes 786436
  57.3 15.3 %collective-permute-start.6 = (bf16[16,8,1024]{2,1,0:T(8,128)(2,1)S(1)}, bf16[16,8,1024]{2,1,0:T(8,128)(2,1)S(1)}, u32[]{:S(2)}, u32[]{:S(2)}) collective-permute-start(bf16[16,8,1024]{2,1,0:T(8,128)(2,1)S(1)} %get-tuple-element.13), channel_id=1, source_target_pairs={{0,8},{4,12},{8,0},{12,4},{1,9},{5,13},{9,1},{13,5},{2,10},{6,14},... | collective-permute-start | bytes 786440 | tf_op jit(solution)/shard_map/ppermute | solution.py:13
  59.8 7.9 %copy-start.8 = (bf16[16,8,1024]{2,1,0:T(8,128)(2,1)}, bf16[16,8,1024]{2,1,0:T(8,128)(2,1)S(1)}, u32[]{:S(2)}) copy-start(bf16[16,8,1024]{2,1,0:T(8,128)(2,1)S(1)} %collective-permute-done.23.refs_5_) | copy-start | bytes 786436
  59.8 11.3 %collective-permute-start.14 = (bf16[16,8,1024]{2,1,0:T(8,128)(2,1)S(1)}, bf16[16,8,1024]{2,1,0:T(8,128)(2,1)S(1)}, u32[]{:S(2)}, u32[]{:S(2)}) collective-permute-start(bf16[16,8,1024]{2,1,0:T(8,128)(2,1)S(1)} %collective-permute-done.5.refs_0_), channel_id=1, source_target_pairs={{0,2},{1,3},{2,0},{3,1},{4,6},{5,7},{6,4},{7,5},{8,10},{9,11},{10,... | collective-permute-start | bytes 786440 | tf_op jit(solution)/shard_map/ppermute | solution.py:13
  60.3 7.3 %copy-start.9 = (bf16[16,8,1024]{2,1,0:T(8,128)(2,1)}, bf16[16,8,1024]{2,1,0:T(8,128)(2,1)S(1)}, u32[]{:S(2)}) copy-start(bf16[16,8,1024]{2,1,0:T(8,128)(2,1)S(1)} %collective-permute-done.24.refs_6_) | copy-start | bytes 786436
  60.3 10.8 %collective-permute-start.16 = (bf16[16,8,1024]{2,1,0:T(8,128)(2,1)S(1)}, bf16[16,8,1024]{2,1,0:T(8,128)(2,1)S(1)}, u32[]{:S(2)}, u32[]{:S(2)}) collective-permute-start(bf16[16,8,1024]{2,1,0:T(8,128)(2,1)S(1)} %collective-permute-done.5.refs_0_), channel_id=1, source_target_pairs={{0,1},{1,0},{2,3},{3,2},{4,5},{5,4},{6,7},{7,6},{8,9},{9,8},{10,11... | collective-permute-start | bytes 786440 | tf_op jit(solution)/shard_map/ppermute | solution.py:13
  60.4 0.7 copy-start.29
  61.1 6.5 %collective-permute-start.25 = (bf16[16,8,1024]{2,1,0:T(8,128)(2,1)S(1)}, bf16[16,8,1024]{2,1,0:T(8,128)(2,1)S(1)}, u32[]{:S(2)}, u32[]{:S(2)}) collective-permute-start(bf16[16,8,1024]{2,1,0:T(8,128)(2,1)S(1)} %collective-permute-done.21.refs_3_), channel_id=1, source_target_pairs={{0,1},{1,0},{2,3},{3,2},{4,5},{5,4},{6,7},{7,6},{8,9},{9,8},{10,11... | collective-permute-start | bytes 786440 | tf_op jit(solution)/shard_map/ppermute | solution.py:13
  67.7 4.9 %copy-start.14 = (bf16[16,8,1024]{2,1,0:T(8,128)(2,1)}, bf16[16,8,1024]{2,1,0:T(8,128)(2,1)S(1)}, u32[]{:S(2)}) copy-start(bf16[16,8,1024]{2,1,0:T(8,128)(2,1)S(1)} %collective-permute-done.25.refs_7_) | copy-start | bytes 786436
  67.7 9.2 %collective-permute-start.7 = (bf16[16,8,1024]{2,1,0:T(8,128)(2,1)S(1)}, bf16[16,8,1024]{2,1,0:T(8,128)(2,1)S(1)}, u32[]{:S(2)}, u32[]{:S(2)}) collective-permute-start(bf16[16,8,1024]{2,1,0:T(8,128)(2,1)S(1)} %collective-permute-done.4.refs_0_), channel_id=1, source_target_pairs={{0,2},{1,3},{2,0},{3,1},{4,6},{5,7},{6,4},{7,5},{8,10},{9,11},{10,... | collective-permute-start | bytes 786440 | tf_op jit(solution)/shard_map/ppermute | solution.py:13
  70.6 22.5 %copy-start.10 = (bf16[16,8,1024]{2,1,0:T(8,128)(2,1)}, bf16[16,8,1024]{2,1,0:T(8,128)(2,1)S(1)}, u32[]{:S(2)}) copy-start(bf16[16,8,1024]{2,1,0:T(8,128)(2,1)S(1)} %collective-permute-done.13.refs_1_) | copy-start | bytes 786436
  70.6 12.0 %collective-permute-start.15 = (bf16[16,8,1024]{2,1,0:T(8,128)(2,1)S(1)}, bf16[16,8,1024]{2,1,0:T(8,128)(2,1)S(1)}, u32[]{:S(2)}, u32[]{:S(2)}) collective-permute-start(bf16[16,8,1024]{2,1,0:T(8,128)(2,1)S(1)} %collective-permute-done.13.refs_1_), channel_id=1, source_target_pairs={{0,2},{1,3},{2,0},{3,1},{4,6},{5,7},{6,4},{7,5},{8,10},{9,11},{10,... | collective-permute-start | bytes 786440 | tf_op jit(solution)/shard_map/ppermute | solution.py:13
  71.1 22.0 %copy-start.12 = (bf16[16,8,1024]{2,1,0:T(8,128)(2,1)}, bf16[16,8,1024]{2,1,0:T(8,128)(2,1)S(1)}, u32[]{:S(2)}) copy-start(bf16[16,8,1024]{2,1,0:T(8,128)(2,1)S(1)} %collective-permute-done.14.refs_2_) | copy-start | bytes 786436
  71.1 11.4 %collective-permute-start.17 = (bf16[16,8,1024]{2,1,0:T(8,128)(2,1)S(1)}, bf16[16,8,1024]{2,1,0:T(8,128)(2,1)S(1)}, u32[]{:S(2)}, u32[]{:S(2)}) collective-permute-start(bf16[16,8,1024]{2,1,0:T(8,128)(2,1)S(1)} %collective-permute-done.13.refs_1_), channel_id=1, source_target_pairs={{0,1},{1,0},{2,3},{3,2},{4,5},{5,4},{6,7},{7,6},{8,9},{9,8},{10,11... | collective-permute-start | bytes 786440 | tf_op jit(solution)/shard_map/ppermute | solution.py:13
  71.1 22.0 %copy-start.13 = (bf16[16,8,1024]{2,1,0:T(8,128)(2,1)}, bf16[16,8,1024]{2,1,0:T(8,128)(2,1)S(1)}, u32[]{:S(2)}) copy-start(bf16[16,8,1024]{2,1,0:T(8,128)(2,1)S(1)} %collective-permute-done.16.refs_4_) | copy-start | bytes 786436
  71.1 11.9 %collective-permute-start.18 = (bf16[16,8,1024]{2,1,0:T(8,128)(2,1)S(1)}, bf16[16,8,1024]{2,1,0:T(8,128)(2,1)S(1)}, u32[]{:S(2)}, u32[]{:S(2)}) collective-permute-start(bf16[16,8,1024]{2,1,0:T(8,128)(2,1)S(1)} %collective-permute-done.14.refs_2_), channel_id=1, source_target_pairs={{0,1},{1,0},{2,3},{3,2},{4,5},{5,4},{6,7},{7,6},{8,9},{9,8},{10,11... | collective-permute-start | bytes 786440 | tf_op jit(solution)/shard_map/ppermute | solution.py:13
  72.6 20.5 %copy-start.6 = (bf16[16,8,1024]{2,1,0:T(8,128)(2,1)}, bf16[16,8,1024]{2,1,0:T(8,128)(2,1)S(1)}, u32[]{:S(2)}) copy-start(bf16[16,8,1024]{2,1,0:T(8,128)(2,1)S(1)} %collective-permute-done.6.refs_1_) | copy-start | bytes 786436
  72.6 14.7 %collective-permute-start.8 = (bf16[16,8,1024]{2,1,0:T(8,128)(2,1)S(1)}, bf16[16,8,1024]{2,1,0:T(8,128)(2,1)S(1)}, u32[]{:S(2)}, u32[]{:S(2)}) collective-permute-start(bf16[16,8,1024]{2,1,0:T(8,128)(2,1)S(1)} %collective-permute-done.6.refs_1_), channel_id=1, source_target_pairs={{0,2},{1,3},{2,0},{3,1},{4,6},{5,7},{6,4},{7,5},{8,10},{9,11},{10,... | collective-permute-start | bytes 786440 | tf_op jit(solution)/shard_map/ppermute | solution.py:13
  76.9 16.2 %copy-start.11 = (bf16[16,8,1024]{2,1,0:T(8,128)(2,1)}, bf16[16,8,1024]{2,1,0:T(8,128)(2,1)S(1)}, u32[]{:S(2)}) copy-start(bf16[16,8,1024]{2,1,0:T(8,128)(2,1)S(1)} %collective-permute-done.7.refs_2_) | copy-start | bytes 786436
  76.9 25.3 %collective-permute-start.9 = (bf16[16,8,1024]{2,1,0:T(8,128)(2,1)S(1)}, bf16[16,8,1024]{2,1,0:T(8,128)(2,1)S(1)}, u32[]{:S(2)}, u32[]{:S(2)}) collective-permute-start(bf16[16,8,1024]{2,1,0:T(8,128)(2,1)S(1)} %collective-permute-done.4.refs_0_), channel_id=1, source_target_pairs={{0,1},{1,0},{2,3},{3,2},{4,5},{5,4},{6,7},{7,6},{8,9},{9,8},{10,11... | collective-permute-start | bytes 786440 | tf_op jit(solution)/shard_map/ppermute | solution.py:13
  82.5 10.6 %copy-start.16 = (bf16[16,8,1024]{2,1,0:T(8,128)(2,1)}, bf16[16,8,1024]{2,1,0:T(8,128)(2,1)S(1)}, u32[]{:S(2)}) copy-start(bf16[16,8,1024]{2,1,0:T(8,128)(2,1)S(1)} %collective-permute-done.15.refs_3_) | copy-start | bytes 786436
  82.5 19.7 %collective-permute-start.10 = (bf16[16,8,1024]{2,1,0:T(8,128)(2,1)S(1)}, bf16[16,8,1024]{2,1,0:T(8,128)(2,1)S(1)}, u32[]{:S(2)}, u32[]{:S(2)}) collective-permute-start(bf16[16,8,1024]{2,1,0:T(8,128)(2,1)S(1)} %collective-permute-done.6.refs_1_), channel_id=1, source_target_pairs={{0,1},{1,0},{2,3},{3,2},{4,5},{5,4},{6,7},{7,6},{8,9},{9,8},{10,11... | collective-permute-start | bytes 786440 | tf_op jit(solution)/shard_map/ppermute | solution.py:13
  82.5 10.6 %copy-start.17 = (bf16[16,8,1024]{2,1,0:T(8,128)(2,1)}, bf16[16,8,1024]{2,1,0:T(8,128)(2,1)S(1)}, u32[]{:S(2)}) copy-start(bf16[16,8,1024]{2,1,0:T(8,128)(2,1)S(1)} %collective-permute-done.17.refs_5_) | copy-start | bytes 786436
  82.6 19.7 %collective-permute-start.11 = (bf16[16,8,1024]{2,1,0:T(8,128)(2,1)S(1)}, bf16[16,8,1024]{2,1,0:T(8,128)(2,1)S(1)}, u32[]{:S(2)}, u32[]{:S(2)}) collective-permute-start(bf16[16,8,1024]{2,1,0:T(8,128)(2,1)S(1)} %collective-permute-done.7.refs_2_), channel_id=1, source_target_pairs={{0,1},{1,0},{2,3},{3,2},{4,5},{5,4},{6,7},{7,6},{8,9},{9,8},{10,11... | collective-permute-start | bytes 786440 | tf_op jit(solution)/shard_map/ppermute | solution.py:13
  83.1 10.1 %copy-start.18 = (bf16[16,8,1024]{2,1,0:T(8,128)(2,1)}, bf16[16,8,1024]{2,1,0:T(8,128)(2,1)S(1)}, u32[]{:S(2)}) copy-start(bf16[16,8,1024]{2,1,0:T(8,128)(2,1)S(1)} %collective-permute-done.18.refs_6_) | copy-start | bytes 786436
  83.1 14.6 %collective-permute-start.19 = (bf16[16,8,1024]{2,1,0:T(8,128)(2,1)S(1)}, bf16[16,8,1024]{2,1,0:T(8,128)(2,1)}, u32[]{:S(2)}, u32[]{:S(2)}) collective-permute-start(bf16[16,8,1024]{2,1,0:T(8,128)(2,1)S(1)} %collective-permute-done.15.refs_3_), channel_id=1, source_target_pairs={{0,1},{1,0},{2,3},{3,2},{4,5},{5,4},{6,7},{7,6},{8,9},{9,8},{10,11... | collective-permute-start | bytes 786440 | tf_op jit(solution)/shard_map/ppermute | solution.py:13
  87.3 5.9 %copy-start.15 = (bf16[16,8,1024]{2,1,0:T(8,128)(2,1)}, bf16[16,8,1024]{2,1,0:T(8,128)(2,1)S(1)}, u32[]{:S(2)}) copy-start(bf16[16,8,1024]{2,1,0:T(8,128)(2,1)S(1)} %collective-permute-done.8.refs_3_) | copy-start | bytes 786436
  87.3 15.0 %collective-permute-start.12 = (bf16[16,8,1024]{2,1,0:T(8,128)(2,1)S(1)}, bf16[16,8,1024]{2,1,0:T(8,128)(2,1)}, u32[]{:S(2)}, u32[]{:S(2)}) collective-permute-start(bf16[16,8,1024]{2,1,0:T(8,128)(2,1)S(1)} %collective-permute-done.8.refs_3_), channel_id=1, source_target_pairs={{0,1},{1,0},{2,3},{3,2},{4,5},{5,4},{6,7},{7,6},{8,9},{9,8},{10,11... | collective-permute-start | bytes 786440 | tf_op jit(solution)/shard_map/ppermute | solution.py:13
  102.2 0.7 copy-start.19
  102.2 0.8 copy-start.20
  102.2 0.9 copy-start.21

commit v5 on v1

v5 whole, which is shorter than its diff:
```python
import functools

import jax
import jax.numpy as jnp
from jax import lax
from jax.experimental import pallas as pl
from jax.experimental.pallas import tpu as pltpu
from jax.sharding import PartitionSpec as P

ANY = pl.BlockSpec(memory_space=pl.ANY)
SMEM = pl.BlockSpec(memory_space=pltpu.SMEM)
VMEM = pl.BlockSpec(memory_space=pltpu.VMEM)


def swap(value, axis, mask):
    pairs = [(source, source ^ mask) for source in range(lax.axis_size(axis))]
    return lax.ppermute(value, axis, pairs)


def slice_kernel(delays_ref, window_ref, *refs, rounds, levels, steps):
    outs = refs[:rounds]
    sem = refs[rounds]
    me = lax.axis_index("area")
    copies = []
    for rnd in range(rounds):
        start = delays_ref[rnd, me ^ (1 << (rnd % levels))] - steps
        copy = pltpu.make_async_copy(window_ref.at[pl.ds(start, steps)], outs[rnd], sem.at[rnd])
        copy.start()
        copies.append(copy)
    for copy in copies:
        copy.wait()


def send_slices(window, delays, rounds, levels, steps):
    shape = (steps,) + window.shape[1:]
    kernel = functools.partial(slice_kernel, rounds=rounds, levels=levels, steps=steps)
    return pl.pallas_call(
        kernel,
        in_specs=[SMEM, ANY],
        out_specs=[ANY] * rounds,
        out_shape=[jax.ShapeDtypeStruct(shape, window.dtype)] * rounds,
        scratch_shapes=[pltpu.SemaphoreType.DMA((rounds,))],
    )(delays, window)


def gather_neuron(stacked):
    bits = lax.axis_size("neuron").bit_length() - 1
    pieces = [stacked]
    for bit in reversed(range(bits)):
        sent = pieces[0] if len(pieces) == 1 else jnp.concatenate(pieces, axis=0)
        pieces.append(swap(sent, "neuron", 1 << bit))
    return pieces


def chunk_place(p, ri, n_rounds):
    if p == 0:
        return 0, ri
    k = p.bit_length()
    return k, (p - (1 << (k - 1))) * n_rounds + ri


def relative_position(n, me, bits):
    d = n ^ me
    pos = jnp.zeros_like(d)
    for s, bit in enumerate(reversed(range(bits))):
        pos = pos | (((d >> bit) & 1) << s)
    return pos


def stage_kernel(pos_ref, *refs, n_pieces, stage, n_pos, final, has_rec):
    n_rounds = len(stage)
    it = iter(refs)
    piece_hbm = [next(it) for _ in range(n_pieces)]
    w_hbm = next(it)
    rec_hbm = next(it) if has_rec else None
    if final:
        err_hbm, surr_hbm, lv_hbm, la_hbm, alpha_hbm, rho_hbm, beta_hbm = [next(it) for _ in range(7)]
        cur_ref, lv_out, la_out = next(it), next(it), next(it)
    else:
        out_ref = next(it)
    piece_buf = [next(it) for _ in range(n_pieces)]
    w_buf = next(it)
    blocks = next(it)
    sem = next(it)
    if has_rec:
        rec_buf = next(it)
    if final:
        err_buf, surr_buf, lv_buf, la_buf, alpha_buf, rho_buf, beta_buf = [next(it) for _ in range(7)]

    _, steps, batch, width = piece_hbm[0].shape
    local_blocks, nnz, side = w_buf.shape[1], w_buf.shape[2], w_buf.shape[3]
    rows = steps * batch
    n_sem = 0

    def start(src, dst):
        nonlocal n_sem
        copy = pltpu.make_async_copy(src, dst, sem.at[n_sem])
        n_sem += 1
        copy.start()
        return copy

    piece_cp = [start(piece_hbm[k], piece_buf[k]) for k in range(n_pieces)]
    w_cp = [start(w_hbm.at[rnd, 0], w_buf.at[ri]) for ri, rnd in enumerate(stage)]
    rec_cp = start(rec_hbm, rec_buf) if has_rec else None
    if final:
        scan_cp = [
            start(src, dst)
            for src, dst in zip(
                (err_hbm, surr_hbm, lv_hbm, la_hbm, alpha_hbm, rho_hbm, beta_hbm),
                (err_buf, surr_buf, lv_buf, la_buf, alpha_buf, rho_buf, beta_buf),
            )
        ]

    waited = set()
    for ri in range(n_rounds):
        for p in range(n_pos):
            k, e = chunk_place(p, ri, n_rounds)
            if k not in waited:
                piece_cp[k].wait()
                waited.add(k)
            for i in range(local_blocks):
                x = piece_buf[k][e, :, :, i * side:(i + 1) * side].astype(jnp.float32)
                blocks[(ri * n_pos + p) * local_blocks + i] = x.reshape(rows, side).astype(jnp.bfloat16)
    if has_rec:
        rec_cp.wait()
    for ri in range(n_rounds):
        w_cp[ri].wait()
    if final:
        for copy in scan_cp:
            copy.wait()
    for j in range(local_blocks):
        cols = slice(j * side, (j + 1) * side)
        if has_rec:
            acc = rec_buf[:, :, cols].reshape(rows, side)
        else:
            acc = jnp.zeros((rows, side), jnp.float32)
        for ri in range(n_rounds):
            for k in range(nnz):
                x = blocks[ri * n_pos * local_blocks + pos_ref[(ri * local_blocks + j) * nnz + k]]
                acc = acc + jnp.dot(x, w_buf[ri, j, k], preferred_element_type=jnp.float32)
        rec = acc.reshape(steps, batch, side)
        if not final:
            out_ref[:, :, cols] = rec
            continue
        alpha = alpha_buf[:, cols]
        rho = rho_buf[:, cols]
        beta = beta_buf[:, cols]
        lv_now = lv_buf[:, cols]
        la_now = la_buf[:, cols]
        for t in reversed(range(steps)):
            surr = surr_buf[t, :, cols]
            total = err_buf[t, :, cols] + rec[t] - lv_now + la_now
            cur_ref[t, :, cols] = lv_now.astype(cur_ref.dtype)
            lv_next = alpha * lv_now + surr * total
            la_next = rho * la_now - beta * surr * total
            lv_now, la_now = lv_next, la_next
        lv_out[:, cols] = lv_now
        la_out[:, cols] = la_now


def stage_contrib(pos, pieces, weights, stage, n_pos, rec, scan_args):
    _, steps, batch, local = pieces[0].shape
    _, _, local_blocks, nnz, side, _ = weights.shape
    n_rounds = len(stage)
    final = scan_args is not None
    has_rec = rec is not None
    operands = list(pieces) + [weights]
    scratch = [pltpu.VMEM(p.shape, p.dtype) for p in pieces]
    scratch += [
        pltpu.VMEM((n_rounds, local_blocks, nnz, side, side), weights.dtype),
        pltpu.VMEM((n_rounds * n_pos * local_blocks, steps * batch, side), jnp.bfloat16),
    ]
    n_sem = len(pieces) + n_rounds + (1 if has_rec else 0) + (7 if final else 0)
    scratch.append(pltpu.SemaphoreType.DMA((n_sem,)))
    if has_rec:
        operands.append(rec)
        scratch.append(pltpu.VMEM(rec.shape, rec.dtype))
    if final:
        err_grad, surrogate, lv_end, la_end, alpha, rho, beta = scan_args
        rows = [a.reshape(1, local) for a in (alpha, rho, beta)]
        extra = [err_grad, surrogate, lv_end, la_end] + rows
        operands += extra
        scratch += [pltpu.VMEM(a.shape, a.dtype) for a in extra]
        out_specs = (VMEM, VMEM, VMEM)
        out_shape = (
            jax.ShapeDtypeStruct((steps, batch, local), jnp.bfloat16),
            jax.ShapeDtypeStruct((batch, local), jnp.float32),
            jax.ShapeDtypeStruct((batch, local), jnp.float32),
        )
    else:
        out_specs = VMEM
        out_shape = jax.ShapeDtypeStruct((steps, batch, local), jnp.float32)
    kernel = functools.partial(
        stage_kernel, n_pieces=len(pieces), stage=tuple(stage), n_pos=n_pos,
        final=final, has_rec=has_rec,
    )
    return pl.pallas_call(
        kernel,
        in_specs=[SMEM] + [ANY] * len(operands),
        out_specs=out_specs,
        scratch_shapes=scratch,
        out_shape=out_shape,
    )(pos, *operands)


def per_device(
    window, err_grad, surrogate, lv_end, la_end, alpha, rho, beta, weights, block_index, delays
):
    steps = err_grad.shape[0]
    local_neurons = err_grad.shape[2]
    block_side = weights.shape[-1]
    local_blocks = local_neurons // block_side
    rounds = weights.shape[0]
    levels = lax.axis_size("area").bit_length() - 1
    nbits = lax.axis_size("neuron").bit_length() - 1
    n_pos = 1 << nbits
    me_neuron = lax.axis_index("neuron")
    slices = send_slices(window, delays, rounds, levels, steps)
    stages = [list(range(f, min(f + 2, rounds))) for f in range(0, rounds, 2)]
    arrived = []
    gate = None
    for stage in stages:
        pieces = [slices[rnd] for rnd in stage]
        if gate is not None:
            pieces, _ = lax.optimization_barrier((pieces, gate))
        got = [swap(piece, "area", 1 << (rnd % levels)) for piece, rnd in zip(pieces, stage)]
        arrived.append(jnp.stack(got))
        gate = got
    rec = None
    for si, stage in enumerate(stages):
        stacked = arrived[si]
        if rec is not None:
            stacked, _ = lax.optimization_barrier((stacked, rec))
        pieces = gather_neuron(stacked)
        idx = block_index[jnp.array(stage), 0]
        owner = idx // local_blocks
        pos = relative_position(owner, me_neuron, nbits) * local_blocks + idx % local_blocks
        scan_args = None
        if si == len(stages) - 1:
            scan_args = (err_grad, surrogate, lv_end, la_end, alpha, rho, beta)
        rec = stage_contrib(
            pos.reshape(-1).astype(jnp.int32), pieces, weights, stage, n_pos, rec, scan_args
        )
    return rec


def solution(mesh):
    placed = (
        P(None, "groups", ("area", "neuron")),
        P(None, "groups", ("area", "neuron")),
        P(None, "groups", ("area", "neuron")),
        P("groups", ("area", "neuron")),
        P("groups", ("area", "neuron")),
        P(("area", "neuron")),
        P(("area", "neuron")),
        P(("area", "neuron")),
        P(None, "area", "neuron", None, None, None),
        P(None, "area", "neuron", None),
        P(),
    )
    return jax.shard_map(
        per_device,
        mesh=mesh,
        in_specs=placed,
        out_specs=(
            P(None, "groups", ("area", "neuron")),
            P("groups", ("area", "neuron")),
            P("groups", ("area", "neuron")),
        ),
        check_vma=False,
    )
```

time: 132 us -> 192 us (1.45)
  Pallas kernels: 0 us -> 79.2 us
  waiting for transfers between devices: 55 us -> 94.4 us
  local copies, waits for them, and re-layouts: 36.1 us -> 1.56 us
  matrix products: 10.3 us -> 0 us
  other arithmetic: 10.4 us -> 4.5 us
  between operations: 6.41 us -> 0.72 us
    pallas_call x0 -> x3, Pallas kernels: none -> 79.2 us  [the longest x1 65.5 us: send_slices(): pl.pallas_call(kernel, in_specs=[SMEM, ANY], out_specs=[ANY] * rounds, ou...]
    ppermute x12 -> x8, waiting for transfers between devices: 55 us -> 94.4 us  [swap(): return lax.ppermute(value, axis, pairs)]
    gather x4 -> x6, local copies, waits for them, and re-layouts: 12.2 us -> 1.53 us  [per_device(): idx = block_index[jnp.array(stage), 0]]
    dot_general x4 -> x0, matrix products: 10.3 us -> none  [per_device(): jnp.einsum('rjkc,jkcd->rjd', picked, weights[rnd, 0], preferred_element_t...]
    reshape x4 -> x0, local copies, waits for them, and re-layouts: 9.55 us -> none  [per_device(): flat = jnp.moveaxis(flat, 1, 0).reshape(steps * batch, -1, block_side)]
    unnamed x48 -> x12, local copies, waits for them, and re-layouts: 8.94 us -> 0.03 us
    concatenate x8 -> x2, other arithmetic: 8.42 us -> 3.27 us  [gather_neuron(): sent = pieces[0] if len(pieces) == 1 else jnp.concatenate(pieces, axis=0)]
    dynamic_slice x2 -> x0, local copies, waits for them, and re-layouts: 4.29 us -> none  [the longest x1 2.8 us: per_device(): piece = lax.dynamic_slice_in_dim(window, start, steps, 0)]
  transfers between devices with their start and end apart: 12 -> 8, of which waited for: 6 -> 7; matrix products, arithmetic and copies ran while one was open for 18% -> 1% of each run, Pallas kernels for 0% -> 0%
where the time goes in v5:
time: 192 us
  waiting for transfers between devices  94.4 us (49%)
  Pallas kernels  79.2 us (41%)
  starting transfers between devices  11.8 us (6%)
  other arithmetic  4.5 us (2%)
    ppermute x8, waiting for transfers between devices, swap(): return lax.ppermute(value, axis, pairs)  94.4 us
    pallas_call x1, Pallas kernels, send_slices(): pl.pallas_call(kernel, in_specs=[SMEM, ANY], out_specs=[ANY] * rounds, ou...  65.5 us
    pallas_call x2, Pallas kernels, stage_contrib(): pl.pallas_call(kernel, in_specs=[SMEM] + [ANY] * len(operands), out_specs...  13.7 us
    ppermute x8, starting transfers between devices, swap(): return lax.ppermute(value, axis, pairs)  11.8 us
  transfers between devices with their start and end apart: 8, of which 7 were waited for; matrix products, arithmetic and copies ran while one was open for 1% of the time, Pallas kernels for 0%

profile of v5, /device:TPU:0, one launch (start us, length us, event | category | flops | bytes accessed | tf_op | source)
XLA Modules:
  0.0 192.2 jit_solution(18237952126753242702)
XLA Ops:
  0.6 0.0 copy-start
  0.6 65.5 %shard_map.148 = (bf16[16,8,2048]{2,1,0:T(8,128)(2,1)}, bf16[16,8,2048]{2,1,0:T(8,128)(2,1)}, bf16[16,8,2048]{2,1,0:T(8,128)(2,1)}, bf16[16,8,2048]{2,1,0:T(8,128)(2,1)}) custom-call(s32[4,4]{1,0:T(4,128)} %delays_ref.1, bf16[32,8,2048]{2,1,0:T(8,128)(2,1)} %window_ref.1), custom_call_target="tpu_custom_call" | custom-call | tf_op jit(solution)/shard_map/pallas_call | solution.py:37
  66.2 3.1 %collective-permute-start = (bf16[16,8,2048]{2,1,0:T(8,128)(2,1)}, bf16[16,8,2048]{2,1,0:T(8,128)(2,1)S(1)}, u32[]{:S(2)}, u32[]{:S(2)}) collective-permute-start(bf16[16,8,2048]{2,1,0:T(8,128)(2,1)} %get-tuple-element.12), channel_id=1, source_target_pairs={{0,4},{4,0},{8,12},{12,8},{1,5},{5,1},{9,13},{13,9},{2,6},{6,2},{1... | collective-permute-start | bytes 1572872 | tf_op jit(solution)/shard_map/ppermute | solution.py:17
  69.2 2.6 %collective-permute-start.1 = (bf16[16,8,2048]{2,1,0:T(8,128)(2,1)}, bf16[16,8,2048]{2,1,0:T(8,128)(2,1)S(1)}, u32[]{:S(2)}, u32[]{:S(2)}) collective-permute-start(bf16[16,8,2048]{2,1,0:T(8,128)(2,1)} %get-tuple-element.13), channel_id=1, source_target_pairs={{0,8},{4,12},{8,0},{12,4},{1,9},{5,13},{9,1},{13,5},{2,10},{6,14},... | collective-permute-start | bytes 1572872 | tf_op jit(solution)/shard_map/ppermute | solution.py:17
  71.8 20.7 %collective-permute-done = bf16[16,8,2048]{2,1,0:T(8,128)(2,1)S(1)} collective-permute-done((bf16[16,8,2048]{2,1,0:T(8,128)(2,1)}, bf16[16,8,2048]{2,1,0:T(8,128)(2,1)S(1)}, u32[]{:S(2)}, u32[]{:S(2)}) %collective-permute-start) | collective-permute-done | bytes 524320 | tf_op jit(solution)/shard_map/ppermute | solution.py:17
  92.5 2.5 %collective-permute-done.1 = bf16[16,8,2048]{2,1,0:T(8,128)(2,1)S(1)} collective-permute-done((bf16[16,8,2048]{2,1,0:T(8,128)(2,1)}, bf16[16,8,2048]{2,1,0:T(8,128)(2,1)S(1)}, u32[]{:S(2)}, u32[]{:S(2)}) %collective-permute-start.1) | collective-permute-done | bytes 524320 | tf_op jit(solution)/shard_map/ppermute | solution.py:17
  95.0 0.1 pad_maximum_fusion.3.refs_0_
  95.1 0.0 copy-start.3
  95.1 1.6 collective-permute-start.4
  96.7 20.3 %collective-permute-done.4.refs_1_ = bf16[2,16,8,2048]{3,2,1,0:T(8,128)(2,1)S(1)} collective-permute-done((bf16[2,16,8,2048]{3,2,1,0:T(8,128)(2,1)S(1)}, bf16[2,16,8,2048]{3,2,1,0:T(8,128)(2,1)S(1)}, u32[]{:S(2)}, u32[]{:S(2)}) %collective-permute-start.4) | collective-permute-done | bytes 1048608 | tf_op jit(solution)/shard_map/ppermute | solution.py:17
  117.0 0.0 copy-start.4
  117.0 1.6 pad_maximum_fusion
  118.7 0.0 copy-done.3
  118.7 0.0 copy-done.4
  118.7 0.0 collective-permute-start.5
  118.7 2.7 %collective-permute-start.2 = (bf16[16,8,2048]{2,1,0:T(8,128)(2,1)}, bf16[16,8,2048]{2,1,0:T(8,128)(2,1)S(1)}, u32[]{:S(2)}, u32[]{:S(2)}) collective-permute-start(bf16[16,8,2048]{2,1,0:T(8,128)(2,1)} %get-tuple-element.14), channel_id=1, source_target_pairs={{0,4},{4,0},{8,12},{12,8},{1,5},{5,1},{9,13},{13,9},{2,6},{6,2},{1... | collective-permute-start | bytes 1572872 | tf_op jit(solution)/shard_map/ppermute | solution.py:17
  121.3 0.3 collective-permute-start.3
  121.6 0.0 copy-done
  121.7 0.6 gather_fusion.1
  122.2 0.1 copy.19
  122.3 0.1 gather.13
  122.4 0.5 fusion.1.pos_ref
  123.0 21.1 %collective-permute-done.2 = bf16[16,8,2048]{2,1,0:T(8,128)(2,1)S(1)} collective-permute-done((bf16[16,8,2048]{2,1,0:T(8,128)(2,1)}, bf16[16,8,2048]{2,1,0:T(8,128)(2,1)S(1)}, u32[]{:S(2)}, u32[]{:S(2)}) %collective-permute-start.2) | collective-permute-done | bytes 524320 | tf_op jit(solution)/shard_map/ppermute | solution.py:17
  144.1 3.7 %collective-permute-done.3 = bf16[16,8,2048]{2,1,0:T(8,128)(2,1)S(1)} collective-permute-done((bf16[16,8,2048]{2,1,0:T(8,128)(2,1)}, bf16[16,8,2048]{2,1,0:T(8,128)(2,1)S(1)}, u32[]{:S(2)}, u32[]{:S(2)}) %collective-permute-start.3) | collective-permute-done | bytes 524320 | tf_op jit(solution)/shard_map/ppermute | solution.py:17
  147.7 0.1 pad_maximum_fusion.2.refs_0_
  147.8 0.0 copy-start.1
  147.8 0.0 collective-permute-done.5.refs_2_
  147.8 6.4 %shard_map.149.refs_4_ = f32[16,8,2048]{2,1,0:T(8,128)} custom-call(s32[128]{0:T(128)} %fusion.1.pos_ref, bf16[2,16,8,2048]{3,2,1,0:T(8,128)(2,1)} %copy-done.3, bf16[2,16,8,2048]{3,2,1,0:T(8,128)(2,1)} %copy-done.4, bf16[4,16,8,2048]{3,2,1,0:T(8,128)(2,1)} %collective-permute-done.5.refs_2_, bf16[4,1,16,4,128,128]{5,4,3,2,1,0:T(8,128)(2,1)} %refs_3_.3), custom_call_target="tpu_custom_call" | custom-call | tf_op jit(solution)/shard_map/pallas_call | solution.py:197
  154.3 0.0 copy-start.5
  154.3 1.6 collective-permute-start.6
  155.9 22.9 %collective-permute-done.6.refs_1_ = bf16[2,16,8,2048]{3,2,1,0:T(8,128)(2,1)S(1)} collective-permute-done((bf16[2,16,8,2048]{3,2,1,0:T(8,128)(2,1)S(1)}, bf16[2,16,8,2048]{3,2,1,0:T(8,128)(2,1)S(1)}, u32[]{:S(2)}, u32[]{:S(2)}) %collective-permute-start.6) | collective-permute-done | bytes 1048608 | tf_op jit(solution)/shard_map/ppermute | solution.py:17
  178.8 0.0 copy-done.1
  178.8 0.0 copy-start.2
  178.8 1.6 pad_maximum_fusion.1
  180.4 0.0 collective-permute-start.7
  180.4 0.0 copy-done.5
  180.4 0.6 gather_fusion
  181.0 0.0 copy-done.2
  181.0 0.1 copy.18
  181.1 0.1 gather.11
  181.2 0.5 fusion.pos_ref
  181.7 3.2 %collective-permute-done.7.refs_2_ = bf16[4,16,8,2048]{3,2,1,0:T(8,128)(2,1)} collective-permute-done((bf16[4,16,8,2048]{3,2,1,0:T(8,128)(2,1)}, bf16[4,16,8,2048]{3,2,1,0:T(8,128)(2,1)}, u32[]{:S(2)}, u32[]{:S(2)}) %collective-permute-start.7) | collective-permute-done | bytes 2097184 | tf_op jit(solution)/shard_map/ppermute | solution.py:17
  184.9 7.3 %shard_map.150 = (bf16[16,8,2048]{2,1,0:T(8,128)(2,1)}, f32[8,2048]{1,0:T(8,128)}, f32[8,2048]{1,0:T(8,128)}) custom-call(s32[128]{0:T(128)} %fusion.pos_ref, bf16[2,16,8,2048]{3,2,1,0:T(8,128)(2,1)} %copy-done.1, bf16[2,16,8,2048]{3,2,1,0:T(8,128)(2,1)} %copy-done.2, bf16[4,16,8,2048]{3,2,1,0:T(8,128)(2,1)} %collective-permute-done.7.refs_2_, ...), custom_call_target="tpu_custom_call" | custom-call | tf_op jit(solution)/shard_map/pallas_call | solution.py:197
  (1 shorter events, 0.0 us)
Async XLA Ops:
  0.6 121.0 %copy-start = (s32[4,1,16,4]{2,3,1,0:T(4,128)S(1)}, s32[4,1,16,4]{2,3,1,0:T(4,128)}, u32[]{:S(2)}) copy-start(s32[4,1,16,4]{2,3,1,0:T(4,128)} %param.22) | copy-start | bytes 3076
  66.2 26.3 %collective-permute-start = (bf16[16,8,2048]{2,1,0:T(8,128)(2,1)}, bf16[16,8,2048]{2,1,0:T(8,128)(2,1)S(1)}, u32[]{:S(2)}, u32[]{:S(2)}) collective-permute-start(bf16[16,8,2048]{2,1,0:T(8,128)(2,1)} %get-tuple-element.12), channel_id=1, source_target_pairs={{0,4},{4,0},{8,12},{12,8},{1,5},{5,1},{9,13},{13,9},{2,6},{6,2},{1... | collective-permute-start | bytes 1572872 | tf_op jit(solution)/shard_map/ppermute | solution.py:17
  69.2 25.8 %collective-permute-start.1 = (bf16[16,8,2048]{2,1,0:T(8,128)(2,1)}, bf16[16,8,2048]{2,1,0:T(8,128)(2,1)S(1)}, u32[]{:S(2)}, u32[]{:S(2)}) collective-permute-start(bf16[16,8,2048]{2,1,0:T(8,128)(2,1)} %get-tuple-element.13), channel_id=1, source_target_pairs={{0,8},{4,12},{8,0},{12,4},{1,9},{5,13},{9,1},{13,5},{2,10},{6,14},... | collective-permute-start | bytes 1572872 | tf_op jit(solution)/shard_map/ppermute | solution.py:17
  95.1 23.6 %copy-start.3 = (bf16[2,16,8,2048]{3,2,1,0:T(8,128)(2,1)}, bf16[2,16,8,2048]{3,2,1,0:T(8,128)(2,1)S(1)}, u32[]{:S(2)}) copy-start(bf16[2,16,8,2048]{3,2,1,0:T(8,128)(2,1)S(1)} %pad_maximum_fusion.3.refs_0_) | copy-start | bytes 3145732
  95.1 21.9 %collective-permute-start.4 = (bf16[2,16,8,2048]{3,2,1,0:T(8,128)(2,1)S(1)}, bf16[2,16,8,2048]{3,2,1,0:T(8,128)(2,1)S(1)}, u32[]{:S(2)}, u32[]{:S(2)}) collective-permute-start(bf16[2,16,8,2048]{3,2,1,0:T(8,128)(2,1)S(1)} %pad_maximum_fusion.3.refs_0_), channel_id=1, source_target_pairs={{0,2},{1,3},{2,0},{3,1},{4,6},{5,7},{6,4},{7,5},{8,10},{9,11},{10,... | collective-permute-start | bytes 3145736 | tf_op jit(solution)/shard_map/ppermute | solution.py:17
  117.0 1.7 copy-start.4
  118.7 29.2 %collective-permute-start.5 = (bf16[4,16,8,2048]{3,2,1,0:T(8,128)(2,1)}, bf16[4,16,8,2048]{3,2,1,0:T(8,128)(2,1)}, u32[]{:S(2)}, u32[]{:S(2)}) collective-permute-start(bf16[4,16,8,2048]{3,2,1,0:T(8,128)(2,1)} %pad_maximum_fusion), channel_id=1, source_target_pairs={{0,1},{1,0},{2,3},{3,2},{4,5},{5,4},{6,7},{7,6},{8,9},{9,8},{10,11... | collective-permute-start | bytes 6291464 | tf_op jit(solution)/shard_map/ppermute | solution.py:17
  118.7 25.4 %collective-permute-start.2 = (bf16[16,8,2048]{2,1,0:T(8,128)(2,1)}, bf16[16,8,2048]{2,1,0:T(8,128)(2,1)S(1)}, u32[]{:S(2)}, u32[]{:S(2)}) collective-permute-start(bf16[16,8,2048]{2,1,0:T(8,128)(2,1)} %get-tuple-element.14), channel_id=1, source_target_pairs={{0,4},{4,0},{8,12},{12,8},{1,5},{5,1},{9,13},{13,9},{2,6},{6,2},{1... | collective-permute-start | bytes 1572872 | tf_op jit(solution)/shard_map/ppermute | solution.py:17
  121.3 26.4 %collective-permute-start.3 = (bf16[16,8,2048]{2,1,0:T(8,128)(2,1)}, bf16[16,8,2048]{2,1,0:T(8,128)(2,1)S(1)}, u32[]{:S(2)}, u32[]{:S(2)}) collective-permute-start(bf16[16,8,2048]{2,1,0:T(8,128)(2,1)} %get-tuple-element.15), channel_id=1, source_target_pairs={{0,8},{4,12},{8,0},{12,4},{1,9},{5,13},{9,1},{13,5},{2,10},{6,14},... | collective-permute-start | bytes 1572872 | tf_op jit(solution)/shard_map/ppermute | solution.py:17
  147.8 31.0 %copy-start.1 = (bf16[2,16,8,2048]{3,2,1,0:T(8,128)(2,1)}, bf16[2,16,8,2048]{3,2,1,0:T(8,128)(2,1)S(1)}, u32[]{:S(2)}) copy-start(bf16[2,16,8,2048]{3,2,1,0:T(8,128)(2,1)S(1)} %pad_maximum_fusion.2.refs_0_) | copy-start | bytes 3145732
  154.3 26.1 %copy-start.5 = (s32[2]{0:T(128)S(1)}, s32[2]{0:T(128)}, u32[]{:S(2)}) copy-start(s32[2]{0:T(128)} %constant.101) | copy-start | bytes 28
  154.3 24.5 %collective-permute-start.6 = (bf16[2,16,8,2048]{3,2,1,0:T(8,128)(2,1)S(1)}, bf16[2,16,8,2048]{3,2,1,0:T(8,128)(2,1)S(1)}, u32[]{:S(2)}, u32[]{:S(2)}) collective-permute-start(bf16[2,16,8,2048]{3,2,1,0:T(8,128)(2,1)S(1)} %pad_maximum_fusion.2.refs_0_), channel_id=1, source_target_pairs={{0,2},{1,3},{2,0},{3,1},{4,6},{5,7},{6,4},{7,5},{8,10},{9,11},{10,... | collective-permute-start | bytes 3145736 | tf_op jit(solution)/shard_map/ppermute | solution.py:17
  178.8 2.2 %copy-start.2 = (bf16[2,16,8,2048]{3,2,1,0:T(8,128)(2,1)}, bf16[2,16,8,2048]{3,2,1,0:T(8,128)(2,1)S(1)}, u32[]{:S(2)}) copy-start(bf16[2,16,8,2048]{3,2,1,0:T(8,128)(2,1)S(1)} %collective-permute-done.6.refs_1_) | copy-start | bytes 3145732
  180.4 4.5 %collective-permute-start.7 = (bf16[4,16,8,2048]{3,2,1,0:T(8,128)(2,1)}, bf16[4,16,8,2048]{3,2,1,0:T(8,128)(2,1)}, u32[]{:S(2)}, u32[]{:S(2)}) collective-permute-start(bf16[4,16,8,2048]{3,2,1,0:T(8,128)(2,1)} %pad_maximum_fusion.1), channel_id=1, source_target_pairs={{0,1},{1,0},{2,3},{3,2},{4,5},{5,4},{6,7},{7,6},{8,9},{9,8},{10,11... | collective-permute-start | bytes 6291464 | tf_op jit(solution)/shard_map/ppermute | solution.py:17

commit v6 on v5

--- a/solution.py
+++ b/solution.py
@@ -17,46 +17,32 @@
     return lax.ppermute(value, axis, pairs)
 
 
-def slice_kernel(delays_ref, window_ref, *refs, rounds, levels, steps):
-    outs = refs[:rounds]
-    sem = refs[rounds]
+def slice_kernel(delays_ref, window_ref, *outs, levels, steps):
     me = lax.axis_index("area")
-    copies = []
-    for rnd in range(rounds):
+    for rnd, out in enumerate(outs):
         start = delays_ref[rnd, me ^ (1 << (rnd % levels))] - steps
-        copy = pltpu.make_async_copy(window_ref.at[pl.ds(start, steps)], outs[rnd], sem.at[rnd])
-        copy.start()
-        copies.append(copy)
-    for copy in copies:
-        copy.wait()
+        out[...] = window_ref[pl.ds(start, steps)]
 
 
 def send_slices(window, delays, rounds, levels, steps):
     shape = (steps,) + window.shape[1:]
-    kernel = functools.partial(slice_kernel, rounds=rounds, levels=levels, steps=steps)
+    kernel = functools.partial(slice_kernel, levels=levels, steps=steps)
     return pl.pallas_call(
         kernel,
-        in_specs=[SMEM, ANY],
-        out_specs=[ANY] * rounds,
+        in_specs=[SMEM, VMEM],
+        out_specs=[VMEM] * rounds,
         out_shape=[jax.ShapeDtypeStruct(shape, window.dtype)] * rounds,
-        scratch_shapes=[pltpu.SemaphoreType.DMA((rounds,))],
     )(delays, window)
 
 
-def gather_neuron(stacked):
+def gather_neuron(piece, gate=None):
     bits = lax.axis_size("neuron").bit_length() - 1
-    pieces = [stacked]
+    held = [piece]
     for bit in reversed(range(bits)):
-        sent = pieces[0] if len(pieces) == 1 else jnp.concatenate(pieces, axis=0)
-        pieces.append(swap(sent, "neuron", 1 << bit))
-    return pieces
-
-
-def chunk_place(p, ri, n_rounds):
-    if p == 0:
-        return 0, ri
-    k = p.bit_length()
-    return k, (p - (1 << (k - 1))) * n_rounds + ri
+        if bit == 0 and gate is not None:
+            held, _ = lax.optimization_barrier((held, gate))
+        held = held + [swap(chunk, "neuron", 1 << bit) for chunk in held]
+    return held
 
 
 def relative_position(n, me, bits):
@@ -87,7 +73,7 @@
     if final:
         err_buf, surr_buf, lv_buf, la_buf, alpha_buf, rho_buf, beta_buf = [next(it) for _ in range(7)]
 
-    _, steps, batch, width = piece_hbm[0].shape
+    steps, batch, width = piece_hbm[0].shape
     local_blocks, nnz, side = w_buf.shape[1], w_buf.shape[2], w_buf.shape[3]
     rows = steps * batch
     n_sem = 0
@@ -111,15 +97,12 @@
             )
         ]
 
-    waited = set()
     for ri in range(n_rounds):
         for p in range(n_pos):
-            k, e = chunk_place(p, ri, n_rounds)
-            if k not in waited:
-                piece_cp[k].wait()
-                waited.add(k)
+            k = ri * n_pos + p
+            piece_cp[k].wait()
             for i in range(local_blocks):
-                x = piece_buf[k][e, :, :, i * side:(i + 1) * side].astype(jnp.float32)
+                x = piece_buf[k][:, :, i * side:(i + 1) * side].astype(jnp.float32)
                 blocks[(ri * n_pos + p) * local_blocks + i] = x.reshape(rows, side).astype(jnp.bfloat16)
     if has_rec:
         rec_cp.wait()
@@ -159,7 +142,7 @@
 
 
 def stage_contrib(pos, pieces, weights, stage, n_pos, rec, scan_args):
-    _, steps, batch, local = pieces[0].shape
+    steps, batch, local = pieces[0].shape
     _, _, local_blocks, nnz, side, _ = weights.shape
     n_rounds = len(stage)
     final = scan_args is not None
@@ -224,14 +207,13 @@
         if gate is not None:
             pieces, _ = lax.optimization_barrier((pieces, gate))
         got = [swap(piece, "area", 1 << (rnd % levels)) for piece, rnd in zip(pieces, stage)]
-        arrived.append(jnp.stack(got))
+        arrived += got
         gate = got
     rec = None
     for si, stage in enumerate(stages):
-        stacked = arrived[si]
-        if rec is not None:
-            stacked, _ = lax.optimization_barrier((stacked, rec))
-        pieces = gather_neuron(stacked)
+        chunks = []
+        for rnd in stage:
+            chunks += gather_neuron(arrived[rnd], rec)
         idx = block_index[jnp.array(stage), 0]
         owner = idx // local_blocks
         pos = relative_position(owner, me_neuron, nbits) * local_blocks + idx % local_blocks
@@ -239,7 +221,7 @@
         if si == len(stages) - 1:
             scan_args = (err_grad, surrogate, lv_end, la_end, alpha, rho, beta)
         rec = stage_contrib(
-            pos.reshape(-1).astype(jnp.int32), pieces, weights, stage, n_pos, rec, scan_args
+            pos.reshape(-1).astype(jnp.int32), chunks, weights, stage, n_pos, rec, scan_args
         )
     return rec
 

time: 192 us -> 93.3 us (0.49)
  Pallas kernels: 79.2 us -> 16.6 us
  waiting for transfers between devices: 94.4 us -> 57.5 us
  starting transfers between devices: 11.8 us -> 15.4 us
  other arithmetic: 4.5 us -> 1.08 us
    pallas_call x1, Pallas kernels: 65.5 us -> 2.72 us  [send_slices(): pl.pallas_call(kernel, in_specs=[SMEM, VMEM], out_specs=[VMEM] * rounds,...]
    ppermute x8 -> x16, waiting for transfers between devices: 94.4 us -> 57.5 us  [swap(): return lax.ppermute(value, axis, pairs)]
    ppermute x8 -> x16, starting transfers between devices: 11.8 us -> 15.4 us  [swap(): return lax.ppermute(value, axis, pairs)]
    concatenate x2 -> x0, other arithmetic: 3.27 us -> none  [gather_neuron(): sent = pieces[0] if len(pieces) == 1 else jnp.concatenate(pieces, axis=0)]
  transfers between devices with their start and end apart: 8 -> 16, of which waited for: 7 -> 9; matrix products, arithmetic and copies ran while one was open for 1% -> 3% of each run, Pallas kernels for 0% -> 7%
where the time goes in v6:
time: 93.3 us; the launch traced here: 93.2 us
  waiting for transfers between devices  57.5 us (62%)
  Pallas kernels  16.6 us (18%)
  starting transfers between devices  15.4 us (17%)
  local copies, waits for them, and re-layouts  1.87 us (2%)
  other arithmetic  1.08 us (1%)
    ppermute x16, waiting for transfers between devices, swap(): return lax.ppermute(value, axis, pairs)  57.5 us
    ppermute x16, starting transfers between devices, swap(): return lax.ppermute(value, axis, pairs)  15.4 us
    pallas_call x2, Pallas kernels, stage_contrib(): pl.pallas_call(kernel, in_specs=[SMEM] + [ANY] * len(operands), out_specs...  13.9 us
    pallas_call x1, Pallas kernels, send_slices(): pl.pallas_call(kernel, in_specs=[SMEM, VMEM], out_specs=[VMEM] * rounds,...  2.72 us
  transfers between devices with their start and end apart: 16, of which 9 were waited for; matrix products, arithmetic and copies ran while one was open for 3% of the time, Pallas kernels for 7%

profile of v6, /device:TPU:0, one launch (start us, length us, event | category | flops | bytes accessed | tf_op | source)
XLA Modules:
  0.0 93.2 jit_solution(15444773371291057118)
XLA Ops:
  0.6 0.0 copy-start
  0.6 0.0 copy-start.10
  0.7 2.7 %shard_map.148 = (bf16[16,8,2048]{2,1,0:T(8,128)(2,1)}, bf16[16,8,2048]{2,1,0:T(8,128)(2,1)}, bf16[16,8,2048]{2,1,0:T(8,128)(2,1)}, bf16[16,8,2048]{2,1,0:T(8,128)(2,1)}) custom-call(s32[4,4]{1,0:T(4,128)} %delays_ref.1, bf16[32,8,2048]{2,1,0:T(8,128)(2,1)} %window_ref.1), custom_call_target="tpu_custom_call" | custom-call | tf_op jit(solution)/shard_map/pallas_call | solution.py:30
  3.4 3.0 %collective-permute-start = (bf16[16,8,2048]{2,1,0:T(8,128)(2,1)}, bf16[16,8,2048]{2,1,0:T(8,128)(2,1)S(1)}, u32[]{:S(2)}, u32[]{:S(2)}) collective-permute-start(bf16[16,8,2048]{2,1,0:T(8,128)(2,1)} %get-tuple-element.15), channel_id=1, source_target_pairs={{0,4},{4,0},{8,12},{12,8},{1,5},{5,1},{9,13},{13,9},{2,6},{6,2},{1... | collective-permute-start | bytes 1572872 | tf_op jit(solution)/shard_map/ppermute | solution.py:17
  6.4 2.6 %collective-permute-start.1 = (bf16[16,8,2048]{2,1,0:T(8,128)(2,1)}, bf16[16,8,2048]{2,1,0:T(8,128)(2,1)S(1)}, u32[]{:S(2)}, u32[]{:S(2)}) collective-permute-start(bf16[16,8,2048]{2,1,0:T(8,128)(2,1)} %get-tuple-element.16), channel_id=1, source_target_pairs={{0,8},{4,12},{8,0},{12,4},{1,9},{5,13},{9,1},{13,5},{2,10},{6,14},... | collective-permute-start | bytes 1572872 | tf_op jit(solution)/shard_map/ppermute | solution.py:17
  9.0 20.7 %collective-permute-done.refs_0_ = bf16[16,8,2048]{2,1,0:T(8,128)(2,1)S(1)} collective-permute-done((bf16[16,8,2048]{2,1,0:T(8,128)(2,1)}, bf16[16,8,2048]{2,1,0:T(8,128)(2,1)S(1)}, u32[]{:S(2)}, u32[]{:S(2)}) %collective-permute-start) | collective-permute-done | bytes 524320 | tf_op jit(solution)/shard_map/ppermute | solution.py:17
  29.7 0.0 copy-start.7
  29.7 1.7 %collective-permute-start.4 = (bf16[16,8,2048]{2,1,0:T(8,128)(2,1)S(1)}, bf16[16,8,2048]{2,1,0:T(8,128)(2,1)}, u32[]{:S(2)}, u32[]{:S(2)}) collective-permute-start(bf16[16,8,2048]{2,1,0:T(8,128)(2,1)S(1)} %collective-permute-done.refs_0_), channel_id=1, source_target_pairs={{0,2},{1,3},{2,0},{3,1},{4,6},{5,7},{6,4},{7,5},{8,10},{9,11},{10,... | collective-permute-start | bytes 1572872 | tf_op jit(solution)/shard_map/ppermute | solution.py:17
  31.3 0.0 collective-permute-start.5
  31.3 0.9 collective-permute-done.1.refs_4_
  32.2 0.0 copy-start.8
  32.2 1.5 %collective-permute-start.7 = (bf16[16,8,2048]{2,1,0:T(8,128)(2,1)S(1)}, bf16[16,8,2048]{2,1,0:T(8,128)(2,1)}, u32[]{:S(2)}, u32[]{:S(2)}) collective-permute-start(bf16[16,8,2048]{2,1,0:T(8,128)(2,1)S(1)} %collective-permute-done.1.refs_4_), channel_id=1, source_target_pairs={{0,2},{1,3},{2,0},{3,1},{4,6},{5,7},{6,4},{7,5},{8,10},{9,11},{10,... | collective-permute-start | bytes 1572872 | tf_op jit(solution)/shard_map/ppermute | solution.py:17
  33.7 0.3 collective-permute-start.12
  34.0 2.7 %collective-permute-start.2 = (bf16[16,8,2048]{2,1,0:T(8,128)(2,1)}, bf16[16,8,2048]{2,1,0:T(8,128)(2,1)S(1)}, u32[]{:S(2)}, u32[]{:S(2)}) collective-permute-start(bf16[16,8,2048]{2,1,0:T(8,128)(2,1)} %get-tuple-element.17), channel_id=1, source_target_pairs={{0,4},{4,0},{8,12},{12,8},{1,5},{5,1},{9,13},{13,9},{2,6},{6,2},{1... | collective-permute-start | bytes 1572872 | tf_op jit(solution)/shard_map/ppermute | solution.py:17
  36.7 7.9 %collective-permute-done.4.refs_1_ = bf16[16,8,2048]{2,1,0:T(8,128)(2,1)} collective-permute-done((bf16[16,8,2048]{2,1,0:T(8,128)(2,1)S(1)}, bf16[16,8,2048]{2,1,0:T(8,128)(2,1)}, u32[]{:S(2)}, u32[]{:S(2)}) %collective-permute-start.4) | collective-permute-done | bytes 524320 | tf_op jit(solution)/shard_map/ppermute | solution.py:17
  44.6 0.0 collective-permute-start.8
  44.6 9.5 %collective-permute-done.7.refs_5_ = bf16[16,8,2048]{2,1,0:T(8,128)(2,1)} collective-permute-done((bf16[16,8,2048]{2,1,0:T(8,128)(2,1)S(1)}, bf16[16,8,2048]{2,1,0:T(8,128)(2,1)}, u32[]{:S(2)}, u32[]{:S(2)}) %collective-permute-start.7) | collective-permute-done | bytes 524320 | tf_op jit(solution)/shard_map/ppermute | solution.py:17
  54.1 0.0 collective-permute-start.6
  54.1 0.0 collective-permute-done.5.refs_2_
  54.1 0.0 copy-start.9
  54.1 0.5 collective-permute-start.9
  54.6 0.3 copy-done.9
  54.9 3.2 %collective-permute-done.12.refs_4_ = bf16[16,8,2048]{2,1,0:T(8,128)(2,1)S(1)} collective-permute-done((bf16[16,8,2048]{2,1,0:T(8,128)(2,1)}, bf16[16,8,2048]{2,1,0:T(8,128)(2,1)S(1)}, u32[]{:S(2)}, u32[]{:S(2)}) %collective-permute-start.12) | collective-permute-done | bytes 524320 | tf_op jit(solution)/shard_map/ppermute | solution.py:17
  58.1 0.0 copy-start.1
  58.1 1.6 %collective-permute-start.13 = (bf16[16,8,2048]{2,1,0:T(8,128)(2,1)S(1)}, bf16[16,8,2048]{2,1,0:T(8,128)(2,1)S(1)}, u32[]{:S(2)}, u32[]{:S(2)}) collective-permute-start(bf16[16,8,2048]{2,1,0:T(8,128)(2,1)S(1)} %collective-permute-done.12.refs_4_), channel_id=1, source_target_pairs={{0,2},{1,3},{2,0},{3,1},{4,6},{5,7},{6,4},{7,5},{8,10},{9,11},{10,... | collective-permute-start | bytes 1572872 | tf_op jit(solution)/shard_map/ppermute | solution.py:17
  59.7 0.0 collective-permute-done.2.refs_0_
  59.7 0.0 copy-start.2
  59.7 0.4 collective-permute-start.3
  60.1 0.0 copy-done
  60.1 0.6 gather_fusion.1
  60.7 0.1 copy.19
  60.8 0.1 gather.13
  60.9 0.5 fusion.1.pos_ref
  61.4 0.0 collective-permute-done.8.refs_6_
  61.4 0.0 collective-permute-done.6.refs_3_
  61.5 0.0 collective-permute-done.9.refs_7_
  61.5 0.0 copy-done.7
  61.5 0.0 copy-done.8
  61.5 6.5 %shard_map.149.refs_9_ = f32[16,8,2048]{2,1,0:T(8,128)} custom-call(s32[128]{0:T(128)} %fusion.1.pos_ref, bf16[16,8,2048]{2,1,0:T(8,128)(2,1)} %copy-done.7, bf16[16,8,2048]{2,1,0:T(8,128)(2,1)} %collective-permute-done.4.refs_1_, bf16[16,8,2048]{2,1,0:T(8,128)(2,1)} %copy-done.9, bf16[16,8,2048]{2,1,0:T(8,128)(2,1)} %collective-permute-done.6.refs_3_, ...), custom_call_target="tpu_custom_call" | custom-call | tf_op jit(solution)/shard_map/pallas_call | solution.py:180
  68.0 4.9 %collective-permute-done.13.refs_5_ = bf16[16,8,2048]{2,1,0:T(8,128)(2,1)S(1)} collective-permute-done((bf16[16,8,2048]{2,1,0:T(8,128)(2,1)S(1)}, bf16[16,8,2048]{2,1,0:T(8,128)(2,1)S(1)}, u32[]{:S(2)}, u32[]{:S(2)}) %collective-permute-start.13) | collective-permute-done | bytes 524320 | tf_op jit(solution)/shard_map/ppermute | solution.py:17
  72.9 0.0 copy-start.3
  72.9 0.0 collective-permute-start.14
  72.9 0.5 collective-permute-start.15
  73.4 9.5 %collective-permute-done.3.refs_1_ = bf16[16,8,2048]{2,1,0:T(8,128)(2,1)S(1)} collective-permute-done((bf16[16,8,2048]{2,1,0:T(8,128)(2,1)S(1)}, bf16[16,8,2048]{2,1,0:T(8,128)(2,1)S(1)}, u32[]{:S(2)}, u32[]{:S(2)}) %collective-permute-start.3) | collective-permute-done | bytes 524320 | tf_op jit(solution)/shard_map/ppermute | solution.py:17
  83.0 0.0 copy-start.4
  83.0 0.0 collective-permute-start.10
  83.0 0.5 collective-permute-start.11
  83.5 0.0 copy-done.10
  83.5 0.6 gather_fusion
  84.1 0.1 copy.18
  84.1 0.1 gather.11
  84.3 0.5 fusion.pos_ref
  84.8 0.0 collective-permute-done.14.refs_6_
  84.8 0.0 collective-permute-done.15.refs_7_
  84.8 0.0 copy-start.6
  84.8 0.2 collective-permute-done.10.refs_2_
  85.0 0.7 collective-permute-done.11.refs_3_
  85.8 0.0 copy-done.1
  85.8 0.0 copy-done.2
  85.8 0.0 copy-done.3
  85.8 0.0 copy-done.4
  85.8 0.0 copy-done.5
  85.8 0.0 copy-done.6
  85.8 7.4 %shard_map.150 = (bf16[16,8,2048]{2,1,0:T(8,128)(2,1)}, f32[8,2048]{1,0:T(8,128)}, f32[8,2048]{1,0:T(8,128)}) custom-call(s32[128]{0:T(128)} %fusion.pos_ref, bf16[16,8,2048]{2,1,0:T(8,128)(2,1)} %copy-done.2, bf16[16,8,2048]{2,1,0:T(8,128)(2,1)} %copy-done.4, bf16[16,8,2048]{2,1,0:T(8,128)(2,1)} %collective-permute-done.10.refs_2_, ...), custom_call_target="tpu_custom_call" | custom-call | tf_op jit(solution)/shard_map/pallas_call | solution.py:180
  (2 shorter events, 0.0 us)
Async XLA Ops:
  0.6 59.5 %copy-start = (s32[4,1,16,4]{2,3,1,0:T(4,128)S(1)}, s32[4,1,16,4]{2,3,1,0:T(4,128)}, u32[]{:S(2)}) copy-start(s32[4,1,16,4]{2,3,1,0:T(4,128)} %param.22) | copy-start | bytes 3076
  0.6 82.8 %copy-start.10 = (s32[2]{0:T(128)S(1)}, s32[2]{0:T(128)}, u32[]{:S(2)}) copy-start(s32[2]{0:T(128)} %constant.101) | copy-start | bytes 28
  3.4 26.3 %collective-permute-start = (bf16[16,8,2048]{2,1,0:T(8,128)(2,1)}, bf16[16,8,2048]{2,1,0:T(8,128)(2,1)S(1)}, u32[]{:S(2)}, u32[]{:S(2)}) collective-permute-start(bf16[16,8,2048]{2,1,0:T(8,128)(2,1)} %get-tuple-element.15), channel_id=1, source_target_pairs={{0,4},{4,0},{8,12},{12,8},{1,5},{5,1},{9,13},{13,9},{2,6},{6,2},{1... | collective-permute-start | bytes 1572872 | tf_op jit(solution)/shard_map/ppermute | solution.py:17
  6.4 25.8 %collective-permute-start.1 = (bf16[16,8,2048]{2,1,0:T(8,128)(2,1)}, bf16[16,8,2048]{2,1,0:T(8,128)(2,1)S(1)}, u32[]{:S(2)}, u32[]{:S(2)}) collective-permute-start(bf16[16,8,2048]{2,1,0:T(8,128)(2,1)} %get-tuple-element.16), channel_id=1, source_target_pairs={{0,8},{4,12},{8,0},{12,4},{1,9},{5,13},{9,1},{13,5},{2,10},{6,14},... | collective-permute-start | bytes 1572872 | tf_op jit(solution)/shard_map/ppermute | solution.py:17
  29.7 31.8 %copy-start.7 = (bf16[16,8,2048]{2,1,0:T(8,128)(2,1)}, bf16[16,8,2048]{2,1,0:T(8,128)(2,1)S(1)}, u32[]{:S(2)}) copy-start(bf16[16,8,2048]{2,1,0:T(8,128)(2,1)S(1)} %collective-permute-done.refs_0_) | copy-start | bytes 1572868
  29.7 15.0 %collective-permute-start.4 = (bf16[16,8,2048]{2,1,0:T(8,128)(2,1)S(1)}, bf16[16,8,2048]{2,1,0:T(8,128)(2,1)}, u32[]{:S(2)}, u32[]{:S(2)}) collective-permute-start(bf16[16,8,2048]{2,1,0:T(8,128)(2,1)S(1)} %collective-permute-done.refs_0_), channel_id=1, source_target_pairs={{0,2},{1,3},{2,0},{3,1},{4,6},{5,7},{6,4},{7,5},{8,10},{9,11},{10,... | collective-permute-start | bytes 1572872 | tf_op jit(solution)/shard_map/ppermute | solution.py:17
  31.3 22.8 %collective-permute-start.5 = (bf16[16,8,2048]{2,1,0:T(8,128)(2,1)S(1)}, bf16[16,8,2048]{2,1,0:T(8,128)(2,1)S(1)}, u32[]{:S(2)}, u32[]{:S(2)}) collective-permute-start(bf16[16,8,2048]{2,1,0:T(8,128)(2,1)S(1)} %collective-permute-done.refs_0_), channel_id=1, source_target_pairs={{0,1},{1,0},{2,3},{3,2},{4,5},{5,4},{6,7},{7,6},{8,9},{9,8},{10,11... | collective-permute-start | bytes 1572872 | tf_op jit(solution)/shard_map/ppermute | solution.py:17
  32.2 29.3 %copy-start.8 = (bf16[16,8,2048]{2,1,0:T(8,128)(2,1)}, bf16[16,8,2048]{2,1,0:T(8,128)(2,1)S(1)}, u32[]{:S(2)}) copy-start(bf16[16,8,2048]{2,1,0:T(8,128)(2,1)S(1)} %collective-permute-done.1.refs_4_) | copy-start | bytes 1572868
  32.2 21.9 %collective-permute-start.7 = (bf16[16,8,2048]{2,1,0:T(8,128)(2,1)S(1)}, bf16[16,8,2048]{2,1,0:T(8,128)(2,1)}, u32[]{:S(2)}, u32[]{:S(2)}) collective-permute-start(bf16[16,8,2048]{2,1,0:T(8,128)(2,1)S(1)} %collective-permute-done.1.refs_4_), channel_id=1, source_target_pairs={{0,2},{1,3},{2,0},{3,1},{4,6},{5,7},{6,4},{7,5},{8,10},{9,11},{10,... | collective-permute-start | bytes 1572872 | tf_op jit(solution)/shard_map/ppermute | solution.py:17
  33.7 24.4 %collective-permute-start.12 = (bf16[16,8,2048]{2,1,0:T(8,128)(2,1)}, bf16[16,8,2048]{2,1,0:T(8,128)(2,1)S(1)}, u32[]{:S(2)}, u32[]{:S(2)}) collective-permute-start(bf16[16,8,2048]{2,1,0:T(8,128)(2,1)} %get-tuple-element.20), channel_id=1, source_target_pairs={{0,8},{4,12},{8,0},{12,4},{1,9},{5,13},{9,1},{13,5},{2,10},{6,14},... | collective-permute-start | bytes 1572872 | tf_op jit(solution)/shard_map/ppermute | solution.py:17
  34.0 25.7 %collective-permute-start.2 = (bf16[16,8,2048]{2,1,0:T(8,128)(2,1)}, bf16[16,8,2048]{2,1,0:T(8,128)(2,1)S(1)}, u32[]{:S(2)}, u32[]{:S(2)}) collective-permute-start(bf16[16,8,2048]{2,1,0:T(8,128)(2,1)} %get-tuple-element.17), channel_id=1, source_target_pairs={{0,4},{4,0},{8,12},{12,8},{1,5},{5,1},{9,13},{13,9},{2,6},{6,2},{1... | collective-permute-start | bytes 1572872 | tf_op jit(solution)/shard_map/ppermute | solution.py:17
  44.6 16.8 %collective-permute-start.8 = (bf16[16,8,2048]{2,1,0:T(8,128)(2,1)S(1)}, bf16[16,8,2048]{2,1,0:T(8,128)(2,1)}, u32[]{:S(2)}, u32[]{:S(2)}) collective-permute-start(bf16[16,8,2048]{2,1,0:T(8,128)(2,1)S(1)} %collective-permute-done.1.refs_4_), channel_id=1, source_target_pairs={{0,1},{1,0},{2,3},{3,2},{4,5},{5,4},{6,7},{7,6},{8,9},{9,8},{10,11... | collective-permute-start | bytes 1572872 | tf_op jit(solution)/shard_map/ppermute | solution.py:17
  54.1 7.3 %collective-permute-start.6 = (bf16[16,8,2048]{2,1,0:T(8,128)(2,1)}, bf16[16,8,2048]{2,1,0:T(8,128)(2,1)}, u32[]{:S(2)}, u32[]{:S(2)}) collective-permute-start(bf16[16,8,2048]{2,1,0:T(8,128)(2,1)} %collective-permute-done.4.refs_1_), channel_id=1, source_target_pairs={{0,1},{1,0},{2,3},{3,2},{4,5},{5,4},{6,7},{7,6},{8,9},{9,8},{10,11... | collective-permute-start | bytes 1572872 | tf_op jit(solution)/shard_map/ppermute | solution.py:17
  54.1 0.8 copy-start.9
  54.1 7.3 %collective-permute-start.9 = (bf16[16,8,2048]{2,1,0:T(8,128)(2,1)}, bf16[16,8,2048]{2,1,0:T(8,128)(2,1)}, u32[]{:S(2)}, u32[]{:S(2)}) collective-permute-start(bf16[16,8,2048]{2,1,0:T(8,128)(2,1)} %collective-permute-done.7.refs_5_), channel_id=1, source_target_pairs={{0,1},{1,0},{2,3},{3,2},{4,5},{5,4},{6,7},{7,6},{8,9},{9,8},{10,11... | collective-permute-start | bytes 1572872 | tf_op jit(solution)/shard_map/ppermute | solution.py:17
  58.1 27.7 %copy-start.1 = (bf16[16,8,2048]{2,1,0:T(8,128)(2,1)}, bf16[16,8,2048]{2,1,0:T(8,128)(2,1)S(1)}, u32[]{:S(2)}) copy-start(bf16[16,8,2048]{2,1,0:T(8,128)(2,1)S(1)} %collective-permute-done.12.refs_4_) | copy-start | bytes 1572868
  58.1 14.8 %collective-permute-start.13 = (bf16[16,8,2048]{2,1,0:T(8,128)(2,1)S(1)}, bf16[16,8,2048]{2,1,0:T(8,128)(2,1)S(1)}, u32[]{:S(2)}, u32[]{:S(2)}) collective-permute-start(bf16[16,8,2048]{2,1,0:T(8,128)(2,1)S(1)} %collective-permute-done.12.refs_4_), channel_id=1, source_target_pairs={{0,2},{1,3},{2,0},{3,1},{4,6},{5,7},{6,4},{7,5},{8,10},{9,11},{10,... | collective-permute-start | bytes 1572872 | tf_op jit(solution)/shard_map/ppermute | solution.py:17
  59.7 26.1 %copy-start.2 = (bf16[16,8,2048]{2,1,0:T(8,128)(2,1)}, bf16[16,8,2048]{2,1,0:T(8,128)(2,1)S(1)}, u32[]{:S(2)}) copy-start(bf16[16,8,2048]{2,1,0:T(8,128)(2,1)S(1)} %collective-permute-done.2.refs_0_) | copy-start | bytes 1572868
  59.7 23.3 %collective-permute-start.3 = (bf16[16,8,2048]{2,1,0:T(8,128)(2,1)S(1)}, bf16[16,8,2048]{2,1,0:T(8,128)(2,1)S(1)}, u32[]{:S(2)}, u32[]{:S(2)}) collective-permute-start(bf16[16,8,2048]{2,1,0:T(8,128)(2,1)S(1)} %collective-permute-done.2.refs_0_), channel_id=1, source_target_pairs={{0,2},{1,3},{2,0},{3,1},{4,6},{5,7},{6,4},{7,5},{8,10},{9,11},{10,... | collective-permute-start | bytes 1572872 | tf_op jit(solution)/shard_map/ppermute | solution.py:17
  72.9 12.8 %copy-start.3 = (bf16[16,8,2048]{2,1,0:T(8,128)(2,1)}, bf16[16,8,2048]{2,1,0:T(8,128)(2,1)S(1)}, u32[]{:S(2)}) copy-start(bf16[16,8,2048]{2,1,0:T(8,128)(2,1)S(1)} %collective-permute-done.13.refs_5_) | copy-start | bytes 1572868
  72.9 11.9 %collective-permute-start.14 = (bf16[16,8,2048]{2,1,0:T(8,128)(2,1)S(1)}, bf16[16,8,2048]{2,1,0:T(8,128)(2,1)S(1)}, u32[]{:S(2)}, u32[]{:S(2)}) collective-permute-start(bf16[16,8,2048]{2,1,0:T(8,128)(2,1)S(1)} %collective-permute-done.12.refs_4_), channel_id=1, source_target_pairs={{0,1},{1,0},{2,3},{3,2},{4,5},{5,4},{6,7},{7,6},{8,9},{9,8},{10,11... | collective-permute-start | bytes 1572872 | tf_op jit(solution)/shard_map/ppermute | solution.py:17
  72.9 11.9 %collective-permute-start.15 = (bf16[16,8,2048]{2,1,0:T(8,128)(2,1)S(1)}, bf16[16,8,2048]{2,1,0:T(8,128)(2,1)S(1)}, u32[]{:S(2)}, u32[]{:S(2)}) collective-permute-start(bf16[16,8,2048]{2,1,0:T(8,128)(2,1)S(1)} %collective-permute-done.13.refs_5_), channel_id=1, source_target_pairs={{0,1},{1,0},{2,3},{3,2},{4,5},{5,4},{6,7},{7,6},{8,9},{9,8},{10,11... | collective-permute-start | bytes 1572872 | tf_op jit(solution)/shard_map/ppermute | solution.py:17
  83.0 2.8 %copy-start.4 = (bf16[16,8,2048]{2,1,0:T(8,128)(2,1)}, bf16[16,8,2048]{2,1,0:T(8,128)(2,1)S(1)}, u32[]{:S(2)}) copy-start(bf16[16,8,2048]{2,1,0:T(8,128)(2,1)S(1)} %collective-permute-done.3.refs_1_) | copy-start | bytes 1572868
  83.0 2.0 %collective-permute-start.10 = (bf16[16,8,2048]{2,1,0:T(8,128)(2,1)S(1)}, bf16[16,8,2048]{2,1,0:T(8,128)(2,1)}, u32[]{:S(2)}, u32[]{:S(2)}) collective-permute-start(bf16[16,8,2048]{2,1,0:T(8,128)(2,1)S(1)} %collective-permute-done.2.refs_0_), channel_id=1, source_target_pairs={{0,1},{1,0},{2,3},{3,2},{4,5},{5,4},{6,7},{7,6},{8,9},{9,8},{10,11... | collective-permute-start | bytes 1572872 | tf_op jit(solution)/shard_map/ppermute | solution.py:17
  83.0 2.8 %collective-permute-start.11 = (bf16[16,8,2048]{2,1,0:T(8,128)(2,1)S(1)}, bf16[16,8,2048]{2,1,0:T(8,128)(2,1)}, u32[]{:S(2)}, u32[]{:S(2)}) collective-permute-start(bf16[16,8,2048]{2,1,0:T(8,128)(2,1)S(1)} %collective-permute-done.3.refs_1_), channel_id=1, source_target_pairs={{0,1},{1,0},{2,3},{3,2},{4,5},{5,4},{6,7},{7,6},{8,9},{9,8},{10,11... | collective-permute-start | bytes 1572872 | tf_op jit(solution)/shard_map/ppermute | solution.py:17
  84.8 1.0 %copy-start.5 = (bf16[16,8,2048]{2,1,0:T(8,128)(2,1)}, bf16[16,8,2048]{2,1,0:T(8,128)(2,1)S(1)}, u32[]{:S(2)}) copy-start(bf16[16,8,2048]{2,1,0:T(8,128)(2,1)S(1)} %collective-permute-done.14.refs_6_) | copy-start | bytes 1572868
  84.8 1.0 %copy-start.6 = (bf16[16,8,2048]{2,1,0:T(8,128)(2,1)}, bf16[16,8,2048]{2,1,0:T(8,128)(2,1)S(1)}, u32[]{:S(2)}) copy-start(bf16[16,8,2048]{2,1,0:T(8,128)(2,1)S(1)} %collective-permute-done.15.refs_7_) | copy-start | bytes 1572868

commit v7 on v6

--- a/solution.py
+++ b/solution.py
@@ -45,22 +45,14 @@
     return held
 
 
-def relative_position(n, me, bits):
-    d = n ^ me
-    pos = jnp.zeros_like(d)
-    for s, bit in enumerate(reversed(range(bits))):
-        pos = pos | (((d >> bit) & 1) << s)
-    return pos
-
-
-def stage_kernel(pos_ref, *refs, n_pieces, stage, n_pos, final, has_rec):
+def stage_kernel(bi_ref, *refs, n_pieces, stage, n_pos, final, has_rec):
     n_rounds = len(stage)
     it = iter(refs)
     piece_hbm = [next(it) for _ in range(n_pieces)]
     w_hbm = next(it)
     rec_hbm = next(it) if has_rec else None
     if final:
-        err_hbm, surr_hbm, lv_hbm, la_hbm, alpha_hbm, rho_hbm, beta_hbm = [next(it) for _ in range(7)]
+        scan_hbm = [next(it) for _ in range(7)]
         cur_ref, lv_out, la_out = next(it), next(it), next(it)
     else:
         out_ref = next(it)
@@ -68,14 +60,15 @@
     w_buf = next(it)
     blocks = next(it)
     sem = next(it)
-    if has_rec:
-        rec_buf = next(it)
-    if final:
-        err_buf, surr_buf, lv_buf, la_buf, alpha_buf, rho_buf, beta_buf = [next(it) for _ in range(7)]
+    rec_buf = next(it)
+    if final:
+        scan_buf = [next(it) for _ in range(7)]
 
     steps, batch, width = piece_hbm[0].shape
     local_blocks, nnz, side = w_buf.shape[1], w_buf.shape[2], w_buf.shape[3]
     rows = steps * batch
+    bits = n_pos.bit_length() - 1
+    me = lax.axis_index("neuron")
     n_sem = 0
 
     def start(src, dst):
@@ -85,63 +78,70 @@
         copy.start()
         return copy
 
-    piece_cp = [start(piece_hbm[k], piece_buf[k]) for k in range(n_pieces)]
-    w_cp = [start(w_hbm.at[rnd, 0], w_buf.at[ri]) for ri, rnd in enumerate(stage)]
-    rec_cp = start(rec_hbm, rec_buf) if has_rec else None
-    if final:
-        scan_cp = [
-            start(src, dst)
-            for src, dst in zip(
-                (err_hbm, surr_hbm, lv_hbm, la_hbm, alpha_hbm, rho_hbm, beta_hbm),
-                (err_buf, surr_buf, lv_buf, la_buf, alpha_buf, rho_buf, beta_buf),
-            )
-        ]
-
-    for ri in range(n_rounds):
+    piece_cp, w_cp = [], []
+    rec_cp = None
+    scan_cp = []
+    for ri, rnd in enumerate(stage):
+        piece_cp += [start(piece_hbm[ri * n_pos + p], piece_buf[ri * n_pos + p]) for p in range(n_pos)]
+        w_cp.append(start(w_hbm.at[rnd, 0], w_buf.at[ri]))
+        if ri == 0 and has_rec:
+            rec_cp = start(rec_hbm, rec_buf)
+    if final:
+        scan_cp = [start(src, dst) for src, dst in zip(scan_hbm, scan_buf)]
+
+    for ri, rnd in enumerate(stage):
         for p in range(n_pos):
             k = ri * n_pos + p
             piece_cp[k].wait()
             for i in range(local_blocks):
                 x = piece_buf[k][:, :, i * side:(i + 1) * side].astype(jnp.float32)
-                blocks[(ri * n_pos + p) * local_blocks + i] = x.reshape(rows, side).astype(jnp.bfloat16)
-    if has_rec:
-        rec_cp.wait()
-    for ri in range(n_rounds):
+                blocks[p * local_blocks + i] = x.reshape(rows, side).astype(jnp.bfloat16)
         w_cp[ri].wait()
-    if final:
-        for copy in scan_cp:
-            copy.wait()
-    for j in range(local_blocks):
-        cols = slice(j * side, (j + 1) * side)
-        if has_rec:
-            acc = rec_buf[:, :, cols].reshape(rows, side)
-        else:
-            acc = jnp.zeros((rows, side), jnp.float32)
-        for ri in range(n_rounds):
+        if ri == 0 and has_rec:
+            rec_cp.wait()
+        last = ri == n_rounds - 1
+        if last and final:
+            for copy in scan_cp:
+                copy.wait()
+            err_buf, surr_buf, lv_buf, la_buf, alpha_buf, rho_buf, beta_buf = scan_buf
+        for j in range(local_blocks):
+            cols = slice(j * side, (j + 1) * side)
+            if ri == 0 and not has_rec:
+                acc = jnp.zeros((rows, side), jnp.float32)
+            else:
+                acc = rec_buf[:, :, cols].reshape(rows, side)
             for k in range(nnz):
-                x = blocks[ri * n_pos * local_blocks + pos_ref[(ri * local_blocks + j) * nnz + k]]
+                idx = bi_ref[rnd, 0, j, k]
+                d = (idx // local_blocks) ^ me
+                rel = 0
+                for s_, bit in enumerate(reversed(range(bits))):
+                    rel = rel | (((d >> bit) & 1) << s_)
+                x = blocks[rel * local_blocks + idx % local_blocks]
                 acc = acc + jnp.dot(x, w_buf[ri, j, k], preferred_element_type=jnp.float32)
-        rec = acc.reshape(steps, batch, side)
-        if not final:
-            out_ref[:, :, cols] = rec
-            continue
-        alpha = alpha_buf[:, cols]
-        rho = rho_buf[:, cols]
-        beta = beta_buf[:, cols]
-        lv_now = lv_buf[:, cols]
-        la_now = la_buf[:, cols]
-        for t in reversed(range(steps)):
-            surr = surr_buf[t, :, cols]
-            total = err_buf[t, :, cols] + rec[t] - lv_now + la_now
-            cur_ref[t, :, cols] = lv_now.astype(cur_ref.dtype)
-            lv_next = alpha * lv_now + surr * total
-            la_next = rho * la_now - beta * surr * total
-            lv_now, la_now = lv_next, la_next
-        lv_out[:, cols] = lv_now
-        la_out[:, cols] = la_now
-
-
-def stage_contrib(pos, pieces, weights, stage, n_pos, rec, scan_args):
+            rec = acc.reshape(steps, batch, side)
+            if not last:
+                rec_buf[:, :, cols] = rec
+                continue
+            if not final:
+                out_ref[:, :, cols] = rec
+                continue
+            alpha = alpha_buf[:, cols]
+            rho = rho_buf[:, cols]
+            beta = beta_buf[:, cols]
+            lv_now = lv_buf[:, cols]
+            la_now = la_buf[:, cols]
+            for t in reversed(range(steps)):
+                surr = surr_buf[t, :, cols]
+                total = err_buf[t, :, cols] + rec[t] - lv_now + la_now
+                cur_ref[t, :, cols] = lv_now.astype(cur_ref.dtype)
+                lv_next = alpha * lv_now + surr * total
+                la_next = rho * la_now - beta * surr * total
+                lv_now, la_now = lv_next, la_next
+            lv_out[:, cols] = lv_now
+            la_out[:, cols] = la_now
+
+
+def stage_contrib(block_index, pieces, weights, stage, n_pos, rec, scan_args):
     steps, batch, local = pieces[0].shape
     _, _, local_blocks, nnz, side, _ = weights.shape
     n_rounds = len(stage)
@@ -151,13 +151,13 @@
     scratch = [pltpu.VMEM(p.shape, p.dtype) for p in pieces]
     scratch += [
         pltpu.VMEM((n_rounds, local_blocks, nnz, side, side), weights.dtype),
-        pltpu.VMEM((n_rounds * n_pos * local_blocks, steps * batch, side), jnp.bfloat16),
+        pltpu.VMEM((n_pos * local_blocks, steps * batch, side), jnp.bfloat16),
     ]
     n_sem = len(pieces) + n_rounds + (1 if has_rec else 0) + (7 if final else 0)
     scratch.append(pltpu.SemaphoreType.DMA((n_sem,)))
+    scratch.append(pltpu.VMEM((steps, batch, local), jnp.float32))
     if has_rec:
         operands.append(rec)
-        scratch.append(pltpu.VMEM(rec.shape, rec.dtype))
     if final:
         err_grad, surrogate, lv_end, la_end, alpha, rho, beta = scan_args
         rows = [a.reshape(1, local) for a in (alpha, rho, beta)]
@@ -183,7 +183,7 @@
         out_specs=out_specs,
         scratch_shapes=scratch,
         out_shape=out_shape,
-    )(pos, *operands)
+    )(block_index, *operands)
 
 
 def per_device(
@@ -197,7 +197,6 @@
     levels = lax.axis_size("area").bit_length() - 1
     nbits = lax.axis_size("neuron").bit_length() - 1
     n_pos = 1 << nbits
-    me_neuron = lax.axis_index("neuron")
     slices = send_slices(window, delays, rounds, levels, steps)
     stages = [list(range(f, min(f + 2, rounds))) for f in range(0, rounds, 2)]
     arrived = []
@@ -214,15 +213,10 @@
         chunks = []
         for rnd in stage:
             chunks += gather_neuron(arrived[rnd], rec)
-        idx = block_index[jnp.array(stage), 0]
-        owner = idx // local_blocks
-        pos = relative_position(owner, me_neuron, nbits) * local_blocks + idx % local_blocks
         scan_args = None
         if si == len(stages) - 1:
             scan_args = (err_grad, surrogate, lv_end, la_end, alpha, rho, beta)
-        rec = stage_contrib(
-            pos.reshape(-1).astype(jnp.int32), chunks, weights, stage, n_pos, rec, scan_args
-        )
+        rec = stage_contrib(block_index, chunks, weights, stage, n_pos, rec, scan_args)
     return rec
 
 

time: 93.3 us -> 94.3 us (1.011)
  waiting for transfers between devices: 57.5 us -> 58.6 us
  other arithmetic: 1.08 us -> 0 us
    unnamed x22 -> x23, local copies, waits for them, and re-layouts: 0.34 us -> 2.54 us
    gather x6 -> x0, local copies, waits for them, and re-layouts: 1.53 us -> none  [per_device(): idx = block_index[jnp.array(stage), 0]]
    ppermute x16, waiting for transfers between devices: 57.5 us -> 58.6 us  [swap(): return lax.ppermute(value, axis, pairs)]
    add x2 -> x0, other arithmetic: 1.08 us -> none  [per_device(): relative_position(owner, me_neuron, nbits) * local_blocks]
  transfers between devices with their start and end apart: 16 -> 16, of which waited for: 9 -> 9; matrix products, arithmetic and copies ran while one was open for 3% -> 1% of each run, Pallas kernels for 7% -> 7%
where the time goes in v7:
time: 94.3 us; the launch traced here: 93.9 us
  waiting for transfers between devices  58.6 us (62%)
  Pallas kernels  16.6 us (18%)
  starting transfers between devices  15.4 us (16%)
  local copies, waits for them, and re-layouts  2.54 us (3%)
    ppermute x16, waiting for transfers between devices, swap(): return lax.ppermute(value, axis, pairs)  58.6 us
    ppermute x16, starting transfers between devices, swap(): return lax.ppermute(value, axis, pairs)  15.4 us
    pallas_call x2, Pallas kernels, stage_contrib(): pl.pallas_call(kernel, in_specs=[SMEM] + [ANY] * len(operands), out_specs...  13.9 us
    pallas_call x1, Pallas kernels, send_slices(): pl.pallas_call(kernel, in_specs=[SMEM, VMEM], out_specs=[VMEM] * rounds,...  2.71 us
    unnamed x23, local copies, waits for them, and re-layouts  2.54 us
  transfers between devices with their start and end apart: 16, of which 9 were waited for; matrix products, arithmetic and copies ran while one was open for 1% of the time, Pallas kernels for 7%

profile of v7, /device:TPU:0, one launch (start us, length us, event | category | flops | bytes accessed | tf_op | source)
XLA Modules:
  0.0 93.9 jit_solution(15664429326776260506)
XLA Ops:
  0.6 2.7 %shard_map.130 = (bf16[16,8,2048]{2,1,0:T(8,128)(2,1)}, bf16[16,8,2048]{2,1,0:T(8,128)(2,1)}, bf16[16,8,2048]{2,1,0:T(8,128)(2,1)}, bf16[16,8,2048]{2,1,0:T(8,128)(2,1)}) custom-call(s32[4,4]{1,0:T(4,128)} %delays_ref.1, bf16[32,8,2048]{2,1,0:T(8,128)(2,1)} %window_ref.1), custom_call_target="tpu_custom_call" | custom-call | tf_op jit(solution)/shard_map/pallas_call | solution.py:30
  3.3 3.0 %collective-permute-start = (bf16[16,8,2048]{2,1,0:T(8,128)(2,1)}, bf16[16,8,2048]{2,1,0:T(8,128)(2,1)S(1)}, u32[]{:S(2)}, u32[]{:S(2)}) collective-permute-start(bf16[16,8,2048]{2,1,0:T(8,128)(2,1)} %get-tuple-element.15), channel_id=1, source_target_pairs={{0,4},{4,0},{8,12},{12,8},{1,5},{5,1},{9,13},{13,9},{2,6},{6,2},{1... | collective-permute-start | bytes 1572872 | tf_op jit(solution)/shard_map/ppermute | solution.py:17
  6.4 2.6 %collective-permute-start.1 = (bf16[16,8,2048]{2,1,0:T(8,128)(2,1)}, bf16[16,8,2048]{2,1,0:T(8,128)(2,1)S(1)}, u32[]{:S(2)}, u32[]{:S(2)}) collective-permute-start(bf16[16,8,2048]{2,1,0:T(8,128)(2,1)} %get-tuple-element.16), channel_id=1, source_target_pairs={{0,8},{4,12},{8,0},{12,4},{1,9},{5,13},{9,1},{13,5},{2,10},{6,14},... | collective-permute-start | bytes 1572872 | tf_op jit(solution)/shard_map/ppermute | solution.py:17
  9.0 20.7 %collective-permute-done.refs_0_ = bf16[16,8,2048]{2,1,0:T(8,128)(2,1)S(1)} collective-permute-done((bf16[16,8,2048]{2,1,0:T(8,128)(2,1)}, bf16[16,8,2048]{2,1,0:T(8,128)(2,1)S(1)}, u32[]{:S(2)}, u32[]{:S(2)}) %collective-permute-start) | collective-permute-done | bytes 524320 | tf_op jit(solution)/shard_map/ppermute | solution.py:17
  29.6 0.0 copy-start.8
  29.6 1.7 %collective-permute-start.4 = (bf16[16,8,2048]{2,1,0:T(8,128)(2,1)S(1)}, bf16[16,8,2048]{2,1,0:T(8,128)(2,1)}, u32[]{:S(2)}, u32[]{:S(2)}) collective-permute-start(bf16[16,8,2048]{2,1,0:T(8,128)(2,1)S(1)} %collective-permute-done.refs_0_), channel_id=1, source_target_pairs={{0,2},{1,3},{2,0},{3,1},{4,6},{5,7},{6,4},{7,5},{8,10},{9,11},{10,... | collective-permute-start | bytes 1572872 | tf_op jit(solution)/shard_map/ppermute | solution.py:17
  31.3 0.0 collective-permute-start.5
  31.3 0.9 collective-permute-done.1.refs_4_
  32.1 0.0 copy-start.9
  32.1 1.5 %collective-permute-start.7 = (bf16[16,8,2048]{2,1,0:T(8,128)(2,1)S(1)}, bf16[16,8,2048]{2,1,0:T(8,128)(2,1)}, u32[]{:S(2)}, u32[]{:S(2)}) collective-permute-start(bf16[16,8,2048]{2,1,0:T(8,128)(2,1)S(1)} %collective-permute-done.1.refs_4_), channel_id=1, source_target_pairs={{0,2},{1,3},{2,0},{3,1},{4,6},{5,7},{6,4},{7,5},{8,10},{9,11},{10,... | collective-permute-start | bytes 1572872 | tf_op jit(solution)/shard_map/ppermute | solution.py:17
  33.6 0.3 collective-permute-start.12
  34.0 2.7 %collective-permute-start.2 = (bf16[16,8,2048]{2,1,0:T(8,128)(2,1)}, bf16[16,8,2048]{2,1,0:T(8,128)(2,1)S(1)}, u32[]{:S(2)}, u32[]{:S(2)}) collective-permute-start(bf16[16,8,2048]{2,1,0:T(8,128)(2,1)} %get-tuple-element.17), channel_id=1, source_target_pairs={{0,4},{4,0},{8,12},{12,8},{1,5},{5,1},{9,13},{13,9},{2,6},{6,2},{1... | collective-permute-start | bytes 1572872 | tf_op jit(solution)/shard_map/ppermute | solution.py:17
  36.7 7.9 %collective-permute-done.4.refs_1_ = bf16[16,8,2048]{2,1,0:T(8,128)(2,1)} collective-permute-done((bf16[16,8,2048]{2,1,0:T(8,128)(2,1)S(1)}, bf16[16,8,2048]{2,1,0:T(8,128)(2,1)}, u32[]{:S(2)}, u32[]{:S(2)}) %collective-permute-start.4) | collective-permute-done | bytes 524320 | tf_op jit(solution)/shard_map/ppermute | solution.py:17
  44.6 0.0 collective-permute-start.8
  44.6 9.5 %collective-permute-done.7.refs_5_ = bf16[16,8,2048]{2,1,0:T(8,128)(2,1)} collective-permute-done((bf16[16,8,2048]{2,1,0:T(8,128)(2,1)S(1)}, bf16[16,8,2048]{2,1,0:T(8,128)(2,1)}, u32[]{:S(2)}, u32[]{:S(2)}) %collective-permute-start.7) | collective-permute-done | bytes 524320 | tf_op jit(solution)/shard_map/ppermute | solution.py:17
  54.1 0.0 collective-permute-start.6
  54.1 0.0 collective-permute-done.5.refs_2_
  54.1 0.0 copy-start.10
  54.1 0.5 collective-permute-start.9
  54.6 0.3 copy-done.10
  54.9 3.2 %collective-permute-done.12.refs_4_ = bf16[16,8,2048]{2,1,0:T(8,128)(2,1)S(1)} collective-permute-done((bf16[16,8,2048]{2,1,0:T(8,128)(2,1)}, bf16[16,8,2048]{2,1,0:T(8,128)(2,1)S(1)}, u32[]{:S(2)}, u32[]{:S(2)}) %collective-permute-start.12) | collective-permute-done | bytes 524320 | tf_op jit(solution)/shard_map/ppermute | solution.py:17
  58.1 0.0 copy-start
  58.1 1.6 %collective-permute-start.13 = (bf16[16,8,2048]{2,1,0:T(8,128)(2,1)S(1)}, bf16[16,8,2048]{2,1,0:T(8,128)(2,1)S(1)}, u32[]{:S(2)}, u32[]{:S(2)}) collective-permute-start(bf16[16,8,2048]{2,1,0:T(8,128)(2,1)S(1)} %collective-permute-done.12.refs_4_), channel_id=1, source_target_pairs={{0,2},{1,3},{2,0},{3,1},{4,6},{5,7},{6,4},{7,5},{8,10},{9,11},{10,... | collective-permute-start | bytes 1572872 | tf_op jit(solution)/shard_map/ppermute | solution.py:17
  59.7 0.0 collective-permute-done.2.refs_0_
  59.7 0.0 copy-start.1
  59.7 0.4 collective-permute-start.3
  60.1 1.4 %copy.15.bi_ref = s32[4,1,16,4]{3,2,1,0:T(8,128)} copy(s32[4,1,16,4]{2,3,1,0:T(4,128)} %param.20) | data formatting | bytes 2048 | tf_op args[9]
  61.5 0.0 collective-permute-done.8.refs_6_
  61.5 0.0 collective-permute-done.6.refs_3_
  61.5 0.0 collective-permute-done.9.refs_7_
  61.5 0.0 copy-done.8
  61.5 0.0 copy-done.9
  61.5 6.5 %shard_map.131.refs_9_ = f32[16,8,2048]{2,1,0:T(8,128)} custom-call(s32[4,1,16,4]{3,2,1,0:T(8,128)} %copy.15.bi_ref, bf16[16,8,2048]{2,1,0:T(8,128)(2,1)} %copy-done.8, bf16[16,8,2048]{2,1,0:T(8,128)(2,1)} %collective-permute-done.4.refs_1_, bf16[16,8,2048]{2,1,0:T(8,128)(2,1)} %copy-done.10, bf16[16,8,2048]{2,1,0:T(8,128)(2,1)} %collective-permute-done.6.refs_3_, ...), custom_call_target="tpu_custom_call" | custom-call | tf_op jit(solution)/shard_map/pallas_call | solution.py:180
  68.0 4.9 %collective-permute-done.13.refs_5_ = bf16[16,8,2048]{2,1,0:T(8,128)(2,1)S(1)} collective-permute-done((bf16[16,8,2048]{2,1,0:T(8,128)(2,1)S(1)}, bf16[16,8,2048]{2,1,0:T(8,128)(2,1)S(1)}, u32[]{:S(2)}, u32[]{:S(2)}) %collective-permute-start.13) | collective-permute-done | bytes 524320 | tf_op jit(solution)/shard_map/ppermute | solution.py:17
  72.9 0.0 copy-start.2
  72.9 0.0 collective-permute-start.14
  72.9 0.5 collective-permute-start.15
  73.4 9.5 %collective-permute-done.3.refs_1_ = bf16[16,8,2048]{2,1,0:T(8,128)(2,1)S(1)} collective-permute-done((bf16[16,8,2048]{2,1,0:T(8,128)(2,1)S(1)}, bf16[16,8,2048]{2,1,0:T(8,128)(2,1)S(1)}, u32[]{:S(2)}, u32[]{:S(2)}) %collective-permute-start.3) | collective-permute-done | bytes 524320 | tf_op jit(solution)/shard_map/ppermute | solution.py:17
  82.9 0.0 copy-start.3
  82.9 0.0 collective-permute-start.10
  82.9 0.5 collective-permute-start.11
  83.4 0.0 collective-permute-done.14.refs_6_
  83.5 0.0 copy-start.4
  83.5 0.0 collective-permute-done.15.refs_7_
  83.5 0.0 copy-start.5
  83.5 1.4 %collective-permute-done.10.refs_2_ = bf16[16,8,2048]{2,1,0:T(8,128)(2,1)S(1)} collective-permute-done((bf16[16,8,2048]{2,1,0:T(8,128)(2,1)S(1)}, bf16[16,8,2048]{2,1,0:T(8,128)(2,1)S(1)}, u32[]{:S(2)}, u32[]{:S(2)}) %collective-permute-start.10) | collective-permute-done | bytes 524320 | tf_op jit(solution)/shard_map/ppermute | solution.py:17
  84.8 0.0 copy-start.6
  84.9 0.7 collective-permute-done.11.refs_3_
  85.6 0.0 copy-done.6
  85.6 0.0 copy-start.7
  85.6 0.8 copy-done.7
  86.4 0.0 copy-done
  86.4 0.0 copy-done.1
  86.4 0.0 copy-done.2
  86.4 0.0 copy-done.3
  86.5 0.0 copy-done.4
  86.5 0.0 copy-done.5
  86.5 7.4 %shard_map.132 = (bf16[16,8,2048]{2,1,0:T(8,128)(2,1)}, f32[8,2048]{1,0:T(8,128)}, f32[8,2048]{1,0:T(8,128)}) custom-call(s32[4,1,16,4]{3,2,1,0:T(8,128)} %copy.15.bi_ref, bf16[16,8,2048]{2,1,0:T(8,128)(2,1)} %copy-done.1, bf16[16,8,2048]{2,1,0:T(8,128)(2,1)} %copy-done.3, bf16[16,8,2048]{2,1,0:T(8,128)(2,1)} %copy-done.6, bf16[16,8,2048]{2,1,0:T(8,128)(2,1)} %copy-done.7, ...), custom_call_target="tpu_custom_call" | custom-call | tf_op jit(solution)/shard_map/pallas_call | solution.py:180
Async XLA Ops:
  3.3 26.3 %collective-permute-start = (bf16[16,8,2048]{2,1,0:T(8,128)(2,1)}, bf16[16,8,2048]{2,1,0:T(8,128)(2,1)S(1)}, u32[]{:S(2)}, u32[]{:S(2)}) collective-permute-start(bf16[16,8,2048]{2,1,0:T(8,128)(2,1)} %get-tuple-element.15), channel_id=1, source_target_pairs={{0,4},{4,0},{8,12},{12,8},{1,5},{5,1},{9,13},{13,9},{2,6},{6,2},{1... | collective-permute-start | bytes 1572872 | tf_op jit(solution)/shard_map/ppermute | solution.py:17
  6.4 25.8 %collective-permute-start.1 = (bf16[16,8,2048]{2,1,0:T(8,128)(2,1)}, bf16[16,8,2048]{2,1,0:T(8,128)(2,1)S(1)}, u32[]{:S(2)}, u32[]{:S(2)}) collective-permute-start(bf16[16,8,2048]{2,1,0:T(8,128)(2,1)} %get-tuple-element.16), channel_id=1, source_target_pairs={{0,8},{4,12},{8,0},{12,4},{1,9},{5,13},{9,1},{13,5},{2,10},{6,14},... | collective-permute-start | bytes 1572872 | tf_op jit(solution)/shard_map/ppermute | solution.py:17
  29.6 31.9 %copy-start.8 = (bf16[16,8,2048]{2,1,0:T(8,128)(2,1)}, bf16[16,8,2048]{2,1,0:T(8,128)(2,1)S(1)}, u32[]{:S(2)}) copy-start(bf16[16,8,2048]{2,1,0:T(8,128)(2,1)S(1)} %collective-permute-done.refs_0_) | copy-start | bytes 1572868
  29.6 15.0 %collective-permute-start.4 = (bf16[16,8,2048]{2,1,0:T(8,128)(2,1)S(1)}, bf16[16,8,2048]{2,1,0:T(8,128)(2,1)}, u32[]{:S(2)}, u32[]{:S(2)}) collective-permute-start(bf16[16,8,2048]{2,1,0:T(8,128)(2,1)S(1)} %collective-permute-done.refs_0_), channel_id=1, source_target_pairs={{0,2},{1,3},{2,0},{3,1},{4,6},{5,7},{6,4},{7,5},{8,10},{9,11},{10,... | collective-permute-start | bytes 1572872 | tf_op jit(solution)/shard_map/ppermute | solution.py:17
  31.3 22.8 %collective-permute-start.5 = (bf16[16,8,2048]{2,1,0:T(8,128)(2,1)S(1)}, bf16[16,8,2048]{2,1,0:T(8,128)(2,1)S(1)}, u32[]{:S(2)}, u32[]{:S(2)}) collective-permute-start(bf16[16,8,2048]{2,1,0:T(8,128)(2,1)S(1)} %collective-permute-done.refs_0_), channel_id=1, source_target_pairs={{0,1},{1,0},{2,3},{3,2},{4,5},{5,4},{6,7},{7,6},{8,9},{9,8},{10,11... | collective-permute-start | bytes 1572872 | tf_op jit(solution)/shard_map/ppermute | solution.py:17
  32.1 29.4 %copy-start.9 = (bf16[16,8,2048]{2,1,0:T(8,128)(2,1)}, bf16[16,8,2048]{2,1,0:T(8,128)(2,1)S(1)}, u32[]{:S(2)}) copy-start(bf16[16,8,2048]{2,1,0:T(8,128)(2,1)S(1)} %collective-permute-done.1.refs_4_) | copy-start | bytes 1572868
  32.1 21.9 %collective-permute-start.7 = (bf16[16,8,2048]{2,1,0:T(8,128)(2,1)S(1)}, bf16[16,8,2048]{2,1,0:T(8,128)(2,1)}, u32[]{:S(2)}, u32[]{:S(2)}) collective-permute-start(bf16[16,8,2048]{2,1,0:T(8,128)(2,1)S(1)} %collective-permute-done.1.refs_4_), channel_id=1, source_target_pairs={{0,2},{1,3},{2,0},{3,1},{4,6},{5,7},{6,4},{7,5},{8,10},{9,11},{10,... | collective-permute-start | bytes 1572872 | tf_op jit(solution)/shard_map/ppermute | solution.py:17
  33.6 24.4 %collective-permute-start.12 = (bf16[16,8,2048]{2,1,0:T(8,128)(2,1)}, bf16[16,8,2048]{2,1,0:T(8,128)(2,1)S(1)}, u32[]{:S(2)}, u32[]{:S(2)}) collective-permute-start(bf16[16,8,2048]{2,1,0:T(8,128)(2,1)} %get-tuple-element.20), channel_id=1, source_target_pairs={{0,8},{4,12},{8,0},{12,4},{1,9},{5,13},{9,1},{13,5},{2,10},{6,14},... | collective-permute-start | bytes 1572872 | tf_op jit(solution)/shard_map/ppermute | solution.py:17
  34.0 25.7 %collective-permute-start.2 = (bf16[16,8,2048]{2,1,0:T(8,128)(2,1)}, bf16[16,8,2048]{2,1,0:T(8,128)(2,1)S(1)}, u32[]{:S(2)}, u32[]{:S(2)}) collective-permute-start(bf16[16,8,2048]{2,1,0:T(8,128)(2,1)} %get-tuple-element.17), channel_id=1, source_target_pairs={{0,4},{4,0},{8,12},{12,8},{1,5},{5,1},{9,13},{13,9},{2,6},{6,2},{1... | collective-permute-start | bytes 1572872 | tf_op jit(solution)/shard_map/ppermute | solution.py:17
  44.6 16.9 %collective-permute-start.8 = (bf16[16,8,2048]{2,1,0:T(8,128)(2,1)S(1)}, bf16[16,8,2048]{2,1,0:T(8,128)(2,1)}, u32[]{:S(2)}, u32[]{:S(2)}) collective-permute-start(bf16[16,8,2048]{2,1,0:T(8,128)(2,1)S(1)} %collective-permute-done.1.refs_4_), channel_id=1, source_target_pairs={{0,1},{1,0},{2,3},{3,2},{4,5},{5,4},{6,7},{7,6},{8,9},{9,8},{10,11... | collective-permute-start | bytes 1572872 | tf_op jit(solution)/shard_map/ppermute | solution.py:17
  54.1 7.4 %collective-permute-start.6 = (bf16[16,8,2048]{2,1,0:T(8,128)(2,1)}, bf16[16,8,2048]{2,1,0:T(8,128)(2,1)}, u32[]{:S(2)}, u32[]{:S(2)}) collective-permute-start(bf16[16,8,2048]{2,1,0:T(8,128)(2,1)} %collective-permute-done.4.refs_1_), channel_id=1, source_target_pairs={{0,1},{1,0},{2,3},{3,2},{4,5},{5,4},{6,7},{7,6},{8,9},{9,8},{10,11... | collective-permute-start | bytes 1572872 | tf_op jit(solution)/shard_map/ppermute | solution.py:17
  54.1 0.8 copy-start.10
  54.1 7.4 %collective-permute-start.9 = (bf16[16,8,2048]{2,1,0:T(8,128)(2,1)}, bf16[16,8,2048]{2,1,0:T(8,128)(2,1)}, u32[]{:S(2)}, u32[]{:S(2)}) collective-permute-start(bf16[16,8,2048]{2,1,0:T(8,128)(2,1)} %collective-permute-done.7.refs_5_), channel_id=1, source_target_pairs={{0,1},{1,0},{2,3},{3,2},{4,5},{5,4},{6,7},{7,6},{8,9},{9,8},{10,11... | collective-permute-start | bytes 1572872 | tf_op jit(solution)/shard_map/ppermute | solution.py:17
  58.1 28.4 %copy-start = (bf16[16,8,2048]{2,1,0:T(8,128)(2,1)}, bf16[16,8,2048]{2,1,0:T(8,128)(2,1)S(1)}, u32[]{:S(2)}) copy-start(bf16[16,8,2048]{2,1,0:T(8,128)(2,1)S(1)} %collective-permute-done.12.refs_4_) | copy-start | bytes 1572868
  58.1 14.8 %collective-permute-start.13 = (bf16[16,8,2048]{2,1,0:T(8,128)(2,1)S(1)}, bf16[16,8,2048]{2,1,0:T(8,128)(2,1)S(1)}, u32[]{:S(2)}, u32[]{:S(2)}) collective-permute-start(bf16[16,8,2048]{2,1,0:T(8,128)(2,1)S(1)} %collective-permute-done.12.refs_4_), channel_id=1, source_target_pairs={{0,2},{1,3},{2,0},{3,1},{4,6},{5,7},{6,4},{7,5},{8,10},{9,11},{10,... | collective-permute-start | bytes 1572872 | tf_op jit(solution)/shard_map/ppermute | solution.py:17
  59.7 26.8 %copy-start.1 = (bf16[16,8,2048]{2,1,0:T(8,128)(2,1)}, bf16[16,8,2048]{2,1,0:T(8,128)(2,1)S(1)}, u32[]{:S(2)}) copy-start(bf16[16,8,2048]{2,1,0:T(8,128)(2,1)S(1)} %collective-permute-done.2.refs_0_) | copy-start | bytes 1572868
  59.7 23.3 %collective-permute-start.3 = (bf16[16,8,2048]{2,1,0:T(8,128)(2,1)S(1)}, bf16[16,8,2048]{2,1,0:T(8,128)(2,1)S(1)}, u32[]{:S(2)}, u32[]{:S(2)}) collective-permute-start(bf16[16,8,2048]{2,1,0:T(8,128)(2,1)S(1)} %collective-permute-done.2.refs_0_), channel_id=1, source_target_pairs={{0,2},{1,3},{2,0},{3,1},{4,6},{5,7},{6,4},{7,5},{8,10},{9,11},{10,... | collective-permute-start | bytes 1572872 | tf_op jit(solution)/shard_map/ppermute | solution.py:17
  72.9 13.6 %copy-start.2 = (bf16[16,8,2048]{2,1,0:T(8,128)(2,1)}, bf16[16,8,2048]{2,1,0:T(8,128)(2,1)S(1)}, u32[]{:S(2)}) copy-start(bf16[16,8,2048]{2,1,0:T(8,128)(2,1)S(1)} %collective-permute-done.13.refs_5_) | copy-start | bytes 1572868
  72.9 10.6 %collective-permute-start.14 = (bf16[16,8,2048]{2,1,0:T(8,128)(2,1)S(1)}, bf16[16,8,2048]{2,1,0:T(8,128)(2,1)S(1)}, u32[]{:S(2)}, u32[]{:S(2)}) collective-permute-start(bf16[16,8,2048]{2,1,0:T(8,128)(2,1)S(1)} %collective-permute-done.12.refs_4_), channel_id=1, source_target_pairs={{0,1},{1,0},{2,3},{3,2},{4,5},{5,4},{6,7},{7,6},{8,9},{9,8},{10,11... | collective-permute-start | bytes 1572872 | tf_op jit(solution)/shard_map/ppermute | solution.py:17
  72.9 10.6 %collective-permute-start.15 = (bf16[16,8,2048]{2,1,0:T(8,128)(2,1)S(1)}, bf16[16,8,2048]{2,1,0:T(8,128)(2,1)S(1)}, u32[]{:S(2)}, u32[]{:S(2)}) collective-permute-start(bf16[16,8,2048]{2,1,0:T(8,128)(2,1)S(1)} %collective-permute-done.13.refs_5_), channel_id=1, source_target_pairs={{0,1},{1,0},{2,3},{3,2},{4,5},{5,4},{6,7},{7,6},{8,9},{9,8},{10,11... | collective-permute-start | bytes 1572872 | tf_op jit(solution)/shard_map/ppermute | solution.py:17
  82.9 3.5 %copy-start.3 = (bf16[16,8,2048]{2,1,0:T(8,128)(2,1)}, bf16[16,8,2048]{2,1,0:T(8,128)(2,1)S(1)}, u32[]{:S(2)}) copy-start(bf16[16,8,2048]{2,1,0:T(8,128)(2,1)S(1)} %collective-permute-done.3.refs_1_) | copy-start | bytes 1572868
  82.9 1.9 %collective-permute-start.10 = (bf16[16,8,2048]{2,1,0:T(8,128)(2,1)S(1)}, bf16[16,8,2048]{2,1,0:T(8,128)(2,1)S(1)}, u32[]{:S(2)}, u32[]{:S(2)}) collective-permute-start(bf16[16,8,2048]{2,1,0:T(8,128)(2,1)S(1)} %collective-permute-done.2.refs_0_), channel_id=1, source_target_pairs={{0,1},{1,0},{2,3},{3,2},{4,5},{5,4},{6,7},{7,6},{8,9},{9,8},{10,11... | collective-permute-start | bytes 1572872 | tf_op jit(solution)/shard_map/ppermute | solution.py:17
  82.9 2.7 %collective-permute-start.11 = (bf16[16,8,2048]{2,1,0:T(8,128)(2,1)S(1)}, bf16[16,8,2048]{2,1,0:T(8,128)(2,1)S(1)}, u32[]{:S(2)}, u32[]{:S(2)}) collective-permute-start(bf16[16,8,2048]{2,1,0:T(8,128)(2,1)S(1)} %collective-permute-done.3.refs_1_), channel_id=1, source_target_pairs={{0,1},{1,0},{2,3},{3,2},{4,5},{5,4},{6,7},{7,6},{8,9},{9,8},{10,11... | collective-permute-start | bytes 1572872 | tf_op jit(solution)/shard_map/ppermute | solution.py:17
  83.5 3.0 %copy-start.4 = (bf16[16,8,2048]{2,1,0:T(8,128)(2,1)}, bf16[16,8,2048]{2,1,0:T(8,128)(2,1)S(1)}, u32[]{:S(2)}) copy-start(bf16[16,8,2048]{2,1,0:T(8,128)(2,1)S(1)} %collective-permute-done.14.refs_6_) | copy-start | bytes 1572868
  83.5 3.0 %copy-start.5 = (bf16[16,8,2048]{2,1,0:T(8,128)(2,1)}, bf16[16,8,2048]{2,1,0:T(8,128)(2,1)S(1)}, u32[]{:S(2)}) copy-start(bf16[16,8,2048]{2,1,0:T(8,128)(2,1)S(1)} %collective-permute-done.15.refs_7_) | copy-start | bytes 1572868
  84.8 0.8 copy-start.6
  85.6 0.8 copy-start.7

commit v8 on v7

--- a/solution.py
+++ b/solution.py
@@ -17,21 +17,24 @@
     return lax.ppermute(value, axis, pairs)
 
 
-def slice_kernel(delays_ref, window_ref, *outs, levels, steps):
+def slice_kernel(delays_ref, window_ref, *outs, levels, steps, n_halves):
     me = lax.axis_index("area")
-    for rnd, out in enumerate(outs):
+    width = outs[0].shape[-1]
+    for n, out in enumerate(outs):
+        rnd, h = divmod(n, n_halves)
         start = delays_ref[rnd, me ^ (1 << (rnd % levels))] - steps
-        out[...] = window_ref[pl.ds(start, steps)]
-
-
-def send_slices(window, delays, rounds, levels, steps):
-    shape = (steps,) + window.shape[1:]
-    kernel = functools.partial(slice_kernel, levels=levels, steps=steps)
+        out[...] = window_ref[pl.ds(start, steps), :, h * width:(h + 1) * width]
+
+
+def send_slices(window, delays, rounds, levels, steps, n_halves):
+    shape = (steps,) + window.shape[1:-1] + (window.shape[-1] // n_halves,)
+    kernel = functools.partial(slice_kernel, levels=levels, steps=steps, n_halves=n_halves)
+    n_out = rounds * n_halves
     return pl.pallas_call(
         kernel,
         in_specs=[SMEM, VMEM],
-        out_specs=[VMEM] * rounds,
-        out_shape=[jax.ShapeDtypeStruct(shape, window.dtype)] * rounds,
+        out_specs=[VMEM] * n_out,
+        out_shape=[jax.ShapeDtypeStruct(shape, window.dtype)] * n_out,
     )(delays, window)
 
 
@@ -45,7 +48,7 @@
     return held
 
 
-def stage_kernel(bi_ref, *refs, n_pieces, stage, n_pos, final, has_rec):
+def stage_kernel(bi_ref, *refs, n_pieces, stage, n_pos, n_halves, final, has_rec):
     n_rounds = len(stage)
     it = iter(refs)
     piece_hbm = [next(it) for _ in range(n_pieces)]
@@ -81,8 +84,10 @@
     piece_cp, w_cp = [], []
     rec_cp = None
     scan_cp = []
+    per_round = n_pos * n_halves
     for ri, rnd in enumerate(stage):
-        piece_cp += [start(piece_hbm[ri * n_pos + p], piece_buf[ri * n_pos + p]) for p in range(n_pos)]
+        piece_cp += [start(piece_hbm[ri * per_round + q], piece_buf[ri * per_round + q])
+                     for q in range(per_round)]
         w_cp.append(start(w_hbm.at[rnd, 0], w_buf.at[ri]))
         if ri == 0 and has_rec:
             rec_cp = start(rec_hbm, rec_buf)
@@ -90,12 +95,15 @@
         scan_cp = [start(src, dst) for src, dst in zip(scan_hbm, scan_buf)]
 
     for ri, rnd in enumerate(stage):
+        per_half = local_blocks // n_halves
         for p in range(n_pos):
-            k = ri * n_pos + p
-            piece_cp[k].wait()
-            for i in range(local_blocks):
-                x = piece_buf[k][:, :, i * side:(i + 1) * side].astype(jnp.float32)
-                blocks[p * local_blocks + i] = x.reshape(rows, side).astype(jnp.bfloat16)
+            for h in range(n_halves):
+                k = (ri * n_pos + p) * n_halves + h
+                piece_cp[k].wait()
+                for i in range(per_half):
+                    x = piece_buf[k][:, :, i * side:(i + 1) * side].astype(jnp.float32)
+                    x = x.reshape(rows, side).astype(jnp.bfloat16)
+                    blocks[p * local_blocks + h * per_half + i] = x
         w_cp[ri].wait()
         if ri == 0 and has_rec:
             rec_cp.wait()
@@ -141,8 +149,9 @@
             la_out[:, cols] = la_now
 
 
-def stage_contrib(block_index, pieces, weights, stage, n_pos, rec, scan_args):
-    steps, batch, local = pieces[0].shape
+def stage_contrib(block_index, pieces, weights, stage, n_pos, n_halves, rec, scan_args):
+    steps, batch, width = pieces[0].shape
+    local = width * n_halves
     _, _, local_blocks, nnz, side, _ = weights.shape
     n_rounds = len(stage)
     final = scan_args is not None
@@ -175,7 +184,7 @@
         out_shape = jax.ShapeDtypeStruct((steps, batch, local), jnp.float32)
     kernel = functools.partial(
         stage_kernel, n_pieces=len(pieces), stage=tuple(stage), n_pos=n_pos,
-        final=final, has_rec=has_rec,
+        n_halves=n_halves, final=final, has_rec=has_rec,
     )
     return pl.pallas_call(
         kernel,
@@ -197,26 +206,30 @@
     levels = lax.axis_size("area").bit_length() - 1
     nbits = lax.axis_size("neuron").bit_length() - 1
     n_pos = 1 << nbits
-    slices = send_slices(window, delays, rounds, levels, steps)
+    n_halves = 2 if local_blocks % 2 == 0 else 1
+    slices = send_slices(window, delays, rounds, levels, steps, n_halves)
     stages = [list(range(f, min(f + 2, rounds))) for f in range(0, rounds, 2)]
-    arrived = []
+    arrived = {}
     gate = None
     for stage in stages:
-        pieces = [slices[rnd] for rnd in stage]
-        if gate is not None:
-            pieces, _ = lax.optimization_barrier((pieces, gate))
-        got = [swap(piece, "area", 1 << (rnd % levels)) for piece, rnd in zip(pieces, stage)]
-        arrived += got
-        gate = got
+        for h in range(n_halves):
+            pieces = [slices[rnd * n_halves + h] for rnd in stage]
+            if gate is not None:
+                pieces, _ = lax.optimization_barrier((pieces, gate))
+            got = [swap(piece, "area", 1 << (rnd % levels)) for piece, rnd in zip(pieces, stage)]
+            for rnd, g in zip(stage, got):
+                arrived[(rnd, h)] = g
+            gate = got
     rec = None
     for si, stage in enumerate(stages):
         chunks = []
         for rnd in stage:
-            chunks += gather_neuron(arrived[rnd], rec)
+            halves = [gather_neuron(arrived[(rnd, h)], rec) for h in range(n_halves)]
+            chunks += [halves[h][p] for p in range(n_pos) for h in range(n_halves)]
         scan_args = None
         if si == len(stages) - 1:
             scan_args = (err_grad, surrogate, lv_end, la_end, alpha, rho, beta)
-        rec = stage_contrib(block_index, chunks, weights, stage, n_pos, rec, scan_args)
+        rec = stage_contrib(block_index, chunks, weights, stage, n_pos, n_halves, rec, scan_args)
     return rec
 
 

time: 94.3 us -> 93.4 us (level)
  waiting for transfers between devices: 58.6 us -> 49.1 us
  starting transfers between devices: 15.4 us -> 24.1 us
    ppermute x16 -> x32, waiting for transfers between devices: 58.6 us -> 49.1 us  [swap(): return lax.ppermute(value, axis, pairs)]
    ppermute x16 -> x32, starting transfers between devices: 15.4 us -> 24.1 us  [swap(): return lax.ppermute(value, axis, pairs)]
    unnamed x23 -> x59, local copies, waits for them, and re-layouts: 2.54 us -> 2.19 us
  transfers between devices with their start and end apart: 16 -> 32, of which waited for: 9 -> 14; matrix products, arithmetic and copies ran while one was open for 1% -> 1% of each run, Pallas kernels for 7% -> 7%
where the time goes in v8:
time: 93.4 us; the launch traced here: 93 us
  waiting for transfers between devices  49.1 us (53%)
  starting transfers between devices  24.1 us (26%)
  Pallas kernels  16.8 us (18%)
  local copies, waits for them, and re-layouts  2.19 us (2%)
    ppermute x32, waiting for transfers between devices, swap(): return lax.ppermute(value, axis, pairs)  49.1 us
    ppermute x32, starting transfers between devices, swap(): return lax.ppermute(value, axis, pairs)  24.1 us
    pallas_call x2, Pallas kernels, stage_contrib(): pl.pallas_call(kernel, in_specs=[SMEM] + [ANY] * len(operands), out_specs...  14.1 us
    pallas_call x1, Pallas kernels, send_slices(): pl.pallas_call(kernel, in_specs=[SMEM, VMEM], out_specs=[VMEM] * n_out, o...  2.69 us
    unnamed x59, local copies, waits for them, and re-layouts  2.19 us
  transfers between devices with their start and end apart: 32, of which 14 were waited for; matrix products, arithmetic and copies ran while one was open for 1% of the time, Pallas kernels for 7%

profile of v8, /device:TPU:0, one launch (start us, length us, event | category | flops | bytes accessed | tf_op | source)
XLA Modules:
  0.0 93.0 jit_solution(1275052938644696669)
XLA Ops:
  0.6 2.7 %shard_map.130 = (bf16[16,8,1024]{2,1,0:T(8,128)(2,1)}, bf16[16,8,1024]{2,1,0:T(8,128)(2,1)}, bf16[16,8,1024]{2,1,0:T(8,128)(2,1)}, bf16[16,8,1024]{2,1,0:T(8,12...) custom-call(s32[4,4]{1,0:T(4,128)} %delays_ref.1, ...), custom_call_target="tpu_custom_call" | custom-call | tf_op jit(solution)/shard_map/pallas_call | solution.py:33
  3.3 3.0 %collective-permute-start = (bf16[16,8,1024]{2,1,0:T(8,128)(2,1)}, bf16[16,8,1024]{2,1,0:T(8,128)(2,1)S(1)}, u32[]{:S(2)}, u32[]{:S(2)}) collective-permute-start(bf16[16,8,1024]{2,1,0:T(8,128)(2,1)} %get-tuple-element.29), channel_id=1, source_target_pairs={{0,4},{4,0},{8,12},{12,8},{1,5},{5,1},{9,13},{13,9},{2,6},{6,2},{1... | collective-permute-start | bytes 786440 | tf_op jit(solution)/shard_map/ppermute | solution.py:17
  6.3 2.6 %collective-permute-start.1 = (bf16[16,8,1024]{2,1,0:T(8,128)(2,1)}, bf16[16,8,1024]{2,1,0:T(8,128)(2,1)S(1)}, u32[]{:S(2)}, u32[]{:S(2)}) collective-permute-start(bf16[16,8,1024]{2,1,0:T(8,128)(2,1)} %get-tuple-element.30), channel_id=1, source_target_pairs={{0,8},{4,12},{8,0},{12,4},{1,9},{5,13},{9,1},{13,5},{2,10},{6,14},... | collective-permute-start | bytes 786440 | tf_op jit(solution)/shard_map/ppermute | solution.py:17
  8.9 9.4 %collective-permute-done.refs_0_ = bf16[16,8,1024]{2,1,0:T(8,128)(2,1)S(1)} collective-permute-done((bf16[16,8,1024]{2,1,0:T(8,128)(2,1)}, bf16[16,8,1024]{2,1,0:T(8,128)(2,1)S(1)}, u32[]{:S(2)}, u32[]{:S(2)}) %collective-permute-start) | collective-permute-done | bytes 262176 | tf_op jit(solution)/shard_map/ppermute | solution.py:17
  18.4 2.5 %collective-permute-done.1.refs_8_ = bf16[16,8,1024]{2,1,0:T(8,128)(2,1)S(1)} collective-permute-done((bf16[16,8,1024]{2,1,0:T(8,128)(2,1)}, bf16[16,8,1024]{2,1,0:T(8,128)(2,1)S(1)}, u32[]{:S(2)}, u32[]{:S(2)}) %collective-permute-start.1) | collective-permute-done | bytes 262176 | tf_op jit(solution)/shard_map/ppermute | solution.py:17
  20.9 0.4 collective-permute-start.2
  21.3 2.6 %collective-permute-start.3 = (bf16[16,8,1024]{2,1,0:T(8,128)(2,1)}, bf16[16,8,1024]{2,1,0:T(8,128)(2,1)S(1)}, u32[]{:S(2)}, u32[]{:S(2)}) collective-permute-start(bf16[16,8,1024]{2,1,0:T(8,128)(2,1)} %get-tuple-element.32), channel_id=1, source_target_pairs={{0,8},{4,12},{8,0},{12,4},{1,9},{5,13},{9,1},{13,5},{2,10},{6,14},... | collective-permute-start | bytes 786440 | tf_op jit(solution)/shard_map/ppermute | solution.py:17
  24.0 1.5 %collective-permute-start.6 = (bf16[16,8,1024]{2,1,0:T(8,128)(2,1)S(1)}, bf16[16,8,1024]{2,1,0:T(8,128)(2,1)S(1)}, u32[]{:S(2)}, u32[]{:S(2)}) collective-permute-start(bf16[16,8,1024]{2,1,0:T(8,128)(2,1)S(1)} %collective-permute-done.refs_0_), channel_id=1, source_target_pairs={{0,2},{1,3},{2,0},{3,1},{4,6},{5,7},{6,4},{7,5},{8,10},{9,11},{10,... | collective-permute-start | bytes 786440 | tf_op jit(solution)/shard_map/ppermute | solution.py:17
  25.5 0.5 collective-permute-start.12
  26.0 0.0 collective-permute-start.14
  26.0 5.2 %collective-permute-done.2.refs_1_ = bf16[16,8,1024]{2,1,0:T(8,128)(2,1)S(1)} collective-permute-done((bf16[16,8,1024]{2,1,0:T(8,128)(2,1)}, bf16[16,8,1024]{2,1,0:T(8,128)(2,1)S(1)}, u32[]{:S(2)}, u32[]{:S(2)}) %collective-permute-start.2) | collective-permute-done | bytes 262176 | tf_op jit(solution)/shard_map/ppermute | solution.py:17
  31.2 0.0 collective-permute-start.8
  31.2 3.7 %collective-permute-done.3.refs_9_ = bf16[16,8,1024]{2,1,0:T(8,128)(2,1)S(1)} collective-permute-done((bf16[16,8,1024]{2,1,0:T(8,128)(2,1)}, bf16[16,8,1024]{2,1,0:T(8,128)(2,1)S(1)}, u32[]{:S(2)}, u32[]{:S(2)}) %collective-permute-start.3) | collective-permute-done | bytes 262176 | tf_op jit(solution)/shard_map/ppermute | solution.py:17
  34.9 0.3 collective-permute-start.18
  35.3 0.0 collective-permute-done.6.refs_2_
  35.3 1.8 %collective-permute-start.4 = (bf16[16,8,1024]{2,1,0:T(8,128)(2,1)}, bf16[16,8,1024]{2,1,0:T(8,128)(2,1)S(1)}, u32[]{:S(2)}, u32[]{:S(2)}) collective-permute-start(bf16[16,8,1024]{2,1,0:T(8,128)(2,1)} %get-tuple-element.33), channel_id=1, source_target_pairs={{0,4},{4,0},{8,12},{12,8},{1,5},{5,1},{9,13},{13,9},{2,6},{6,2},{1... | collective-permute-start | bytes 786440 | tf_op jit(solution)/shard_map/ppermute | solution.py:17
  37.1 0.0 collective-permute-done.12.refs_10_
  37.1 1.5 %collective-permute-start.7 = (bf16[16,8,1024]{2,1,0:T(8,128)(2,1)S(1)}, bf16[16,8,1024]{2,1,0:T(8,128)(2,1)S(1)}, u32[]{:S(2)}, u32[]{:S(2)}) collective-permute-start(bf16[16,8,1024]{2,1,0:T(8,128)(2,1)S(1)} %collective-permute-done.2.refs_1_), channel_id=1, source_target_pairs={{0,2},{1,3},{2,0},{3,1},{4,6},{5,7},{6,4},{7,5},{8,10},{9,11},{10,... | collective-permute-start | bytes 786440 | tf_op jit(solution)/shard_map/ppermute | solution.py:17
  38.6 0.0 collective-permute-done.14.refs_12_
  38.6 0.5 collective-permute-start.13
  39.1 0.0 collective-permute-done.8.refs_4_
  39.1 0.0 collective-permute-start.15
  39.1 7.6 %collective-permute-done.18.refs_8_ = bf16[16,8,1024]{2,1,0:T(8,128)(2,1)S(1)} collective-permute-done((bf16[16,8,1024]{2,1,0:T(8,128)(2,1)}, bf16[16,8,1024]{2,1,0:T(8,128)(2,1)S(1)}, u32[]{:S(2)}, u32[]{:S(2)}) %collective-permute-start.18) | collective-permute-done | bytes 262176 | tf_op jit(solution)/shard_map/ppermute | solution.py:17
  46.8 0.0 collective-permute-start.9
  46.8 0.2 collective-permute-done.4.refs_0_
  47.0 0.3 collective-permute-start.10
  47.3 0.2 collective-permute-start.16
  47.5 1.2 %collective-permute-done.13.refs_11_ = bf16[16,8,1024]{2,1,0:T(8,128)(2,1)} collective-permute-done((bf16[16,8,1024]{2,1,0:T(8,128)(2,1)S(1)}, bf16[16,8,1024]{2,1,0:T(8,128)(2,1)}, u32[]{:S(2)}, u32[]{:S(2)}) %collective-permute-start.13) | collective-permute-done | bytes 262176 | tf_op jit(solution)/shard_map/ppermute | solution.py:17
  48.7 0.4 collective-permute-start.26
  49.1 0.0 collective-permute-start.11
  49.1 0.0 collective-permute-done.9.refs_5_
  49.1 1.4 %collective-permute-start.19 = (bf16[16,8,1024]{2,1,0:T(8,128)(2,1)}, bf16[16,8,1024]{2,1,0:T(8,128)(2,1)S(1)}, u32[]{:S(2)}, u32[]{:S(2)}) collective-permute-start(bf16[16,8,1024]{2,1,0:T(8,128)(2,1)} %get-tuple-element.38), channel_id=1, source_target_pairs={{0,4},{4,0},{8,12},{12,8},{1,5},{5,1},{9,13},{13,9},{2,6},{6,2},{1... | collective-permute-start | bytes 786440 | tf_op jit(solution)/shard_map/ppermute | solution.py:17
  50.6 0.1 collective-permute-start.17
  50.6 0.0 collective-permute-done.16.refs_14_
  50.6 1.6 %collective-permute-start.25 = (bf16[16,8,1024]{2,1,0:T(8,128)(2,1)S(1)}, bf16[16,8,1024]{2,1,0:T(8,128)(2,1)S(1)}, u32[]{:S(2)}, u32[]{:S(2)}) collective-permute-start(bf16[16,8,1024]{2,1,0:T(8,128)(2,1)S(1)} %collective-permute-done.18.refs_8_), channel_id=1, source_target_pairs={{0,2},{1,3},{2,0},{3,1},{4,6},{5,7},{6,4},{7,5},{8,10},{9,11},{10,... | collective-permute-start | bytes 786440 | tf_op jit(solution)/shard_map/ppermute | solution.py:17
  52.2 10.4 %collective-permute-done.26.refs_9_ = bf16[16,8,1024]{2,1,0:T(8,128)(2,1)S(1)} collective-permute-done((bf16[16,8,1024]{2,1,0:T(8,128)(2,1)}, bf16[16,8,1024]{2,1,0:T(8,128)(2,1)S(1)}, u32[]{:S(2)}, u32[]{:S(2)}) %collective-permute-start.26) | collective-permute-done | bytes 262176 | tf_op jit(solution)/shard_map/ppermute | solution.py:17
  62.6 1.6 %collective-permute-start.5 = (bf16[16,8,1024]{2,1,0:T(8,128)(2,1)S(1)}, bf16[16,8,1024]{2,1,0:T(8,128)(2,1)S(1)}, u32[]{:S(2)}, u32[]{:S(2)}) collective-permute-start(bf16[16,8,1024]{2,1,0:T(8,128)(2,1)S(1)} %collective-permute-done.4.refs_0_), channel_id=1, source_target_pairs={{0,2},{1,3},{2,0},{3,1},{4,6},{5,7},{6,4},{7,5},{8,10},{9,11},{10,... | collective-permute-start | bytes 786440 | tf_op jit(solution)/shard_map/ppermute | solution.py:17
  64.1 1.4 %copy.15.bi_ref = s32[4,1,16,4]{3,2,1,0:T(8,128)} copy(s32[4,1,16,4]{2,3,1,0:T(4,128)} %param.20) | data formatting | bytes 2048 | tf_op args[9]
  65.5 0.0 collective-permute-done.11.refs_7_
  65.5 0.5 collective-permute-start.27
  66.1 0.0 collective-permute-done.19.refs_1_
  66.1 1.6 %collective-permute-start.20 = (bf16[16,8,1024]{2,1,0:T(8,128)(2,1)S(1)}, bf16[16,8,1024]{2,1,0:T(8,128)(2,1)S(1)}, u32[]{:S(2)}, u32[]{:S(2)}) collective-permute-start(bf16[16,8,1024]{2,1,0:T(8,128)(2,1)S(1)} %collective-permute-done.19.refs_1_), channel_id=1, source_target_pairs={{0,2},{1,3},{2,0},{3,1},{4,6},{5,7},{6,4},{7,5},{8,10},{9,11},{10,... | collective-permute-start | bytes 786440 | tf_op jit(solution)/shard_map/ppermute | solution.py:17
  67.7 6.6 %shard_map.131.refs_17_ = f32[16,8,2048]{2,1,0:T(8,128)} custom-call(s32[4,1,16,4]{3,2,1,0:T(8,128)} %copy.15.bi_ref, bf16[16,8,1024]{2,1,0:T(8,128)(2,1)} %copy-done.16, bf16[16,8,1024]{2,1,0:T(8,128)(2,1)} %copy-done.18, bf16[16,8,1024]{2,1,0:T(8,128)(2,1)} %copy-done.20, bf16[16,8,1024]{2,1,0:T(8,128)(2,1)} %copy-done.24, ...), custom_call_target="tpu_custom_call" | custom-call | tf_op jit(solution)/shard_map/pallas_call | solution.py:189
  74.3 0.0 collective-permute-done.25.refs_10_
  74.3 0.1 collective-permute-start.28
  74.4 0.5 collective-permute-start.30
  74.9 0.0 collective-permute-done.5.refs_2_
  74.9 0.1 collective-permute-start.21
  75.0 2.5 %collective-permute-done.27.refs_11_ = bf16[16,8,1024]{2,1,0:T(8,128)(2,1)S(1)} collective-permute-done((bf16[16,8,1024]{2,1,0:T(8,128)(2,1)S(1)}, bf16[16,8,1024]{2,1,0:T(8,128)(2,1)S(1)}, u32[]{:S(2)}, u32[]{:S(2)}) %collective-permute-start.27) | collective-permute-done | bytes 262176 | tf_op jit(solution)/shard_map/ppermute | solution.py:17
  77.4 4.6 %collective-permute-done.20.refs_3_ = bf16[16,8,1024]{2,1,0:T(8,128)(2,1)S(1)} collective-permute-done((bf16[16,8,1024]{2,1,0:T(8,128)(2,1)S(1)}, bf16[16,8,1024]{2,1,0:T(8,128)(2,1)S(1)}, u32[]{:S(2)}, u32[]{:S(2)}) %collective-permute-start.20) | collective-permute-done | bytes 262176 | tf_op jit(solution)/shard_map/ppermute | solution.py:17
  82.0 0.0 collective-permute-start.29
  82.1 0.0 collective-permute-done.28.refs_12_
  82.1 0.5 collective-permute-start.31
  82.6 0.1 collective-permute-start.22
  82.7 0.0 collective-permute-done.21.refs_4_
  82.7 0.4 collective-permute-start.24
  83.1 0.0 collective-permute-done.23.refs_6_
  83.1 0.5 collective-permute-done.29.refs_13_
  83.6 0.4 collective-permute-done.31.refs_15_
  84.0 0.4 collective-permute-done.22.refs_5_
  84.3 0.4 collective-permute-done.24.refs_7_
  84.7 0.3 copy-done.14
  85.1 0.4 copy-done.15
  85.5 7.5 %shard_map.132 = (bf16[16,8,2048]{2,1,0:T(8,128)(2,1)}, f32[8,2048]{1,0:T(8,128)}, f32[8,2048]{1,0:T(8,128)}) custom-call(s32[4,1,16,4]{3,2,1,0:T(8,128)} %copy.15.bi_ref, bf16[16,8,1024]{2,1,0:T(8,128)(2,1)} %copy-done.1, bf16[16,8,1024]{2,1,0:T(8,128)(2,1)} %copy-done.3, bf16[16,8,1024]{2,1,0:T(8,128)(2,1)} %copy-done.5, bf16[16,8,1024]{2,1,0:T(8,128)(2,1)} %copy-done.7, ...), custom_call_target="tpu_custom_call" | custom-call | tf_op jit(solution)/shard_map/pallas_call | solution.py:189
  (62 shorter events, 0.1 us)
Async XLA Ops:
  3.3 15.0 %collective-permute-start = (bf16[16,8,1024]{2,1,0:T(8,128)(2,1)}, bf16[16,8,1024]{2,1,0:T(8,128)(2,1)S(1)}, u32[]{:S(2)}, u32[]{:S(2)}) collective-permute-start(bf16[16,8,1024]{2,1,0:T(8,128)(2,1)} %get-tuple-element.29), channel_id=1, source_target_pairs={{0,4},{4,0},{8,12},{12,8},{1,5},{5,1},{9,13},{13,9},{2,6},{6,2},{1... | collective-permute-start | bytes 786440 | tf_op jit(solution)/shard_map/ppermute | solution.py:17
  6.3 14.5 %collective-permute-start.1 = (bf16[16,8,1024]{2,1,0:T(8,128)(2,1)}, bf16[16,8,1024]{2,1,0:T(8,128)(2,1)S(1)}, u32[]{:S(2)}, u32[]{:S(2)}) collective-permute-start(bf16[16,8,1024]{2,1,0:T(8,128)(2,1)} %get-tuple-element.30), channel_id=1, source_target_pairs={{0,8},{4,12},{8,0},{12,4},{1,9},{5,13},{9,1},{13,5},{2,10},{6,14},... | collective-permute-start | bytes 786440 | tf_op jit(solution)/shard_map/ppermute | solution.py:17
  18.4 49.3 %copy-start.16 = (bf16[16,8,1024]{2,1,0:T(8,128)(2,1)}, bf16[16,8,1024]{2,1,0:T(8,128)(2,1)S(1)}, u32[]{:S(2)}) copy-start(bf16[16,8,1024]{2,1,0:T(8,128)(2,1)S(1)} %collective-permute-done.refs_0_) | copy-start | bytes 786436
  20.9 46.8 %copy-start.17 = (bf16[16,8,1024]{2,1,0:T(8,128)(2,1)}, bf16[16,8,1024]{2,1,0:T(8,128)(2,1)S(1)}, u32[]{:S(2)}) copy-start(bf16[16,8,1024]{2,1,0:T(8,128)(2,1)S(1)} %collective-permute-done.1.refs_8_) | copy-start | bytes 786436
  20.9 10.3 %collective-permute-start.2 = (bf16[16,8,1024]{2,1,0:T(8,128)(2,1)}, bf16[16,8,1024]{2,1,0:T(8,128)(2,1)S(1)}, u32[]{:S(2)}, u32[]{:S(2)}) collective-permute-start(bf16[16,8,1024]{2,1,0:T(8,128)(2,1)} %get-tuple-element.31), channel_id=1, source_target_pairs={{0,4},{4,0},{8,12},{12,8},{1,5},{5,1},{9,13},{13,9},{2,6},{6,2},{1... | collective-permute-start | bytes 786440 | tf_op jit(solution)/shard_map/ppermute | solution.py:17
  21.3 13.6 %collective-permute-start.3 = (bf16[16,8,1024]{2,1,0:T(8,128)(2,1)}, bf16[16,8,1024]{2,1,0:T(8,128)(2,1)S(1)}, u32[]{:S(2)}, u32[]{:S(2)}) collective-permute-start(bf16[16,8,1024]{2,1,0:T(8,128)(2,1)} %get-tuple-element.32), channel_id=1, source_target_pairs={{0,8},{4,12},{8,0},{12,4},{1,9},{5,13},{9,1},{13,5},{2,10},{6,14},... | collective-permute-start | bytes 786440 | tf_op jit(solution)/shard_map/ppermute | solution.py:17
  24.0 11.3 %collective-permute-start.6 = (bf16[16,8,1024]{2,1,0:T(8,128)(2,1)S(1)}, bf16[16,8,1024]{2,1,0:T(8,128)(2,1)S(1)}, u32[]{:S(2)}, u32[]{:S(2)}) collective-permute-start(bf16[16,8,1024]{2,1,0:T(8,128)(2,1)S(1)} %collective-permute-done.refs_0_), channel_id=1, source_target_pairs={{0,2},{1,3},{2,0},{3,1},{4,6},{5,7},{6,4},{7,5},{8,10},{9,11},{10,... | collective-permute-start | bytes 786440 | tf_op jit(solution)/shard_map/ppermute | solution.py:17
  25.5 11.6 %collective-permute-start.12 = (bf16[16,8,1024]{2,1,0:T(8,128)(2,1)S(1)}, bf16[16,8,1024]{2,1,0:T(8,128)(2,1)S(1)}, u32[]{:S(2)}, u32[]{:S(2)}) collective-permute-start(bf16[16,8,1024]{2,1,0:T(8,128)(2,1)S(1)} %collective-permute-done.1.refs_8_), channel_id=1, source_target_pairs={{0,2},{1,3},{2,0},{3,1},{4,6},{5,7},{6,4},{7,5},{8,10},{9,11},{10,... | collective-permute-start | bytes 786440 | tf_op jit(solution)/shard_map/ppermute | solution.py:17
  26.0 12.6 %collective-permute-start.14 = (bf16[16,8,1024]{2,1,0:T(8,128)(2,1)S(1)}, bf16[16,8,1024]{2,1,0:T(8,128)(2,1)S(1)}, u32[]{:S(2)}, u32[]{:S(2)}) collective-permute-start(bf16[16,8,1024]{2,1,0:T(8,128)(2,1)S(1)} %collective-permute-done.1.refs_8_), channel_id=1, source_target_pairs={{0,1},{1,0},{2,3},{3,2},{4,5},{5,4},{6,7},{7,6},{8,9},{9,8},{10,11... | collective-permute-start | bytes 786440 | tf_op jit(solution)/shard_map/ppermute | solution.py:17
  31.2 36.4 %copy-start.18 = (bf16[16,8,1024]{2,1,0:T(8,128)(2,1)}, bf16[16,8,1024]{2,1,0:T(8,128)(2,1)S(1)}, u32[]{:S(2)}) copy-start(bf16[16,8,1024]{2,1,0:T(8,128)(2,1)S(1)} %collective-permute-done.2.refs_1_) | copy-start | bytes 786436
  31.2 7.9 %collective-permute-start.8 = (bf16[16,8,1024]{2,1,0:T(8,128)(2,1)S(1)}, bf16[16,8,1024]{2,1,0:T(8,128)(2,1)S(1)}, u32[]{:S(2)}, u32[]{:S(2)}) collective-permute-start(bf16[16,8,1024]{2,1,0:T(8,128)(2,1)S(1)} %collective-permute-done.refs_0_), channel_id=1, source_target_pairs={{0,1},{1,0},{2,3},{3,2},{4,5},{5,4},{6,7},{7,6},{8,9},{9,8},{10,11... | collective-permute-start | bytes 786440 | tf_op jit(solution)/shard_map/ppermute | solution.py:17
  34.9 32.7 %copy-start.19 = (bf16[16,8,1024]{2,1,0:T(8,128)(2,1)}, bf16[16,8,1024]{2,1,0:T(8,128)(2,1)S(1)}, u32[]{:S(2)}) copy-start(bf16[16,8,1024]{2,1,0:T(8,128)(2,1)S(1)} %collective-permute-done.3.refs_9_) | copy-start | bytes 786436
  34.9 11.8 %collective-permute-start.18 = (bf16[16,8,1024]{2,1,0:T(8,128)(2,1)}, bf16[16,8,1024]{2,1,0:T(8,128)(2,1)S(1)}, u32[]{:S(2)}, u32[]{:S(2)}) collective-permute-start(bf16[16,8,1024]{2,1,0:T(8,128)(2,1)} %get-tuple-element.37), channel_id=1, source_target_pairs={{0,8},{4,12},{8,0},{12,4},{1,9},{5,13},{9,1},{13,5},{2,10},{6,14},... | collective-permute-start | bytes 786440 | tf_op jit(solution)/shard_map/ppermute | solution.py:17
  35.3 32.4 %copy-start.20 = (bf16[16,8,1024]{2,1,0:T(8,128)(2,1)}, bf16[16,8,1024]{2,1,0:T(8,128)(2,1)S(1)}, u32[]{:S(2)}) copy-start(bf16[16,8,1024]{2,1,0:T(8,128)(2,1)S(1)} %collective-permute-done.6.refs_2_) | copy-start | bytes 786436
  35.3 11.7 %collective-permute-start.4 = (bf16[16,8,1024]{2,1,0:T(8,128)(2,1)}, bf16[16,8,1024]{2,1,0:T(8,128)(2,1)S(1)}, u32[]{:S(2)}, u32[]{:S(2)}) collective-permute-start(bf16[16,8,1024]{2,1,0:T(8,128)(2,1)} %get-tuple-element.33), channel_id=1, source_target_pairs={{0,4},{4,0},{8,12},{12,8},{1,5},{5,1},{9,13},{13,9},{2,6},{6,2},{1... | collective-permute-start | bytes 786440 | tf_op jit(solution)/shard_map/ppermute | solution.py:17
  37.1 13.5 %copy-start.21 = (bf16[16,8,1024]{2,1,0:T(8,128)(2,1)}, bf16[16,8,1024]{2,1,0:T(8,128)(2,1)S(1)}, u32[]{:S(2)}) copy-start(bf16[16,8,1024]{2,1,0:T(8,128)(2,1)S(1)} %collective-permute-done.12.refs_10_) | copy-start | bytes 786436
  37.1 10.2 %collective-permute-start.7 = (bf16[16,8,1024]{2,1,0:T(8,128)(2,1)S(1)}, bf16[16,8,1024]{2,1,0:T(8,128)(2,1)S(1)}, u32[]{:S(2)}, u32[]{:S(2)}) collective-permute-start(bf16[16,8,1024]{2,1,0:T(8,128)(2,1)S(1)} %collective-permute-done.2.refs_1_), channel_id=1, source_target_pairs={{0,2},{1,3},{2,0},{3,1},{4,6},{5,7},{6,4},{7,5},{8,10},{9,11},{10,... | collective-permute-start | bytes 786440 | tf_op jit(solution)/shard_map/ppermute | solution.py:17
  38.6 8.9 %copy-start.22 = (bf16[16,8,1024]{2,1,0:T(8,128)(2,1)}, bf16[16,8,1024]{2,1,0:T(8,128)(2,1)S(1)}, u32[]{:S(2)}) copy-start(bf16[16,8,1024]{2,1,0:T(8,128)(2,1)S(1)} %collective-permute-done.14.refs_12_) | copy-start | bytes 786436
  38.6 10.1 %collective-permute-start.13 = (bf16[16,8,1024]{2,1,0:T(8,128)(2,1)S(1)}, bf16[16,8,1024]{2,1,0:T(8,128)(2,1)}, u32[]{:S(2)}, u32[]{:S(2)}) collective-permute-start(bf16[16,8,1024]{2,1,0:T(8,128)(2,1)S(1)} %collective-permute-done.3.refs_9_), channel_id=1, source_target_pairs={{0,2},{1,3},{2,0},{3,1},{4,6},{5,7},{6,4},{7,5},{8,10},{9,11},{10,... | collective-permute-start | bytes 786440 | tf_op jit(solution)/shard_map/ppermute | solution.py:17
  39.1 10.0 %copy-start.23 = (bf16[16,8,1024]{2,1,0:T(8,128)(2,1)}, bf16[16,8,1024]{2,1,0:T(8,128)(2,1)S(1)}, u32[]{:S(2)}) copy-start(bf16[16,8,1024]{2,1,0:T(8,128)(2,1)S(1)} %collective-permute-done.8.refs_4_) | copy-start | bytes 786436
  39.1 10.0 %collective-permute-start.15 = (bf16[16,8,1024]{2,1,0:T(8,128)(2,1)S(1)}, bf16[16,8,1024]{2,1,0:T(8,128)(2,1)S(1)}, u32[]{:S(2)}, u32[]{:S(2)}) collective-permute-start(bf16[16,8,1024]{2,1,0:T(8,128)(2,1)S(1)} %collective-permute-done.3.refs_9_), channel_id=1, source_target_pairs={{0,1},{1,0},{2,3},{3,2},{4,5},{5,4},{6,7},{7,6},{8,9},{9,8},{10,11... | collective-permute-start | bytes 786440 | tf_op jit(solution)/shard_map/ppermute | solution.py:17
  46.8 38.7 %copy-start = (bf16[16,8,1024]{2,1,0:T(8,128)(2,1)}, bf16[16,8,1024]{2,1,0:T(8,128)(2,1)S(1)}, u32[]{:S(2)}) copy-start(bf16[16,8,1024]{2,1,0:T(8,128)(2,1)S(1)} %collective-permute-done.18.refs_8_) | copy-start | bytes 786436
  46.8 2.4 %collective-permute-start.9 = (bf16[16,8,1024]{2,1,0:T(8,128)(2,1)S(1)}, bf16[16,8,1024]{2,1,0:T(8,128)(2,1)S(1)}, u32[]{:S(2)}, u32[]{:S(2)}) collective-permute-start(bf16[16,8,1024]{2,1,0:T(8,128)(2,1)S(1)} %collective-permute-done.2.refs_1_), channel_id=1, source_target_pairs={{0,1},{1,0},{2,3},{3,2},{4,5},{5,4},{6,7},{7,6},{8,9},{9,8},{10,11... | collective-permute-start | bytes 786440 | tf_op jit(solution)/shard_map/ppermute | solution.py:17
  47.0 38.4 %copy-start.1 = (bf16[16,8,1024]{2,1,0:T(8,128)(2,1)}, bf16[16,8,1024]{2,1,0:T(8,128)(2,1)S(1)}, u32[]{:S(2)}) copy-start(bf16[16,8,1024]{2,1,0:T(8,128)(2,1)S(1)} %collective-permute-done.4.refs_0_) | copy-start | bytes 786436
  47.0 3.6 %collective-permute-start.10 = (bf16[16,8,1024]{2,1,0:T(8,128)(2,1)S(1)}, bf16[16,8,1024]{2,1,0:T(8,128)(2,1)S(1)}, u32[]{:S(2)}, u32[]{:S(2)}) collective-permute-start(bf16[16,8,1024]{2,1,0:T(8,128)(2,1)S(1)} %collective-permute-done.6.refs_2_), channel_id=1, source_target_pairs={{0,1},{1,0},{2,3},{3,2},{4,5},{5,4},{6,7},{7,6},{8,9},{9,8},{10,11... | collective-permute-start | bytes 786440 | tf_op jit(solution)/shard_map/ppermute | solution.py:17
  47.3 18.2 %copy-start.24 = (bf16[16,8,1024]{2,1,0:T(8,128)(2,1)}, bf16[16,8,1024]{2,1,0:T(8,128)(2,1)S(1)}, u32[]{:S(2)}) copy-start(bf16[16,8,1024]{2,1,0:T(8,128)(2,1)S(1)} %collective-permute-done.7.refs_3_) | copy-start | bytes 786436
  47.3 3.3 %collective-permute-start.16 = (bf16[16,8,1024]{2,1,0:T(8,128)(2,1)S(1)}, bf16[16,8,1024]{2,1,0:T(8,128)(2,1)S(1)}, u32[]{:S(2)}, u32[]{:S(2)}) collective-permute-start(bf16[16,8,1024]{2,1,0:T(8,128)(2,1)S(1)} %collective-permute-done.12.refs_10_), channel_id=1, source_target_pairs={{0,1},{1,0},{2,3},{3,2},{4,5},{5,4},{6,7},{7,6},{8,9},{9,8},{10,11... | collective-permute-start | bytes 786440 | tf_op jit(solution)/shard_map/ppermute | solution.py:17
  48.7 13.9 %collective-permute-start.26 = (bf16[16,8,1024]{2,1,0:T(8,128)(2,1)}, bf16[16,8,1024]{2,1,0:T(8,128)(2,1)S(1)}, u32[]{:S(2)}, u32[]{:S(2)}) collective-permute-start(bf16[16,8,1024]{2,1,0:T(8,128)(2,1)} %get-tuple-element.43), channel_id=1, source_target_pairs={{0,8},{4,12},{8,0},{12,4},{1,9},{5,13},{9,1},{13,5},{2,10},{6,14},... | collective-permute-start | bytes 786440 | tf_op jit(solution)/shard_map/ppermute | solution.py:17
  49.1 3.1 %copy-start.25 = (bf16[16,8,1024]{2,1,0:T(8,128)(2,1)}, bf16[16,8,1024]{2,1,0:T(8,128)(2,1)S(1)}, u32[]{:S(2)}) copy-start(bf16[16,8,1024]{2,1,0:T(8,128)(2,1)S(1)} %collective-permute-done.15.refs_13_) | copy-start | bytes 786436
  49.1 16.4 %collective-permute-start.11 = (bf16[16,8,1024]{2,1,0:T(8,128)(2,1)S(1)}, bf16[16,8,1024]{2,1,0:T(8,128)(2,1)}, u32[]{:S(2)}, u32[]{:S(2)}) collective-permute-start(bf16[16,8,1024]{2,1,0:T(8,128)(2,1)S(1)} %collective-permute-done.7.refs_3_), channel_id=1, source_target_pairs={{0,1},{1,0},{2,3},{3,2},{4,5},{5,4},{6,7},{7,6},{8,9},{9,8},{10,11... | collective-permute-start | bytes 786440 | tf_op jit(solution)/shard_map/ppermute | solution.py:17
  49.1 17.0 %copy-start.26 = (bf16[16,8,1024]{2,1,0:T(8,128)(2,1)}, bf16[16,8,1024]{2,1,0:T(8,128)(2,1)S(1)}, u32[]{:S(2)}) copy-start(bf16[16,8,1024]{2,1,0:T(8,128)(2,1)S(1)} %collective-permute-done.9.refs_5_) | copy-start | bytes 786436
  49.1 16.9 %collective-permute-start.19 = (bf16[16,8,1024]{2,1,0:T(8,128)(2,1)}, bf16[16,8,1024]{2,1,0:T(8,128)(2,1)S(1)}, u32[]{:S(2)}, u32[]{:S(2)}) collective-permute-start(bf16[16,8,1024]{2,1,0:T(8,128)(2,1)} %get-tuple-element.38), channel_id=1, source_target_pairs={{0,4},{4,0},{8,12},{12,8},{1,5},{5,1},{9,13},{13,9},{2,6},{6,2},{1... | collective-permute-start | bytes 786440 | tf_op jit(solution)/shard_map/ppermute | solution.py:17
  50.6 12.0 %copy-start.27 = (bf16[16,8,1024]{2,1,0:T(8,128)(2,1)}, bf16[16,8,1024]{2,1,0:T(8,128)(2,1)S(1)}, u32[]{:S(2)}) copy-start(bf16[16,8,1024]{2,1,0:T(8,128)(2,1)S(1)} %collective-permute-done.10.refs_6_) | copy-start | bytes 786436
  50.6 17.1 %collective-permute-start.17 = (bf16[16,8,1024]{2,1,0:T(8,128)(2,1)}, bf16[16,8,1024]{2,1,0:T(8,128)(2,1)}, u32[]{:S(2)}, u32[]{:S(2)}) collective-permute-start(bf16[16,8,1024]{2,1,0:T(8,128)(2,1)} %collective-permute-done.13.refs_11_), channel_id=1, source_target_pairs={{0,1},{1,0},{2,3},{3,2},{4,5},{5,4},{6,7},{7,6},{8,9},{9,8},{10,11... | collective-permute-start | bytes 786440 | tf_op jit(solution)/shard_map/ppermute | solution.py:17
  50.6 12.0 %copy-start.28 = (bf16[16,8,1024]{2,1,0:T(8,128)(2,1)}, bf16[16,8,1024]{2,1,0:T(8,128)(2,1)S(1)}, u32[]{:S(2)}) copy-start(bf16[16,8,1024]{2,1,0:T(8,128)(2,1)S(1)} %collective-permute-done.16.refs_14_) | copy-start | bytes 786436
  50.6 23.6 %collective-permute-start.25 = (bf16[16,8,1024]{2,1,0:T(8,128)(2,1)S(1)}, bf16[16,8,1024]{2,1,0:T(8,128)(2,1)S(1)}, u32[]{:S(2)}, u32[]{:S(2)}) collective-permute-start(bf16[16,8,1024]{2,1,0:T(8,128)(2,1)S(1)} %collective-permute-done.18.refs_8_), channel_id=1, source_target_pairs={{0,2},{1,3},{2,0},{3,1},{4,6},{5,7},{6,4},{7,5},{8,10},{9,11},{10,... | collective-permute-start | bytes 786440 | tf_op jit(solution)/shard_map/ppermute | solution.py:17
  62.6 22.8 %copy-start.2 = (bf16[16,8,1024]{2,1,0:T(8,128)(2,1)}, bf16[16,8,1024]{2,1,0:T(8,128)(2,1)S(1)}, u32[]{:S(2)}) copy-start(bf16[16,8,1024]{2,1,0:T(8,128)(2,1)S(1)} %collective-permute-done.26.refs_9_) | copy-start | bytes 786436
  62.6 12.3 %collective-permute-start.5 = (bf16[16,8,1024]{2,1,0:T(8,128)(2,1)S(1)}, bf16[16,8,1024]{2,1,0:T(8,128)(2,1)S(1)}, u32[]{:S(2)}, u32[]{:S(2)}) collective-permute-start(bf16[16,8,1024]{2,1,0:T(8,128)(2,1)S(1)} %collective-permute-done.4.refs_0_), channel_id=1, source_target_pairs={{0,2},{1,3},{2,0},{3,1},{4,6},{5,7},{6,4},{7,5},{8,10},{9,11},{10,... | collective-permute-start | bytes 786440 | tf_op jit(solution)/shard_map/ppermute | solution.py:17
  65.5 11.9 %collective-permute-start.27 = (bf16[16,8,1024]{2,1,0:T(8,128)(2,1)S(1)}, bf16[16,8,1024]{2,1,0:T(8,128)(2,1)S(1)}, u32[]{:S(2)}, u32[]{:S(2)}) collective-permute-start(bf16[16,8,1024]{2,1,0:T(8,128)(2,1)S(1)} %collective-permute-done.26.refs_9_), channel_id=1, source_target_pairs={{0,2},{1,3},{2,0},{3,1},{4,6},{5,7},{6,4},{7,5},{8,10},{9,11},{10,... | collective-permute-start | bytes 786440 | tf_op jit(solution)/shard_map/ppermute | solution.py:17
  66.1 19.3 %copy-start.3 = (bf16[16,8,1024]{2,1,0:T(8,128)(2,1)}, bf16[16,8,1024]{2,1,0:T(8,128)(2,1)S(1)}, u32[]{:S(2)}) copy-start(bf16[16,8,1024]{2,1,0:T(8,128)(2,1)S(1)} %collective-permute-done.19.refs_1_) | copy-start | bytes 786436
  66.1 16.0 %collective-permute-start.20 = (bf16[16,8,1024]{2,1,0:T(8,128)(2,1)S(1)}, bf16[16,8,1024]{2,1,0:T(8,128)(2,1)S(1)}, u32[]{:S(2)}, u32[]{:S(2)}) collective-permute-start(bf16[16,8,1024]{2,1,0:T(8,128)(2,1)S(1)} %collective-permute-done.19.refs_1_), channel_id=1, source_target_pairs={{0,2},{1,3},{2,0},{3,1},{4,6},{5,7},{6,4},{7,5},{8,10},{9,11},{10,... | collective-permute-start | bytes 786440 | tf_op jit(solution)/shard_map/ppermute | solution.py:17
  74.3 11.1 %copy-start.4 = (bf16[16,8,1024]{2,1,0:T(8,128)(2,1)}, bf16[16,8,1024]{2,1,0:T(8,128)(2,1)S(1)}, u32[]{:S(2)}) copy-start(bf16[16,8,1024]{2,1,0:T(8,128)(2,1)S(1)} %collective-permute-done.25.refs_10_) | copy-start | bytes 786436
  74.3 7.8 %collective-permute-start.28 = (bf16[16,8,1024]{2,1,0:T(8,128)(2,1)S(1)}, bf16[16,8,1024]{2,1,0:T(8,128)(2,1)S(1)}, u32[]{:S(2)}, u32[]{:S(2)}) collective-permute-start(bf16[16,8,1024]{2,1,0:T(8,128)(2,1)S(1)} %collective-permute-done.18.refs_8_), channel_id=1, source_target_pairs={{0,1},{1,0},{2,3},{3,2},{4,5},{5,4},{6,7},{7,6},{8,9},{9,8},{10,11... | collective-permute-start | bytes 786440 | tf_op jit(solution)/shard_map/ppermute | solution.py:17
  74.4 8.2 %collective-permute-start.30 = (bf16[16,8,1024]{2,1,0:T(8,128)(2,1)S(1)}, bf16[16,8,1024]{2,1,0:T(8,128)(2,1)S(1)}, u32[]{:S(2)}, u32[]{:S(2)}) collective-permute-start(bf16[16,8,1024]{2,1,0:T(8,128)(2,1)S(1)} %collective-permute-done.25.refs_10_), channel_id=1, source_target_pairs={{0,1},{1,0},{2,3},{3,2},{4,5},{5,4},{6,7},{7,6},{8,9},{9,8},{10,11... | collective-permute-start | bytes 786440 | tf_op jit(solution)/shard_map/ppermute | solution.py:17
  74.9 10.6 %copy-start.5 = (bf16[16,8,1024]{2,1,0:T(8,128)(2,1)}, bf16[16,8,1024]{2,1,0:T(8,128)(2,1)S(1)}, u32[]{:S(2)}) copy-start(bf16[16,8,1024]{2,1,0:T(8,128)(2,1)S(1)} %collective-permute-done.5.refs_2_) | copy-start | bytes 786436
  74.9 7.8 %collective-permute-start.21 = (bf16[16,8,1024]{2,1,0:T(8,128)(2,1)S(1)}, bf16[16,8,1024]{2,1,0:T(8,128)(2,1)S(1)}, u32[]{:S(2)}, u32[]{:S(2)}) collective-permute-start(bf16[16,8,1024]{2,1,0:T(8,128)(2,1)S(1)} %collective-permute-done.4.refs_0_), channel_id=1, source_target_pairs={{0,1},{1,0},{2,3},{3,2},{4,5},{5,4},{6,7},{7,6},{8,9},{9,8},{10,11... | collective-permute-start | bytes 786440 | tf_op jit(solution)/shard_map/ppermute | solution.py:17
  77.4 8.0 %copy-start.6 = (bf16[16,8,1024]{2,1,0:T(8,128)(2,1)}, bf16[16,8,1024]{2,1,0:T(8,128)(2,1)S(1)}, u32[]{:S(2)}) copy-start(bf16[16,8,1024]{2,1,0:T(8,128)(2,1)S(1)} %collective-permute-done.27.refs_11_) | copy-start | bytes 786436
  77.4 5.7 %collective-permute-start.23 = (bf16[16,8,1024]{2,1,0:T(8,128)(2,1)S(1)}, bf16[16,8,1024]{2,1,0:T(8,128)(2,1)S(1)}, u32[]{:S(2)}, u32[]{:S(2)}) collective-permute-start(bf16[16,8,1024]{2,1,0:T(8,128)(2,1)S(1)} %collective-permute-done.5.refs_2_), channel_id=1, source_target_pairs={{0,1},{1,0},{2,3},{3,2},{4,5},{5,4},{6,7},{7,6},{8,9},{9,8},{10,11... | collective-permute-start | bytes 786440 | tf_op jit(solution)/shard_map/ppermute | solution.py:17
  82.0 3.4 %copy-start.7 = (bf16[16,8,1024]{2,1,0:T(8,128)(2,1)}, bf16[16,8,1024]{2,1,0:T(8,128)(2,1)S(1)}, u32[]{:S(2)}) copy-start(bf16[16,8,1024]{2,1,0:T(8,128)(2,1)S(1)} %collective-permute-done.20.refs_3_) | copy-start | bytes 786436
  82.0 1.5 %collective-permute-start.29 = (bf16[16,8,1024]{2,1,0:T(8,128)(2,1)S(1)}, bf16[16,8,1024]{2,1,0:T(8,128)(2,1)S(1)}, u32[]{:S(2)}, u32[]{:S(2)}) collective-permute-start(bf16[16,8,1024]{2,1,0:T(8,128)(2,1)S(1)} %collective-permute-done.26.refs_9_), channel_id=1, source_target_pairs={{0,1},{1,0},{2,3},{3,2},{4,5},{5,4},{6,7},{7,6},{8,9},{9,8},{10,11... | collective-permute-start | bytes 786440 | tf_op jit(solution)/shard_map/ppermute | solution.py:17
  82.1 3.4 %copy-start.8 = (bf16[16,8,1024]{2,1,0:T(8,128)(2,1)}, bf16[16,8,1024]{2,1,0:T(8,128)(2,1)S(1)}, u32[]{:S(2)}) copy-start(bf16[16,8,1024]{2,1,0:T(8,128)(2,1)S(1)} %collective-permute-done.28.refs_12_) | copy-start | bytes 786436
  82.1 1.9 %collective-permute-start.31 = (bf16[16,8,1024]{2,1,0:T(8,128)(2,1)S(1)}, bf16[16,8,1024]{2,1,0:T(8,128)(2,1)S(1)}, u32[]{:S(2)}, u32[]{:S(2)}) collective-permute-start(bf16[16,8,1024]{2,1,0:T(8,128)(2,1)S(1)} %collective-permute-done.27.refs_11_), channel_id=1, source_target_pairs={{0,1},{1,0},{2,3},{3,2},{4,5},{5,4},{6,7},{7,6},{8,9},{9,8},{10,11... | collective-permute-start | bytes 786440 | tf_op jit(solution)/shard_map/ppermute | solution.py:17
  82.6 2.9 %copy-start.9 = (bf16[16,8,1024]{2,1,0:T(8,128)(2,1)}, bf16[16,8,1024]{2,1,0:T(8,128)(2,1)S(1)}, u32[]{:S(2)}) copy-start(bf16[16,8,1024]{2,1,0:T(8,128)(2,1)S(1)} %collective-permute-done.30.refs_14_) | copy-start | bytes 786436
  82.6 1.8 %collective-permute-start.22 = (bf16[16,8,1024]{2,1,0:T(8,128)(2,1)S(1)}, bf16[16,8,1024]{2,1,0:T(8,128)(2,1)S(1)}, u32[]{:S(2)}, u32[]{:S(2)}) collective-permute-start(bf16[16,8,1024]{2,1,0:T(8,128)(2,1)S(1)} %collective-permute-done.19.refs_1_), channel_id=1, source_target_pairs={{0,1},{1,0},{2,3},{3,2},{4,5},{5,4},{6,7},{7,6},{8,9},{9,8},{10,11... | collective-permute-start | bytes 786440 | tf_op jit(solution)/shard_map/ppermute | solution.py:17
  82.7 2.8 %copy-start.10 = (bf16[16,8,1024]{2,1,0:T(8,128)(2,1)}, bf16[16,8,1024]{2,1,0:T(8,128)(2,1)S(1)}, u32[]{:S(2)}) copy-start(bf16[16,8,1024]{2,1,0:T(8,128)(2,1)S(1)} %collective-permute-done.21.refs_4_) | copy-start | bytes 786436
  82.7 2.0 %collective-permute-start.24 = (bf16[16,8,1024]{2,1,0:T(8,128)(2,1)S(1)}, bf16[16,8,1024]{2,1,0:T(8,128)(2,1)S(1)}, u32[]{:S(2)}, u32[]{:S(2)}) collective-permute-start(bf16[16,8,1024]{2,1,0:T(8,128)(2,1)S(1)} %collective-permute-done.20.refs_3_), channel_id=1, source_target_pairs={{0,1},{1,0},{2,3},{3,2},{4,5},{5,4},{6,7},{7,6},{8,9},{9,8},{10,11... | collective-permute-start | bytes 786440 | tf_op jit(solution)/shard_map/ppermute | solution.py:17
  83.1 2.4 %copy-start.11 = (bf16[16,8,1024]{2,1,0:T(8,128)(2,1)}, bf16[16,8,1024]{2,1,0:T(8,128)(2,1)S(1)}, u32[]{:S(2)}) copy-start(bf16[16,8,1024]{2,1,0:T(8,128)(2,1)S(1)} %collective-permute-done.23.refs_6_) | copy-start | bytes 786436
  83.6 1.9 %copy-start.12 = (bf16[16,8,1024]{2,1,0:T(8,128)(2,1)}, bf16[16,8,1024]{2,1,0:T(8,128)(2,1)S(1)}, u32[]{:S(2)}) copy-start(bf16[16,8,1024]{2,1,0:T(8,128)(2,1)S(1)} %collective-permute-done.29.refs_13_) | copy-start | bytes 786436
  84.0 0.8 copy-start.13
  84.3 0.7 copy-start.14
  84.7 0.7 copy-start.15

commit v9 on v7

--- a/solution.py
+++ b/solution.py
@@ -19,13 +19,17 @@
 
 def slice_kernel(delays_ref, window_ref, *outs, levels, steps):
     me = lax.axis_index("area")
+    rows, width = outs[0].shape
+    side = 128 if width % 128 == 0 else width
     for rnd, out in enumerate(outs):
         start = delays_ref[rnd, me ^ (1 << (rnd % levels))] - steps
-        out[...] = window_ref[pl.ds(start, steps)]
+        for c in range(0, width, side):
+            x = window_ref[pl.ds(start, steps), :, c:c + side].astype(jnp.float32)
+            out[:, c:c + side] = x.reshape(rows, side).astype(out.dtype)
 
 
 def send_slices(window, delays, rounds, levels, steps):
-    shape = (steps,) + window.shape[1:]
+    shape = (steps * window.shape[1], window.shape[2])
     kernel = functools.partial(slice_kernel, levels=levels, steps=steps)
     return pl.pallas_call(
         kernel,
@@ -56,15 +60,14 @@
         cur_ref, lv_out, la_out = next(it), next(it), next(it)
     else:
         out_ref = next(it)
-    piece_buf = [next(it) for _ in range(n_pieces)]
+    piece_buf = next(it)
     w_buf = next(it)
-    blocks = next(it)
     sem = next(it)
     rec_buf = next(it)
     if final:
         scan_buf = [next(it) for _ in range(7)]
 
-    steps, batch, width = piece_hbm[0].shape
+    steps, batch = rec_buf.shape[0], rec_buf.shape[1]
     local_blocks, nnz, side = w_buf.shape[1], w_buf.shape[2], w_buf.shape[3]
     rows = steps * batch
     bits = n_pos.bit_length() - 1
@@ -82,7 +85,7 @@
     rec_cp = None
     scan_cp = []
     for ri, rnd in enumerate(stage):
-        piece_cp += [start(piece_hbm[ri * n_pos + p], piece_buf[ri * n_pos + p]) for p in range(n_pos)]
+        piece_cp += [start(piece_hbm[ri * n_pos + p], piece_buf.at[ri * n_pos + p]) for p in range(n_pos)]
         w_cp.append(start(w_hbm.at[rnd, 0], w_buf.at[ri]))
         if ri == 0 and has_rec:
             rec_cp = start(rec_hbm, rec_buf)
@@ -91,11 +94,7 @@
 
     for ri, rnd in enumerate(stage):
         for p in range(n_pos):
-            k = ri * n_pos + p
-            piece_cp[k].wait()
-            for i in range(local_blocks):
-                x = piece_buf[k][:, :, i * side:(i + 1) * side].astype(jnp.float32)
-                blocks[p * local_blocks + i] = x.reshape(rows, side).astype(jnp.bfloat16)
+            piece_cp[ri * n_pos + p].wait()
         w_cp[ri].wait()
         if ri == 0 and has_rec:
             rec_cp.wait()
@@ -116,7 +115,8 @@
                 rel = 0
                 for s_, bit in enumerate(reversed(range(bits))):
                     rel = rel | (((d >> bit) & 1) << s_)
-                x = blocks[rel * local_blocks + idx % local_blocks]
+                off = pl.multiple_of((idx % local_blocks) * side, side)
+                x = piece_buf[ri * n_pos + rel, :, pl.ds(off, side)]
                 acc = acc + jnp.dot(x, w_buf[ri, j, k], preferred_element_type=jnp.float32)
             rec = acc.reshape(steps, batch, side)
             if not last:
@@ -141,17 +141,17 @@
             la_out[:, cols] = la_now
 
 
-def stage_contrib(block_index, pieces, weights, stage, n_pos, rec, scan_args):
-    steps, batch, local = pieces[0].shape
+def stage_contrib(block_index, pieces, weights, stage, n_pos, rec, scan_args, steps):
+    rows, local = pieces[0].shape
     _, _, local_blocks, nnz, side, _ = weights.shape
+    batch = rows // steps
     n_rounds = len(stage)
     final = scan_args is not None
     has_rec = rec is not None
     operands = list(pieces) + [weights]
-    scratch = [pltpu.VMEM(p.shape, p.dtype) for p in pieces]
-    scratch += [
+    scratch = [
+        pltpu.VMEM((len(pieces), rows, local), pieces[0].dtype),
         pltpu.VMEM((n_rounds, local_blocks, nnz, side, side), weights.dtype),
-        pltpu.VMEM((n_pos * local_blocks, steps * batch, side), jnp.bfloat16),
     ]
     n_sem = len(pieces) + n_rounds + (1 if has_rec else 0) + (7 if final else 0)
     scratch.append(pltpu.SemaphoreType.DMA((n_sem,)))
@@ -216,7 +216,7 @@
         scan_args = None
         if si == len(stages) - 1:
             scan_args = (err_grad, surrogate, lv_end, la_end, alpha, rho, beta)
-        rec = stage_contrib(block_index, chunks, weights, stage, n_pos, rec, scan_args)
+        rec = stage_contrib(block_index, chunks, weights, stage, n_pos, rec, scan_args, steps)
     return rec
 
 

time: 94.3 us -> 94.8 us (level)
  no operation moved by 1% of the time
where the time goes in v9:
time: 94.8 us; the launch traced here: 94.3 us
  waiting for transfers between devices  58.6 us (62%)
  Pallas kernels  17.2 us (18%)
  starting transfers between devices  15.4 us (16%)
  local copies, waits for them, and re-layouts  2.54 us (3%)
    ppermute x16, waiting for transfers between devices, swap(): return lax.ppermute(value, axis, pairs)  58.6 us
    ppermute x16, starting transfers between devices, swap(): return lax.ppermute(value, axis, pairs)  15.4 us
    pallas_call x2, Pallas kernels, stage_contrib(): pl.pallas_call(kernel, in_specs=[SMEM] + [ANY] * len(operands), out_specs...  14.1 us
    pallas_call x1, Pallas kernels, send_slices(): pl.pallas_call(kernel, in_specs=[SMEM, VMEM], out_specs=[VMEM] * rounds,...  3.05 us
    unnamed x23, local copies, waits for them, and re-layouts  2.54 us
  transfers between devices with their start and end apart: 16, of which 9 were waited for; matrix products, arithmetic and copies ran while one was open for 1% of the time, Pallas kernels for 7%

profile of v9, /device:TPU:0, one launch (start us, length us, event | category | flops | bytes accessed | tf_op | source)
XLA Modules:
  0.0 94.3 jit_solution(4173345323436209019)
XLA Ops:
  0.6 3.0 %shard_map.130 = (bf16[128,2048]{1,0:T(8,128)(2,1)}, bf16[128,2048]{1,0:T(8,128)(2,1)}, bf16[128,2048]{1,0:T(8,128)(2,1)}, bf16[128,2048]{1,0:T(8,128)(2,1)}) custom-call(s32[4,4]{1,0:T(4,128)} %delays_ref.1, bf16[32,8,2048]{2,1,0:T(8,128)(2,1)} %window_ref.1), custom_call_target="tpu_custom_call" | custom-call | tf_op jit(solution)/shard_map/pallas_call | solution.py:34
  3.7 3.0 %collective-permute-start = (bf16[128,2048]{1,0:T(8,128)(2,1)}, bf16[128,2048]{1,0:T(8,128)(2,1)S(1)}, u32[]{:S(2)}, u32[]{:S(2)}) collective-permute-start(bf16[128,2048]{1,0:T(8,128)(2,1)} %get-tuple-element.15), channel_id=1, source_target_pairs={{0,4},{4,0},{8,12},{12,8},{1,5},{5,1},{9,13},{13,9},{2,6},{6,2},{1... | collective-permute-start | bytes 1572872 | tf_op jit(solution)/shard_map/ppermute | solution.py:17
  6.7 2.6 %collective-permute-start.1 = (bf16[128,2048]{1,0:T(8,128)(2,1)}, bf16[128,2048]{1,0:T(8,128)(2,1)S(1)}, u32[]{:S(2)}, u32[]{:S(2)}) collective-permute-start(bf16[128,2048]{1,0:T(8,128)(2,1)} %get-tuple-element.16), channel_id=1, source_target_pairs={{0,8},{4,12},{8,0},{12,4},{1,9},{5,13},{9,1},{13,5},{2,10},{6,14},... | collective-permute-start | bytes 1572872 | tf_op jit(solution)/shard_map/ppermute | solution.py:17
  9.3 20.7 %collective-permute-done.refs_0_ = bf16[128,2048]{1,0:T(8,128)(2,1)S(1)} collective-permute-done((bf16[128,2048]{1,0:T(8,128)(2,1)}, bf16[128,2048]{1,0:T(8,128)(2,1)S(1)}, u32[]{:S(2)}, u32[]{:S(2)}) %collective-permute-start) | collective-permute-done | bytes 524320 | tf_op jit(solution)/shard_map/ppermute | solution.py:17
  30.0 0.0 copy-start.8
  30.0 1.7 %collective-permute-start.4 = (bf16[128,2048]{1,0:T(8,128)(2,1)S(1)}, bf16[128,2048]{1,0:T(8,128)(2,1)}, u32[]{:S(2)}, u32[]{:S(2)}) collective-permute-start(bf16[128,2048]{1,0:T(8,128)(2,1)S(1)} %collective-permute-done.refs_0_), channel_id=1, source_target_pairs={{0,2},{1,3},{2,0},{3,1},{4,6},{5,7},{6,4},{7,5},{8,10},{9,11},{10,... | collective-permute-start | bytes 1572872 | tf_op jit(solution)/shard_map/ppermute | solution.py:17
  31.6 0.0 collective-permute-start.5
  31.6 0.9 collective-permute-done.1.refs_4_
  32.5 0.0 copy-start.9
  32.5 1.5 %collective-permute-start.7 = (bf16[128,2048]{1,0:T(8,128)(2,1)S(1)}, bf16[128,2048]{1,0:T(8,128)(2,1)}, u32[]{:S(2)}, u32[]{:S(2)}) collective-permute-start(bf16[128,2048]{1,0:T(8,128)(2,1)S(1)} %collective-permute-done.1.refs_4_), channel_id=1, source_target_pairs={{0,2},{1,3},{2,0},{3,1},{4,6},{5,7},{6,4},{7,5},{8,10},{9,11},{10,... | collective-permute-start | bytes 1572872 | tf_op jit(solution)/shard_map/ppermute | solution.py:17
  34.0 0.3 collective-permute-start.12
  34.3 2.7 %collective-permute-start.2 = (bf16[128,2048]{1,0:T(8,128)(2,1)}, bf16[128,2048]{1,0:T(8,128)(2,1)S(1)}, u32[]{:S(2)}, u32[]{:S(2)}) collective-permute-start(bf16[128,2048]{1,0:T(8,128)(2,1)} %get-tuple-element.17), channel_id=1, source_target_pairs={{0,4},{4,0},{8,12},{12,8},{1,5},{5,1},{9,13},{13,9},{2,6},{6,2},{1... | collective-permute-start | bytes 1572872 | tf_op jit(solution)/shard_map/ppermute | solution.py:17
  37.0 7.9 %collective-permute-done.4.refs_1_ = bf16[128,2048]{1,0:T(8,128)(2,1)} collective-permute-done((bf16[128,2048]{1,0:T(8,128)(2,1)S(1)}, bf16[128,2048]{1,0:T(8,128)(2,1)}, u32[]{:S(2)}, u32[]{:S(2)}) %collective-permute-start.4) | collective-permute-done | bytes 524320 | tf_op jit(solution)/shard_map/ppermute | solution.py:17
  44.9 0.0 collective-permute-start.8
  44.9 9.5 %collective-permute-done.7.refs_5_ = bf16[128,2048]{1,0:T(8,128)(2,1)} collective-permute-done((bf16[128,2048]{1,0:T(8,128)(2,1)S(1)}, bf16[128,2048]{1,0:T(8,128)(2,1)}, u32[]{:S(2)}, u32[]{:S(2)}) %collective-permute-start.7) | collective-permute-done | bytes 524320 | tf_op jit(solution)/shard_map/ppermute | solution.py:17
  54.4 0.0 collective-permute-start.6
  54.4 0.0 collective-permute-done.5.refs_2_
  54.4 0.0 copy-start.10
  54.4 0.5 collective-permute-start.9
  54.9 0.3 copy-done.10
  55.2 3.2 %collective-permute-done.12.refs_4_ = bf16[128,2048]{1,0:T(8,128)(2,1)S(1)} collective-permute-done((bf16[128,2048]{1,0:T(8,128)(2,1)}, bf16[128,2048]{1,0:T(8,128)(2,1)S(1)}, u32[]{:S(2)}, u32[]{:S(2)}) %collective-permute-start.12) | collective-permute-done | bytes 524320 | tf_op jit(solution)/shard_map/ppermute | solution.py:17
  58.4 0.0 copy-start
  58.4 1.6 %collective-permute-start.13 = (bf16[128,2048]{1,0:T(8,128)(2,1)S(1)}, bf16[128,2048]{1,0:T(8,128)(2,1)S(1)}, u32[]{:S(2)}, u32[]{:S(2)}) collective-permute-start(bf16[128,2048]{1,0:T(8,128)(2,1)S(1)} %collective-permute-done.12.refs_4_), channel_id=1, source_target_pairs={{0,2},{1,3},{2,0},{3,1},{4,6},{5,7},{6,4},{7,5},{8,10},{9,11},{10,... | collective-permute-start | bytes 1572872 | tf_op jit(solution)/shard_map/ppermute | solution.py:17
  60.0 0.0 collective-permute-done.2.refs_0_
  60.0 0.0 copy-start.1
  60.0 0.4 collective-permute-start.3
  60.4 1.4 %copy.15.bi_ref = s32[4,1,16,4]{3,2,1,0:T(8,128)} copy(s32[4,1,16,4]{2,3,1,0:T(4,128)} %param.20) | data formatting | bytes 2048 | tf_op args[9]
  61.8 0.0 collective-permute-done.8.refs_6_
  61.8 0.0 collective-permute-done.6.refs_3_
  61.8 0.0 collective-permute-done.9.refs_7_
  61.8 0.0 copy-done.8
  61.8 0.0 copy-done.9
  61.9 6.6 %shard_map.131.refs_9_ = f32[16,8,2048]{2,1,0:T(8,128)} custom-call(s32[4,1,16,4]{3,2,1,0:T(8,128)} %copy.15.bi_ref, bf16[128,2048]{1,0:T(8,128)(2,1)} %copy-done.8, bf16[128,2048]{1,0:T(8,128)(2,1)} %collective-permute-done.4.refs_1_, bf16[128,2048]{1,0:T(8,128)(2,1)} %copy-done.10, bf16[128,2048]{1,0:T(8,128)(2,1)} %collective-permute-done.6.refs_3_, ...), custom_call_target="tpu_custom_call" | custom-call | tf_op jit(solution)/shard_map/pallas_call | solution.py:180
  68.5 4.8 %collective-permute-done.13.refs_5_ = bf16[128,2048]{1,0:T(8,128)(2,1)S(1)} collective-permute-done((bf16[128,2048]{1,0:T(8,128)(2,1)S(1)}, bf16[128,2048]{1,0:T(8,128)(2,1)S(1)}, u32[]{:S(2)}, u32[]{:S(2)}) %collective-permute-start.13) | collective-permute-done | bytes 524320 | tf_op jit(solution)/shard_map/ppermute | solution.py:17
  73.2 0.0 copy-start.2
  73.2 0.0 collective-permute-start.14
  73.2 0.5 collective-permute-start.15
  73.7 9.5 %collective-permute-done.3.refs_1_ = bf16[128,2048]{1,0:T(8,128)(2,1)S(1)} collective-permute-done((bf16[128,2048]{1,0:T(8,128)(2,1)S(1)}, bf16[128,2048]{1,0:T(8,128)(2,1)S(1)}, u32[]{:S(2)}, u32[]{:S(2)}) %collective-permute-start.3) | collective-permute-done | bytes 524320 | tf_op jit(solution)/shard_map/ppermute | solution.py:17
  83.3 0.0 copy-start.3
  83.3 0.0 collective-permute-start.10
  83.3 0.5 collective-permute-start.11
  83.8 0.0 collective-permute-done.14.refs_6_
  83.8 0.0 copy-start.4
  83.8 0.0 collective-permute-done.15.refs_7_
  83.8 0.0 copy-start.5
  83.8 1.4 %collective-permute-done.10.refs_2_ = bf16[128,2048]{1,0:T(8,128)(2,1)S(1)} collective-permute-done((bf16[128,2048]{1,0:T(8,128)(2,1)S(1)}, bf16[128,2048]{1,0:T(8,128)(2,1)S(1)}, u32[]{:S(2)}, u32[]{:S(2)}) %collective-permute-start.10) | collective-permute-done | bytes 524320 | tf_op jit(solution)/shard_map/ppermute | solution.py:17
  85.2 0.0 copy-start.6
  85.2 0.7 collective-permute-done.11.refs_3_
  85.9 0.0 copy-done.6
  86.0 0.0 copy-start.7
  86.0 0.8 copy-done.7
  86.8 0.0 copy-done
  86.8 0.0 copy-done.1
  86.8 0.0 copy-done.2
  86.8 0.0 copy-done.3
  86.8 0.0 copy-done.4
  86.8 0.0 copy-done.5
  86.8 7.5 %shard_map.132 = (bf16[16,8,2048]{2,1,0:T(8,128)(2,1)}, f32[8,2048]{1,0:T(8,128)}, f32[8,2048]{1,0:T(8,128)}) custom-call(s32[4,1,16,4]{3,2,1,0:T(8,128)} %copy.15.bi_ref, bf16[128,2048]{1,0:T(8,128)(2,1)} %copy-done.1, bf16[128,2048]{1,0:T(8,128)(2,1)} %copy-done.3, bf16[128,2048]{1,0:T(8,128)(2,1)} %copy-done.6, bf16[128,2048]{1,0:T(8,128)(2,1)} %copy-done.7, ...), custom_call_target="tpu_custom_call" | custom-call | tf_op jit(solution)/shard_map/pallas_call | solution.py:180
Async XLA Ops:
  3.7 26.3 %collective-permute-start = (bf16[128,2048]{1,0:T(8,128)(2,1)}, bf16[128,2048]{1,0:T(8,128)(2,1)S(1)}, u32[]{:S(2)}, u32[]{:S(2)}) collective-permute-start(bf16[128,2048]{1,0:T(8,128)(2,1)} %get-tuple-element.15), channel_id=1, source_target_pairs={{0,4},{4,0},{8,12},{12,8},{1,5},{5,1},{9,13},{13,9},{2,6},{6,2},{1... | collective-permute-start | bytes 1572872 | tf_op jit(solution)/shard_map/ppermute | solution.py:17
  6.7 25.8 %collective-permute-start.1 = (bf16[128,2048]{1,0:T(8,128)(2,1)}, bf16[128,2048]{1,0:T(8,128)(2,1)S(1)}, u32[]{:S(2)}, u32[]{:S(2)}) collective-permute-start(bf16[128,2048]{1,0:T(8,128)(2,1)} %get-tuple-element.16), channel_id=1, source_target_pairs={{0,8},{4,12},{8,0},{12,4},{1,9},{5,13},{9,1},{13,5},{2,10},{6,14},... | collective-permute-start | bytes 1572872 | tf_op jit(solution)/shard_map/ppermute | solution.py:17
  30.0 31.9 %copy-start.8 = (bf16[128,2048]{1,0:T(8,128)(2,1)}, bf16[128,2048]{1,0:T(8,128)(2,1)S(1)}, u32[]{:S(2)}) copy-start(bf16[128,2048]{1,0:T(8,128)(2,1)S(1)} %collective-permute-done.refs_0_) | copy-start | bytes 1572868
  30.0 15.0 %collective-permute-start.4 = (bf16[128,2048]{1,0:T(8,128)(2,1)S(1)}, bf16[128,2048]{1,0:T(8,128)(2,1)}, u32[]{:S(2)}, u32[]{:S(2)}) collective-permute-start(bf16[128,2048]{1,0:T(8,128)(2,1)S(1)} %collective-permute-done.refs_0_), channel_id=1, source_target_pairs={{0,2},{1,3},{2,0},{3,1},{4,6},{5,7},{6,4},{7,5},{8,10},{9,11},{10,... | collective-permute-start | bytes 1572872 | tf_op jit(solution)/shard_map/ppermute | solution.py:17
  31.6 22.8 %collective-permute-start.5 = (bf16[128,2048]{1,0:T(8,128)(2,1)S(1)}, bf16[128,2048]{1,0:T(8,128)(2,1)S(1)}, u32[]{:S(2)}, u32[]{:S(2)}) collective-permute-start(bf16[128,2048]{1,0:T(8,128)(2,1)S(1)} %collective-permute-done.refs_0_), channel_id=1, source_target_pairs={{0,1},{1,0},{2,3},{3,2},{4,5},{5,4},{6,7},{7,6},{8,9},{9,8},{10,11... | collective-permute-start | bytes 1572872 | tf_op jit(solution)/shard_map/ppermute | solution.py:17
  32.5 29.4 %copy-start.9 = (bf16[128,2048]{1,0:T(8,128)(2,1)}, bf16[128,2048]{1,0:T(8,128)(2,1)S(1)}, u32[]{:S(2)}) copy-start(bf16[128,2048]{1,0:T(8,128)(2,1)S(1)} %collective-permute-done.1.refs_4_) | copy-start | bytes 1572868
  32.5 21.9 %collective-permute-start.7 = (bf16[128,2048]{1,0:T(8,128)(2,1)S(1)}, bf16[128,2048]{1,0:T(8,128)(2,1)}, u32[]{:S(2)}, u32[]{:S(2)}) collective-permute-start(bf16[128,2048]{1,0:T(8,128)(2,1)S(1)} %collective-permute-done.1.refs_4_), channel_id=1, source_target_pairs={{0,2},{1,3},{2,0},{3,1},{4,6},{5,7},{6,4},{7,5},{8,10},{9,11},{10,... | collective-permute-start | bytes 1572872 | tf_op jit(solution)/shard_map/ppermute | solution.py:17
  34.0 24.4 %collective-permute-start.12 = (bf16[128,2048]{1,0:T(8,128)(2,1)}, bf16[128,2048]{1,0:T(8,128)(2,1)S(1)}, u32[]{:S(2)}, u32[]{:S(2)}) collective-permute-start(bf16[128,2048]{1,0:T(8,128)(2,1)} %get-tuple-element.20), channel_id=1, source_target_pairs={{0,8},{4,12},{8,0},{12,4},{1,9},{5,13},{9,1},{13,5},{2,10},{6,14},... | collective-permute-start | bytes 1572872 | tf_op jit(solution)/shard_map/ppermute | solution.py:17
  34.3 25.7 %collective-permute-start.2 = (bf16[128,2048]{1,0:T(8,128)(2,1)}, bf16[128,2048]{1,0:T(8,128)(2,1)S(1)}, u32[]{:S(2)}, u32[]{:S(2)}) collective-permute-start(bf16[128,2048]{1,0:T(8,128)(2,1)} %get-tuple-element.17), channel_id=1, source_target_pairs={{0,4},{4,0},{8,12},{12,8},{1,5},{5,1},{9,13},{13,9},{2,6},{6,2},{1... | collective-permute-start | bytes 1572872 | tf_op jit(solution)/shard_map/ppermute | solution.py:17
  44.9 16.9 %collective-permute-start.8 = (bf16[128,2048]{1,0:T(8,128)(2,1)S(1)}, bf16[128,2048]{1,0:T(8,128)(2,1)}, u32[]{:S(2)}, u32[]{:S(2)}) collective-permute-start(bf16[128,2048]{1,0:T(8,128)(2,1)S(1)} %collective-permute-done.1.refs_4_), channel_id=1, source_target_pairs={{0,1},{1,0},{2,3},{3,2},{4,5},{5,4},{6,7},{7,6},{8,9},{9,8},{10,11... | collective-permute-start | bytes 1572872 | tf_op jit(solution)/shard_map/ppermute | solution.py:17
  54.4 7.4 %collective-permute-start.6 = (bf16[128,2048]{1,0:T(8,128)(2,1)}, bf16[128,2048]{1,0:T(8,128)(2,1)}, u32[]{:S(2)}, u32[]{:S(2)}) collective-permute-start(bf16[128,2048]{1,0:T(8,128)(2,1)} %collective-permute-done.4.refs_1_), channel_id=1, source_target_pairs={{0,1},{1,0},{2,3},{3,2},{4,5},{5,4},{6,7},{7,6},{8,9},{9,8},{10,11... | collective-permute-start | bytes 1572872 | tf_op jit(solution)/shard_map/ppermute | solution.py:17
  54.4 0.8 copy-start.10
  54.4 7.4 %collective-permute-start.9 = (bf16[128,2048]{1,0:T(8,128)(2,1)}, bf16[128,2048]{1,0:T(8,128)(2,1)}, u32[]{:S(2)}, u32[]{:S(2)}) collective-permute-start(bf16[128,2048]{1,0:T(8,128)(2,1)} %collective-permute-done.7.refs_5_), channel_id=1, source_target_pairs={{0,1},{1,0},{2,3},{3,2},{4,5},{5,4},{6,7},{7,6},{8,9},{9,8},{10,11... | collective-permute-start | bytes 1572872 | tf_op jit(solution)/shard_map/ppermute | solution.py:17
  58.4 28.4 %copy-start = (bf16[128,2048]{1,0:T(8,128)(2,1)}, bf16[128,2048]{1,0:T(8,128)(2,1)S(1)}, u32[]{:S(2)}) copy-start(bf16[128,2048]{1,0:T(8,128)(2,1)S(1)} %collective-permute-done.12.refs_4_) | copy-start | bytes 1572868
  58.4 14.8 %collective-permute-start.13 = (bf16[128,2048]{1,0:T(8,128)(2,1)S(1)}, bf16[128,2048]{1,0:T(8,128)(2,1)S(1)}, u32[]{:S(2)}, u32[]{:S(2)}) collective-permute-start(bf16[128,2048]{1,0:T(8,128)(2,1)S(1)} %collective-permute-done.12.refs_4_), channel_id=1, source_target_pairs={{0,2},{1,3},{2,0},{3,1},{4,6},{5,7},{6,4},{7,5},{8,10},{9,11},{10,... | collective-permute-start | bytes 1572872 | tf_op jit(solution)/shard_map/ppermute | solution.py:17
  60.0 26.8 %copy-start.1 = (bf16[128,2048]{1,0:T(8,128)(2,1)}, bf16[128,2048]{1,0:T(8,128)(2,1)S(1)}, u32[]{:S(2)}) copy-start(bf16[128,2048]{1,0:T(8,128)(2,1)S(1)} %collective-permute-done.2.refs_0_) | copy-start | bytes 1572868
  60.0 23.3 %collective-permute-start.3 = (bf16[128,2048]{1,0:T(8,128)(2,1)S(1)}, bf16[128,2048]{1,0:T(8,128)(2,1)S(1)}, u32[]{:S(2)}, u32[]{:S(2)}) collective-permute-start(bf16[128,2048]{1,0:T(8,128)(2,1)S(1)} %collective-permute-done.2.refs_0_), channel_id=1, source_target_pairs={{0,2},{1,3},{2,0},{3,1},{4,6},{5,7},{6,4},{7,5},{8,10},{9,11},{10,... | collective-permute-start | bytes 1572872 | tf_op jit(solution)/shard_map/ppermute | solution.py:17
  73.2 13.6 %copy-start.2 = (bf16[128,2048]{1,0:T(8,128)(2,1)}, bf16[128,2048]{1,0:T(8,128)(2,1)S(1)}, u32[]{:S(2)}) copy-start(bf16[128,2048]{1,0:T(8,128)(2,1)S(1)} %collective-permute-done.13.refs_5_) | copy-start | bytes 1572868
  73.2 10.6 %collective-permute-start.14 = (bf16[128,2048]{1,0:T(8,128)(2,1)S(1)}, bf16[128,2048]{1,0:T(8,128)(2,1)S(1)}, u32[]{:S(2)}, u32[]{:S(2)}) collective-permute-start(bf16[128,2048]{1,0:T(8,128)(2,1)S(1)} %collective-permute-done.12.refs_4_), channel_id=1, source_target_pairs={{0,1},{1,0},{2,3},{3,2},{4,5},{5,4},{6,7},{7,6},{8,9},{9,8},{10,11... | collective-permute-start | bytes 1572872 | tf_op jit(solution)/shard_map/ppermute | solution.py:17
  73.2 10.6 %collective-permute-start.15 = (bf16[128,2048]{1,0:T(8,128)(2,1)S(1)}, bf16[128,2048]{1,0:T(8,128)(2,1)S(1)}, u32[]{:S(2)}, u32[]{:S(2)}) collective-permute-start(bf16[128,2048]{1,0:T(8,128)(2,1)S(1)} %collective-permute-done.13.refs_5_), channel_id=1, source_target_pairs={{0,1},{1,0},{2,3},{3,2},{4,5},{5,4},{6,7},{7,6},{8,9},{9,8},{10,11... | collective-permute-start | bytes 1572872 | tf_op jit(solution)/shard_map/ppermute | solution.py:17
  83.3 3.5 %copy-start.3 = (bf16[128,2048]{1,0:T(8,128)(2,1)}, bf16[128,2048]{1,0:T(8,128)(2,1)S(1)}, u32[]{:S(2)}) copy-start(bf16[128,2048]{1,0:T(8,128)(2,1)S(1)} %collective-permute-done.3.refs_1_) | copy-start | bytes 1572868
  83.3 1.9 %collective-permute-start.10 = (bf16[128,2048]{1,0:T(8,128)(2,1)S(1)}, bf16[128,2048]{1,0:T(8,128)(2,1)S(1)}, u32[]{:S(2)}, u32[]{:S(2)}) collective-permute-start(bf16[128,2048]{1,0:T(8,128)(2,1)S(1)} %collective-permute-done.2.refs_0_), channel_id=1, source_target_pairs={{0,1},{1,0},{2,3},{3,2},{4,5},{5,4},{6,7},{7,6},{8,9},{9,8},{10,11... | collective-permute-start | bytes 1572872 | tf_op jit(solution)/shard_map/ppermute | solution.py:17
  83.3 2.7 %collective-permute-start.11 = (bf16[128,2048]{1,0:T(8,128)(2,1)S(1)}, bf16[128,2048]{1,0:T(8,128)(2,1)S(1)}, u32[]{:S(2)}, u32[]{:S(2)}) collective-permute-start(bf16[128,2048]{1,0:T(8,128)(2,1)S(1)} %collective-permute-done.3.refs_1_), channel_id=1, source_target_pairs={{0,1},{1,0},{2,3},{3,2},{4,5},{5,4},{6,7},{7,6},{8,9},{9,8},{10,11... | collective-permute-start | bytes 1572872 | tf_op jit(solution)/shard_map/ppermute | solution.py:17
  83.8 3.0 %copy-start.4 = (bf16[128,2048]{1,0:T(8,128)(2,1)}, bf16[128,2048]{1,0:T(8,128)(2,1)S(1)}, u32[]{:S(2)}) copy-start(bf16[128,2048]{1,0:T(8,128)(2,1)S(1)} %collective-permute-done.14.refs_6_) | copy-start | bytes 1572868
  83.8 3.0 %copy-start.5 = (bf16[128,2048]{1,0:T(8,128)(2,1)}, bf16[128,2048]{1,0:T(8,128)(2,1)S(1)}, u32[]{:S(2)}) copy-start(bf16[128,2048]{1,0:T(8,128)(2,1)S(1)} %collective-permute-done.15.refs_7_) | copy-start | bytes 1572868
  85.2 0.8 copy-start.6
  86.0 0.8 copy-start.7

commit v10 on v9

--- a/solution.py
+++ b/solution.py
@@ -177,9 +177,13 @@
         stage_kernel, n_pieces=len(pieces), stage=tuple(stage), n_pos=n_pos,
         final=final, has_rec=has_rec,
     )
+    pinned = [final and i > len(pieces) + has_rec for i in range(len(operands))]
+    specs = [VMEM if p else ANY for p in pinned]
+    operands = [pltpu.with_memory_space_constraint(x, pltpu.VMEM) if p else x
+                for x, p in zip(operands, pinned)]
     return pl.pallas_call(
         kernel,
-        in_specs=[SMEM] + [ANY] * len(operands),
+        in_specs=[SMEM] + specs,
         out_specs=out_specs,
         scratch_shapes=scratch,
         out_shape=out_shape,

time: 94.8 us -> 94.7 us (level)
    unnamed x23 -> x31, local copies, waits for them, and re-layouts: 2.54 us -> 2.24 us
where the time goes in v10:
time: 94.7 us; the launch traced here: 94.3 us
  waiting for transfers between devices  59.1 us (62%)
  Pallas kernels  16.8 us (18%)
  starting transfers between devices  15.4 us (16%)
  local copies, waits for them, and re-layouts  2.24 us (2%)
    ppermute x16, waiting for transfers between devices, swap(): return lax.ppermute(value, axis, pairs)  59.1 us
    ppermute x16, starting transfers between devices, swap(): return lax.ppermute(value, axis, pairs)  15.4 us
    pallas_call x2, Pallas kernels, stage_contrib(): pl.pallas_call(kernel, in_specs=[SMEM] + specs, out_specs=out_specs, scra...  13.6 us
    pallas_call x1, Pallas kernels, send_slices(): pl.pallas_call(kernel, in_specs=[SMEM, VMEM], out_specs=[VMEM] * rounds,...  3.2 us
    unnamed x31, local copies, waits for them, and re-layouts  2.24 us
  transfers between devices with their start and end apart: 16, of which 9 were waited for; matrix products, arithmetic and copies ran while one was open for 1% of the time, Pallas kernels for 7%

profile of v10, /device:TPU:0, one launch (start us, length us, event | category | flops | bytes accessed | tf_op | source)
XLA Modules:
  0.0 94.3 jit_solution(4580032345765685548)
XLA Ops:
  0.6 0.0 copy-start.4
  0.6 0.0 copy-start.5
  0.7 0.0 copy-start.6
  0.7 0.0 copy-start
  0.7 0.0 copy-start.1
  0.7 0.0 copy-start.2
  0.7 0.0 copy-start.3
  0.7 3.2 %shard_map.130 = (bf16[128,2048]{1,0:T(8,128)(2,1)}, bf16[128,2048]{1,0:T(8,128)(2,1)}, bf16[128,2048]{1,0:T(8,128)(2,1)}, bf16[128,2048]{1,0:T(8,128)(2,1)}) custom-call(s32[4,4]{1,0:T(4,128)} %delays_ref.1, bf16[32,8,2048]{2,1,0:T(8,128)(2,1)} %window_ref.1), custom_call_target="tpu_custom_call" | custom-call | tf_op jit(solution)/shard_map/pallas_call | solution.py:34
  3.9 3.0 %collective-permute-start = (bf16[128,2048]{1,0:T(8,128)(2,1)}, bf16[128,2048]{1,0:T(8,128)(2,1)S(1)}, u32[]{:S(2)}, u32[]{:S(2)}) collective-permute-start(bf16[128,2048]{1,0:T(8,128)(2,1)} %get-tuple-element.15), channel_id=1, source_target_pairs={{0,4},{4,0},{8,12},{12,8},{1,5},{5,1},{9,13},{13,9},{2,6},{6,2},{1... | collective-permute-start | bytes 1572872 | tf_op jit(solution)/shard_map/ppermute | solution.py:17
  6.9 2.6 %collective-permute-start.1 = (bf16[128,2048]{1,0:T(8,128)(2,1)}, bf16[128,2048]{1,0:T(8,128)(2,1)}, u32[]{:S(2)}, u32[]{:S(2)}) collective-permute-start(bf16[128,2048]{1,0:T(8,128)(2,1)} %get-tuple-element.16), channel_id=1, source_target_pairs={{0,8},{4,12},{8,0},{12,4},{1,9},{5,13},{9,1},{13,5},{2,10},{6,14},... | collective-permute-start | bytes 1572872 | tf_op jit(solution)/shard_map/ppermute | solution.py:17
  9.5 20.7 %collective-permute-done.refs_0_ = bf16[128,2048]{1,0:T(8,128)(2,1)S(1)} collective-permute-done((bf16[128,2048]{1,0:T(8,128)(2,1)}, bf16[128,2048]{1,0:T(8,128)(2,1)S(1)}, u32[]{:S(2)}, u32[]{:S(2)}) %collective-permute-start) | collective-permute-done | bytes 524320 | tf_op jit(solution)/shard_map/ppermute | solution.py:17
  30.2 0.0 copy-start.13
  30.2 1.7 %collective-permute-start.4 = (bf16[128,2048]{1,0:T(8,128)(2,1)S(1)}, bf16[128,2048]{1,0:T(8,128)(2,1)}, u32[]{:S(2)}, u32[]{:S(2)}) collective-permute-start(bf16[128,2048]{1,0:T(8,128)(2,1)S(1)} %collective-permute-done.refs_0_), channel_id=1, source_target_pairs={{0,2},{1,3},{2,0},{3,1},{4,6},{5,7},{6,4},{7,5},{8,10},{9,11},{10,... | collective-permute-start | bytes 1572872 | tf_op jit(solution)/shard_map/ppermute | solution.py:17
  31.8 0.0 collective-permute-start.5
  31.8 1.0 %collective-permute-done.1.refs_4_ = bf16[128,2048]{1,0:T(8,128)(2,1)} collective-permute-done((bf16[128,2048]{1,0:T(8,128)(2,1)}, bf16[128,2048]{1,0:T(8,128)(2,1)}, u32[]{:S(2)}, u32[]{:S(2)}) %collective-permute-start.1) | collective-permute-done | bytes 524320 | tf_op jit(solution)/shard_map/ppermute | solution.py:17
  32.8 1.5 %collective-permute-start.7 = (bf16[128,2048]{1,0:T(8,128)(2,1)}, bf16[128,2048]{1,0:T(8,128)(2,1)}, u32[]{:S(2)}, u32[]{:S(2)}) collective-permute-start(bf16[128,2048]{1,0:T(8,128)(2,1)} %collective-permute-done.1.refs_4_), channel_id=1, source_target_pairs={{0,2},{1,3},{2,0},{3,1},{4,6},{5,7},{6,4},{7,5},{8,10},{9,11},{10,... | collective-permute-start | bytes 1572872 | tf_op jit(solution)/shard_map/ppermute | solution.py:17
  34.3 0.3 collective-permute-start.12
  34.6 2.7 %collective-permute-start.2 = (bf16[128,2048]{1,0:T(8,128)(2,1)}, bf16[128,2048]{1,0:T(8,128)(2,1)S(1)}, u32[]{:S(2)}, u32[]{:S(2)}) collective-permute-start(bf16[128,2048]{1,0:T(8,128)(2,1)} %get-tuple-element.17), channel_id=1, source_target_pairs={{0,4},{4,0},{8,12},{12,8},{1,5},{5,1},{9,13},{13,9},{2,6},{6,2},{1... | collective-permute-start | bytes 1572872 | tf_op jit(solution)/shard_map/ppermute | solution.py:17
  37.3 7.8 %collective-permute-done.4.refs_1_ = bf16[128,2048]{1,0:T(8,128)(2,1)} collective-permute-done((bf16[128,2048]{1,0:T(8,128)(2,1)S(1)}, bf16[128,2048]{1,0:T(8,128)(2,1)}, u32[]{:S(2)}, u32[]{:S(2)}) %collective-permute-start.4) | collective-permute-done | bytes 524320 | tf_op jit(solution)/shard_map/ppermute | solution.py:17
  45.2 0.0 collective-permute-start.8
  45.2 9.6 %collective-permute-done.7.refs_5_ = bf16[128,2048]{1,0:T(8,128)(2,1)} collective-permute-done((bf16[128,2048]{1,0:T(8,128)(2,1)}, bf16[128,2048]{1,0:T(8,128)(2,1)}, u32[]{:S(2)}, u32[]{:S(2)}) %collective-permute-start.7) | collective-permute-done | bytes 524320 | tf_op jit(solution)/shard_map/ppermute | solution.py:17
  54.7 0.0 collective-permute-start.6
  54.7 0.0 collective-permute-done.5.refs_2_
  54.7 0.0 copy-start.14
  54.8 0.5 collective-permute-start.9
  55.3 3.4 %collective-permute-done.12.refs_4_ = bf16[128,2048]{1,0:T(8,128)(2,1)S(1)} collective-permute-done((bf16[128,2048]{1,0:T(8,128)(2,1)}, bf16[128,2048]{1,0:T(8,128)(2,1)S(1)}, u32[]{:S(2)}, u32[]{:S(2)}) %collective-permute-start.12) | collective-permute-done | bytes 524320 | tf_op jit(solution)/shard_map/ppermute | solution.py:17
  58.6 0.0 copy-start.7
  58.6 1.6 %collective-permute-start.13 = (bf16[128,2048]{1,0:T(8,128)(2,1)S(1)}, bf16[128,2048]{1,0:T(8,128)(2,1)}, u32[]{:S(2)}, u32[]{:S(2)}) collective-permute-start(bf16[128,2048]{1,0:T(8,128)(2,1)S(1)} %collective-permute-done.12.refs_4_), channel_id=1, source_target_pairs={{0,2},{1,3},{2,0},{3,1},{4,6},{5,7},{6,4},{7,5},{8,10},{9,11},{10,... | collective-permute-start | bytes 1572872 | tf_op jit(solution)/shard_map/ppermute | solution.py:17
  60.2 0.0 collective-permute-done.2.refs_0_
  60.2 0.0 copy-done.13
  60.2 0.0 copy-done.14
  60.2 0.0 copy-start.8
  60.2 0.5 collective-permute-start.3
  60.7 1.4 %copy.15.bi_ref = s32[4,1,16,4]{3,2,1,0:T(8,128)} copy(s32[4,1,16,4]{2,3,1,0:T(4,128)} %param.20) | data formatting | bytes 2048 | tf_op args[9]
  62.1 0.0 collective-permute-done.8.refs_6_
  62.1 0.0 collective-permute-done.6.refs_3_
  62.1 0.0 collective-permute-done.9.refs_7_
  62.1 6.6 %shard_map.131.refs_9_ = f32[16,8,2048]{2,1,0:T(8,128)} custom-call(s32[4,1,16,4]{3,2,1,0:T(8,128)} %copy.15.bi_ref, bf16[128,2048]{1,0:T(8,128)(2,1)} %copy-done.13, bf16[128,2048]{1,0:T(8,128)(2,1)} %collective-permute-done.4.refs_1_, bf16[128,2048]{1,0:T(8,128)(2,1)} %copy-done.14, bf16[128,2048]{1,0:T(8,128)(2,1)} %collective-permute-done.6.refs_3_, ...), custom_call_target="tpu_custom_call" | custom-call | tf_op jit(solution)/shard_map/pallas_call | solution.py:184
  68.7 4.8 %collective-permute-done.13.refs_5_ = bf16[128,2048]{1,0:T(8,128)(2,1)} collective-permute-done((bf16[128,2048]{1,0:T(8,128)(2,1)S(1)}, bf16[128,2048]{1,0:T(8,128)(2,1)}, u32[]{:S(2)}, u32[]{:S(2)}) %collective-permute-start.13) | collective-permute-done | bytes 524320 | tf_op jit(solution)/shard_map/ppermute | solution.py:17
  73.5 0.0 collective-permute-start.14
  73.5 0.5 collective-permute-start.15
  74.1 9.5 %collective-permute-done.3.refs_1_ = bf16[128,2048]{1,0:T(8,128)(2,1)} collective-permute-done((bf16[128,2048]{1,0:T(8,128)(2,1)S(1)}, bf16[128,2048]{1,0:T(8,128)(2,1)}, u32[]{:S(2)}, u32[]{:S(2)}) %collective-permute-start.3) | collective-permute-done | bytes 524320 | tf_op jit(solution)/shard_map/ppermute | solution.py:17
  83.6 0.0 collective-permute-start.10
  83.6 0.5 collective-permute-start.11
  84.1 0.0 collective-permute-done.14.refs_6_
  84.1 0.0 copy-start.9
  84.1 0.0 collective-permute-done.15.refs_7_
  84.1 0.0 copy-start.10
  84.1 2.1 %collective-permute-done.10.refs_2_ = bf16[128,2048]{1,0:T(8,128)(2,1)S(1)} collective-permute-done((bf16[128,2048]{1,0:T(8,128)(2,1)S(1)}, bf16[128,2048]{1,0:T(8,128)(2,1)S(1)}, u32[]{:S(2)}, u32[]{:S(2)}) %collective-permute-start.10) | collective-permute-done | bytes 524320 | tf_op jit(solution)/shard_map/ppermute | solution.py:17
  86.2 0.0 copy-done.9
  86.2 0.2 collective-permute-done.11.refs_3_
  86.5 0.0 copy-done.10
  86.5 0.6 copy-done.11
  87.0 0.2 copy-done.12
  87.3 0.0 copy-done.7
  87.3 0.0 copy-done.8
  87.3 0.0 copy-done.4
  87.3 0.0 copy-done.5
  87.3 0.0 copy-done.6
  87.3 0.0 copy-done
  87.3 0.0 copy-done.1
  87.3 0.0 copy-done.2
  87.3 0.0 copy-done.3
  87.3 7.0 %shard_map.132 = (bf16[16,8,2048]{2,1,0:T(8,128)(2,1)}, f32[8,2048]{1,0:T(8,128)}, f32[8,2048]{1,0:T(8,128)}) custom-call(s32[4,1,16,4]{3,2,1,0:T(8,128)} %copy.15.bi_ref, bf16[128,2048]{1,0:T(8,128)(2,1)} %copy-done.8, bf16[128,2048]{1,0:T(8,128)(2,1)} %collective-permute-done.3.refs_1_, bf16[128,2048]{1,0:T(8,128)(2,1)} %copy-done.11, ...), custom_call_target="tpu_custom_call" | custom-call | tf_op jit(solution)/shard_map/pallas_call | solution.py:184
  (2 shorter events, 0.0 us)
Async XLA Ops:
  0.6 86.6 %copy-start.4 = (f32[2048]{0:T(1024)S(1)}, f32[2048]{0:T(1024)}, u32[]{:S(2)}) copy-start(f32[2048]{0:T(1024)} %param.16) | copy-start | bytes 24580
  0.6 86.6 %copy-start.5 = (f32[2048]{0:T(1024)S(1)}, f32[2048]{0:T(1024)}, u32[]{:S(2)}) copy-start(f32[2048]{0:T(1024)} %param.17) | copy-start | bytes 24580
  0.7 86.6 %copy-start.6 = (f32[2048]{0:T(1024)S(1)}, f32[2048]{0:T(1024)}, u32[]{:S(2)}) copy-start(f32[2048]{0:T(1024)} %param.18) | copy-start | bytes 24580
  0.7 86.6 %copy-start = (f32[16,8,2048]{2,1,0:T(8,128)S(1)}, f32[16,8,2048]{2,1,0:T(8,128)}, u32[]{:S(2)}) copy-start(f32[16,8,2048]{2,1,0:T(8,128)} %refs_10_.1) | copy-start | bytes 3145732
  0.7 86.6 %copy-start.1 = (f32[16,8,2048]{2,1,0:T(8,128)S(1)}, f32[16,8,2048]{2,1,0:T(8,128)}, u32[]{:S(2)}) copy-start(f32[16,8,2048]{2,1,0:T(8,128)} %refs_11_.1) | copy-start | bytes 3145732
  0.7 86.6 %copy-start.2 = (f32[8,2048]{1,0:T(8,128)S(1)}, f32[8,2048]{1,0:T(8,128)}, u32[]{:S(2)}) copy-start(f32[8,2048]{1,0:T(8,128)} %refs_12_.1) | copy-start | bytes 196612
  0.7 86.6 %copy-start.3 = (f32[8,2048]{1,0:T(8,128)S(1)}, f32[8,2048]{1,0:T(8,128)}, u32[]{:S(2)}) copy-start(f32[8,2048]{1,0:T(8,128)} %refs_13_.1) | copy-start | bytes 196612
  3.9 26.3 %collective-permute-start = (bf16[128,2048]{1,0:T(8,128)(2,1)}, bf16[128,2048]{1,0:T(8,128)(2,1)S(1)}, u32[]{:S(2)}, u32[]{:S(2)}) collective-permute-start(bf16[128,2048]{1,0:T(8,128)(2,1)} %get-tuple-element.15), channel_id=1, source_target_pairs={{0,4},{4,0},{8,12},{12,8},{1,5},{5,1},{9,13},{13,9},{2,6},{6,2},{1... | collective-permute-start | bytes 1572872 | tf_op jit(solution)/shard_map/ppermute | solution.py:17
  6.9 25.9 %collective-permute-start.1 = (bf16[128,2048]{1,0:T(8,128)(2,1)}, bf16[128,2048]{1,0:T(8,128)(2,1)}, u32[]{:S(2)}, u32[]{:S(2)}) collective-permute-start(bf16[128,2048]{1,0:T(8,128)(2,1)} %get-tuple-element.16), channel_id=1, source_target_pairs={{0,8},{4,12},{8,0},{12,4},{1,9},{5,13},{9,1},{13,5},{2,10},{6,14},... | collective-permute-start | bytes 1572872 | tf_op jit(solution)/shard_map/ppermute | solution.py:17
  30.2 30.0 %copy-start.13 = (bf16[128,2048]{1,0:T(8,128)(2,1)}, bf16[128,2048]{1,0:T(8,128)(2,1)S(1)}, u32[]{:S(2)}) copy-start(bf16[128,2048]{1,0:T(8,128)(2,1)S(1)} %collective-permute-done.refs_0_) | copy-start | bytes 1572868
  30.2 15.0 %collective-permute-start.4 = (bf16[128,2048]{1,0:T(8,128)(2,1)S(1)}, bf16[128,2048]{1,0:T(8,128)(2,1)}, u32[]{:S(2)}, u32[]{:S(2)}) collective-permute-start(bf16[128,2048]{1,0:T(8,128)(2,1)S(1)} %collective-permute-done.refs_0_), channel_id=1, source_target_pairs={{0,2},{1,3},{2,0},{3,1},{4,6},{5,7},{6,4},{7,5},{8,10},{9,11},{10,... | collective-permute-start | bytes 1572872 | tf_op jit(solution)/shard_map/ppermute | solution.py:17
  31.8 22.9 %collective-permute-start.5 = (bf16[128,2048]{1,0:T(8,128)(2,1)S(1)}, bf16[128,2048]{1,0:T(8,128)(2,1)S(1)}, u32[]{:S(2)}, u32[]{:S(2)}) collective-permute-start(bf16[128,2048]{1,0:T(8,128)(2,1)S(1)} %collective-permute-done.refs_0_), channel_id=1, source_target_pairs={{0,1},{1,0},{2,3},{3,2},{4,5},{5,4},{6,7},{7,6},{8,9},{9,8},{10,11... | collective-permute-start | bytes 1572872 | tf_op jit(solution)/shard_map/ppermute | solution.py:17
  32.8 21.9 %collective-permute-start.7 = (bf16[128,2048]{1,0:T(8,128)(2,1)}, bf16[128,2048]{1,0:T(8,128)(2,1)}, u32[]{:S(2)}, u32[]{:S(2)}) collective-permute-start(bf16[128,2048]{1,0:T(8,128)(2,1)} %collective-permute-done.1.refs_4_), channel_id=1, source_target_pairs={{0,2},{1,3},{2,0},{3,1},{4,6},{5,7},{6,4},{7,5},{8,10},{9,11},{10,... | collective-permute-start | bytes 1572872 | tf_op jit(solution)/shard_map/ppermute | solution.py:17
  34.3 24.3 %collective-permute-start.12 = (bf16[128,2048]{1,0:T(8,128)(2,1)}, bf16[128,2048]{1,0:T(8,128)(2,1)S(1)}, u32[]{:S(2)}, u32[]{:S(2)}) collective-permute-start(bf16[128,2048]{1,0:T(8,128)(2,1)} %get-tuple-element.20), channel_id=1, source_target_pairs={{0,8},{4,12},{8,0},{12,4},{1,9},{5,13},{9,1},{13,5},{2,10},{6,14},... | collective-permute-start | bytes 1572872 | tf_op jit(solution)/shard_map/ppermute | solution.py:17
  34.6 25.6 %collective-permute-start.2 = (bf16[128,2048]{1,0:T(8,128)(2,1)}, bf16[128,2048]{1,0:T(8,128)(2,1)S(1)}, u32[]{:S(2)}, u32[]{:S(2)}) collective-permute-start(bf16[128,2048]{1,0:T(8,128)(2,1)} %get-tuple-element.17), channel_id=1, source_target_pairs={{0,4},{4,0},{8,12},{12,8},{1,5},{5,1},{9,13},{13,9},{2,6},{6,2},{1... | collective-permute-start | bytes 1572872 | tf_op jit(solution)/shard_map/ppermute | solution.py:17
  45.2 17.0 %collective-permute-start.8 = (bf16[128,2048]{1,0:T(8,128)(2,1)}, bf16[128,2048]{1,0:T(8,128)(2,1)}, u32[]{:S(2)}, u32[]{:S(2)}) collective-permute-start(bf16[128,2048]{1,0:T(8,128)(2,1)} %collective-permute-done.1.refs_4_), channel_id=1, source_target_pairs={{0,1},{1,0},{2,3},{3,2},{4,5},{5,4},{6,7},{7,6},{8,9},{9,8},{10,11... | collective-permute-start | bytes 1572872 | tf_op jit(solution)/shard_map/ppermute | solution.py:17
  54.7 7.4 %collective-permute-start.6 = (bf16[128,2048]{1,0:T(8,128)(2,1)}, bf16[128,2048]{1,0:T(8,128)(2,1)}, u32[]{:S(2)}, u32[]{:S(2)}) collective-permute-start(bf16[128,2048]{1,0:T(8,128)(2,1)} %collective-permute-done.4.refs_1_), channel_id=1, source_target_pairs={{0,1},{1,0},{2,3},{3,2},{4,5},{5,4},{6,7},{7,6},{8,9},{9,8},{10,11... | collective-permute-start | bytes 1572872 | tf_op jit(solution)/shard_map/ppermute | solution.py:17
  54.7 5.5 %copy-start.14 = (bf16[128,2048]{1,0:T(8,128)(2,1)}, bf16[128,2048]{1,0:T(8,128)(2,1)S(1)}, u32[]{:S(2)}) copy-start(bf16[128,2048]{1,0:T(8,128)(2,1)S(1)} %collective-permute-done.5.refs_2_) | copy-start | bytes 1572868
  54.8 7.4 %collective-permute-start.9 = (bf16[128,2048]{1,0:T(8,128)(2,1)}, bf16[128,2048]{1,0:T(8,128)(2,1)}, u32[]{:S(2)}, u32[]{:S(2)}) collective-permute-start(bf16[128,2048]{1,0:T(8,128)(2,1)} %collective-permute-done.7.refs_5_), channel_id=1, source_target_pairs={{0,1},{1,0},{2,3},{3,2},{4,5},{5,4},{6,7},{7,6},{8,9},{9,8},{10,11... | collective-permute-start | bytes 1572872 | tf_op jit(solution)/shard_map/ppermute | solution.py:17
  58.6 28.7 %copy-start.7 = (bf16[128,2048]{1,0:T(8,128)(2,1)}, bf16[128,2048]{1,0:T(8,128)(2,1)S(1)}, u32[]{:S(2)}) copy-start(bf16[128,2048]{1,0:T(8,128)(2,1)S(1)} %collective-permute-done.12.refs_4_) | copy-start | bytes 1572868
  58.6 14.9 %collective-permute-start.13 = (bf16[128,2048]{1,0:T(8,128)(2,1)S(1)}, bf16[128,2048]{1,0:T(8,128)(2,1)}, u32[]{:S(2)}, u32[]{:S(2)}) collective-permute-start(bf16[128,2048]{1,0:T(8,128)(2,1)S(1)} %collective-permute-done.12.refs_4_), channel_id=1, source_target_pairs={{0,2},{1,3},{2,0},{3,1},{4,6},{5,7},{6,4},{7,5},{8,10},{9,11},{10,... | collective-permute-start | bytes 1572872 | tf_op jit(solution)/shard_map/ppermute | solution.py:17
  60.2 27.0 %copy-start.8 = (bf16[128,2048]{1,0:T(8,128)(2,1)}, bf16[128,2048]{1,0:T(8,128)(2,1)S(1)}, u32[]{:S(2)}) copy-start(bf16[128,2048]{1,0:T(8,128)(2,1)S(1)} %collective-permute-done.2.refs_0_) | copy-start | bytes 1572868
  60.2 23.4 %collective-permute-start.3 = (bf16[128,2048]{1,0:T(8,128)(2,1)S(1)}, bf16[128,2048]{1,0:T(8,128)(2,1)}, u32[]{:S(2)}, u32[]{:S(2)}) collective-permute-start(bf16[128,2048]{1,0:T(8,128)(2,1)S(1)} %collective-permute-done.2.refs_0_), channel_id=1, source_target_pairs={{0,2},{1,3},{2,0},{3,1},{4,6},{5,7},{6,4},{7,5},{8,10},{9,11},{10,... | collective-permute-start | bytes 1572872 | tf_op jit(solution)/shard_map/ppermute | solution.py:17
  73.5 10.6 %collective-permute-start.14 = (bf16[128,2048]{1,0:T(8,128)(2,1)S(1)}, bf16[128,2048]{1,0:T(8,128)(2,1)S(1)}, u32[]{:S(2)}, u32[]{:S(2)}) collective-permute-start(bf16[128,2048]{1,0:T(8,128)(2,1)S(1)} %collective-permute-done.12.refs_4_), channel_id=1, source_target_pairs={{0,1},{1,0},{2,3},{3,2},{4,5},{5,4},{6,7},{7,6},{8,9},{9,8},{10,11... | collective-permute-start | bytes 1572872 | tf_op jit(solution)/shard_map/ppermute | solution.py:17
  73.5 10.6 %collective-permute-start.15 = (bf16[128,2048]{1,0:T(8,128)(2,1)}, bf16[128,2048]{1,0:T(8,128)(2,1)S(1)}, u32[]{:S(2)}, u32[]{:S(2)}) collective-permute-start(bf16[128,2048]{1,0:T(8,128)(2,1)} %collective-permute-done.13.refs_5_), channel_id=1, source_target_pairs={{0,1},{1,0},{2,3},{3,2},{4,5},{5,4},{6,7},{7,6},{8,9},{9,8},{10,11... | collective-permute-start | bytes 1572872 | tf_op jit(solution)/shard_map/ppermute | solution.py:17
  83.6 2.6 %collective-permute-start.10 = (bf16[128,2048]{1,0:T(8,128)(2,1)S(1)}, bf16[128,2048]{1,0:T(8,128)(2,1)S(1)}, u32[]{:S(2)}, u32[]{:S(2)}) collective-permute-start(bf16[128,2048]{1,0:T(8,128)(2,1)S(1)} %collective-permute-done.2.refs_0_), channel_id=1, source_target_pairs={{0,1},{1,0},{2,3},{3,2},{4,5},{5,4},{6,7},{7,6},{8,9},{9,8},{10,11... | collective-permute-start | bytes 1572872 | tf_op jit(solution)/shard_map/ppermute | solution.py:17
  83.6 2.9 %collective-permute-start.11 = (bf16[128,2048]{1,0:T(8,128)(2,1)}, bf16[128,2048]{1,0:T(8,128)(2,1)S(1)}, u32[]{:S(2)}, u32[]{:S(2)}) collective-permute-start(bf16[128,2048]{1,0:T(8,128)(2,1)} %collective-permute-done.3.refs_1_), channel_id=1, source_target_pairs={{0,1},{1,0},{2,3},{3,2},{4,5},{5,4},{6,7},{7,6},{8,9},{9,8},{10,11... | collective-permute-start | bytes 1572872 | tf_op jit(solution)/shard_map/ppermute | solution.py:17
  84.1 2.1 %copy-start.9 = (bf16[128,2048]{1,0:T(8,128)(2,1)}, bf16[128,2048]{1,0:T(8,128)(2,1)S(1)}, u32[]{:S(2)}) copy-start(bf16[128,2048]{1,0:T(8,128)(2,1)S(1)} %collective-permute-done.14.refs_6_) | copy-start | bytes 1572868
  84.1 2.4 %copy-start.10 = (bf16[128,2048]{1,0:T(8,128)(2,1)}, bf16[128,2048]{1,0:T(8,128)(2,1)S(1)}, u32[]{:S(2)}) copy-start(bf16[128,2048]{1,0:T(8,128)(2,1)S(1)} %collective-permute-done.15.refs_7_) | copy-start | bytes 1572868
  86.2 0.8 copy-start.11
  86.5 0.8 copy-start.12

commit v11 on v10

--- a/solution.py
+++ b/solution.py
@@ -17,11 +17,11 @@
     return lax.ppermute(value, axis, pairs)
 
 
-def slice_kernel(delays_ref, window_ref, *outs, levels, steps):
+def slice_kernel(delays_ref, window_ref, *outs, rounds, levels, steps):
     me = lax.axis_index("area")
     rows, width = outs[0].shape
     side = 128 if width % 128 == 0 else width
-    for rnd, out in enumerate(outs):
+    for rnd, out in zip(rounds, outs):
         start = delays_ref[rnd, me ^ (1 << (rnd % levels))] - steps
         for c in range(0, width, side):
             x = window_ref[pl.ds(start, steps), :, c:c + side].astype(jnp.float32)
@@ -30,12 +30,12 @@
 
 def send_slices(window, delays, rounds, levels, steps):
     shape = (steps * window.shape[1], window.shape[2])
-    kernel = functools.partial(slice_kernel, levels=levels, steps=steps)
+    kernel = functools.partial(slice_kernel, rounds=tuple(rounds), levels=levels, steps=steps)
     return pl.pallas_call(
         kernel,
         in_specs=[SMEM, VMEM],
-        out_specs=[VMEM] * rounds,
-        out_shape=[jax.ShapeDtypeStruct(shape, window.dtype)] * rounds,
+        out_specs=[VMEM] * len(rounds),
+        out_shape=[jax.ShapeDtypeStruct(shape, window.dtype)] * len(rounds),
     )(delays, window)
 
 
@@ -201,12 +201,11 @@
     levels = lax.axis_size("area").bit_length() - 1
     nbits = lax.axis_size("neuron").bit_length() - 1
     n_pos = 1 << nbits
-    slices = send_slices(window, delays, rounds, levels, steps)
     stages = [list(range(f, min(f + 2, rounds))) for f in range(0, rounds, 2)]
     arrived = []
     gate = None
     for stage in stages:
-        pieces = [slices[rnd] for rnd in stage]
+        pieces = send_slices(window, delays, stage, levels, steps)
         if gate is not None:
             pieces, _ = lax.optimization_barrier((pieces, gate))
         got = [swap(piece, "area", 1 << (rnd % levels)) for piece, rnd in zip(pieces, stage)]

time: 94.7 us -> 92.5 us (0.977)
  waiting for transfers between devices: 59.1 us -> 54.4 us
  Pallas kernels: 16.8 us -> 18.7 us
    ppermute x16, waiting for transfers between devices: 59.1 us -> 54.4 us  [swap(): return lax.ppermute(value, axis, pairs)]
    pallas_call x1 -> x2, Pallas kernels: 3.2 us -> 5.12 us  [send_slices(): pl.pallas_call(kernel, in_specs=[SMEM, VMEM], out_specs=[VMEM] * len(roun...]
    unnamed x31 -> x29, local copies, waits for them, and re-layouts: 2.24 us -> 2.25 us
  transfers between devices with their start and end apart: 16 -> 16, of which waited for: 9 -> 10; matrix products, arithmetic and copies ran while one was open for 1% -> 2% of each run, Pallas kernels for 7% -> 10%
where the time goes in v11:
time: 92.5 us; the launch traced here: 92.1 us
  waiting for transfers between devices  54.4 us (59%)
  Pallas kernels  18.7 us (20%)
  starting transfers between devices  16 us (17%)
  local copies, waits for them, and re-layouts  2.25 us (2%)
    ppermute x16, waiting for transfers between devices, swap(): return lax.ppermute(value, axis, pairs)  54.4 us
    ppermute x16, starting transfers between devices, swap(): return lax.ppermute(value, axis, pairs)  16 us
    pallas_call x2, Pallas kernels, stage_contrib(): pl.pallas_call(kernel, in_specs=[SMEM] + specs, out_specs=out_specs, scra...  13.6 us
    pallas_call x2, Pallas kernels, send_slices(): pl.pallas_call(kernel, in_specs=[SMEM, VMEM], out_specs=[VMEM] * len(roun...  5.12 us
    unnamed x29, local copies, waits for them, and re-layouts  2.25 us
  transfers between devices with their start and end apart: 16, of which 10 were waited for; matrix products, arithmetic and copies ran while one was open for 2% of the time, Pallas kernels for 10%

profile of v11, /device:TPU:0, one launch (start us, length us, event | category | flops | bytes accessed | tf_op | source)
XLA Modules:
  0.0 92.1 jit_solution(4336609719438131107)
XLA Ops:
  0.6 0.0 copy-start.6
  0.6 0.0 copy-start.5
  0.7 0.0 copy-start.4
  0.7 0.0 copy-start.3
  0.7 0.0 copy-start.2
  0.7 0.0 copy-start.1
  0.7 0.0 copy-start
  0.7 2.7 %shard_map.131 = (bf16[128,2048]{1,0:T(8,128)(2,1)}, bf16[128,2048]{1,0:T(8,128)(2,1)}) custom-call(s32[4,4]{1,0:T(4,128)} %delays_ref.3, bf16[32,8,2048]{2,1,0:T(8,128)(2,1)} %window_ref.3), custom_call_target="tpu_custom_call" | custom-call | tf_op jit(solution)/shard_map/pallas_call | solution.py:34
  3.4 3.0 %collective-permute-start = (bf16[128,2048]{1,0:T(8,128)(2,1)}, bf16[128,2048]{1,0:T(8,128)(2,1)}, u32[]{:S(2)}, u32[]{:S(2)}) collective-permute-start(bf16[128,2048]{1,0:T(8,128)(2,1)} %get-tuple-element.15), channel_id=1, source_target_pairs={{0,4},{4,0},{8,12},{12,8},{1,5},{5,1},{9,13},{13,9},{2,6},{6,2},{1... | collective-permute-start | bytes 1572872 | tf_op jit(solution)/shard_map/ppermute | solution.py:17
  6.4 2.6 %collective-permute-start.1 = (bf16[128,2048]{1,0:T(8,128)(2,1)}, bf16[128,2048]{1,0:T(8,128)(2,1)}, u32[]{:S(2)}, u32[]{:S(2)}) collective-permute-start(bf16[128,2048]{1,0:T(8,128)(2,1)} %get-tuple-element.16), channel_id=1, source_target_pairs={{0,8},{4,12},{8,0},{12,4},{1,9},{5,13},{9,1},{13,5},{2,10},{6,14},... | collective-permute-start | bytes 1572872 | tf_op jit(solution)/shard_map/ppermute | solution.py:17
  9.0 2.5 %shard_map.130 = (bf16[128,2048]{1,0:T(8,128)(2,1)}, bf16[128,2048]{1,0:T(8,128)(2,1)}) custom-call(s32[4,4]{1,0:T(4,128)} %delays_ref.3, bf16[32,8,2048]{2,1,0:T(8,128)(2,1)} %window_ref.3), custom_call_target="tpu_custom_call" | custom-call | tf_op jit(solution)/shard_map/pallas_call | solution.py:34
  11.4 18.3 %collective-permute-done.refs_0_ = bf16[128,2048]{1,0:T(8,128)(2,1)} collective-permute-done((bf16[128,2048]{1,0:T(8,128)(2,1)}, bf16[128,2048]{1,0:T(8,128)(2,1)}, u32[]{:S(2)}, u32[]{:S(2)}) %collective-permute-start) | collective-permute-done | bytes 524320 | tf_op jit(solution)/shard_map/ppermute | solution.py:17
  29.7 0.0 collective-permute-start.5
  29.7 1.7 %collective-permute-start.4 = (bf16[128,2048]{1,0:T(8,128)(2,1)}, bf16[128,2048]{1,0:T(8,128)(2,1)}, u32[]{:S(2)}, u32[]{:S(2)}) collective-permute-start(bf16[128,2048]{1,0:T(8,128)(2,1)} %collective-permute-done.refs_0_), channel_id=1, source_target_pairs={{0,2},{1,3},{2,0},{3,1},{4,6},{5,7},{6,4},{7,5},{8,10},{9,11},{10,... | collective-permute-start | bytes 1572872 | tf_op jit(solution)/shard_map/ppermute | solution.py:17
  31.4 0.9 collective-permute-done.1.refs_4_
  32.3 1.5 %collective-permute-start.7 = (bf16[128,2048]{1,0:T(8,128)(2,1)}, bf16[128,2048]{1,0:T(8,128)(2,1)}, u32[]{:S(2)}, u32[]{:S(2)}) collective-permute-start(bf16[128,2048]{1,0:T(8,128)(2,1)} %collective-permute-done.1.refs_4_), channel_id=1, source_target_pairs={{0,2},{1,3},{2,0},{3,1},{4,6},{5,7},{6,4},{7,5},{8,10},{9,11},{10,... | collective-permute-start | bytes 1572872 | tf_op jit(solution)/shard_map/ppermute | solution.py:17
  33.8 0.4 collective-permute-start.2
  34.2 2.6 %collective-permute-start.12 = (bf16[128,2048]{1,0:T(8,128)(2,1)}, bf16[128,2048]{1,0:T(8,128)(2,1)S(1)}, u32[]{:S(2)}, u32[]{:S(2)}) collective-permute-start(bf16[128,2048]{1,0:T(8,128)(2,1)} %get-tuple-element.20), channel_id=1, source_target_pairs={{0,8},{4,12},{8,0},{12,4},{1,9},{5,13},{9,1},{13,5},{2,10},{6,14},... | collective-permute-start | bytes 1572872 | tf_op jit(solution)/shard_map/ppermute | solution.py:17
  36.8 0.0 collective-permute-done.5.refs_2_
  36.8 0.0 copy-start.13
  36.8 0.0 collective-permute-start.8
  36.8 8.0 %collective-permute-done.4.refs_1_ = bf16[128,2048]{1,0:T(8,128)(2,1)} collective-permute-done((bf16[128,2048]{1,0:T(8,128)(2,1)}, bf16[128,2048]{1,0:T(8,128)(2,1)}, u32[]{:S(2)}, u32[]{:S(2)}) %collective-permute-start.4) | collective-permute-done | bytes 524320 | tf_op jit(solution)/shard_map/ppermute | solution.py:17
  44.8 0.0 collective-permute-start.6
  44.8 10.8 %collective-permute-done.7.refs_5_ = bf16[128,2048]{1,0:T(8,128)(2,1)} collective-permute-done((bf16[128,2048]{1,0:T(8,128)(2,1)}, bf16[128,2048]{1,0:T(8,128)(2,1)}, u32[]{:S(2)}, u32[]{:S(2)}) %collective-permute-start.7) | collective-permute-done | bytes 524320 | tf_op jit(solution)/shard_map/ppermute | solution.py:17
  55.6 0.0 collective-permute-start.9
  55.6 0.6 collective-permute-done.2.refs_0_
  56.2 0.0 copy-start.7
  56.2 2.2 %collective-permute-start.3 = (bf16[128,2048]{1,0:T(8,128)(2,1)S(1)}, bf16[128,2048]{1,0:T(8,128)(2,1)}, u32[]{:S(2)}, u32[]{:S(2)}) collective-permute-start(bf16[128,2048]{1,0:T(8,128)(2,1)S(1)} %collective-permute-done.2.refs_0_), channel_id=1, source_target_pairs={{0,2},{1,3},{2,0},{3,1},{4,6},{5,7},{6,4},{7,5},{8,10},{9,11},{10,... | collective-permute-start | bytes 1572872 | tf_op jit(solution)/shard_map/ppermute | solution.py:17
  58.4 0.3 collective-permute-done.12.refs_4_
  58.8 0.0 copy-done.13
  58.8 0.0 copy-start.8
  58.8 0.9 %collective-permute-start.13 = (bf16[128,2048]{1,0:T(8,128)(2,1)S(1)}, bf16[128,2048]{1,0:T(8,128)(2,1)}, u32[]{:S(2)}, u32[]{:S(2)}) collective-permute-start(bf16[128,2048]{1,0:T(8,128)(2,1)S(1)} %collective-permute-done.12.refs_4_), channel_id=1, source_target_pairs={{0,2},{1,3},{2,0},{3,1},{4,6},{5,7},{6,4},{7,5},{8,10},{9,11},{10,... | collective-permute-start | bytes 1572872 | tf_op jit(solution)/shard_map/ppermute | solution.py:17
  59.7 1.4 %copy.15.bi_ref = s32[4,1,16,4]{3,2,1,0:T(8,128)} copy(s32[4,1,16,4]{2,3,1,0:T(4,128)} %param.20) | data formatting | bytes 2048 | tf_op args[9]
  61.1 0.0 collective-permute-done.8.refs_6_
  61.1 0.0 collective-permute-done.6.refs_3_
  61.1 0.0 collective-permute-done.9.refs_7_
  61.1 6.6 %shard_map.132.refs_9_ = f32[16,8,2048]{2,1,0:T(8,128)} custom-call(s32[4,1,16,4]{3,2,1,0:T(8,128)} %copy.15.bi_ref, bf16[128,2048]{1,0:T(8,128)(2,1)} %collective-permute-done.refs_0_, bf16[128,2048]{1,0:T(8,128)(2,1)} %collective-permute-done.4.refs_1_, bf16[128,2048]{1,0:T(8,128)(2,1)} %copy-done.13, bf16[128,2048]{1,0:T(8,128)(2,1)} %collective-permute-done.6.refs_3_, ...), custom_call_target="tpu_custom_call" | custom-call | tf_op jit(solution)/shard_map/pallas_call | solution.py:184
  67.7 3.6 %collective-permute-done.3.refs_1_ = bf16[128,2048]{1,0:T(8,128)(2,1)} collective-permute-done((bf16[128,2048]{1,0:T(8,128)(2,1)S(1)}, bf16[128,2048]{1,0:T(8,128)(2,1)}, u32[]{:S(2)}, u32[]{:S(2)}) %collective-permute-start.3) | collective-permute-done | bytes 524320 | tf_op jit(solution)/shard_map/ppermute | solution.py:17
  71.3 0.0 collective-permute-start.10
  71.3 0.5 collective-permute-start.11
  71.8 9.5 %collective-permute-done.13.refs_5_ = bf16[128,2048]{1,0:T(8,128)(2,1)} collective-permute-done((bf16[128,2048]{1,0:T(8,128)(2,1)S(1)}, bf16[128,2048]{1,0:T(8,128)(2,1)}, u32[]{:S(2)}, u32[]{:S(2)}) %collective-permute-start.13) | collective-permute-done | bytes 524320 | tf_op jit(solution)/shard_map/ppermute | solution.py:17
  81.3 0.0 collective-permute-start.14
  81.3 0.5 collective-permute-start.15
  81.8 0.0 collective-permute-done.10.refs_2_
  81.8 0.0 copy-start.9
  81.8 0.0 collective-permute-done.11.refs_3_
  81.8 0.0 copy-start.10
  81.8 2.1 %collective-permute-done.14.refs_6_ = bf16[128,2048]{1,0:T(8,128)(2,1)S(1)} collective-permute-done((bf16[128,2048]{1,0:T(8,128)(2,1)S(1)}, bf16[128,2048]{1,0:T(8,128)(2,1)S(1)}, u32[]{:S(2)}, u32[]{:S(2)}) %collective-permute-start.14) | collective-permute-done | bytes 524320 | tf_op jit(solution)/shard_map/ppermute | solution.py:17
  83.9 0.0 copy-done.9
  83.9 0.0 copy-start.11
  83.9 0.2 collective-permute-done.15.refs_7_
  84.2 0.0 copy-done.10
  84.2 0.6 copy-done.11
  84.8 0.2 copy-done.12
  85.0 0.0 copy-done.7
  85.0 0.0 copy-done.8
  85.0 0.0 copy-done.6
  85.0 0.0 copy-done.5
  85.0 0.0 copy-done.4
  85.0 0.0 copy-done.3
  85.0 0.0 copy-done.2
  85.0 0.0 copy-done.1
  85.0 0.0 copy-done
  85.1 7.0 %shard_map.133 = (bf16[16,8,2048]{2,1,0:T(8,128)(2,1)}, f32[8,2048]{1,0:T(8,128)}, f32[8,2048]{1,0:T(8,128)}) custom-call(s32[4,1,16,4]{3,2,1,0:T(8,128)} %copy.15.bi_ref, bf16[128,2048]{1,0:T(8,128)(2,1)} %copy-done.7, bf16[128,2048]{1,0:T(8,128)(2,1)} %collective-permute-done.3.refs_1_, bf16[128,2048]{1,0:T(8,128)(2,1)} %copy-done.9, ...), custom_call_target="tpu_custom_call" | custom-call | tf_op jit(solution)/shard_map/pallas_call | solution.py:184
  (1 shorter events, 0.0 us)
Async XLA Ops:
  0.6 84.4 %copy-start.6 = (f32[2048]{0:T(1024)S(1)}, f32[2048]{0:T(1024)}, u32[]{:S(2)}) copy-start(f32[2048]{0:T(1024)} %param.18) | copy-start | bytes 24580
  0.6 84.4 %copy-start.5 = (f32[2048]{0:T(1024)S(1)}, f32[2048]{0:T(1024)}, u32[]{:S(2)}) copy-start(f32[2048]{0:T(1024)} %param.17) | copy-start | bytes 24580
  0.7 84.4 %copy-start.4 = (f32[2048]{0:T(1024)S(1)}, f32[2048]{0:T(1024)}, u32[]{:S(2)}) copy-start(f32[2048]{0:T(1024)} %param.16) | copy-start | bytes 24580
  0.7 84.4 %copy-start.3 = (f32[8,2048]{1,0:T(8,128)S(1)}, f32[8,2048]{1,0:T(8,128)}, u32[]{:S(2)}) copy-start(f32[8,2048]{1,0:T(8,128)} %refs_13_.1) | copy-start | bytes 196612
  0.7 84.4 %copy-start.2 = (f32[8,2048]{1,0:T(8,128)S(1)}, f32[8,2048]{1,0:T(8,128)}, u32[]{:S(2)}) copy-start(f32[8,2048]{1,0:T(8,128)} %refs_12_.1) | copy-start | bytes 196612
  0.7 84.4 %copy-start.1 = (f32[16,8,2048]{2,1,0:T(8,128)S(1)}, f32[16,8,2048]{2,1,0:T(8,128)}, u32[]{:S(2)}) copy-start(f32[16,8,2048]{2,1,0:T(8,128)} %refs_11_.1) | copy-start | bytes 3145732
  0.7 84.4 %copy-start = (f32[16,8,2048]{2,1,0:T(8,128)S(1)}, f32[16,8,2048]{2,1,0:T(8,128)}, u32[]{:S(2)}) copy-start(f32[16,8,2048]{2,1,0:T(8,128)} %refs_10_.1) | copy-start | bytes 3145732
  3.4 26.4 %collective-permute-start = (bf16[128,2048]{1,0:T(8,128)(2,1)}, bf16[128,2048]{1,0:T(8,128)(2,1)}, u32[]{:S(2)}, u32[]{:S(2)}) collective-permute-start(bf16[128,2048]{1,0:T(8,128)(2,1)} %get-tuple-element.15), channel_id=1, source_target_pairs={{0,4},{4,0},{8,12},{12,8},{1,5},{5,1},{9,13},{13,9},{2,6},{6,2},{1... | collective-permute-start | bytes 1572872 | tf_op jit(solution)/shard_map/ppermute | solution.py:17
  6.4 25.9 %collective-permute-start.1 = (bf16[128,2048]{1,0:T(8,128)(2,1)}, bf16[128,2048]{1,0:T(8,128)(2,1)}, u32[]{:S(2)}, u32[]{:S(2)}) collective-permute-start(bf16[128,2048]{1,0:T(8,128)(2,1)} %get-tuple-element.16), channel_id=1, source_target_pairs={{0,8},{4,12},{8,0},{12,4},{1,9},{5,13},{9,1},{13,5},{2,10},{6,14},... | collective-permute-start | bytes 1572872 | tf_op jit(solution)/shard_map/ppermute | solution.py:17
  29.7 7.1 %collective-permute-start.5 = (bf16[128,2048]{1,0:T(8,128)(2,1)}, bf16[128,2048]{1,0:T(8,128)(2,1)S(1)}, u32[]{:S(2)}, u32[]{:S(2)}) collective-permute-start(bf16[128,2048]{1,0:T(8,128)(2,1)} %collective-permute-done.refs_0_), channel_id=1, source_target_pairs={{0,1},{1,0},{2,3},{3,2},{4,5},{5,4},{6,7},{7,6},{8,9},{9,8},{10,11... | collective-permute-start | bytes 1572872 | tf_op jit(solution)/shard_map/ppermute | solution.py:17
  29.7 15.0 %collective-permute-start.4 = (bf16[128,2048]{1,0:T(8,128)(2,1)}, bf16[128,2048]{1,0:T(8,128)(2,1)}, u32[]{:S(2)}, u32[]{:S(2)}) collective-permute-start(bf16[128,2048]{1,0:T(8,128)(2,1)} %collective-permute-done.refs_0_), channel_id=1, source_target_pairs={{0,2},{1,3},{2,0},{3,1},{4,6},{5,7},{6,4},{7,5},{8,10},{9,11},{10,... | collective-permute-start | bytes 1572872 | tf_op jit(solution)/shard_map/ppermute | solution.py:17
  32.3 23.4 %collective-permute-start.7 = (bf16[128,2048]{1,0:T(8,128)(2,1)}, bf16[128,2048]{1,0:T(8,128)(2,1)}, u32[]{:S(2)}, u32[]{:S(2)}) collective-permute-start(bf16[128,2048]{1,0:T(8,128)(2,1)} %collective-permute-done.1.refs_4_), channel_id=1, source_target_pairs={{0,2},{1,3},{2,0},{3,1},{4,6},{5,7},{6,4},{7,5},{8,10},{9,11},{10,... | collective-permute-start | bytes 1572872 | tf_op jit(solution)/shard_map/ppermute | solution.py:17
  33.8 22.5 %collective-permute-start.2 = (bf16[128,2048]{1,0:T(8,128)(2,1)}, bf16[128,2048]{1,0:T(8,128)(2,1)S(1)}, u32[]{:S(2)}, u32[]{:S(2)}) collective-permute-start(bf16[128,2048]{1,0:T(8,128)(2,1)} %get-tuple-element.17), channel_id=1, source_target_pairs={{0,4},{4,0},{8,12},{12,8},{1,5},{5,1},{9,13},{13,9},{2,6},{6,2},{1... | collective-permute-start | bytes 1572872 | tf_op jit(solution)/shard_map/ppermute | solution.py:17
  34.2 24.6 %collective-permute-start.12 = (bf16[128,2048]{1,0:T(8,128)(2,1)}, bf16[128,2048]{1,0:T(8,128)(2,1)S(1)}, u32[]{:S(2)}, u32[]{:S(2)}) collective-permute-start(bf16[128,2048]{1,0:T(8,128)(2,1)} %get-tuple-element.20), channel_id=1, source_target_pairs={{0,8},{4,12},{8,0},{12,4},{1,9},{5,13},{9,1},{13,5},{2,10},{6,14},... | collective-permute-start | bytes 1572872 | tf_op jit(solution)/shard_map/ppermute | solution.py:17
  36.8 22.0 %copy-start.13 = (bf16[128,2048]{1,0:T(8,128)(2,1)}, bf16[128,2048]{1,0:T(8,128)(2,1)S(1)}, u32[]{:S(2)}) copy-start(bf16[128,2048]{1,0:T(8,128)(2,1)S(1)} %collective-permute-done.5.refs_2_) | copy-start | bytes 1572868
  36.8 24.3 %collective-permute-start.8 = (bf16[128,2048]{1,0:T(8,128)(2,1)}, bf16[128,2048]{1,0:T(8,128)(2,1)}, u32[]{:S(2)}, u32[]{:S(2)}) collective-permute-start(bf16[128,2048]{1,0:T(8,128)(2,1)} %collective-permute-done.1.refs_4_), channel_id=1, source_target_pairs={{0,1},{1,0},{2,3},{3,2},{4,5},{5,4},{6,7},{7,6},{8,9},{9,8},{10,11... | collective-permute-start | bytes 1572872 | tf_op jit(solution)/shard_map/ppermute | solution.py:17
  44.8 16.3 %collective-permute-start.6 = (bf16[128,2048]{1,0:T(8,128)(2,1)}, bf16[128,2048]{1,0:T(8,128)(2,1)}, u32[]{:S(2)}, u32[]{:S(2)}) collective-permute-start(bf16[128,2048]{1,0:T(8,128)(2,1)} %collective-permute-done.4.refs_1_), channel_id=1, source_target_pairs={{0,1},{1,0},{2,3},{3,2},{4,5},{5,4},{6,7},{7,6},{8,9},{9,8},{10,11... | collective-permute-start | bytes 1572872 | tf_op jit(solution)/shard_map/ppermute | solution.py:17
  55.6 5.5 %collective-permute-start.9 = (bf16[128,2048]{1,0:T(8,128)(2,1)}, bf16[128,2048]{1,0:T(8,128)(2,1)}, u32[]{:S(2)}, u32[]{:S(2)}) collective-permute-start(bf16[128,2048]{1,0:T(8,128)(2,1)} %collective-permute-done.7.refs_5_), channel_id=1, source_target_pairs={{0,1},{1,0},{2,3},{3,2},{4,5},{5,4},{6,7},{7,6},{8,9},{9,8},{10,11... | collective-permute-start | bytes 1572872 | tf_op jit(solution)/shard_map/ppermute | solution.py:17
  56.2 28.8 %copy-start.7 = (bf16[128,2048]{1,0:T(8,128)(2,1)}, bf16[128,2048]{1,0:T(8,128)(2,1)S(1)}, u32[]{:S(2)}) copy-start(bf16[128,2048]{1,0:T(8,128)(2,1)S(1)} %collective-permute-done.2.refs_0_) | copy-start | bytes 1572868
  56.2 15.1 %collective-permute-start.3 = (bf16[128,2048]{1,0:T(8,128)(2,1)S(1)}, bf16[128,2048]{1,0:T(8,128)(2,1)}, u32[]{:S(2)}, u32[]{:S(2)}) collective-permute-start(bf16[128,2048]{1,0:T(8,128)(2,1)S(1)} %collective-permute-done.2.refs_0_), channel_id=1, source_target_pairs={{0,2},{1,3},{2,0},{3,1},{4,6},{5,7},{6,4},{7,5},{8,10},{9,11},{10,... | collective-permute-start | bytes 1572872 | tf_op jit(solution)/shard_map/ppermute | solution.py:17
  58.8 26.2 %copy-start.8 = (bf16[128,2048]{1,0:T(8,128)(2,1)}, bf16[128,2048]{1,0:T(8,128)(2,1)S(1)}, u32[]{:S(2)}) copy-start(bf16[128,2048]{1,0:T(8,128)(2,1)S(1)} %collective-permute-done.12.refs_4_) | copy-start | bytes 1572868
  58.8 22.5 %collective-permute-start.13 = (bf16[128,2048]{1,0:T(8,128)(2,1)S(1)}, bf16[128,2048]{1,0:T(8,128)(2,1)}, u32[]{:S(2)}, u32[]{:S(2)}) collective-permute-start(bf16[128,2048]{1,0:T(8,128)(2,1)S(1)} %collective-permute-done.12.refs_4_), channel_id=1, source_target_pairs={{0,2},{1,3},{2,0},{3,1},{4,6},{5,7},{6,4},{7,5},{8,10},{9,11},{10,... | collective-permute-start | bytes 1572872 | tf_op jit(solution)/shard_map/ppermute | solution.py:17
  71.3 10.5 %collective-permute-start.10 = (bf16[128,2048]{1,0:T(8,128)(2,1)S(1)}, bf16[128,2048]{1,0:T(8,128)(2,1)S(1)}, u32[]{:S(2)}, u32[]{:S(2)}) collective-permute-start(bf16[128,2048]{1,0:T(8,128)(2,1)S(1)} %collective-permute-done.2.refs_0_), channel_id=1, source_target_pairs={{0,1},{1,0},{2,3},{3,2},{4,5},{5,4},{6,7},{7,6},{8,9},{9,8},{10,11... | collective-permute-start | bytes 1572872 | tf_op jit(solution)/shard_map/ppermute | solution.py:17
  71.3 10.5 %collective-permute-start.11 = (bf16[128,2048]{1,0:T(8,128)(2,1)}, bf16[128,2048]{1,0:T(8,128)(2,1)S(1)}, u32[]{:S(2)}, u32[]{:S(2)}) collective-permute-start(bf16[128,2048]{1,0:T(8,128)(2,1)} %collective-permute-done.3.refs_1_), channel_id=1, source_target_pairs={{0,1},{1,0},{2,3},{3,2},{4,5},{5,4},{6,7},{7,6},{8,9},{9,8},{10,11... | collective-permute-start | bytes 1572872 | tf_op jit(solution)/shard_map/ppermute | solution.py:17
  81.3 2.6 %collective-permute-start.14 = (bf16[128,2048]{1,0:T(8,128)(2,1)S(1)}, bf16[128,2048]{1,0:T(8,128)(2,1)S(1)}, u32[]{:S(2)}, u32[]{:S(2)}) collective-permute-start(bf16[128,2048]{1,0:T(8,128)(2,1)S(1)} %collective-permute-done.12.refs_4_), channel_id=1, source_target_pairs={{0,1},{1,0},{2,3},{3,2},{4,5},{5,4},{6,7},{7,6},{8,9},{9,8},{10,11... | collective-permute-start | bytes 1572872 | tf_op jit(solution)/shard_map/ppermute | solution.py:17
  81.3 2.9 %collective-permute-start.15 = (bf16[128,2048]{1,0:T(8,128)(2,1)}, bf16[128,2048]{1,0:T(8,128)(2,1)S(1)}, u32[]{:S(2)}, u32[]{:S(2)}) collective-permute-start(bf16[128,2048]{1,0:T(8,128)(2,1)} %collective-permute-done.13.refs_5_), channel_id=1, source_target_pairs={{0,1},{1,0},{2,3},{3,2},{4,5},{5,4},{6,7},{7,6},{8,9},{9,8},{10,11... | collective-permute-start | bytes 1572872 | tf_op jit(solution)/shard_map/ppermute | solution.py:17
  81.8 2.1 %copy-start.9 = (bf16[128,2048]{1,0:T(8,128)(2,1)}, bf16[128,2048]{1,0:T(8,128)(2,1)S(1)}, u32[]{:S(2)}) copy-start(bf16[128,2048]{1,0:T(8,128)(2,1)S(1)} %collective-permute-done.10.refs_2_) | copy-start | bytes 1572868
  81.8 2.4 %copy-start.10 = (bf16[128,2048]{1,0:T(8,128)(2,1)}, bf16[128,2048]{1,0:T(8,128)(2,1)S(1)}, u32[]{:S(2)}) copy-start(bf16[128,2048]{1,0:T(8,128)(2,1)S(1)} %collective-permute-done.11.refs_3_) | copy-start | bytes 1572868
  83.9 0.8 copy-start.11
  84.2 0.8 copy-start.12

commit v12 on v11

--- a/solution.py
+++ b/solution.py
@@ -211,13 +211,14 @@
         got = [swap(piece, "area", 1 << (rnd % levels)) for piece, rnd in zip(pieces, stage)]
         arrived += got
         gate = got
+    groups = stages[:-1] + [[rnd] for rnd in stages[-1]]
     rec = None
-    for si, stage in enumerate(stages):
+    for si, stage in enumerate(groups):
         chunks = []
         for rnd in stage:
             chunks += gather_neuron(arrived[rnd], rec)
         scan_args = None
-        if si == len(stages) - 1:
+        if si == len(groups) - 1:
             scan_args = (err_grad, surrogate, lv_end, la_end, alpha, rho, beta)
         rec = stage_contrib(block_index, chunks, weights, stage, n_pos, rec, scan_args, steps)
     return rec

time: 92.5 us -> 106 us (1.15)
  waiting for transfers between devices: 54.4 us -> 64.9 us
  Pallas kernels: 18.7 us -> 22.7 us
  starting transfers between devices: 16 us -> 13.4 us
  local copies, waits for them, and re-layouts: 2.25 us -> 3.49 us
    ppermute x16, waiting for transfers between devices: 54.4 us -> 64.9 us  [swap(): return lax.ppermute(value, axis, pairs)]
    pallas_call x2 -> x3, Pallas kernels: 13.6 us -> 17.8 us  [stage_contrib(): pl.pallas_call(kernel, in_specs=[SMEM] + specs, out_specs=out_specs, scra...]
    ppermute x16, starting transfers between devices: 16 us -> 13.4 us  [swap(): return lax.ppermute(value, axis, pairs)]
    unnamed x29 -> x33, local copies, waits for them, and re-layouts: 2.25 us -> 3.49 us
  transfers between devices with their start and end apart: 16 -> 16, of which waited for: 10 -> 9; matrix products, arithmetic and copies ran while one was open for 2% -> 1% of each run, Pallas kernels for 10% -> 14%
where the time goes in v12:
time: 106 us; the launch traced here: 105 us
  waiting for transfers between devices  64.9 us (61%)
  Pallas kernels  22.7 us (21%)
  starting transfers between devices  13.4 us (13%)
  local copies, waits for them, and re-layouts  3.49 us (3%)
    ppermute x16, waiting for transfers between devices, swap(): return lax.ppermute(value, axis, pairs)  64.9 us
    pallas_call x3, Pallas kernels, stage_contrib(): pl.pallas_call(kernel, in_specs=[SMEM] + specs, out_specs=out_specs, scra...  17.8 us
    ppermute x16, starting transfers between devices, swap(): return lax.ppermute(value, axis, pairs)  13.4 us
    pallas_call x2, Pallas kernels, send_slices(): pl.pallas_call(kernel, in_specs=[SMEM, VMEM], out_specs=[VMEM] * len(roun...  4.94 us
    unnamed x33, local copies, waits for them, and re-layouts  3.49 us
  transfers between devices with their start and end apart: 16, of which 9 were waited for; matrix products, arithmetic and copies ran while one was open for 1% of the time, Pallas kernels for 14%

profile of v12, /device:TPU:0, one launch (start us, length us, event | category | flops | bytes accessed | tf_op | source)
XLA Modules:
  0.0 105.3 jit_solution(17692975386742719584)
XLA Ops:
  0.6 2.5 %shard_map.131 = (bf16[128,2048]{1,0:T(8,128)(2,1)}, bf16[128,2048]{1,0:T(8,128)(2,1)}) custom-call(s32[4,4]{1,0:T(4,128)} %delays_ref.3, bf16[32,8,2048]{2,1,0:T(8,128)(2,1)} %window_ref.3), custom_call_target="tpu_custom_call" | custom-call | tf_op jit(solution)/shard_map/pallas_call | solution.py:34
  3.1 3.0 %collective-permute-start = (bf16[128,2048]{1,0:T(8,128)(2,1)}, bf16[128,2048]{1,0:T(8,128)(2,1)S(1)}, u32[]{:S(2)}, u32[]{:S(2)}) collective-permute-start(bf16[128,2048]{1,0:T(8,128)(2,1)} %get-tuple-element.15), channel_id=1, source_target_pairs={{0,4},{4,0},{8,12},{12,8},{1,5},{5,1},{9,13},{13,9},{2,6},{6,2},{1... | collective-permute-start | bytes 1572872 | tf_op jit(solution)/shard_map/ppermute | solution.py:17
  6.1 2.6 %collective-permute-start.1 = (bf16[128,2048]{1,0:T(8,128)(2,1)}, bf16[128,2048]{1,0:T(8,128)(2,1)S(1)}, u32[]{:S(2)}, u32[]{:S(2)}) collective-permute-start(bf16[128,2048]{1,0:T(8,128)(2,1)} %get-tuple-element.16), channel_id=1, source_target_pairs={{0,8},{4,12},{8,0},{12,4},{1,9},{5,13},{9,1},{13,5},{2,10},{6,14},... | collective-permute-start | bytes 1572872 | tf_op jit(solution)/shard_map/ppermute | solution.py:17
  8.7 2.5 %shard_map.130 = (bf16[128,2048]{1,0:T(8,128)(2,1)}, bf16[128,2048]{1,0:T(8,128)(2,1)}) custom-call(s32[4,4]{1,0:T(4,128)} %delays_ref.3, bf16[32,8,2048]{2,1,0:T(8,128)(2,1)} %window_ref.3), custom_call_target="tpu_custom_call" | custom-call | tf_op jit(solution)/shard_map/pallas_call | solution.py:34
  11.2 18.2 %collective-permute-done.refs_0_ = bf16[128,2048]{1,0:T(8,128)(2,1)S(1)} collective-permute-done((bf16[128,2048]{1,0:T(8,128)(2,1)}, bf16[128,2048]{1,0:T(8,128)(2,1)S(1)}, u32[]{:S(2)}, u32[]{:S(2)}) %collective-permute-start) | collective-permute-done | bytes 524320 | tf_op jit(solution)/shard_map/ppermute | solution.py:17
  29.4 0.0 copy-start.11
  29.4 1.7 %collective-permute-start.6 = (bf16[128,2048]{1,0:T(8,128)(2,1)S(1)}, bf16[128,2048]{1,0:T(8,128)(2,1)S(1)}, u32[]{:S(2)}, u32[]{:S(2)}) collective-permute-start(bf16[128,2048]{1,0:T(8,128)(2,1)S(1)} %collective-permute-done.refs_0_), channel_id=1, source_target_pairs={{0,2},{1,3},{2,0},{3,1},{4,6},{5,7},{6,4},{7,5},{8,10},{9,11},{10,... | collective-permute-start | bytes 1572872 | tf_op jit(solution)/shard_map/ppermute | solution.py:17
  31.0 0.9 collective-permute-done.1.refs_4_
  31.9 0.0 copy-start.12
  31.9 1.5 %collective-permute-start.9 = (bf16[128,2048]{1,0:T(8,128)(2,1)S(1)}, bf16[128,2048]{1,0:T(8,128)(2,1)S(1)}, u32[]{:S(2)}, u32[]{:S(2)}) collective-permute-start(bf16[128,2048]{1,0:T(8,128)(2,1)S(1)} %collective-permute-done.1.refs_4_), channel_id=1, source_target_pairs={{0,2},{1,3},{2,0},{3,1},{4,6},{5,7},{6,4},{7,5},{8,10},{9,11},{10,... | collective-permute-start | bytes 1572872 | tf_op jit(solution)/shard_map/ppermute | solution.py:17
  33.4 0.4 collective-permute-start.4
  33.9 0.0 collective-permute-start.7
  33.9 0.5 collective-permute-start.10
  34.4 9.9 %collective-permute-done.6.refs_1_ = bf16[128,2048]{1,0:T(8,128)(2,1)S(1)} collective-permute-done((bf16[128,2048]{1,0:T(8,128)(2,1)S(1)}, bf16[128,2048]{1,0:T(8,128)(2,1)S(1)}, u32[]{:S(2)}, u32[]{:S(2)}) %collective-permute-start.6) | collective-permute-done | bytes 524320 | tf_op jit(solution)/shard_map/ppermute | solution.py:17
  44.2 0.0 collective-permute-start.8
  44.3 9.5 %collective-permute-done.9.refs_5_ = bf16[128,2048]{1,0:T(8,128)(2,1)S(1)} collective-permute-done((bf16[128,2048]{1,0:T(8,128)(2,1)S(1)}, bf16[128,2048]{1,0:T(8,128)(2,1)S(1)}, u32[]{:S(2)}, u32[]{:S(2)}) %collective-permute-start.9) | collective-permute-done | bytes 524320 | tf_op jit(solution)/shard_map/ppermute | solution.py:17
  53.7 0.0 collective-permute-start.11
  53.7 0.0 collective-permute-done.4.refs_0_
  53.7 0.0 copy-start.7
  53.8 1.4 %collective-permute-start.5 = (bf16[128,2048]{1,0:T(8,128)(2,1)S(1)}, bf16[128,2048]{1,0:T(8,128)(2,1)}, u32[]{:S(2)}, u32[]{:S(2)}) collective-permute-start(bf16[128,2048]{1,0:T(8,128)(2,1)S(1)} %collective-permute-done.4.refs_0_), channel_id=1, source_target_pairs={{0,2},{1,3},{2,0},{3,1},{4,6},{5,7},{6,4},{7,5},{8,10},{9,11},{10,... | collective-permute-start | bytes 1572872 | tf_op jit(solution)/shard_map/ppermute | solution.py:17
  55.2 0.0 collective-permute-done.7.refs_2_
  55.2 0.8 copy-done.15
  56.0 0.7 collective-permute-start.2
  56.6 1.4 %copy.16.bi_ref = s32[4,1,16,4]{3,2,1,0:T(8,128)} copy(s32[4,1,16,4]{2,3,1,0:T(4,128)} %param.20) | data formatting | bytes 2048 | tf_op args[9]
  58.0 0.0 collective-permute-done.10.refs_6_
  58.0 0.0 collective-permute-done.8.refs_3_
  58.0 0.0 collective-permute-done.11.refs_7_
  58.0 0.0 copy-done.11
  58.1 0.0 copy-done.12
  58.1 0.0 copy-done.13
  58.1 0.0 copy-done.14
  58.1 6.6 %shard_map.132.refs_5_ = f32[16,8,2048]{2,1,0:T(8,128)} custom-call(s32[4,1,16,4]{3,2,1,0:T(8,128)} %copy.16.bi_ref, bf16[128,2048]{1,0:T(8,128)(2,1)} %copy-done.11, bf16[128,2048]{1,0:T(8,128)(2,1)} %copy-done.13, bf16[128,2048]{1,0:T(8,128)(2,1)} %copy-done.15, bf16[128,2048]{1,0:T(8,128)(2,1)} %collective-permute-done.8.refs_3_, ...), custom_call_target="tpu_custom_call" | custom-call | tf_op jit(solution)/shard_map/pallas_call | solution.py:184
  64.7 0.0 copy-start
  64.7 0.0 copy-start.1
  64.7 0.0 copy-start.2
  64.7 0.0 copy-start.3
  64.7 0.0 copy-start.4
  64.7 0.0 copy-start.5
  64.7 0.0 copy-start.6
  64.7 3.5 %collective-permute-done.5.refs_1_ = bf16[128,2048]{1,0:T(8,128)(2,1)} collective-permute-done((bf16[128,2048]{1,0:T(8,128)(2,1)S(1)}, bf16[128,2048]{1,0:T(8,128)(2,1)}, u32[]{:S(2)}, u32[]{:S(2)}) %collective-permute-start.5) | collective-permute-done | bytes 524320 | tf_op jit(solution)/shard_map/ppermute | solution.py:17
  68.2 0.0 collective-permute-start.12
  68.2 0.5 collective-permute-start.13
  68.7 13.4 %collective-permute-done.2.refs_0_ = bf16[128,2048]{1,0:T(8,128)(2,1)S(1)} collective-permute-done((bf16[128,2048]{1,0:T(8,128)(2,1)}, bf16[128,2048]{1,0:T(8,128)(2,1)S(1)}, u32[]{:S(2)}, u32[]{:S(2)}) %collective-permute-start.2) | collective-permute-done | bytes 524320 | tf_op jit(solution)/shard_map/ppermute | solution.py:17
  82.1 0.5 collective-permute-start.3
  82.7 0.0 collective-permute-done.12.refs_2_
  82.7 0.8 copy-done.9
  83.5 0.0 collective-permute-done.13.refs_3_
  83.5 0.0 copy-done.7
  83.5 5.6 %shard_map.133.refs_5_ = f32[16,8,2048]{2,1,0:T(8,128)} custom-call(s32[4,1,16,4]{3,2,1,0:T(8,128)} %copy.16.bi_ref, bf16[128,2048]{1,0:T(8,128)(2,1)} %copy-done.7, bf16[128,2048]{1,0:T(8,128)(2,1)} %collective-permute-done.5.refs_1_, bf16[128,2048]{1,0:T(8,128)(2,1)} %copy-done.9, bf16[128,2048]{1,0:T(8,128)(2,1)} %collective-permute-done.13.refs_3_, ...), custom_call_target="tpu_custom_call" | custom-call | tf_op jit(solution)/shard_map/pallas_call | solution.py:184
  89.1 7.0 %collective-permute-done.3.refs_1_ = bf16[128,2048]{1,0:T(8,128)(2,1)} collective-permute-done((bf16[128,2048]{1,0:T(8,128)(2,1)S(1)}, bf16[128,2048]{1,0:T(8,128)(2,1)}, u32[]{:S(2)}, u32[]{:S(2)}) %collective-permute-start.3) | collective-permute-done | bytes 524320 | tf_op jit(solution)/shard_map/ppermute | solution.py:17
  96.1 0.0 collective-permute-start.14
  96.1 0.5 collective-permute-start.15
  96.6 2.1 %collective-permute-done.14.refs_2_ = bf16[128,2048]{1,0:T(8,128)(2,1)S(1)} collective-permute-done((bf16[128,2048]{1,0:T(8,128)(2,1)S(1)}, bf16[128,2048]{1,0:T(8,128)(2,1)S(1)}, u32[]{:S(2)}, u32[]{:S(2)}) %collective-permute-start.14) | collective-permute-done | bytes 524320 | tf_op jit(solution)/shard_map/ppermute | solution.py:17
  98.7 0.4 collective-permute-done.15.refs_3_
  99.1 0.0 copy-done.8
  99.1 0.4 copy-done.10
  99.5 0.0 copy-done
  99.6 0.0 copy-done.1
  99.6 0.0 copy-done.2
  99.6 0.0 copy-done.3
  99.6 0.0 copy-done.4
  99.6 0.0 copy-done.5
  99.6 0.0 copy-done.6
  99.6 5.7 %shard_map.134 = (bf16[16,8,2048]{2,1,0:T(8,128)(2,1)}, f32[8,2048]{1,0:T(8,128)}, f32[8,2048]{1,0:T(8,128)}) custom-call(s32[4,1,16,4]{3,2,1,0:T(8,128)} %copy.16.bi_ref, bf16[128,2048]{1,0:T(8,128)(2,1)} %copy-done.8, bf16[128,2048]{1,0:T(8,128)(2,1)} %collective-permute-done.3.refs_1_, bf16[128,2048]{1,0:T(8,128)(2,1)} %copy-done.10, ...), custom_call_target="tpu_custom_call" | custom-call | tf_op jit(solution)/shard_map/pallas_call | solution.py:184
  (6 shorter events, 0.0 us)
Async XLA Ops:
  3.1 26.3 %collective-permute-start = (bf16[128,2048]{1,0:T(8,128)(2,1)}, bf16[128,2048]{1,0:T(8,128)(2,1)S(1)}, u32[]{:S(2)}, u32[]{:S(2)}) collective-permute-start(bf16[128,2048]{1,0:T(8,128)(2,1)} %get-tuple-element.15), channel_id=1, source_target_pairs={{0,4},{4,0},{8,12},{12,8},{1,5},{5,1},{9,13},{13,9},{2,6},{6,2},{1... | collective-permute-start | bytes 1572872 | tf_op jit(solution)/shard_map/ppermute | solution.py:17
  6.1 25.8 %collective-permute-start.1 = (bf16[128,2048]{1,0:T(8,128)(2,1)}, bf16[128,2048]{1,0:T(8,128)(2,1)S(1)}, u32[]{:S(2)}, u32[]{:S(2)}) collective-permute-start(bf16[128,2048]{1,0:T(8,128)(2,1)} %get-tuple-element.16), channel_id=1, source_target_pairs={{0,8},{4,12},{8,0},{12,4},{1,9},{5,13},{9,1},{13,5},{2,10},{6,14},... | collective-permute-start | bytes 1572872 | tf_op jit(solution)/shard_map/ppermute | solution.py:17
  29.4 28.7 %copy-start.11 = (bf16[128,2048]{1,0:T(8,128)(2,1)}, bf16[128,2048]{1,0:T(8,128)(2,1)S(1)}, u32[]{:S(2)}) copy-start(bf16[128,2048]{1,0:T(8,128)(2,1)S(1)} %collective-permute-done.refs_0_) | copy-start | bytes 1572868
  29.4 14.9 %collective-permute-start.6 = (bf16[128,2048]{1,0:T(8,128)(2,1)S(1)}, bf16[128,2048]{1,0:T(8,128)(2,1)S(1)}, u32[]{:S(2)}, u32[]{:S(2)}) collective-permute-start(bf16[128,2048]{1,0:T(8,128)(2,1)S(1)} %collective-permute-done.refs_0_), channel_id=1, source_target_pairs={{0,2},{1,3},{2,0},{3,1},{4,6},{5,7},{6,4},{7,5},{8,10},{9,11},{10,... | collective-permute-start | bytes 1572872 | tf_op jit(solution)/shard_map/ppermute | solution.py:17
  31.9 26.2 %copy-start.12 = (bf16[128,2048]{1,0:T(8,128)(2,1)}, bf16[128,2048]{1,0:T(8,128)(2,1)S(1)}, u32[]{:S(2)}) copy-start(bf16[128,2048]{1,0:T(8,128)(2,1)S(1)} %collective-permute-done.1.refs_4_) | copy-start | bytes 1572868
  31.9 21.8 %collective-permute-start.9 = (bf16[128,2048]{1,0:T(8,128)(2,1)S(1)}, bf16[128,2048]{1,0:T(8,128)(2,1)S(1)}, u32[]{:S(2)}, u32[]{:S(2)}) collective-permute-start(bf16[128,2048]{1,0:T(8,128)(2,1)S(1)} %collective-permute-done.1.refs_4_), channel_id=1, source_target_pairs={{0,2},{1,3},{2,0},{3,1},{4,6},{5,7},{6,4},{7,5},{8,10},{9,11},{10,... | collective-permute-start | bytes 1572872 | tf_op jit(solution)/shard_map/ppermute | solution.py:17
  33.4 20.3 %collective-permute-start.4 = (bf16[128,2048]{1,0:T(8,128)(2,1)}, bf16[128,2048]{1,0:T(8,128)(2,1)S(1)}, u32[]{:S(2)}, u32[]{:S(2)}) collective-permute-start(bf16[128,2048]{1,0:T(8,128)(2,1)} %get-tuple-element.18), channel_id=1, source_target_pairs={{0,4},{4,0},{8,12},{12,8},{1,5},{5,1},{9,13},{13,9},{2,6},{6,2},{1... | collective-permute-start | bytes 1572872 | tf_op jit(solution)/shard_map/ppermute | solution.py:17
  33.9 21.3 %collective-permute-start.7 = (bf16[128,2048]{1,0:T(8,128)(2,1)S(1)}, bf16[128,2048]{1,0:T(8,128)(2,1)S(1)}, u32[]{:S(2)}, u32[]{:S(2)}) collective-permute-start(bf16[128,2048]{1,0:T(8,128)(2,1)S(1)} %collective-permute-done.refs_0_), channel_id=1, source_target_pairs={{0,1},{1,0},{2,3},{3,2},{4,5},{5,4},{6,7},{7,6},{8,9},{9,8},{10,11... | collective-permute-start | bytes 1572872 | tf_op jit(solution)/shard_map/ppermute | solution.py:17
  33.9 24.2 %collective-permute-start.10 = (bf16[128,2048]{1,0:T(8,128)(2,1)S(1)}, bf16[128,2048]{1,0:T(8,128)(2,1)}, u32[]{:S(2)}, u32[]{:S(2)}) collective-permute-start(bf16[128,2048]{1,0:T(8,128)(2,1)S(1)} %collective-permute-done.1.refs_4_), channel_id=1, source_target_pairs={{0,1},{1,0},{2,3},{3,2},{4,5},{5,4},{6,7},{7,6},{8,9},{9,8},{10,11... | collective-permute-start | bytes 1572872 | tf_op jit(solution)/shard_map/ppermute | solution.py:17
  44.2 13.8 %copy-start.13 = (bf16[128,2048]{1,0:T(8,128)(2,1)}, bf16[128,2048]{1,0:T(8,128)(2,1)S(1)}, u32[]{:S(2)}) copy-start(bf16[128,2048]{1,0:T(8,128)(2,1)S(1)} %collective-permute-done.6.refs_1_) | copy-start | bytes 1572868
  44.2 13.8 %collective-permute-start.8 = (bf16[128,2048]{1,0:T(8,128)(2,1)S(1)}, bf16[128,2048]{1,0:T(8,128)(2,1)}, u32[]{:S(2)}, u32[]{:S(2)}) collective-permute-start(bf16[128,2048]{1,0:T(8,128)(2,1)S(1)} %collective-permute-done.6.refs_1_), channel_id=1, source_target_pairs={{0,1},{1,0},{2,3},{3,2},{4,5},{5,4},{6,7},{7,6},{8,9},{9,8},{10,11... | collective-permute-start | bytes 1572872 | tf_op jit(solution)/shard_map/ppermute | solution.py:17
  53.7 4.3 %copy-start.14 = (bf16[128,2048]{1,0:T(8,128)(2,1)}, bf16[128,2048]{1,0:T(8,128)(2,1)S(1)}, u32[]{:S(2)}) copy-start(bf16[128,2048]{1,0:T(8,128)(2,1)S(1)} %collective-permute-done.9.refs_5_) | copy-start | bytes 1572868
  53.7 4.3 %collective-permute-start.11 = (bf16[128,2048]{1,0:T(8,128)(2,1)S(1)}, bf16[128,2048]{1,0:T(8,128)(2,1)}, u32[]{:S(2)}, u32[]{:S(2)}) collective-permute-start(bf16[128,2048]{1,0:T(8,128)(2,1)S(1)} %collective-permute-done.9.refs_5_), channel_id=1, source_target_pairs={{0,1},{1,0},{2,3},{3,2},{4,5},{5,4},{6,7},{7,6},{8,9},{9,8},{10,11... | collective-permute-start | bytes 1572872 | tf_op jit(solution)/shard_map/ppermute | solution.py:17
  53.7 29.8 %copy-start.7 = (bf16[128,2048]{1,0:T(8,128)(2,1)}, bf16[128,2048]{1,0:T(8,128)(2,1)S(1)}, u32[]{:S(2)}) copy-start(bf16[128,2048]{1,0:T(8,128)(2,1)S(1)} %collective-permute-done.4.refs_0_) | copy-start | bytes 1572868
  53.8 14.4 %collective-permute-start.5 = (bf16[128,2048]{1,0:T(8,128)(2,1)S(1)}, bf16[128,2048]{1,0:T(8,128)(2,1)}, u32[]{:S(2)}, u32[]{:S(2)}) collective-permute-start(bf16[128,2048]{1,0:T(8,128)(2,1)S(1)} %collective-permute-done.4.refs_0_), channel_id=1, source_target_pairs={{0,2},{1,3},{2,0},{3,1},{4,6},{5,7},{6,4},{7,5},{8,10},{9,11},{10,... | collective-permute-start | bytes 1572872 | tf_op jit(solution)/shard_map/ppermute | solution.py:17
  55.2 0.8 copy-start.15
  56.0 26.2 %collective-permute-start.2 = (bf16[128,2048]{1,0:T(8,128)(2,1)}, bf16[128,2048]{1,0:T(8,128)(2,1)S(1)}, u32[]{:S(2)}, u32[]{:S(2)}) collective-permute-start(bf16[128,2048]{1,0:T(8,128)(2,1)} %get-tuple-element.17), channel_id=1, source_target_pairs={{0,8},{4,12},{8,0},{12,4},{1,9},{5,13},{9,1},{13,5},{2,10},{6,14},... | collective-permute-start | bytes 1572872 | tf_op jit(solution)/shard_map/ppermute | solution.py:17
  64.7 34.9 %copy-start = (f32[16,8,2048]{2,1,0:T(8,128)S(1)}, f32[16,8,2048]{2,1,0:T(8,128)}, u32[]{:S(2)}) copy-start(f32[16,8,2048]{2,1,0:T(8,128)} %refs_6_.1) | copy-start | bytes 3145732
  64.7 34.9 %copy-start.1 = (f32[16,8,2048]{2,1,0:T(8,128)S(1)}, f32[16,8,2048]{2,1,0:T(8,128)}, u32[]{:S(2)}) copy-start(f32[16,8,2048]{2,1,0:T(8,128)} %refs_7_.1) | copy-start | bytes 3145732
  64.7 34.9 %copy-start.2 = (f32[8,2048]{1,0:T(8,128)S(1)}, f32[8,2048]{1,0:T(8,128)}, u32[]{:S(2)}) copy-start(f32[8,2048]{1,0:T(8,128)} %refs_8_.3) | copy-start | bytes 196612
  64.7 34.9 %copy-start.3 = (f32[8,2048]{1,0:T(8,128)S(1)}, f32[8,2048]{1,0:T(8,128)}, u32[]{:S(2)}) copy-start(f32[8,2048]{1,0:T(8,128)} %refs_9_.1) | copy-start | bytes 196612
  64.7 34.9 %copy-start.4 = (f32[2048]{0:T(1024)S(1)}, f32[2048]{0:T(1024)}, u32[]{:S(2)}) copy-start(f32[2048]{0:T(1024)} %param.16) | copy-start | bytes 24580
  64.7 34.9 %copy-start.5 = (f32[2048]{0:T(1024)S(1)}, f32[2048]{0:T(1024)}, u32[]{:S(2)}) copy-start(f32[2048]{0:T(1024)} %param.17) | copy-start | bytes 24580
  64.7 34.9 %copy-start.6 = (f32[2048]{0:T(1024)S(1)}, f32[2048]{0:T(1024)}, u32[]{:S(2)}) copy-start(f32[2048]{0:T(1024)} %param.18) | copy-start | bytes 24580
  68.2 14.5 %collective-permute-start.12 = (bf16[128,2048]{1,0:T(8,128)(2,1)S(1)}, bf16[128,2048]{1,0:T(8,128)(2,1)S(1)}, u32[]{:S(2)}, u32[]{:S(2)}) collective-permute-start(bf16[128,2048]{1,0:T(8,128)(2,1)S(1)} %collective-permute-done.4.refs_0_), channel_id=1, source_target_pairs={{0,1},{1,0},{2,3},{3,2},{4,5},{5,4},{6,7},{7,6},{8,9},{9,8},{10,11... | collective-permute-start | bytes 1572872 | tf_op jit(solution)/shard_map/ppermute | solution.py:17
  68.2 15.3 %collective-permute-start.13 = (bf16[128,2048]{1,0:T(8,128)(2,1)}, bf16[128,2048]{1,0:T(8,128)(2,1)}, u32[]{:S(2)}, u32[]{:S(2)}) collective-permute-start(bf16[128,2048]{1,0:T(8,128)(2,1)} %collective-permute-done.5.refs_1_), channel_id=1, source_target_pairs={{0,1},{1,0},{2,3},{3,2},{4,5},{5,4},{6,7},{7,6},{8,9},{9,8},{10,11... | collective-permute-start | bytes 1572872 | tf_op jit(solution)/shard_map/ppermute | solution.py:17
  82.1 17.0 %copy-start.8 = (bf16[128,2048]{1,0:T(8,128)(2,1)}, bf16[128,2048]{1,0:T(8,128)(2,1)S(1)}, u32[]{:S(2)}) copy-start(bf16[128,2048]{1,0:T(8,128)(2,1)S(1)} %collective-permute-done.2.refs_0_) | copy-start | bytes 1572868
  82.1 14.0 %collective-permute-start.3 = (bf16[128,2048]{1,0:T(8,128)(2,1)S(1)}, bf16[128,2048]{1,0:T(8,128)(2,1)}, u32[]{:S(2)}, u32[]{:S(2)}) collective-permute-start(bf16[128,2048]{1,0:T(8,128)(2,1)S(1)} %collective-permute-done.2.refs_0_), channel_id=1, source_target_pairs={{0,2},{1,3},{2,0},{3,1},{4,6},{5,7},{6,4},{7,5},{8,10},{9,11},{10,... | collective-permute-start | bytes 1572872 | tf_op jit(solution)/shard_map/ppermute | solution.py:17
  82.7 0.8 copy-start.9
  96.1 2.6 %collective-permute-start.14 = (bf16[128,2048]{1,0:T(8,128)(2,1)S(1)}, bf16[128,2048]{1,0:T(8,128)(2,1)S(1)}, u32[]{:S(2)}, u32[]{:S(2)}) collective-permute-start(bf16[128,2048]{1,0:T(8,128)(2,1)S(1)} %collective-permute-done.2.refs_0_), channel_id=1, source_target_pairs={{0,1},{1,0},{2,3},{3,2},{4,5},{5,4},{6,7},{7,6},{8,9},{9,8},{10,11... | collective-permute-start | bytes 1572872 | tf_op jit(solution)/shard_map/ppermute | solution.py:17
  96.1 3.0 %collective-permute-start.15 = (bf16[128,2048]{1,0:T(8,128)(2,1)}, bf16[128,2048]{1,0:T(8,128)(2,1)}, u32[]{:S(2)}, u32[]{:S(2)}) collective-permute-start(bf16[128,2048]{1,0:T(8,128)(2,1)} %collective-permute-done.3.refs_1_), channel_id=1, source_target_pairs={{0,1},{1,0},{2,3},{3,2},{4,5},{5,4},{6,7},{7,6},{8,9},{9,8},{10,11... | collective-permute-start | bytes 1572872 | tf_op jit(solution)/shard_map/ppermute | solution.py:17
  98.7 0.8 copy-start.10

commit v13 on v11

--- a/solution.py
+++ b/solution.py
@@ -39,14 +39,24 @@
     )(delays, window)
 
 
-def gather_neuron(piece, gate=None):
+def gather_neuron(held, gate=None, skip=0):
     bits = lax.axis_size("neuron").bit_length() - 1
-    held = [piece]
-    for bit in reversed(range(bits)):
+    held = list(held)
+    for bit in list(reversed(range(bits)))[skip:]:
         if bit == 0 and gate is not None:
             held, _ = lax.optimization_barrier((held, gate))
         held = held + [swap(chunk, "neuron", 1 << bit) for chunk in held]
     return held
+
+
+def swap_diagonal(value, mask, high):
+    n_area, n_neuron = lax.axis_size("area"), lax.axis_size("neuron")
+    pairs = [
+        (a * n_neuron + n, (a ^ mask) * n_neuron + (n ^ high))
+        for a in range(n_area)
+        for n in range(n_neuron)
+    ]
+    return lax.ppermute(value, ("area", "neuron"), pairs)
 
 
 def stage_kernel(bi_ref, *refs, n_pieces, stage, n_pos, final, has_rec):
@@ -202,20 +212,26 @@
     nbits = lax.axis_size("neuron").bit_length() - 1
     n_pos = 1 << nbits
     stages = [list(range(f, min(f + 2, rounds))) for f in range(0, rounds, 2)]
-    arrived = []
+    high = (1 << (nbits - 1)) if nbits > 0 else 0
+    arrived = {}
     gate = None
-    for stage in stages:
+    for si, stage in enumerate(stages):
         pieces = send_slices(window, delays, stage, levels, steps)
         if gate is not None:
             pieces, _ = lax.optimization_barrier((pieces, gate))
-        got = [swap(piece, "area", 1 << (rnd % levels)) for piece, rnd in zip(pieces, stage)]
-        arrived += got
+        diagonal = si == len(stages) - 1 and si > 0 and high > 0
+        got = []
+        for piece, rnd in zip(pieces, stage):
+            mask = 1 << (rnd % levels)
+            straight = swap(piece, "area", mask)
+            arrived[rnd] = [straight, swap_diagonal(piece, mask, high)] if diagonal else [straight]
+            got.append(straight)
         gate = got
     rec = None
     for si, stage in enumerate(stages):
         chunks = []
         for rnd in stage:
-            chunks += gather_neuron(arrived[rnd], rec)
+            chunks += gather_neuron(arrived[rnd], rec, len(arrived[rnd]) - 1)
         scan_args = None
         if si == len(stages) - 1:
             scan_args = (err_grad, surrogate, lv_end, la_end, alpha, rho, beta)

time: 92.5 us -> 117 us (1.26)
  waiting for transfers between devices: 54.4 us -> 78 us
    ppermute x0 -> x2, waiting for transfers between devices: none -> 22 us  [swap_diagonal(): return lax.ppermute(value, ('area', 'neuron'), pairs)]
    ppermute x16 -> x14, waiting for transfers between devices: 54.4 us -> 56 us  [swap(): return lax.ppermute(value, axis, pairs)]
    ppermute x0 -> x2, starting transfers between devices: none -> 1.43 us  [swap_diagonal(): return lax.ppermute(value, ('area', 'neuron'), pairs)]
    ppermute x16 -> x14, starting transfers between devices: 16 us -> 14.7 us  [swap(): return lax.ppermute(value, axis, pairs)]
  transfers between devices with their start and end apart: 16 -> 16, of which waited for: 10 -> 9; matrix products, arithmetic and copies ran while one was open for 2% -> 1% of each run, Pallas kernels for 10% -> 8%
where the time goes in v13:
time: 117 us
  waiting for transfers between devices  78 us (67%)
  Pallas kernels  18.7 us (16%)
  starting transfers between devices  16.2 us (14%)
  local copies, waits for them, and re-layouts  3.12 us (3%)
    ppermute x14, waiting for transfers between devices, swap(): return lax.ppermute(value, axis, pairs)  56 us
    ppermute x2, waiting for transfers between devices, swap_diagonal(): return lax.ppermute(value, ('area', 'neuron'), pairs)  22 us
    ppermute x14, starting transfers between devices, swap(): return lax.ppermute(value, axis, pairs)  14.7 us
    pallas_call x2, Pallas kernels, stage_contrib(): pl.pallas_call(kernel, in_specs=[SMEM] + specs, out_specs=out_specs, scra...  13.6 us
    pallas_call x2, Pallas kernels, send_slices(): pl.pallas_call(kernel, in_specs=[SMEM, VMEM], out_specs=[VMEM] * len(roun...  5.09 us
    unnamed x29, local copies, waits for them, and re-layouts  3.12 us
  transfers between devices with their start and end apart: 16, of which 9 were waited for; matrix products, arithmetic and copies ran while one was open for 1% of the time, Pallas kernels for 8%

profile of v13, /device:TPU:0, one launch (start us, length us, event | category | flops | bytes accessed | tf_op | source)
XLA Modules:
  0.0 116.7 jit_solution(7457724959257551350)
XLA Ops:
  0.6 0.0 copy-start.6
  0.6 0.0 copy-start.5
  0.7 0.0 copy-start.4
  0.7 0.0 copy-start.3
  0.7 0.0 copy-start.2
  0.7 0.0 copy-start.1
  0.7 0.0 copy-start
  0.7 2.6 %shard_map.131 = (bf16[128,2048]{1,0:T(8,128)(2,1)}, bf16[128,2048]{1,0:T(8,128)(2,1)}) custom-call(s32[4,4]{1,0:T(4,128)} %delays_ref.3, bf16[32,8,2048]{2,1,0:T(8,128)(2,1)} %window_ref.3), custom_call_target="tpu_custom_call" | custom-call | tf_op jit(solution)/shard_map/pallas_call | solution.py:34
  3.3 3.0 %collective-permute-start = (bf16[128,2048]{1,0:T(8,128)(2,1)}, bf16[128,2048]{1,0:T(8,128)(2,1)S(1)}, u32[]{:S(2)}, u32[]{:S(2)}) collective-permute-start(bf16[128,2048]{1,0:T(8,128)(2,1)} %get-tuple-element.15), channel_id=1, source_target_pairs={{0,4},{4,0},{8,12},{12,8},{1,5},{5,1},{9,13},{13,9},{2,6},{6,2},{1... | collective-permute-start | bytes 1572872 | tf_op jit(solution)/shard_map/ppermute | solution.py:17
  6.3 2.6 %collective-permute-start.1 = (bf16[128,2048]{1,0:T(8,128)(2,1)}, bf16[128,2048]{1,0:T(8,128)(2,1)}, u32[]{:S(2)}, u32[]{:S(2)}) collective-permute-start(bf16[128,2048]{1,0:T(8,128)(2,1)} %get-tuple-element.16), channel_id=1, source_target_pairs={{0,8},{4,12},{8,0},{12,4},{1,9},{5,13},{9,1},{13,5},{2,10},{6,14},... | collective-permute-start | bytes 1572872 | tf_op jit(solution)/shard_map/ppermute | solution.py:17
  8.9 20.7 %collective-permute-done.refs_0_ = bf16[128,2048]{1,0:T(8,128)(2,1)S(1)} collective-permute-done((bf16[128,2048]{1,0:T(8,128)(2,1)}, bf16[128,2048]{1,0:T(8,128)(2,1)S(1)}, u32[]{:S(2)}, u32[]{:S(2)}) %collective-permute-start) | collective-permute-done | bytes 524320 | tf_op jit(solution)/shard_map/ppermute | solution.py:17
  29.6 0.0 copy-start.13
  29.6 1.7 %collective-permute-start.4 = (bf16[128,2048]{1,0:T(8,128)(2,1)S(1)}, bf16[128,2048]{1,0:T(8,128)(2,1)}, u32[]{:S(2)}, u32[]{:S(2)}) collective-permute-start(bf16[128,2048]{1,0:T(8,128)(2,1)S(1)} %collective-permute-done.refs_0_), channel_id=1, source_target_pairs={{0,2},{1,3},{2,0},{3,1},{4,6},{5,7},{6,4},{7,5},{8,10},{9,11},{10,... | collective-permute-start | bytes 1572872 | tf_op jit(solution)/shard_map/ppermute | solution.py:17
  31.3 1.0 collective-permute-done.1.refs_4_
  32.2 1.5 %collective-permute-start.7 = (bf16[128,2048]{1,0:T(8,128)(2,1)}, bf16[128,2048]{1,0:T(8,128)(2,1)}, u32[]{:S(2)}, u32[]{:S(2)}) collective-permute-start(bf16[128,2048]{1,0:T(8,128)(2,1)} %collective-permute-done.1.refs_4_), channel_id=1, source_target_pairs={{0,2},{1,3},{2,0},{3,1},{4,6},{5,7},{6,4},{7,5},{8,10},{9,11},{10,... | collective-permute-start | bytes 1572872 | tf_op jit(solution)/shard_map/ppermute | solution.py:17
  33.7 0.0 collective-permute-start.5
  33.7 0.5 collective-permute-start.8
  34.2 10.3 %collective-permute-done.4.refs_1_ = bf16[128,2048]{1,0:T(8,128)(2,1)} collective-permute-done((bf16[128,2048]{1,0:T(8,128)(2,1)S(1)}, bf16[128,2048]{1,0:T(8,128)(2,1)}, u32[]{:S(2)}, u32[]{:S(2)}) %collective-permute-start.4) | collective-permute-done | bytes 524320 | tf_op jit(solution)/shard_map/ppermute | solution.py:17
  44.6 0.0 collective-permute-start.6
  44.6 2.5 %shard_map.130 = (bf16[128,2048]{1,0:T(8,128)(2,1)}, bf16[128,2048]{1,0:T(8,128)(2,1)}) custom-call(s32[4,4]{1,0:T(4,128)} %delays_ref.3, bf16[32,8,2048]{2,1,0:T(8,128)(2,1)} %window_ref.3), custom_call_target="tpu_custom_call" | custom-call | tf_op jit(solution)/shard_map/pallas_call | solution.py:34
  47.0 7.1 %collective-permute-done.7.refs_5_ = bf16[128,2048]{1,0:T(8,128)(2,1)} collective-permute-done((bf16[128,2048]{1,0:T(8,128)(2,1)}, bf16[128,2048]{1,0:T(8,128)(2,1)}, u32[]{:S(2)}, u32[]{:S(2)}) %collective-permute-start.7) | collective-permute-done | bytes 524320 | tf_op jit(solution)/shard_map/ppermute | solution.py:17
  54.2 0.0 collective-permute-start.9
  54.2 0.3 collective-permute-start.3
  54.5 0.0 copy-done.13
  54.5 0.0 collective-permute-done.5.refs_2_
  54.5 2.5 %collective-permute-start.2 = (bf16[128,2048]{1,0:T(8,128)(2,1)}, bf16[128,2048]{1,0:T(8,128)(2,1)S(1)}, u32[]{:S(2)}, u32[]{:S(2)}) collective-permute-start(bf16[128,2048]{1,0:T(8,128)(2,1)} %get-tuple-element.17), channel_id=1, source_target_pairs={{0,4},{4,0},{8,12},{12,8},{1,5},{5,1},{9,13},{13,9},{2,6},{6,2},{1... | collective-permute-start | bytes 1572872 | tf_op jit(solution)/shard_map/ppermute | solution.py:17
  57.0 0.0 collective-permute-done.8.refs_6_
  57.0 1.1 collective-permute-start.13
  58.1 0.0 collective-permute-done.6.refs_3_
  58.1 1.9 %collective-permute-start.12 = (bf16[128,2048]{1,0:T(8,128)(2,1)}, bf16[128,2048]{1,0:T(8,128)(2,1)}, u32[]{:S(2)}, u32[]{:S(2)}) collective-permute-start(bf16[128,2048]{1,0:T(8,128)(2,1)} %get-tuple-element.20), channel_id=1, source_target_pairs={{0,8},{4,12},{8,0},{12,4},{1,9},{5,13},{9,1},{13,5},{2,10},{6,14},... | collective-permute-start | bytes 1572872 | tf_op jit(solution)/shard_map/ppermute | solution.py:17
  60.0 1.4 %copy.15.bi_ref = s32[4,1,16,4]{3,2,1,0:T(8,128)} copy(s32[4,1,16,4]{2,3,1,0:T(4,128)} %param.20) | data formatting | bytes 2048 | tf_op args[9]
  61.4 0.0 collective-permute-done.9.refs_7_
  61.4 6.6 %shard_map.132.refs_9_ = f32[16,8,2048]{2,1,0:T(8,128)} custom-call(s32[4,1,16,4]{3,2,1,0:T(8,128)} %copy.15.bi_ref, bf16[128,2048]{1,0:T(8,128)(2,1)} %copy-done.13, bf16[128,2048]{1,0:T(8,128)(2,1)} %collective-permute-done.4.refs_1_, bf16[128,2048]{1,0:T(8,128)(2,1)} %collective-permute-done.5.refs_2_, bf16[128,2048]{1,0:T(8,128)(2,1)} %collective-permute-done.6.refs_3_, ...), custom_call_target="tpu_custom_call" | custom-call | tf_op jit(solution)/shard_map/pallas_call | solution.py:194
  68.0 22.0 %collective-permute-done.3.refs_1_ = bf16[128,2048]{1,0:T(8,128)(2,1)S(1)} collective-permute-done((bf16[128,2048]{1,0:T(8,128)(2,1)}, bf16[128,2048]{1,0:T(8,128)(2,1)S(1)}, u32[]{:S(2)}, u32[]{:S(2)}) %collective-permute-start.3) | collective-permute-done | bytes 524320 | tf_op jit(solution)/shard_map/ppermute | solution.py:59
  90.0 0.0 copy-start.7
  90.0 10.8 %collective-permute-done.2.refs_0_ = bf16[128,2048]{1,0:T(8,128)(2,1)S(1)} collective-permute-done((bf16[128,2048]{1,0:T(8,128)(2,1)}, bf16[128,2048]{1,0:T(8,128)(2,1)S(1)}, u32[]{:S(2)}, u32[]{:S(2)}) %collective-permute-start.2) | collective-permute-done | bytes 524320 | tf_op jit(solution)/shard_map/ppermute | solution.py:17
  100.8 0.0 copy-start.8
  100.8 0.0 collective-permute-start.10
  100.8 0.5 collective-permute-start.11
  101.3 0.0 collective-permute-done.13.refs_5_
  101.3 4.6 %collective-permute-done.12.refs_4_ = bf16[128,2048]{1,0:T(8,128)(2,1)} collective-permute-done((bf16[128,2048]{1,0:T(8,128)(2,1)}, bf16[128,2048]{1,0:T(8,128)(2,1)}, u32[]{:S(2)}, u32[]{:S(2)}) %collective-permute-start.12) | collective-permute-done | bytes 524320 | tf_op jit(solution)/shard_map/ppermute | solution.py:17
  105.8 0.0 collective-permute-start.14
  105.8 0.5 collective-permute-start.15
  106.3 0.0 collective-permute-done.10.refs_2_
  106.4 0.0 copy-start.9
  106.4 0.0 collective-permute-done.11.refs_3_
  106.4 0.8 copy-done.9
  107.2 0.0 copy-start.10
  107.2 0.8 collective-permute-done.14.refs_6_
  108.0 0.0 copy-done.10
  108.0 0.0 copy-start.11
  108.0 0.7 collective-permute-done.15.refs_7_
  108.7 0.1 copy-done.11
  108.8 0.8 copy-done.12
  109.6 0.0 copy-done.7
  109.6 0.0 copy-done.8
  109.6 0.0 copy-done.6
  109.6 0.0 copy-done.5
  109.6 0.0 copy-done.4
  109.6 0.0 copy-done.3
  109.6 0.0 copy-done.2
  109.6 0.0 copy-done.1
  109.6 0.0 copy-done
  109.7 7.0 %shard_map.133 = (bf16[16,8,2048]{2,1,0:T(8,128)(2,1)}, f32[8,2048]{1,0:T(8,128)}, f32[8,2048]{1,0:T(8,128)}) custom-call(s32[4,1,16,4]{3,2,1,0:T(8,128)} %copy.15.bi_ref, bf16[128,2048]{1,0:T(8,128)(2,1)} %copy-done.8, bf16[128,2048]{1,0:T(8,128)(2,1)} %copy-done.7, bf16[128,2048]{1,0:T(8,128)(2,1)} %copy-done.9, bf16[128,2048]{1,0:T(8,128)(2,1)} %copy-done.10, ...), custom_call_target="tpu_custom_call" | custom-call | tf_op jit(solution)/shard_map/pallas_call | solution.py:194
  (1 shorter events, 0.0 us)
Async XLA Ops:
  0.6 109.0 %copy-start.6 = (f32[2048]{0:T(1024)S(1)}, f32[2048]{0:T(1024)}, u32[]{:S(2)}) copy-start(f32[2048]{0:T(1024)} %param.18) | copy-start | bytes 24580
  0.6 109.0 %copy-start.5 = (f32[2048]{0:T(1024)S(1)}, f32[2048]{0:T(1024)}, u32[]{:S(2)}) copy-start(f32[2048]{0:T(1024)} %param.17) | copy-start | bytes 24580
  0.7 108.9 %copy-start.4 = (f32[2048]{0:T(1024)S(1)}, f32[2048]{0:T(1024)}, u32[]{:S(2)}) copy-start(f32[2048]{0:T(1024)} %param.16) | copy-start | bytes 24580
  0.7 108.9 %copy-start.3 = (f32[8,2048]{1,0:T(8,128)S(1)}, f32[8,2048]{1,0:T(8,128)}, u32[]{:S(2)}) copy-start(f32[8,2048]{1,0:T(8,128)} %refs_13_.1) | copy-start | bytes 196612
  0.7 108.9 %copy-start.2 = (f32[8,2048]{1,0:T(8,128)S(1)}, f32[8,2048]{1,0:T(8,128)}, u32[]{:S(2)}) copy-start(f32[8,2048]{1,0:T(8,128)} %refs_12_.1) | copy-start | bytes 196612
  0.7 108.9 %copy-start.1 = (f32[16,8,2048]{2,1,0:T(8,128)S(1)}, f32[16,8,2048]{2,1,0:T(8,128)}, u32[]{:S(2)}) copy-start(f32[16,8,2048]{2,1,0:T(8,128)} %refs_11_.1) | copy-start | bytes 3145732
  0.7 108.9 %copy-start = (f32[16,8,2048]{2,1,0:T(8,128)S(1)}, f32[16,8,2048]{2,1,0:T(8,128)}, u32[]{:S(2)}) copy-start(f32[16,8,2048]{2,1,0:T(8,128)} %refs_10_.1) | copy-start | bytes 3145732
  3.3 26.3 %collective-permute-start = (bf16[128,2048]{1,0:T(8,128)(2,1)}, bf16[128,2048]{1,0:T(8,128)(2,1)S(1)}, u32[]{:S(2)}, u32[]{:S(2)}) collective-permute-start(bf16[128,2048]{1,0:T(8,128)(2,1)} %get-tuple-element.15), channel_id=1, source_target_pairs={{0,4},{4,0},{8,12},{12,8},{1,5},{5,1},{9,13},{13,9},{2,6},{6,2},{1... | collective-permute-start | bytes 1572872 | tf_op jit(solution)/shard_map/ppermute | solution.py:17
  6.3 25.9 %collective-permute-start.1 = (bf16[128,2048]{1,0:T(8,128)(2,1)}, bf16[128,2048]{1,0:T(8,128)(2,1)}, u32[]{:S(2)}, u32[]{:S(2)}) collective-permute-start(bf16[128,2048]{1,0:T(8,128)(2,1)} %get-tuple-element.16), channel_id=1, source_target_pairs={{0,8},{4,12},{8,0},{12,4},{1,9},{5,13},{9,1},{13,5},{2,10},{6,14},... | collective-permute-start | bytes 1572872 | tf_op jit(solution)/shard_map/ppermute | solution.py:17
  29.6 24.9 %copy-start.13 = (bf16[128,2048]{1,0:T(8,128)(2,1)}, bf16[128,2048]{1,0:T(8,128)(2,1)S(1)}, u32[]{:S(2)}) copy-start(bf16[128,2048]{1,0:T(8,128)(2,1)S(1)} %collective-permute-done.refs_0_) | copy-start | bytes 1572868
  29.6 15.0 %collective-permute-start.4 = (bf16[128,2048]{1,0:T(8,128)(2,1)S(1)}, bf16[128,2048]{1,0:T(8,128)(2,1)}, u32[]{:S(2)}, u32[]{:S(2)}) collective-permute-start(bf16[128,2048]{1,0:T(8,128)(2,1)S(1)} %collective-permute-done.refs_0_), channel_id=1, source_target_pairs={{0,2},{1,3},{2,0},{3,1},{4,6},{5,7},{6,4},{7,5},{8,10},{9,11},{10,... | collective-permute-start | bytes 1572872 | tf_op jit(solution)/shard_map/ppermute | solution.py:17
  32.2 21.9 %collective-permute-start.7 = (bf16[128,2048]{1,0:T(8,128)(2,1)}, bf16[128,2048]{1,0:T(8,128)(2,1)}, u32[]{:S(2)}, u32[]{:S(2)}) collective-permute-start(bf16[128,2048]{1,0:T(8,128)(2,1)} %collective-permute-done.1.refs_4_), channel_id=1, source_target_pairs={{0,2},{1,3},{2,0},{3,1},{4,6},{5,7},{6,4},{7,5},{8,10},{9,11},{10,... | collective-permute-start | bytes 1572872 | tf_op jit(solution)/shard_map/ppermute | solution.py:17
  33.7 20.8 %collective-permute-start.5 = (bf16[128,2048]{1,0:T(8,128)(2,1)S(1)}, bf16[128,2048]{1,0:T(8,128)(2,1)}, u32[]{:S(2)}, u32[]{:S(2)}) collective-permute-start(bf16[128,2048]{1,0:T(8,128)(2,1)S(1)} %collective-permute-done.refs_0_), channel_id=1, source_target_pairs={{0,1},{1,0},{2,3},{3,2},{4,5},{5,4},{6,7},{7,6},{8,9},{9,8},{10,11... | collective-permute-start | bytes 1572872 | tf_op jit(solution)/shard_map/ppermute | solution.py:17
  33.7 23.2 %collective-permute-start.8 = (bf16[128,2048]{1,0:T(8,128)(2,1)}, bf16[128,2048]{1,0:T(8,128)(2,1)}, u32[]{:S(2)}, u32[]{:S(2)}) collective-permute-start(bf16[128,2048]{1,0:T(8,128)(2,1)} %collective-permute-done.1.refs_4_), channel_id=1, source_target_pairs={{0,1},{1,0},{2,3},{3,2},{4,5},{5,4},{6,7},{7,6},{8,9},{9,8},{10,11... | collective-permute-start | bytes 1572872 | tf_op jit(solution)/shard_map/ppermute | solution.py:17
  44.6 13.5 %collective-permute-start.6 = (bf16[128,2048]{1,0:T(8,128)(2,1)}, bf16[128,2048]{1,0:T(8,128)(2,1)}, u32[]{:S(2)}, u32[]{:S(2)}) collective-permute-start(bf16[128,2048]{1,0:T(8,128)(2,1)} %collective-permute-done.4.refs_1_), channel_id=1, source_target_pairs={{0,1},{1,0},{2,3},{3,2},{4,5},{5,4},{6,7},{7,6},{8,9},{9,8},{10,11... | collective-permute-start | bytes 1572872 | tf_op jit(solution)/shard_map/ppermute | solution.py:17
  54.2 7.3 %collective-permute-start.9 = (bf16[128,2048]{1,0:T(8,128)(2,1)}, bf16[128,2048]{1,0:T(8,128)(2,1)}, u32[]{:S(2)}, u32[]{:S(2)}) collective-permute-start(bf16[128,2048]{1,0:T(8,128)(2,1)} %collective-permute-done.7.refs_5_), channel_id=1, source_target_pairs={{0,1},{1,0},{2,3},{3,2},{4,5},{5,4},{6,7},{7,6},{8,9},{9,8},{10,11... | collective-permute-start | bytes 1572872 | tf_op jit(solution)/shard_map/ppermute | solution.py:17
  54.2 35.8 %collective-permute-start.3 = (bf16[128,2048]{1,0:T(8,128)(2,1)}, bf16[128,2048]{1,0:T(8,128)(2,1)S(1)}, u32[]{:S(2)}, u32[]{:S(2)}) collective-permute-start(bf16[128,2048]{1,0:T(8,128)(2,1)} %get-tuple-element.17), channel_id=1, source_target_pairs={{0,6},{1,7},{2,4},{3,5},{4,2},{5,3},{6,0},{7,1},{8,14},{9,15},{10,... | collective-permute-start | bytes 1572872 | tf_op jit(solution)/shard_map/ppermute | solution.py:59
  54.5 46.3 %collective-permute-start.2 = (bf16[128,2048]{1,0:T(8,128)(2,1)}, bf16[128,2048]{1,0:T(8,128)(2,1)S(1)}, u32[]{:S(2)}, u32[]{:S(2)}) collective-permute-start(bf16[128,2048]{1,0:T(8,128)(2,1)} %get-tuple-element.17), channel_id=1, source_target_pairs={{0,4},{4,0},{8,12},{12,8},{1,5},{5,1},{9,13},{13,9},{2,6},{6,2},{1... | collective-permute-start | bytes 1572872 | tf_op jit(solution)/shard_map/ppermute | solution.py:17
  57.0 44.3 %collective-permute-start.13 = (bf16[128,2048]{1,0:T(8,128)(2,1)}, bf16[128,2048]{1,0:T(8,128)(2,1)}, u32[]{:S(2)}, u32[]{:S(2)}) collective-permute-start(bf16[128,2048]{1,0:T(8,128)(2,1)} %get-tuple-element.20), channel_id=1, source_target_pairs={{0,10},{1,11},{2,8},{3,9},{4,14},{5,15},{6,12},{7,13},{8,2},{9,3},... | collective-permute-start | bytes 1572872 | tf_op jit(solution)/shard_map/ppermute | solution.py:59
  58.1 47.8 %collective-permute-start.12 = (bf16[128,2048]{1,0:T(8,128)(2,1)}, bf16[128,2048]{1,0:T(8,128)(2,1)}, u32[]{:S(2)}, u32[]{:S(2)}) collective-permute-start(bf16[128,2048]{1,0:T(8,128)(2,1)} %get-tuple-element.20), channel_id=1, source_target_pairs={{0,8},{4,12},{8,0},{12,4},{1,9},{5,13},{9,1},{13,5},{2,10},{6,14},... | collective-permute-start | bytes 1572872 | tf_op jit(solution)/shard_map/ppermute | solution.py:17
  90.0 19.6 %copy-start.7 = (bf16[128,2048]{1,0:T(8,128)(2,1)}, bf16[128,2048]{1,0:T(8,128)(2,1)S(1)}, u32[]{:S(2)}) copy-start(bf16[128,2048]{1,0:T(8,128)(2,1)S(1)} %collective-permute-done.3.refs_1_) | copy-start | bytes 1572868
  100.8 8.8 %copy-start.8 = (bf16[128,2048]{1,0:T(8,128)(2,1)}, bf16[128,2048]{1,0:T(8,128)(2,1)S(1)}, u32[]{:S(2)}) copy-start(bf16[128,2048]{1,0:T(8,128)(2,1)S(1)} %collective-permute-done.2.refs_0_) | copy-start | bytes 1572868
  100.8 5.6 %collective-permute-start.10 = (bf16[128,2048]{1,0:T(8,128)(2,1)S(1)}, bf16[128,2048]{1,0:T(8,128)(2,1)S(1)}, u32[]{:S(2)}, u32[]{:S(2)}) collective-permute-start(bf16[128,2048]{1,0:T(8,128)(2,1)S(1)} %collective-permute-done.2.refs_0_), channel_id=1, source_target_pairs={{0,1},{1,0},{2,3},{3,2},{4,5},{5,4},{6,7},{7,6},{8,9},{9,8},{10,11... | collective-permute-start | bytes 1572872 | tf_op jit(solution)/shard_map/ppermute | solution.py:17
  100.8 5.6 %collective-permute-start.11 = (bf16[128,2048]{1,0:T(8,128)(2,1)S(1)}, bf16[128,2048]{1,0:T(8,128)(2,1)S(1)}, u32[]{:S(2)}, u32[]{:S(2)}) collective-permute-start(bf16[128,2048]{1,0:T(8,128)(2,1)S(1)} %collective-permute-done.3.refs_1_), channel_id=1, source_target_pairs={{0,1},{1,0},{2,3},{3,2},{4,5},{5,4},{6,7},{7,6},{8,9},{9,8},{10,11... | collective-permute-start | bytes 1572872 | tf_op jit(solution)/shard_map/ppermute | solution.py:17
  105.8 2.1 %collective-permute-start.14 = (bf16[128,2048]{1,0:T(8,128)(2,1)}, bf16[128,2048]{1,0:T(8,128)(2,1)S(1)}, u32[]{:S(2)}, u32[]{:S(2)}) collective-permute-start(bf16[128,2048]{1,0:T(8,128)(2,1)} %collective-permute-done.12.refs_4_), channel_id=1, source_target_pairs={{0,1},{1,0},{2,3},{3,2},{4,5},{5,4},{6,7},{7,6},{8,9},{9,8},{10,11... | collective-permute-start | bytes 1572872 | tf_op jit(solution)/shard_map/ppermute | solution.py:17
  105.8 2.9 %collective-permute-start.15 = (bf16[128,2048]{1,0:T(8,128)(2,1)}, bf16[128,2048]{1,0:T(8,128)(2,1)S(1)}, u32[]{:S(2)}, u32[]{:S(2)}) collective-permute-start(bf16[128,2048]{1,0:T(8,128)(2,1)} %collective-permute-done.13.refs_5_), channel_id=1, source_target_pairs={{0,1},{1,0},{2,3},{3,2},{4,5},{5,4},{6,7},{7,6},{8,9},{9,8},{10,11... | collective-permute-start | bytes 1572872 | tf_op jit(solution)/shard_map/ppermute | solution.py:17
  106.4 0.8 copy-start.9
  107.2 0.8 copy-start.10
  108.0 0.8 copy-start.11
  108.8 0.8 copy-start.12

commit v14 on v11

--- a/solution.py
+++ b/solution.py
@@ -202,14 +202,15 @@
     nbits = lax.axis_size("neuron").bit_length() - 1
     n_pos = 1 << nbits
     stages = [list(range(f, min(f + 2, rounds))) for f in range(0, rounds, 2)]
-    arrived = []
+    arrived = {}
     gate = None
     for stage in stages:
+        stage = sorted(stage, key=lambda rnd: -(rnd % levels))
         pieces = send_slices(window, delays, stage, levels, steps)
         if gate is not None:
             pieces, _ = lax.optimization_barrier((pieces, gate))
         got = [swap(piece, "area", 1 << (rnd % levels)) for piece, rnd in zip(pieces, stage)]
-        arrived += got
+        arrived.update(zip(stage, got))
         gate = got
     rec = None
     for si, stage in enumerate(stages):

time: 92.5 us -> 93.7 us (1.013)
  waiting for transfers between devices: 54.4 us -> 55.9 us
    ppermute x16, waiting for transfers between devices: 54.4 us -> 55.9 us  [swap(): return lax.ppermute(value, axis, pairs)]
  transfers between devices with their start and end apart: 16 -> 16, of which waited for: 10 -> 9; matrix products, arithmetic and copies ran while one was open for 2% -> 1% of each run, Pallas kernels for 10% -> 10%
where the time goes in v14:
time: 93.7 us; the launch traced here: 93.3 us
  waiting for transfers between devices  55.9 us (60%)
  Pallas kernels  18.7 us (20%)
  starting transfers between devices  15.7 us (17%)
  local copies, waits for them, and re-layouts  2.25 us (2%)
    ppermute x16, waiting for transfers between devices, swap(): return lax.ppermute(value, axis, pairs)  55.9 us
    ppermute x16, starting transfers between devices, swap(): return lax.ppermute(value, axis, pairs)  15.7 us
    pallas_call x2, Pallas kernels, stage_contrib(): pl.pallas_call(kernel, in_specs=[SMEM] + specs, out_specs=out_specs, scra...  13.6 us
    pallas_call x2, Pallas kernels, send_slices(): pl.pallas_call(kernel, in_specs=[SMEM, VMEM], out_specs=[VMEM] * len(roun...  5.12 us
    unnamed x29, local copies, waits for them, and re-layouts  2.25 us
  transfers between devices with their start and end apart: 16, of which 9 were waited for; matrix products, arithmetic and copies ran while one was open for 1% of the time, Pallas kernels for 10%

profile of v14, /device:TPU:0, one launch (start us, length us, event | category | flops | bytes accessed | tf_op | source)
XLA Modules:
  0.0 93.3 jit_solution(1996564629346091865)
XLA Ops:
  0.6 0.0 copy-start.6
  0.6 0.0 copy-start.5
  0.7 0.0 copy-start.4
  0.7 0.0 copy-start.3
  0.7 0.0 copy-start.2
  0.7 0.0 copy-start.1
  0.7 0.0 copy-start
  0.7 2.7 %shard_map.131 = (bf16[128,2048]{1,0:T(8,128)(2,1)}, bf16[128,2048]{1,0:T(8,128)(2,1)}) custom-call(s32[4,4]{1,0:T(4,128)} %delays_ref.3, bf16[32,8,2048]{2,1,0:T(8,128)(2,1)} %window_ref.3), custom_call_target="tpu_custom_call" | custom-call | tf_op jit(solution)/shard_map/pallas_call | solution.py:34
  3.4 4.0 %collective-permute-start = (bf16[128,2048]{1,0:T(8,128)(2,1)}, bf16[128,2048]{1,0:T(8,128)(2,1)}, u32[]{:S(2)}, u32[]{:S(2)}) collective-permute-start(bf16[128,2048]{1,0:T(8,128)(2,1)} %get-tuple-element.15), channel_id=1, source_target_pairs={{0,8},{4,12},{8,0},{12,4},{1,9},{5,13},{9,1},{13,5},{2,10},{6,14},... | collective-permute-start | bytes 1572872 | tf_op jit(solution)/shard_map/ppermute | solution.py:17
  7.4 1.6 %collective-permute-start.1 = (bf16[128,2048]{1,0:T(8,128)(2,1)}, bf16[128,2048]{1,0:T(8,128)(2,1)}, u32[]{:S(2)}, u32[]{:S(2)}) collective-permute-start(bf16[128,2048]{1,0:T(8,128)(2,1)} %get-tuple-element.16), channel_id=1, source_target_pairs={{0,4},{4,0},{8,12},{12,8},{1,5},{5,1},{9,13},{13,9},{2,6},{6,2},{1... | collective-permute-start | bytes 1572872 | tf_op jit(solution)/shard_map/ppermute | solution.py:17
  9.0 2.5 %shard_map.130 = (bf16[128,2048]{1,0:T(8,128)(2,1)}, bf16[128,2048]{1,0:T(8,128)(2,1)}) custom-call(s32[4,4]{1,0:T(4,128)} %delays_ref.3, bf16[32,8,2048]{2,1,0:T(8,128)(2,1)} %window_ref.3), custom_call_target="tpu_custom_call" | custom-call | tf_op jit(solution)/shard_map/pallas_call | solution.py:34
  11.4 19.5 %collective-permute-done.refs_4_ = bf16[128,2048]{1,0:T(8,128)(2,1)} collective-permute-done((bf16[128,2048]{1,0:T(8,128)(2,1)}, bf16[128,2048]{1,0:T(8,128)(2,1)}, u32[]{:S(2)}, u32[]{:S(2)}) %collective-permute-start) | collective-permute-done | bytes 524320 | tf_op jit(solution)/shard_map/ppermute | solution.py:17
  31.0 0.0 collective-permute-start.8
  31.0 1.5 %collective-permute-start.7 = (bf16[128,2048]{1,0:T(8,128)(2,1)}, bf16[128,2048]{1,0:T(8,128)(2,1)}, u32[]{:S(2)}, u32[]{:S(2)}) collective-permute-start(bf16[128,2048]{1,0:T(8,128)(2,1)} %collective-permute-done.refs_4_), channel_id=1, source_target_pairs={{0,2},{1,3},{2,0},{3,1},{4,6},{5,7},{6,4},{7,5},{8,10},{9,11},{10,... | collective-permute-start | bytes 1572872 | tf_op jit(solution)/shard_map/ppermute | solution.py:17
  32.5 0.0 collective-permute-done.1.refs_0_
  32.5 0.5 collective-permute-start.4
  33.0 1.1 %collective-permute-start.2 = (bf16[128,2048]{1,0:T(8,128)(2,1)}, bf16[128,2048]{1,0:T(8,128)(2,1)S(1)}, u32[]{:S(2)}, u32[]{:S(2)}) collective-permute-start(bf16[128,2048]{1,0:T(8,128)(2,1)} %get-tuple-element.17), channel_id=1, source_target_pairs={{0,4},{4,0},{8,12},{12,8},{1,5},{5,1},{9,13},{13,9},{2,6},{6,2},{1... | collective-permute-start | bytes 1572872 | tf_op jit(solution)/shard_map/ppermute | solution.py:17
  34.1 2.9 %collective-permute-start.12 = (bf16[128,2048]{1,0:T(8,128)(2,1)}, bf16[128,2048]{1,0:T(8,128)(2,1)S(1)}, u32[]{:S(2)}, u32[]{:S(2)}) collective-permute-start(bf16[128,2048]{1,0:T(8,128)(2,1)} %get-tuple-element.20), channel_id=1, source_target_pairs={{0,8},{4,12},{8,0},{12,4},{1,9},{5,13},{9,1},{13,5},{2,10},{6,14},... | collective-permute-start | bytes 1572872 | tf_op jit(solution)/shard_map/ppermute | solution.py:17
  37.0 0.0 collective-permute-done.8.refs_6_
  37.0 0.0 copy-start.13
  37.0 0.0 collective-permute-start.5
  37.0 9.0 %collective-permute-done.7.refs_5_ = bf16[128,2048]{1,0:T(8,128)(2,1)} collective-permute-done((bf16[128,2048]{1,0:T(8,128)(2,1)}, bf16[128,2048]{1,0:T(8,128)(2,1)}, u32[]{:S(2)}, u32[]{:S(2)}) %collective-permute-start.7) | collective-permute-done | bytes 524320 | tf_op jit(solution)/shard_map/ppermute | solution.py:17
  46.0 0.0 collective-permute-start.9
  46.0 10.8 %collective-permute-done.4.refs_1_ = bf16[128,2048]{1,0:T(8,128)(2,1)} collective-permute-done((bf16[128,2048]{1,0:T(8,128)(2,1)}, bf16[128,2048]{1,0:T(8,128)(2,1)}, u32[]{:S(2)}, u32[]{:S(2)}) %collective-permute-start.4) | collective-permute-done | bytes 524320 | tf_op jit(solution)/shard_map/ppermute | solution.py:17
  56.9 0.0 collective-permute-start.6
  56.9 1.1 %collective-permute-done.2.refs_0_ = bf16[128,2048]{1,0:T(8,128)(2,1)S(1)} collective-permute-done((bf16[128,2048]{1,0:T(8,128)(2,1)}, bf16[128,2048]{1,0:T(8,128)(2,1)S(1)}, u32[]{:S(2)}, u32[]{:S(2)}) %collective-permute-start.2) | collective-permute-done | bytes 524320 | tf_op jit(solution)/shard_map/ppermute | solution.py:17
  58.0 0.0 copy-start.7
  58.0 1.5 %collective-permute-start.3 = (bf16[128,2048]{1,0:T(8,128)(2,1)S(1)}, bf16[128,2048]{1,0:T(8,128)(2,1)}, u32[]{:S(2)}, u32[]{:S(2)}) collective-permute-start(bf16[128,2048]{1,0:T(8,128)(2,1)S(1)} %collective-permute-done.2.refs_0_), channel_id=1, source_target_pairs={{0,2},{1,3},{2,0},{3,1},{4,6},{5,7},{6,4},{7,5},{8,10},{9,11},{10,... | collective-permute-start | bytes 1572872 | tf_op jit(solution)/shard_map/ppermute | solution.py:17
  59.5 0.7 collective-permute-done.12.refs_4_
  60.2 0.0 copy-done.13
  60.3 0.0 copy-start.8
  60.3 1.5 %collective-permute-start.13 = (bf16[128,2048]{1,0:T(8,128)(2,1)S(1)}, bf16[128,2048]{1,0:T(8,128)(2,1)}, u32[]{:S(2)}, u32[]{:S(2)}) collective-permute-start(bf16[128,2048]{1,0:T(8,128)(2,1)S(1)} %collective-permute-done.12.refs_4_), channel_id=1, source_target_pairs={{0,2},{1,3},{2,0},{3,1},{4,6},{5,7},{6,4},{7,5},{8,10},{9,11},{10,... | collective-permute-start | bytes 1572872 | tf_op jit(solution)/shard_map/ppermute | solution.py:17
  61.7 1.4 %copy.15.bi_ref = s32[4,1,16,4]{3,2,1,0:T(8,128)} copy(s32[4,1,16,4]{2,3,1,0:T(4,128)} %param.20) | data formatting | bytes 2048 | tf_op args[9]
  63.1 0.0 collective-permute-done.5.refs_2_
  63.1 0.0 collective-permute-done.9.refs_7_
  63.1 0.0 collective-permute-done.6.refs_3_
  63.1 6.6 %shard_map.132.refs_9_ = f32[16,8,2048]{2,1,0:T(8,128)} custom-call(s32[4,1,16,4]{3,2,1,0:T(8,128)} %copy.15.bi_ref, bf16[128,2048]{1,0:T(8,128)(2,1)} %collective-permute-done.1.refs_0_, bf16[128,2048]{1,0:T(8,128)(2,1)} %collective-permute-done.4.refs_1_, bf16[128,2048]{1,0:T(8,128)(2,1)} %collective-permute-done.5.refs_2_, ...), custom_call_target="tpu_custom_call" | custom-call | tf_op jit(solution)/shard_map/pallas_call | solution.py:184
  69.7 3.2 %collective-permute-done.3.refs_1_ = bf16[128,2048]{1,0:T(8,128)(2,1)} collective-permute-done((bf16[128,2048]{1,0:T(8,128)(2,1)S(1)}, bf16[128,2048]{1,0:T(8,128)(2,1)}, u32[]{:S(2)}, u32[]{:S(2)}) %collective-permute-start.3) | collective-permute-done | bytes 524320 | tf_op jit(solution)/shard_map/ppermute | solution.py:17
  73.0 0.0 collective-permute-start.10
  73.0 0.5 collective-permute-start.11
  73.5 9.1 %collective-permute-done.13.refs_5_ = bf16[128,2048]{1,0:T(8,128)(2,1)} collective-permute-done((bf16[128,2048]{1,0:T(8,128)(2,1)S(1)}, bf16[128,2048]{1,0:T(8,128)(2,1)}, u32[]{:S(2)}, u32[]{:S(2)}) %collective-permute-start.13) | collective-permute-done | bytes 524320 | tf_op jit(solution)/shard_map/ppermute | solution.py:17
  82.6 0.0 collective-permute-start.14
  82.6 0.5 collective-permute-start.15
  83.1 0.0 collective-permute-done.10.refs_2_
  83.1 0.0 copy-start.9
  83.1 0.0 collective-permute-done.11.refs_3_
  83.1 0.0 copy-start.10
  83.1 2.1 %collective-permute-done.14.refs_6_ = bf16[128,2048]{1,0:T(8,128)(2,1)S(1)} collective-permute-done((bf16[128,2048]{1,0:T(8,128)(2,1)S(1)}, bf16[128,2048]{1,0:T(8,128)(2,1)S(1)}, u32[]{:S(2)}, u32[]{:S(2)}) %collective-permute-start.14) | collective-permute-done | bytes 524320 | tf_op jit(solution)/shard_map/ppermute | solution.py:17
  85.2 0.0 copy-done.9
  85.2 0.0 copy-start.11
  85.2 0.2 collective-permute-done.15.refs_7_
  85.4 0.0 copy-done.10
  85.4 0.6 copy-done.11
  86.0 0.2 copy-done.12
  86.2 0.0 copy-done.7
  86.2 0.0 copy-done.8
  86.2 0.0 copy-done.6
  86.2 0.0 copy-done.5
  86.2 0.0 copy-done.4
  86.3 0.0 copy-done.3
  86.3 0.0 copy-done.2
  86.3 0.0 copy-done.1
  86.3 0.0 copy-done
  86.3 7.0 %shard_map.133 = (bf16[16,8,2048]{2,1,0:T(8,128)(2,1)}, f32[8,2048]{1,0:T(8,128)}, f32[8,2048]{1,0:T(8,128)}) custom-call(s32[4,1,16,4]{3,2,1,0:T(8,128)} %copy.15.bi_ref, bf16[128,2048]{1,0:T(8,128)(2,1)} %copy-done.7, bf16[128,2048]{1,0:T(8,128)(2,1)} %collective-permute-done.3.refs_1_, bf16[128,2048]{1,0:T(8,128)(2,1)} %copy-done.9, ...), custom_call_target="tpu_custom_call" | custom-call | tf_op jit(solution)/shard_map/pallas_call | solution.py:184
  (1 shorter events, 0.0 us)
Async XLA Ops:
  0.6 85.6 %copy-start.6 = (f32[2048]{0:T(1024)S(1)}, f32[2048]{0:T(1024)}, u32[]{:S(2)}) copy-start(f32[2048]{0:T(1024)} %param.18) | copy-start | bytes 24580
  0.6 85.6 %copy-start.5 = (f32[2048]{0:T(1024)S(1)}, f32[2048]{0:T(1024)}, u32[]{:S(2)}) copy-start(f32[2048]{0:T(1024)} %param.17) | copy-start | bytes 24580
  0.7 85.6 %copy-start.4 = (f32[2048]{0:T(1024)S(1)}, f32[2048]{0:T(1024)}, u32[]{:S(2)}) copy-start(f32[2048]{0:T(1024)} %param.16) | copy-start | bytes 24580
  0.7 85.6 %copy-start.3 = (f32[8,2048]{1,0:T(8,128)S(1)}, f32[8,2048]{1,0:T(8,128)}, u32[]{:S(2)}) copy-start(f32[8,2048]{1,0:T(8,128)} %refs_13_.1) | copy-start | bytes 196612
  0.7 85.6 %copy-start.2 = (f32[8,2048]{1,0:T(8,128)S(1)}, f32[8,2048]{1,0:T(8,128)}, u32[]{:S(2)}) copy-start(f32[8,2048]{1,0:T(8,128)} %refs_12_.1) | copy-start | bytes 196612
  0.7 85.6 %copy-start.1 = (f32[16,8,2048]{2,1,0:T(8,128)S(1)}, f32[16,8,2048]{2,1,0:T(8,128)}, u32[]{:S(2)}) copy-start(f32[16,8,2048]{2,1,0:T(8,128)} %refs_11_.1) | copy-start | bytes 3145732
  0.7 85.6 %copy-start = (f32[16,8,2048]{2,1,0:T(8,128)S(1)}, f32[16,8,2048]{2,1,0:T(8,128)}, u32[]{:S(2)}) copy-start(f32[16,8,2048]{2,1,0:T(8,128)} %refs_10_.1) | copy-start | bytes 3145732
  3.4 27.6 %collective-permute-start = (bf16[128,2048]{1,0:T(8,128)(2,1)}, bf16[128,2048]{1,0:T(8,128)(2,1)}, u32[]{:S(2)}, u32[]{:S(2)}) collective-permute-start(bf16[128,2048]{1,0:T(8,128)(2,1)} %get-tuple-element.15), channel_id=1, source_target_pairs={{0,8},{4,12},{8,0},{12,4},{1,9},{5,13},{9,1},{13,5},{2,10},{6,14},... | collective-permute-start | bytes 1572872 | tf_op jit(solution)/shard_map/ppermute | solution.py:17
  7.4 25.1 %collective-permute-start.1 = (bf16[128,2048]{1,0:T(8,128)(2,1)}, bf16[128,2048]{1,0:T(8,128)(2,1)}, u32[]{:S(2)}, u32[]{:S(2)}) collective-permute-start(bf16[128,2048]{1,0:T(8,128)(2,1)} %get-tuple-element.16), channel_id=1, source_target_pairs={{0,4},{4,0},{8,12},{12,8},{1,5},{5,1},{9,13},{13,9},{2,6},{6,2},{1... | collective-permute-start | bytes 1572872 | tf_op jit(solution)/shard_map/ppermute | solution.py:17
  31.0 6.0 %collective-permute-start.8 = (bf16[128,2048]{1,0:T(8,128)(2,1)}, bf16[128,2048]{1,0:T(8,128)(2,1)S(1)}, u32[]{:S(2)}, u32[]{:S(2)}) collective-permute-start(bf16[128,2048]{1,0:T(8,128)(2,1)} %collective-permute-done.refs_4_), channel_id=1, source_target_pairs={{0,1},{1,0},{2,3},{3,2},{4,5},{5,4},{6,7},{7,6},{8,9},{9,8},{10,11... | collective-permute-start | bytes 1572872 | tf_op jit(solution)/shard_map/ppermute | solution.py:17
  31.0 15.0 %collective-permute-start.7 = (bf16[128,2048]{1,0:T(8,128)(2,1)}, bf16[128,2048]{1,0:T(8,128)(2,1)}, u32[]{:S(2)}, u32[]{:S(2)}) collective-permute-start(bf16[128,2048]{1,0:T(8,128)(2,1)} %collective-permute-done.refs_4_), channel_id=1, source_target_pairs={{0,2},{1,3},{2,0},{3,1},{4,6},{5,7},{6,4},{7,5},{8,10},{9,11},{10,... | collective-permute-start | bytes 1572872 | tf_op jit(solution)/shard_map/ppermute | solution.py:17
  32.5 24.3 %collective-permute-start.4 = (bf16[128,2048]{1,0:T(8,128)(2,1)}, bf16[128,2048]{1,0:T(8,128)(2,1)}, u32[]{:S(2)}, u32[]{:S(2)}) collective-permute-start(bf16[128,2048]{1,0:T(8,128)(2,1)} %collective-permute-done.1.refs_0_), channel_id=1, source_target_pairs={{0,2},{1,3},{2,0},{3,1},{4,6},{5,7},{6,4},{7,5},{8,10},{9,11},{10,... | collective-permute-start | bytes 1572872 | tf_op jit(solution)/shard_map/ppermute | solution.py:17
  33.0 25.0 %collective-permute-start.2 = (bf16[128,2048]{1,0:T(8,128)(2,1)}, bf16[128,2048]{1,0:T(8,128)(2,1)S(1)}, u32[]{:S(2)}, u32[]{:S(2)}) collective-permute-start(bf16[128,2048]{1,0:T(8,128)(2,1)} %get-tuple-element.17), channel_id=1, source_target_pairs={{0,4},{4,0},{8,12},{12,8},{1,5},{5,1},{9,13},{13,9},{2,6},{6,2},{1... | collective-permute-start | bytes 1572872 | tf_op jit(solution)/shard_map/ppermute | solution.py:17
  34.1 26.1 %collective-permute-start.12 = (bf16[128,2048]{1,0:T(8,128)(2,1)}, bf16[128,2048]{1,0:T(8,128)(2,1)S(1)}, u32[]{:S(2)}, u32[]{:S(2)}) collective-permute-start(bf16[128,2048]{1,0:T(8,128)(2,1)} %get-tuple-element.20), channel_id=1, source_target_pairs={{0,8},{4,12},{8,0},{12,4},{1,9},{5,13},{9,1},{13,5},{2,10},{6,14},... | collective-permute-start | bytes 1572872 | tf_op jit(solution)/shard_map/ppermute | solution.py:17
  37.0 23.2 %copy-start.13 = (bf16[128,2048]{1,0:T(8,128)(2,1)}, bf16[128,2048]{1,0:T(8,128)(2,1)S(1)}, u32[]{:S(2)}) copy-start(bf16[128,2048]{1,0:T(8,128)(2,1)S(1)} %collective-permute-done.8.refs_6_) | copy-start | bytes 1572868
  37.0 26.1 %collective-permute-start.5 = (bf16[128,2048]{1,0:T(8,128)(2,1)}, bf16[128,2048]{1,0:T(8,128)(2,1)}, u32[]{:S(2)}, u32[]{:S(2)}) collective-permute-start(bf16[128,2048]{1,0:T(8,128)(2,1)} %collective-permute-done.1.refs_0_), channel_id=1, source_target_pairs={{0,1},{1,0},{2,3},{3,2},{4,5},{5,4},{6,7},{7,6},{8,9},{9,8},{10,11... | collective-permute-start | bytes 1572872 | tf_op jit(solution)/shard_map/ppermute | solution.py:17
  46.0 17.1 %collective-permute-start.9 = (bf16[128,2048]{1,0:T(8,128)(2,1)}, bf16[128,2048]{1,0:T(8,128)(2,1)}, u32[]{:S(2)}, u32[]{:S(2)}) collective-permute-start(bf16[128,2048]{1,0:T(8,128)(2,1)} %collective-permute-done.7.refs_5_), channel_id=1, source_target_pairs={{0,1},{1,0},{2,3},{3,2},{4,5},{5,4},{6,7},{7,6},{8,9},{9,8},{10,11... | collective-permute-start | bytes 1572872 | tf_op jit(solution)/shard_map/ppermute | solution.py:17
  56.9 6.3 %collective-permute-start.6 = (bf16[128,2048]{1,0:T(8,128)(2,1)}, bf16[128,2048]{1,0:T(8,128)(2,1)}, u32[]{:S(2)}, u32[]{:S(2)}) collective-permute-start(bf16[128,2048]{1,0:T(8,128)(2,1)} %collective-permute-done.4.refs_1_), channel_id=1, source_target_pairs={{0,1},{1,0},{2,3},{3,2},{4,5},{5,4},{6,7},{7,6},{8,9},{9,8},{10,11... | collective-permute-start | bytes 1572872 | tf_op jit(solution)/shard_map/ppermute | solution.py:17
  58.0 28.2 %copy-start.7 = (bf16[128,2048]{1,0:T(8,128)(2,1)}, bf16[128,2048]{1,0:T(8,128)(2,1)S(1)}, u32[]{:S(2)}) copy-start(bf16[128,2048]{1,0:T(8,128)(2,1)S(1)} %collective-permute-done.2.refs_0_) | copy-start | bytes 1572868
  58.0 15.0 %collective-permute-start.3 = (bf16[128,2048]{1,0:T(8,128)(2,1)S(1)}, bf16[128,2048]{1,0:T(8,128)(2,1)}, u32[]{:S(2)}, u32[]{:S(2)}) collective-permute-start(bf16[128,2048]{1,0:T(8,128)(2,1)S(1)} %collective-permute-done.2.refs_0_), channel_id=1, source_target_pairs={{0,2},{1,3},{2,0},{3,1},{4,6},{5,7},{6,4},{7,5},{8,10},{9,11},{10,... | collective-permute-start | bytes 1572872 | tf_op jit(solution)/shard_map/ppermute | solution.py:17
  60.3 26.0 %copy-start.8 = (bf16[128,2048]{1,0:T(8,128)(2,1)}, bf16[128,2048]{1,0:T(8,128)(2,1)S(1)}, u32[]{:S(2)}) copy-start(bf16[128,2048]{1,0:T(8,128)(2,1)S(1)} %collective-permute-done.12.refs_4_) | copy-start | bytes 1572868
  60.3 22.3 %collective-permute-start.13 = (bf16[128,2048]{1,0:T(8,128)(2,1)S(1)}, bf16[128,2048]{1,0:T(8,128)(2,1)}, u32[]{:S(2)}, u32[]{:S(2)}) collective-permute-start(bf16[128,2048]{1,0:T(8,128)(2,1)S(1)} %collective-permute-done.12.refs_4_), channel_id=1, source_target_pairs={{0,2},{1,3},{2,0},{3,1},{4,6},{5,7},{6,4},{7,5},{8,10},{9,11},{10,... | collective-permute-start | bytes 1572872 | tf_op jit(solution)/shard_map/ppermute | solution.py:17
  73.0 10.1 %collective-permute-start.10 = (bf16[128,2048]{1,0:T(8,128)(2,1)S(1)}, bf16[128,2048]{1,0:T(8,128)(2,1)S(1)}, u32[]{:S(2)}, u32[]{:S(2)}) collective-permute-start(bf16[128,2048]{1,0:T(8,128)(2,1)S(1)} %collective-permute-done.2.refs_0_), channel_id=1, source_target_pairs={{0,1},{1,0},{2,3},{3,2},{4,5},{5,4},{6,7},{7,6},{8,9},{9,8},{10,11... | collective-permute-start | bytes 1572872 | tf_op jit(solution)/shard_map/ppermute | solution.py:17
  73.0 10.1 %collective-permute-start.11 = (bf16[128,2048]{1,0:T(8,128)(2,1)}, bf16[128,2048]{1,0:T(8,128)(2,1)S(1)}, u32[]{:S(2)}, u32[]{:S(2)}) collective-permute-start(bf16[128,2048]{1,0:T(8,128)(2,1)} %collective-permute-done.3.refs_1_), channel_id=1, source_target_pairs={{0,1},{1,0},{2,3},{3,2},{4,5},{5,4},{6,7},{7,6},{8,9},{9,8},{10,11... | collective-permute-start | bytes 1572872 | tf_op jit(solution)/shard_map/ppermute | solution.py:17
  82.6 2.6 %collective-permute-start.14 = (bf16[128,2048]{1,0:T(8,128)(2,1)S(1)}, bf16[128,2048]{1,0:T(8,128)(2,1)S(1)}, u32[]{:S(2)}, u32[]{:S(2)}) collective-permute-start(bf16[128,2048]{1,0:T(8,128)(2,1)S(1)} %collective-permute-done.12.refs_4_), channel_id=1, source_target_pairs={{0,1},{1,0},{2,3},{3,2},{4,5},{5,4},{6,7},{7,6},{8,9},{9,8},{10,11... | collective-permute-start | bytes 1572872 | tf_op jit(solution)/shard_map/ppermute | solution.py:17
  82.6 2.9 %collective-permute-start.15 = (bf16[128,2048]{1,0:T(8,128)(2,1)}, bf16[128,2048]{1,0:T(8,128)(2,1)S(1)}, u32[]{:S(2)}, u32[]{:S(2)}) collective-permute-start(bf16[128,2048]{1,0:T(8,128)(2,1)} %collective-permute-done.13.refs_5_), channel_id=1, source_target_pairs={{0,1},{1,0},{2,3},{3,2},{4,5},{5,4},{6,7},{7,6},{8,9},{9,8},{10,11... | collective-permute-start | bytes 1572872 | tf_op jit(solution)/shard_map/ppermute | solution.py:17
  83.1 2.1 %copy-start.9 = (bf16[128,2048]{1,0:T(8,128)(2,1)}, bf16[128,2048]{1,0:T(8,128)(2,1)S(1)}, u32[]{:S(2)}) copy-start(bf16[128,2048]{1,0:T(8,128)(2,1)S(1)} %collective-permute-done.10.refs_2_) | copy-start | bytes 1572868
  83.1 2.4 %copy-start.10 = (bf16[128,2048]{1,0:T(8,128)(2,1)}, bf16[128,2048]{1,0:T(8,128)(2,1)S(1)}, u32[]{:S(2)}) copy-start(bf16[128,2048]{1,0:T(8,128)(2,1)S(1)} %collective-permute-done.11.refs_3_) | copy-start | bytes 1572868
  85.2 0.8 copy-start.11
  85.4 0.8 copy-start.12

commit v15 on v14

--- a/solution.py
+++ b/solution.py
@@ -17,25 +17,30 @@
     return lax.ppermute(value, axis, pairs)
 
 
-def slice_kernel(delays_ref, window_ref, *outs, rounds, levels, steps):
+def slice_kernel(delays_ref, window_ref, *outs, rounds, levels, steps, n_halves):
     me = lax.axis_index("area")
     rows, width = outs[0].shape
     side = 128 if width % 128 == 0 else width
-    for rnd, out in zip(rounds, outs):
+    for n, out in enumerate(outs):
+        rnd, h = rounds[n // n_halves], n % n_halves
         start = delays_ref[rnd, me ^ (1 << (rnd % levels))] - steps
         for c in range(0, width, side):
-            x = window_ref[pl.ds(start, steps), :, c:c + side].astype(jnp.float32)
+            col = h * width + c
+            x = window_ref[pl.ds(start, steps), :, col:col + side].astype(jnp.float32)
             out[:, c:c + side] = x.reshape(rows, side).astype(out.dtype)
 
 
-def send_slices(window, delays, rounds, levels, steps):
-    shape = (steps * window.shape[1], window.shape[2])
-    kernel = functools.partial(slice_kernel, rounds=tuple(rounds), levels=levels, steps=steps)
+def send_slices(window, delays, rounds, levels, steps, n_halves=1):
+    shape = (steps * window.shape[1], window.shape[2] // n_halves)
+    kernel = functools.partial(
+        slice_kernel, rounds=tuple(rounds), levels=levels, steps=steps, n_halves=n_halves
+    )
+    n_out = len(rounds) * n_halves
     return pl.pallas_call(
         kernel,
         in_specs=[SMEM, VMEM],
-        out_specs=[VMEM] * len(rounds),
-        out_shape=[jax.ShapeDtypeStruct(shape, window.dtype)] * len(rounds),
+        out_specs=[VMEM] * n_out,
+        out_shape=[jax.ShapeDtypeStruct(shape, window.dtype)] * n_out,
     )(delays, window)
 
 
@@ -49,7 +54,7 @@
     return held
 
 
-def stage_kernel(bi_ref, *refs, n_pieces, stage, n_pos, final, has_rec):
+def stage_kernel(bi_ref, *refs, n_pieces, stage, n_pos, n_halves, final, has_rec):
     n_rounds = len(stage)
     it = iter(refs)
     piece_hbm = [next(it) for _ in range(n_pieces)]
@@ -84,8 +89,12 @@
     piece_cp, w_cp = [], []
     rec_cp = None
     scan_cp = []
+    width = piece_buf.shape[-1] // n_halves
     for ri, rnd in enumerate(stage):
-        piece_cp += [start(piece_hbm[ri * n_pos + p], piece_buf.at[ri * n_pos + p]) for p in range(n_pos)]
+        for p in range(n_pos):
+            for h in range(n_halves):
+                dst = piece_buf.at[ri * n_pos + p, :, pl.ds(h * width, width)]
+                piece_cp.append(start(piece_hbm[(ri * n_pos + p) * n_halves + h], dst))
         w_cp.append(start(w_hbm.at[rnd, 0], w_buf.at[ri]))
         if ri == 0 and has_rec:
             rec_cp = start(rec_hbm, rec_buf)
@@ -93,8 +102,8 @@
         scan_cp = [start(src, dst) for src, dst in zip(scan_hbm, scan_buf)]
 
     for ri, rnd in enumerate(stage):
-        for p in range(n_pos):
-            piece_cp[ri * n_pos + p].wait()
+        for q in range(n_pos * n_halves):
+            piece_cp[ri * n_pos * n_halves + q].wait()
         w_cp[ri].wait()
         if ri == 0 and has_rec:
             rec_cp.wait()
@@ -141,8 +150,9 @@
             la_out[:, cols] = la_now
 
 
-def stage_contrib(block_index, pieces, weights, stage, n_pos, rec, scan_args, steps):
-    rows, local = pieces[0].shape
+def stage_contrib(block_index, pieces, weights, stage, n_pos, rec, scan_args, steps, n_halves=1):
+    rows, width = pieces[0].shape
+    local = width * n_halves
     _, _, local_blocks, nnz, side, _ = weights.shape
     batch = rows // steps
     n_rounds = len(stage)
@@ -150,7 +160,7 @@
     has_rec = rec is not None
     operands = list(pieces) + [weights]
     scratch = [
-        pltpu.VMEM((len(pieces), rows, local), pieces[0].dtype),
+        pltpu.VMEM((len(pieces) // n_halves, rows, local), pieces[0].dtype),
         pltpu.VMEM((n_rounds, local_blocks, nnz, side, side), weights.dtype),
     ]
     n_sem = len(pieces) + n_rounds + (1 if has_rec else 0) + (7 if final else 0)
@@ -174,7 +184,7 @@
         out_specs = VMEM
         out_shape = jax.ShapeDtypeStruct((steps, batch, local), jnp.float32)
     kernel = functools.partial(
-        stage_kernel, n_pieces=len(pieces), stage=tuple(stage), n_pos=n_pos,
+        stage_kernel, n_pieces=len(pieces), stage=tuple(stage), n_pos=n_pos, n_halves=n_halves,
         final=final, has_rec=has_rec,
     )
     pinned = [final and i > len(pieces) + has_rec for i in range(len(operands))]
@@ -202,25 +212,33 @@
     nbits = lax.axis_size("neuron").bit_length() - 1
     n_pos = 1 << nbits
     stages = [list(range(f, min(f + 2, rounds))) for f in range(0, rounds, 2)]
+    n_halves = 2 if local_blocks % 2 == 0 and len(stages) > 1 else 1
     arrived = {}
     gate = None
-    for stage in stages:
-        stage = sorted(stage, key=lambda rnd: -(rnd % levels))
-        pieces = send_slices(window, delays, stage, levels, steps)
-        if gate is not None:
-            pieces, _ = lax.optimization_barrier((pieces, gate))
-        got = [swap(piece, "area", 1 << (rnd % levels)) for piece, rnd in zip(pieces, stage)]
-        arrived.update(zip(stage, got))
-        gate = got
+    for si, stage in enumerate(stages):
+        halves = n_halves if si == len(stages) - 1 else 1
+        pieces = send_slices(window, delays, stage, levels, steps, halves)
+        for h in range(halves):
+            part = [pieces[ri * halves + h] for ri in range(len(stage))]
+            if gate is not None:
+                part, _ = lax.optimization_barrier((part, gate))
+            got = [swap(piece, "area", 1 << (rnd % levels)) for piece, rnd in zip(part, stage)]
+            for rnd, g in zip(stage, got):
+                arrived[(rnd, h)] = g
+            gate = got
     rec = None
     for si, stage in enumerate(stages):
+        halves = n_halves if si == len(stages) - 1 else 1
         chunks = []
         for rnd in stage:
-            chunks += gather_neuron(arrived[rnd], rec)
+            parts = [gather_neuron(arrived[(rnd, h)], rec) for h in range(halves)]
+            chunks += [parts[h][p] for p in range(n_pos) for h in range(halves)]
         scan_args = None
         if si == len(stages) - 1:
             scan_args = (err_grad, surrogate, lv_end, la_end, alpha, rho, beta)
-        rec = stage_contrib(block_index, chunks, weights, stage, n_pos, rec, scan_args, steps)
+        rec = stage_contrib(
+            block_index, chunks, weights, stage, n_pos, rec, scan_args, steps, halves
+        )
     return rec
 
 

time: 93.7 us -> 95.1 us (1.015)
  starting transfers between devices: 15.7 us -> 19.1 us
  waiting for transfers between devices: 55.9 us -> 53.9 us
    ppermute x16 -> x24, starting transfers between devices: 15.7 us -> 19.1 us  [swap(): return lax.ppermute(value, axis, pairs)]
    ppermute x16 -> x24, waiting for transfers between devices: 55.9 us -> 53.9 us  [swap(): return lax.ppermute(value, axis, pairs)]
    unnamed x29 -> x33, local copies, waits for them, and re-layouts: 2.25 us -> 2.25 us
  transfers between devices with their start and end apart: 16 -> 24, of which waited for: 9 -> 13; matrix products, arithmetic and copies ran while one was open for 1% -> 1% of each run, Pallas kernels for 10% -> 10%
where the time goes in v15:
time: 95.1 us; the launch traced here: 94.7 us
  waiting for transfers between devices  53.9 us (57%)
  starting transfers between devices  19.1 us (20%)
  Pallas kernels  18.7 us (20%)
  local copies, waits for them, and re-layouts  2.25 us (2%)
    ppermute x24, waiting for transfers between devices, swap(): return lax.ppermute(value, axis, pairs)  53.9 us
    ppermute x24, starting transfers between devices, swap(): return lax.ppermute(value, axis, pairs)  19.1 us
    pallas_call x2, Pallas kernels, stage_contrib(): pl.pallas_call(kernel, in_specs=[SMEM] + specs, out_specs=out_specs, scra...  13.7 us
    pallas_call x2, Pallas kernels, send_slices(): pl.pallas_call(kernel, in_specs=[SMEM, VMEM], out_specs=[VMEM] * n_out, o...  5.04 us
    unnamed x33, local copies, waits for them, and re-layouts  2.25 us
  transfers between devices with their start and end apart: 24, of which 13 were waited for; matrix products, arithmetic and copies ran while one was open for 1% of the time, Pallas kernels for 10%

profile of v15, /device:TPU:0, one launch (start us, length us, event | category | flops | bytes accessed | tf_op | source)
XLA Modules:
  0.0 94.7 jit_solution(6193363614174422092)
XLA Ops:
  0.6 0.0 copy-start.4
  0.6 0.0 copy-start.5
  0.7 0.0 copy-start.6
  0.7 0.0 copy-start
  0.7 0.0 copy-start.1
  0.7 0.0 copy-start.2
  0.7 0.0 copy-start.3
  0.7 2.6 %shard_map.131 = (bf16[128,2048]{1,0:T(8,128)(2,1)}, bf16[128,2048]{1,0:T(8,128)(2,1)}) custom-call(s32[4,4]{1,0:T(4,128)} %delays_ref.3, bf16[32,8,2048]{2,1,0:T(8,128)(2,1)} %window_ref.3), custom_call_target="tpu_custom_call" | custom-call | tf_op jit(solution)/shard_map/pallas_call | solution.py:39
  3.3 3.0 %collective-permute-start = (bf16[128,2048]{1,0:T(8,128)(2,1)}, bf16[128,2048]{1,0:T(8,128)(2,1)S(1)}, u32[]{:S(2)}, u32[]{:S(2)}) collective-permute-start(bf16[128,2048]{1,0:T(8,128)(2,1)} %get-tuple-element.23), channel_id=1, source_target_pairs={{0,4},{4,0},{8,12},{12,8},{1,5},{5,1},{9,13},{13,9},{2,6},{6,2},{1... | collective-permute-start | bytes 1572872 | tf_op jit(solution)/shard_map/ppermute | solution.py:17
  6.3 2.6 %collective-permute-start.1 = (bf16[128,2048]{1,0:T(8,128)(2,1)}, bf16[128,2048]{1,0:T(8,128)(2,1)S(1)}, u32[]{:S(2)}, u32[]{:S(2)}) collective-permute-start(bf16[128,2048]{1,0:T(8,128)(2,1)} %get-tuple-element.24), channel_id=1, source_target_pairs={{0,8},{4,12},{8,0},{12,4},{1,9},{5,13},{9,1},{13,5},{2,10},{6,14},... | collective-permute-start | bytes 1572872 | tf_op jit(solution)/shard_map/ppermute | solution.py:17
  8.9 2.5 %shard_map.130 = (bf16[128,1024]{1,0:T(8,128)(2,1)}, bf16[128,1024]{1,0:T(8,128)(2,1)}, bf16[128,1024]{1,0:T(8,128)(2,1)}, bf16[128,1024]{1,0:T(8,128)(2,1)}) custom-call(s32[4,4]{1,0:T(4,128)} %delays_ref.3, bf16[32,8,2048]{2,1,0:T(8,128)(2,1)} %window_ref.3), custom_call_target="tpu_custom_call" | custom-call | tf_op jit(solution)/shard_map/pallas_call | solution.py:39
  11.4 18.2 %collective-permute-done.refs_0_ = bf16[128,2048]{1,0:T(8,128)(2,1)S(1)} collective-permute-done((bf16[128,2048]{1,0:T(8,128)(2,1)}, bf16[128,2048]{1,0:T(8,128)(2,1)S(1)}, u32[]{:S(2)}, u32[]{:S(2)}) %collective-permute-start) | collective-permute-done | bytes 524320 | tf_op jit(solution)/shard_map/ppermute | solution.py:17
  29.6 2.5 %collective-permute-done.1.refs_4_ = bf16[128,2048]{1,0:T(8,128)(2,1)S(1)} collective-permute-done((bf16[128,2048]{1,0:T(8,128)(2,1)}, bf16[128,2048]{1,0:T(8,128)(2,1)S(1)}, u32[]{:S(2)}, u32[]{:S(2)}) %collective-permute-start.1) | collective-permute-done | bytes 524320 | tf_op jit(solution)/shard_map/ppermute | solution.py:17
  32.1 1.5 %collective-permute-start.4 = (bf16[128,2048]{1,0:T(8,128)(2,1)S(1)}, bf16[128,2048]{1,0:T(8,128)(2,1)}, u32[]{:S(2)}, u32[]{:S(2)}) collective-permute-start(bf16[128,2048]{1,0:T(8,128)(2,1)S(1)} %collective-permute-done.refs_0_), channel_id=1, source_target_pairs={{0,2},{1,3},{2,0},{3,1},{4,6},{5,7},{6,4},{7,5},{8,10},{9,11},{10,... | collective-permute-start | bytes 1572872 | tf_op jit(solution)/shard_map/ppermute | solution.py:17
  33.6 0.3 collective-permute-start.10
  33.9 0.5 collective-permute-start.7
  34.5 2.7 %collective-permute-start.2 = (bf16[128,1024]{1,0:T(8,128)(2,1)}, bf16[128,1024]{1,0:T(8,128)(2,1)S(1)}, u32[]{:S(2)}, u32[]{:S(2)}) collective-permute-start(bf16[128,1024]{1,0:T(8,128)(2,1)} %get-tuple-element.25), channel_id=1, source_target_pairs={{0,4},{4,0},{8,12},{12,8},{1,5},{5,1},{9,13},{13,9},{2,6},{6,2},{1... | collective-permute-start | bytes 786440 | tf_op jit(solution)/shard_map/ppermute | solution.py:17
  37.2 0.0 collective-permute-start.5
  37.2 7.9 %collective-permute-done.10.refs_8_ = bf16[128,1024]{1,0:T(8,128)(2,1)S(1)} collective-permute-done((bf16[128,1024]{1,0:T(8,128)(2,1)}, bf16[128,1024]{1,0:T(8,128)(2,1)S(1)}, u32[]{:S(2)}, u32[]{:S(2)}) %collective-permute-start.10) | collective-permute-done | bytes 262176 | tf_op jit(solution)/shard_map/ppermute | solution.py:17
  45.0 0.1 collective-permute-done.2.refs_0_
  45.1 2.5 %collective-permute-start.18 = (bf16[128,1024]{1,0:T(8,128)(2,1)}, bf16[128,1024]{1,0:T(8,128)(2,1)}, u32[]{:S(2)}, u32[]{:S(2)}) collective-permute-start(bf16[128,1024]{1,0:T(8,128)(2,1)} %get-tuple-element.35), channel_id=1, source_target_pairs={{0,8},{4,12},{8,0},{12,4},{1,9},{5,13},{9,1},{13,5},{2,10},{6,14},... | collective-permute-start | bytes 786440 | tf_op jit(solution)/shard_map/ppermute | solution.py:17
  47.6 0.0 collective-permute-start.8
  47.7 0.0 collective-permute-done.4.refs_1_
  47.7 0.5 collective-permute-start.6
  48.2 5.9 %collective-permute-done.7.refs_5_ = bf16[128,2048]{1,0:T(8,128)(2,1)} collective-permute-done((bf16[128,2048]{1,0:T(8,128)(2,1)S(1)}, bf16[128,2048]{1,0:T(8,128)(2,1)}, u32[]{:S(2)}, u32[]{:S(2)}) %collective-permute-start.7) | collective-permute-done | bytes 524320 | tf_op jit(solution)/shard_map/ppermute | solution.py:17
  54.1 0.0 collective-permute-start.9
  54.1 3.8 %collective-permute-done.18.refs_9_ = bf16[128,1024]{1,0:T(8,128)(2,1)} collective-permute-done((bf16[128,1024]{1,0:T(8,128)(2,1)}, bf16[128,1024]{1,0:T(8,128)(2,1)}, u32[]{:S(2)}, u32[]{:S(2)}) %collective-permute-start.18) | collective-permute-done | bytes 262176 | tf_op jit(solution)/shard_map/ppermute | solution.py:17
  57.9 0.7 collective-permute-start.11
  58.6 0.0 collective-permute-done.5.refs_2_
  58.6 0.8 copy-done.9
  59.4 0.5 collective-permute-start.19
  60.0 0.0 copy-done.10
  60.0 5.5 %collective-permute-done.11.refs_1_ = bf16[128,1024]{1,0:T(8,128)(2,1)} collective-permute-done((bf16[128,1024]{1,0:T(8,128)(2,1)}, bf16[128,1024]{1,0:T(8,128)(2,1)}, u32[]{:S(2)}, u32[]{:S(2)}) %collective-permute-start.11) | collective-permute-done | bytes 262176 | tf_op jit(solution)/shard_map/ppermute | solution.py:17
  65.4 0.4 collective-permute-start.12
  65.8 1.4 %copy.15.bi_ref = s32[4,1,16,4]{3,2,1,0:T(8,128)} copy(s32[4,1,16,4]{2,3,1,0:T(4,128)} %param.20) | data formatting | bytes 2048 | tf_op args[9]
  67.2 0.0 collective-permute-done.8.refs_6_
  67.2 1.6 %collective-permute-start.17 = (bf16[128,1024]{1,0:T(8,128)(2,1)}, bf16[128,1024]{1,0:T(8,128)(2,1)}, u32[]{:S(2)}, u32[]{:S(2)}) collective-permute-start(bf16[128,1024]{1,0:T(8,128)(2,1)} %copy-done.10), channel_id=1, source_target_pairs={{0,2},{1,3},{2,0},{3,1},{4,6},{5,7},{6,4},{7,5},{8,10},{9,11},{10,... | collective-permute-start | bytes 786440 | tf_op jit(solution)/shard_map/ppermute | solution.py:17
  68.9 0.0 collective-permute-done.6.refs_3_
  68.9 0.4 collective-permute-start.3
  69.2 0.0 collective-permute-done.9.refs_7_
  69.3 0.0 copy-done.8
  69.3 6.6 %shard_map.132.refs_17_ = f32[16,8,2048]{2,1,0:T(8,128)} custom-call(s32[4,1,16,4]{3,2,1,0:T(8,128)} %copy.15.bi_ref, bf16[128,2048]{1,0:T(8,128)(2,1)} %copy-done.7, bf16[128,2048]{1,0:T(8,128)(2,1)} %collective-permute-done.4.refs_1_, bf16[128,2048]{1,0:T(8,128)(2,1)} %copy-done.9, bf16[128,2048]{1,0:T(8,128)(2,1)} %collective-permute-done.6.refs_3_, ...), custom_call_target="tpu_custom_call" | custom-call | tf_op jit(solution)/shard_map/pallas_call | solution.py:194
  75.8 0.0 collective-permute-done.19.refs_11_
  75.9 0.1 collective-permute-start.21
  75.9 0.5 collective-permute-start.23
  76.4 0.0 collective-permute-done.12.refs_3_
  76.4 0.1 collective-permute-start.14
  76.5 4.1 %collective-permute-done.17.refs_10_ = bf16[128,1024]{1,0:T(8,128)(2,1)} collective-permute-done((bf16[128,1024]{1,0:T(8,128)(2,1)}, bf16[128,1024]{1,0:T(8,128)(2,1)}, u32[]{:S(2)}, u32[]{:S(2)}) %collective-permute-start.17) | collective-permute-done | bytes 262176 | tf_op jit(solution)/shard_map/ppermute | solution.py:17
  80.6 0.0 collective-permute-start.16
  80.6 3.9 %collective-permute-done.3.refs_2_ = bf16[128,1024]{1,0:T(8,128)(2,1)} collective-permute-done((bf16[128,1024]{1,0:T(8,128)(2,1)}, bf16[128,1024]{1,0:T(8,128)(2,1)}, u32[]{:S(2)}, u32[]{:S(2)}) %collective-permute-start.3) | collective-permute-done | bytes 262176 | tf_op jit(solution)/shard_map/ppermute | solution.py:17
  84.5 0.0 collective-permute-start.20
  84.5 0.0 collective-permute-done.21.refs_13_
  84.6 0.5 collective-permute-start.22
  85.1 0.0 collective-permute-done.23.refs_15_
  85.1 0.1 collective-permute-start.13
  85.1 0.0 collective-permute-done.14.refs_5_
  85.2 0.4 collective-permute-start.15
  85.6 0.0 collective-permute-done.16.refs_7_
  85.6 0.8 collective-permute-done.20.refs_12_
  86.4 0.4 collective-permute-done.22.refs_14_
  86.8 0.4 collective-permute-done.13.refs_4_
  87.2 0.4 collective-permute-done.15.refs_6_
  87.5 0.0 copy-done.13
  87.6 7.1 %shard_map.133 = (bf16[16,8,2048]{2,1,0:T(8,128)(2,1)}, f32[8,2048]{1,0:T(8,128)}, f32[8,2048]{1,0:T(8,128)}) custom-call(s32[4,1,16,4]{3,2,1,0:T(8,128)} %copy.15.bi_ref, bf16[128,1024]{1,0:T(8,128)(2,1)} %copy-done.11, bf16[128,1024]{1,0:T(8,128)(2,1)} %collective-permute-done.11.refs_1_, bf16[128,1024]{1,0:T(8,128)(2,1)} %collective-permute-done.3.refs_2_, ...), custom_call_target="tpu_custom_call" | custom-call | tf_op jit(solution)/shard_map/pallas_call | solution.py:194
  (21 shorter events, 0.0 us)
Async XLA Ops:
  0.6 86.9 %copy-start.4 = (f32[2048]{0:T(1024)S(1)}, f32[2048]{0:T(1024)}, u32[]{:S(2)}) copy-start(f32[2048]{0:T(1024)} %param.16) | copy-start | bytes 24580
  0.6 86.9 %copy-start.5 = (f32[2048]{0:T(1024)S(1)}, f32[2048]{0:T(1024)}, u32[]{:S(2)}) copy-start(f32[2048]{0:T(1024)} %param.17) | copy-start | bytes 24580
  0.7 86.9 %copy-start.6 = (f32[2048]{0:T(1024)S(1)}, f32[2048]{0:T(1024)}, u32[]{:S(2)}) copy-start(f32[2048]{0:T(1024)} %param.18) | copy-start | bytes 24580
  0.7 86.9 %copy-start = (f32[16,8,2048]{2,1,0:T(8,128)S(1)}, f32[16,8,2048]{2,1,0:T(8,128)}, u32[]{:S(2)}) copy-start(f32[16,8,2048]{2,1,0:T(8,128)} %refs_18_.1) | copy-start | bytes 3145732
  0.7 86.9 %copy-start.1 = (f32[16,8,2048]{2,1,0:T(8,128)S(1)}, f32[16,8,2048]{2,1,0:T(8,128)}, u32[]{:S(2)}) copy-start(f32[16,8,2048]{2,1,0:T(8,128)} %refs_19_.1) | copy-start | bytes 3145732
  0.7 86.9 %copy-start.2 = (f32[8,2048]{1,0:T(8,128)S(1)}, f32[8,2048]{1,0:T(8,128)}, u32[]{:S(2)}) copy-start(f32[8,2048]{1,0:T(8,128)} %refs_20_.1) | copy-start | bytes 196612
  0.7 86.9 %copy-start.3 = (f32[8,2048]{1,0:T(8,128)S(1)}, f32[8,2048]{1,0:T(8,128)}, u32[]{:S(2)}) copy-start(f32[8,2048]{1,0:T(8,128)} %refs_21_.1) | copy-start | bytes 196612
  3.3 26.3 %collective-permute-start = (bf16[128,2048]{1,0:T(8,128)(2,1)}, bf16[128,2048]{1,0:T(8,128)(2,1)S(1)}, u32[]{:S(2)}, u32[]{:S(2)}) collective-permute-start(bf16[128,2048]{1,0:T(8,128)(2,1)} %get-tuple-element.23), channel_id=1, source_target_pairs={{0,4},{4,0},{8,12},{12,8},{1,5},{5,1},{9,13},{13,9},{2,6},{6,2},{1... | collective-permute-start | bytes 1572872 | tf_op jit(solution)/shard_map/ppermute | solution.py:17
  6.3 25.8 %collective-permute-start.1 = (bf16[128,2048]{1,0:T(8,128)(2,1)}, bf16[128,2048]{1,0:T(8,128)(2,1)S(1)}, u32[]{:S(2)}, u32[]{:S(2)}) collective-permute-start(bf16[128,2048]{1,0:T(8,128)(2,1)} %get-tuple-element.24), channel_id=1, source_target_pairs={{0,8},{4,12},{8,0},{12,4},{1,9},{5,13},{9,1},{13,5},{2,10},{6,14},... | collective-permute-start | bytes 1572872 | tf_op jit(solution)/shard_map/ppermute | solution.py:17
  29.6 39.7 %copy-start.7 = (bf16[128,2048]{1,0:T(8,128)(2,1)}, bf16[128,2048]{1,0:T(8,128)(2,1)S(1)}, u32[]{:S(2)}) copy-start(bf16[128,2048]{1,0:T(8,128)(2,1)S(1)} %collective-permute-done.refs_0_) | copy-start | bytes 1572868
  32.1 37.2 %copy-start.8 = (bf16[128,2048]{1,0:T(8,128)(2,1)}, bf16[128,2048]{1,0:T(8,128)(2,1)S(1)}, u32[]{:S(2)}) copy-start(bf16[128,2048]{1,0:T(8,128)(2,1)S(1)} %collective-permute-done.1.refs_4_) | copy-start | bytes 1572868
  32.1 15.6 %collective-permute-start.4 = (bf16[128,2048]{1,0:T(8,128)(2,1)S(1)}, bf16[128,2048]{1,0:T(8,128)(2,1)}, u32[]{:S(2)}, u32[]{:S(2)}) collective-permute-start(bf16[128,2048]{1,0:T(8,128)(2,1)S(1)} %collective-permute-done.refs_0_), channel_id=1, source_target_pairs={{0,2},{1,3},{2,0},{3,1},{4,6},{5,7},{6,4},{7,5},{8,10},{9,11},{10,... | collective-permute-start | bytes 1572872 | tf_op jit(solution)/shard_map/ppermute | solution.py:17
  33.6 11.4 %collective-permute-start.10 = (bf16[128,1024]{1,0:T(8,128)(2,1)}, bf16[128,1024]{1,0:T(8,128)(2,1)S(1)}, u32[]{:S(2)}, u32[]{:S(2)}) collective-permute-start(bf16[128,1024]{1,0:T(8,128)(2,1)} %get-tuple-element.29), channel_id=1, source_target_pairs={{0,8},{4,12},{8,0},{12,4},{1,9},{5,13},{9,1},{13,5},{2,10},{6,14},... | collective-permute-start | bytes 786440 | tf_op jit(solution)/shard_map/ppermute | solution.py:17
  33.9 20.2 %collective-permute-start.7 = (bf16[128,2048]{1,0:T(8,128)(2,1)S(1)}, bf16[128,2048]{1,0:T(8,128)(2,1)}, u32[]{:S(2)}, u32[]{:S(2)}) collective-permute-start(bf16[128,2048]{1,0:T(8,128)(2,1)S(1)} %collective-permute-done.1.refs_4_), channel_id=1, source_target_pairs={{0,2},{1,3},{2,0},{3,1},{4,6},{5,7},{6,4},{7,5},{8,10},{9,11},{10,... | collective-permute-start | bytes 1572872 | tf_op jit(solution)/shard_map/ppermute | solution.py:17
  34.5 10.7 %collective-permute-start.2 = (bf16[128,1024]{1,0:T(8,128)(2,1)}, bf16[128,1024]{1,0:T(8,128)(2,1)S(1)}, u32[]{:S(2)}, u32[]{:S(2)}) collective-permute-start(bf16[128,1024]{1,0:T(8,128)(2,1)} %get-tuple-element.25), channel_id=1, source_target_pairs={{0,4},{4,0},{8,12},{12,8},{1,5},{5,1},{9,13},{13,9},{2,6},{6,2},{1... | collective-permute-start | bytes 786440 | tf_op jit(solution)/shard_map/ppermute | solution.py:17
  37.2 21.5 %collective-permute-start.5 = (bf16[128,2048]{1,0:T(8,128)(2,1)S(1)}, bf16[128,2048]{1,0:T(8,128)(2,1)S(1)}, u32[]{:S(2)}, u32[]{:S(2)}) collective-permute-start(bf16[128,2048]{1,0:T(8,128)(2,1)S(1)} %collective-permute-done.refs_0_), channel_id=1, source_target_pairs={{0,1},{1,0},{2,3},{3,2},{4,5},{5,4},{6,7},{7,6},{8,9},{9,8},{10,11... | collective-permute-start | bytes 1572872 | tf_op jit(solution)/shard_map/ppermute | solution.py:17
  45.0 14.9 %copy-start.10 = (bf16[128,1024]{1,0:T(8,128)(2,1)}, bf16[128,1024]{1,0:T(8,128)(2,1)S(1)}, u32[]{:S(2)}) copy-start(bf16[128,1024]{1,0:T(8,128)(2,1)S(1)} %collective-permute-done.10.refs_8_) | copy-start | bytes 786436
  45.1 20.3 %copy-start.11 = (bf16[128,1024]{1,0:T(8,128)(2,1)}, bf16[128,1024]{1,0:T(8,128)(2,1)S(1)}, u32[]{:S(2)}) copy-start(bf16[128,1024]{1,0:T(8,128)(2,1)S(1)} %collective-permute-done.2.refs_0_) | copy-start | bytes 786436
  45.1 12.8 %collective-permute-start.18 = (bf16[128,1024]{1,0:T(8,128)(2,1)}, bf16[128,1024]{1,0:T(8,128)(2,1)}, u32[]{:S(2)}, u32[]{:S(2)}) collective-permute-start(bf16[128,1024]{1,0:T(8,128)(2,1)} %get-tuple-element.35), channel_id=1, source_target_pairs={{0,8},{4,12},{8,0},{12,4},{1,9},{5,13},{9,1},{13,5},{2,10},{6,14},... | collective-permute-start | bytes 786440 | tf_op jit(solution)/shard_map/ppermute | solution.py:17
  47.6 19.6 %collective-permute-start.8 = (bf16[128,2048]{1,0:T(8,128)(2,1)S(1)}, bf16[128,2048]{1,0:T(8,128)(2,1)}, u32[]{:S(2)}, u32[]{:S(2)}) collective-permute-start(bf16[128,2048]{1,0:T(8,128)(2,1)S(1)} %collective-permute-done.1.refs_4_), channel_id=1, source_target_pairs={{0,1},{1,0},{2,3},{3,2},{4,5},{5,4},{6,7},{7,6},{8,9},{9,8},{10,11... | collective-permute-start | bytes 1572872 | tf_op jit(solution)/shard_map/ppermute | solution.py:17
  47.7 21.2 %collective-permute-start.6 = (bf16[128,2048]{1,0:T(8,128)(2,1)}, bf16[128,2048]{1,0:T(8,128)(2,1)}, u32[]{:S(2)}, u32[]{:S(2)}) collective-permute-start(bf16[128,2048]{1,0:T(8,128)(2,1)} %collective-permute-done.4.refs_1_), channel_id=1, source_target_pairs={{0,1},{1,0},{2,3},{3,2},{4,5},{5,4},{6,7},{7,6},{8,9},{9,8},{10,11... | collective-permute-start | bytes 1572872 | tf_op jit(solution)/shard_map/ppermute | solution.py:17
  54.1 15.2 %collective-permute-start.9 = (bf16[128,2048]{1,0:T(8,128)(2,1)}, bf16[128,2048]{1,0:T(8,128)(2,1)}, u32[]{:S(2)}, u32[]{:S(2)}) collective-permute-start(bf16[128,2048]{1,0:T(8,128)(2,1)} %collective-permute-done.7.refs_5_), channel_id=1, source_target_pairs={{0,1},{1,0},{2,3},{3,2},{4,5},{5,4},{6,7},{7,6},{8,9},{9,8},{10,11... | collective-permute-start | bytes 1572872 | tf_op jit(solution)/shard_map/ppermute | solution.py:17
  57.9 7.5 %collective-permute-start.11 = (bf16[128,1024]{1,0:T(8,128)(2,1)}, bf16[128,1024]{1,0:T(8,128)(2,1)}, u32[]{:S(2)}, u32[]{:S(2)}) collective-permute-start(bf16[128,1024]{1,0:T(8,128)(2,1)} %get-tuple-element.30), channel_id=1, source_target_pairs={{0,4},{4,0},{8,12},{12,8},{1,5},{5,1},{9,13},{13,9},{2,6},{6,2},{1... | collective-permute-start | bytes 786440 | tf_op jit(solution)/shard_map/ppermute | solution.py:17
  58.6 0.8 copy-start.9
  59.4 16.4 %collective-permute-start.19 = (bf16[128,1024]{1,0:T(8,128)(2,1)}, bf16[128,1024]{1,0:T(8,128)(2,1)}, u32[]{:S(2)}, u32[]{:S(2)}) collective-permute-start(bf16[128,1024]{1,0:T(8,128)(2,1)} %collective-permute-done.18.refs_9_), channel_id=1, source_target_pairs={{0,2},{1,3},{2,0},{3,1},{4,6},{5,7},{6,4},{7,5},{8,10},{9,11},{10,... | collective-permute-start | bytes 786440 | tf_op jit(solution)/shard_map/ppermute | solution.py:17
  65.4 11.0 %collective-permute-start.12 = (bf16[128,1024]{1,0:T(8,128)(2,1)}, bf16[128,1024]{1,0:T(8,128)(2,1)}, u32[]{:S(2)}, u32[]{:S(2)}) collective-permute-start(bf16[128,1024]{1,0:T(8,128)(2,1)} %collective-permute-done.11.refs_1_), channel_id=1, source_target_pairs={{0,2},{1,3},{2,0},{3,1},{4,6},{5,7},{6,4},{7,5},{8,10},{9,11},{10,... | collective-permute-start | bytes 786440 | tf_op jit(solution)/shard_map/ppermute | solution.py:17
  67.2 13.4 %collective-permute-start.17 = (bf16[128,1024]{1,0:T(8,128)(2,1)}, bf16[128,1024]{1,0:T(8,128)(2,1)}, u32[]{:S(2)}, u32[]{:S(2)}) collective-permute-start(bf16[128,1024]{1,0:T(8,128)(2,1)} %copy-done.10), channel_id=1, source_target_pairs={{0,2},{1,3},{2,0},{3,1},{4,6},{5,7},{6,4},{7,5},{8,10},{9,11},{10,... | collective-permute-start | bytes 786440 | tf_op jit(solution)/shard_map/ppermute | solution.py:17
  68.9 15.7 %collective-permute-start.3 = (bf16[128,1024]{1,0:T(8,128)(2,1)}, bf16[128,1024]{1,0:T(8,128)(2,1)}, u32[]{:S(2)}, u32[]{:S(2)}) collective-permute-start(bf16[128,1024]{1,0:T(8,128)(2,1)} %copy-done.11), channel_id=1, source_target_pairs={{0,2},{1,3},{2,0},{3,1},{4,6},{5,7},{6,4},{7,5},{8,10},{9,11},{10,... | collective-permute-start | bytes 786440 | tf_op jit(solution)/shard_map/ppermute | solution.py:17
  75.9 8.7 %collective-permute-start.21 = (bf16[128,1024]{1,0:T(8,128)(2,1)}, bf16[128,1024]{1,0:T(8,128)(2,1)S(1)}, u32[]{:S(2)}, u32[]{:S(2)}) collective-permute-start(bf16[128,1024]{1,0:T(8,128)(2,1)} %collective-permute-done.18.refs_9_), channel_id=1, source_target_pairs={{0,1},{1,0},{2,3},{3,2},{4,5},{5,4},{6,7},{7,6},{8,9},{9,8},{10,11... | collective-permute-start | bytes 786440 | tf_op jit(solution)/shard_map/ppermute | solution.py:17
  75.9 9.1 %collective-permute-start.23 = (bf16[128,1024]{1,0:T(8,128)(2,1)}, bf16[128,1024]{1,0:T(8,128)(2,1)S(1)}, u32[]{:S(2)}, u32[]{:S(2)}) collective-permute-start(bf16[128,1024]{1,0:T(8,128)(2,1)} %collective-permute-done.19.refs_11_), channel_id=1, source_target_pairs={{0,1},{1,0},{2,3},{3,2},{4,5},{5,4},{6,7},{7,6},{8,9},{9,8},{10,11... | collective-permute-start | bytes 786440 | tf_op jit(solution)/shard_map/ppermute | solution.py:17
  76.4 8.7 %collective-permute-start.14 = (bf16[128,1024]{1,0:T(8,128)(2,1)}, bf16[128,1024]{1,0:T(8,128)(2,1)S(1)}, u32[]{:S(2)}, u32[]{:S(2)}) collective-permute-start(bf16[128,1024]{1,0:T(8,128)(2,1)} %collective-permute-done.11.refs_1_), channel_id=1, source_target_pairs={{0,1},{1,0},{2,3},{3,2},{4,5},{5,4},{6,7},{7,6},{8,9},{9,8},{10,11... | collective-permute-start | bytes 786440 | tf_op jit(solution)/shard_map/ppermute | solution.py:17
  80.6 5.0 %collective-permute-start.16 = (bf16[128,1024]{1,0:T(8,128)(2,1)}, bf16[128,1024]{1,0:T(8,128)(2,1)S(1)}, u32[]{:S(2)}, u32[]{:S(2)}) collective-permute-start(bf16[128,1024]{1,0:T(8,128)(2,1)} %collective-permute-done.12.refs_3_), channel_id=1, source_target_pairs={{0,1},{1,0},{2,3},{3,2},{4,5},{5,4},{6,7},{7,6},{8,9},{9,8},{10,11... | collective-permute-start | bytes 786440 | tf_op jit(solution)/shard_map/ppermute | solution.py:17
  84.5 1.9 %collective-permute-start.20 = (bf16[128,1024]{1,0:T(8,128)(2,1)}, bf16[128,1024]{1,0:T(8,128)(2,1)}, u32[]{:S(2)}, u32[]{:S(2)}) collective-permute-start(bf16[128,1024]{1,0:T(8,128)(2,1)} %copy-done.10), channel_id=1, source_target_pairs={{0,1},{1,0},{2,3},{3,2},{4,5},{5,4},{6,7},{7,6},{8,9},{9,8},{10,11... | collective-permute-start | bytes 786440 | tf_op jit(solution)/shard_map/ppermute | solution.py:17
  84.5 3.0 %copy-start.12 = (bf16[128,1024]{1,0:T(8,128)(2,1)}, bf16[128,1024]{1,0:T(8,128)(2,1)S(1)}, u32[]{:S(2)}) copy-start(bf16[128,1024]{1,0:T(8,128)(2,1)S(1)} %collective-permute-done.21.refs_13_) | copy-start | bytes 786436
  84.6 2.2 %collective-permute-start.22 = (bf16[128,1024]{1,0:T(8,128)(2,1)}, bf16[128,1024]{1,0:T(8,128)(2,1)}, u32[]{:S(2)}, u32[]{:S(2)}) collective-permute-start(bf16[128,1024]{1,0:T(8,128)(2,1)} %collective-permute-done.17.refs_10_), channel_id=1, source_target_pairs={{0,1},{1,0},{2,3},{3,2},{4,5},{5,4},{6,7},{7,6},{8,9},{9,8},{10,11... | collective-permute-start | bytes 786440 | tf_op jit(solution)/shard_map/ppermute | solution.py:17
  85.1 2.5 %copy-start.13 = (bf16[128,1024]{1,0:T(8,128)(2,1)}, bf16[128,1024]{1,0:T(8,128)(2,1)S(1)}, u32[]{:S(2)}) copy-start(bf16[128,1024]{1,0:T(8,128)(2,1)S(1)} %collective-permute-done.23.refs_15_) | copy-start | bytes 786436
  85.1 2.1 %collective-permute-start.13 = (bf16[128,1024]{1,0:T(8,128)(2,1)}, bf16[128,1024]{1,0:T(8,128)(2,1)}, u32[]{:S(2)}, u32[]{:S(2)}) collective-permute-start(bf16[128,1024]{1,0:T(8,128)(2,1)} %copy-done.11), channel_id=1, source_target_pairs={{0,1},{1,0},{2,3},{3,2},{4,5},{5,4},{6,7},{7,6},{8,9},{9,8},{10,11... | collective-permute-start | bytes 786440 | tf_op jit(solution)/shard_map/ppermute | solution.py:17
  85.2 2.4 %copy-start.14 = (bf16[128,1024]{1,0:T(8,128)(2,1)}, bf16[128,1024]{1,0:T(8,128)(2,1)S(1)}, u32[]{:S(2)}) copy-start(bf16[128,1024]{1,0:T(8,128)(2,1)S(1)} %collective-permute-done.14.refs_5_) | copy-start | bytes 786436
  85.2 2.4 %collective-permute-start.15 = (bf16[128,1024]{1,0:T(8,128)(2,1)}, bf16[128,1024]{1,0:T(8,128)(2,1)}, u32[]{:S(2)}, u32[]{:S(2)}) collective-permute-start(bf16[128,1024]{1,0:T(8,128)(2,1)} %collective-permute-done.3.refs_2_), channel_id=1, source_target_pairs={{0,1},{1,0},{2,3},{3,2},{4,5},{5,4},{6,7},{7,6},{8,9},{9,8},{10,11... | collective-permute-start | bytes 786440 | tf_op jit(solution)/shard_map/ppermute | solution.py:17
  85.6 2.0 %copy-start.15 = (bf16[128,1024]{1,0:T(8,128)(2,1)}, bf16[128,1024]{1,0:T(8,128)(2,1)S(1)}, u32[]{:S(2)}) copy-start(bf16[128,1024]{1,0:T(8,128)(2,1)S(1)} %collective-permute-done.16.refs_7_) | copy-start | bytes 786436

commit v16 on v11

--- a/solution.py
+++ b/solution.py
@@ -64,8 +64,6 @@
     w_buf = next(it)
     sem = next(it)
     rec_buf = next(it)
-    if final:
-        scan_buf = [next(it) for _ in range(7)]
 
     steps, batch = rec_buf.shape[0], rec_buf.shape[1]
     local_blocks, nnz, side = w_buf.shape[1], w_buf.shape[2], w_buf.shape[3]
@@ -83,14 +81,11 @@
 
     piece_cp, w_cp = [], []
     rec_cp = None
-    scan_cp = []
     for ri, rnd in enumerate(stage):
         piece_cp += [start(piece_hbm[ri * n_pos + p], piece_buf.at[ri * n_pos + p]) for p in range(n_pos)]
         w_cp.append(start(w_hbm.at[rnd, 0], w_buf.at[ri]))
         if ri == 0 and has_rec:
             rec_cp = start(rec_hbm, rec_buf)
-    if final:
-        scan_cp = [start(src, dst) for src, dst in zip(scan_hbm, scan_buf)]
 
     for ri, rnd in enumerate(stage):
         for p in range(n_pos):
@@ -100,9 +95,7 @@
             rec_cp.wait()
         last = ri == n_rounds - 1
         if last and final:
-            for copy in scan_cp:
-                copy.wait()
-            err_buf, surr_buf, lv_buf, la_buf, alpha_buf, rho_buf, beta_buf = scan_buf
+            err_buf, surr_buf, lv_buf, la_buf, alpha_buf, rho_buf, beta_buf = scan_hbm
         for j in range(local_blocks):
             cols = slice(j * side, (j + 1) * side)
             if ri == 0 and not has_rec:
@@ -153,7 +146,7 @@
         pltpu.VMEM((len(pieces), rows, local), pieces[0].dtype),
         pltpu.VMEM((n_rounds, local_blocks, nnz, side, side), weights.dtype),
     ]
-    n_sem = len(pieces) + n_rounds + (1 if has_rec else 0) + (7 if final else 0)
+    n_sem = len(pieces) + n_rounds + (1 if has_rec else 0)
     scratch.append(pltpu.SemaphoreType.DMA((n_sem,)))
     scratch.append(pltpu.VMEM((steps, batch, local), jnp.float32))
     if has_rec:
@@ -163,7 +156,6 @@
         rows = [a.reshape(1, local) for a in (alpha, rho, beta)]
         extra = [err_grad, surrogate, lv_end, la_end] + rows
         operands += extra
-        scratch += [pltpu.VMEM(a.shape, a.dtype) for a in extra]
         out_specs = (VMEM, VMEM, VMEM)
         out_shape = (
             jax.ShapeDtypeStruct((steps, batch, local), jnp.bfloat16),

time: 92.5 us -> 92.4 us (level)
  no operation moved by 1% of the time
where the time goes in v16:
time: 92.4 us; the launch traced here: 92 us
  waiting for transfers between devices  54.4 us (59%)
  Pallas kernels  18.7 us (20%)
  starting transfers between devices  16 us (17%)
  local copies, waits for them, and re-layouts  2.25 us (2%)
    ppermute x16, waiting for transfers between devices, swap(): return lax.ppermute(value, axis, pairs)  54.4 us
    ppermute x16, starting transfers between devices, swap(): return lax.ppermute(value, axis, pairs)  16 us
    pallas_call x2, Pallas kernels, stage_contrib(): pl.pallas_call(kernel, in_specs=[SMEM] + specs, out_specs=out_specs, scra...  13.5 us
    pallas_call x2, Pallas kernels, send_slices(): pl.pallas_call(kernel, in_specs=[SMEM, VMEM], out_specs=[VMEM] * len(roun...  5.12 us
    unnamed x29, local copies, waits for them, and re-layouts  2.25 us
  transfers between devices with their start and end apart: 16, of which 10 were waited for; matrix products, arithmetic and copies ran while one was open for 2% of the time, Pallas kernels for 10%

profile of v16, /device:TPU:0, one launch (start us, length us, event | category | flops | bytes accessed | tf_op | source)
XLA Modules:
  0.0 92.0 jit_solution(13486490507763843412)
XLA Ops:
  0.6 0.0 copy-start.6
  0.6 0.0 copy-start.5
  0.7 0.0 copy-start.4
  0.7 0.0 copy-start.3
  0.7 0.0 copy-start.2
  0.7 0.0 copy-start.1
  0.7 0.0 copy-start
  0.7 2.7 %shard_map.131 = (bf16[128,2048]{1,0:T(8,128)(2,1)}, bf16[128,2048]{1,0:T(8,128)(2,1)}) custom-call(s32[4,4]{1,0:T(4,128)} %delays_ref.3, bf16[32,8,2048]{2,1,0:T(8,128)(2,1)} %window_ref.3), custom_call_target="tpu_custom_call" | custom-call | tf_op jit(solution)/shard_map/pallas_call | solution.py:34
  3.4 3.0 %collective-permute-start = (bf16[128,2048]{1,0:T(8,128)(2,1)}, bf16[128,2048]{1,0:T(8,128)(2,1)}, u32[]{:S(2)}, u32[]{:S(2)}) collective-permute-start(bf16[128,2048]{1,0:T(8,128)(2,1)} %get-tuple-element.15), channel_id=1, source_target_pairs={{0,4},{4,0},{8,12},{12,8},{1,5},{5,1},{9,13},{13,9},{2,6},{6,2},{1... | collective-permute-start | bytes 1572872 | tf_op jit(solution)/shard_map/ppermute | solution.py:17
  6.4 2.6 %collective-permute-start.1 = (bf16[128,2048]{1,0:T(8,128)(2,1)}, bf16[128,2048]{1,0:T(8,128)(2,1)}, u32[]{:S(2)}, u32[]{:S(2)}) collective-permute-start(bf16[128,2048]{1,0:T(8,128)(2,1)} %get-tuple-element.16), channel_id=1, source_target_pairs={{0,8},{4,12},{8,0},{12,4},{1,9},{5,13},{9,1},{13,5},{2,10},{6,14},... | collective-permute-start | bytes 1572872 | tf_op jit(solution)/shard_map/ppermute | solution.py:17
  9.0 2.5 %shard_map.130 = (bf16[128,2048]{1,0:T(8,128)(2,1)}, bf16[128,2048]{1,0:T(8,128)(2,1)}) custom-call(s32[4,4]{1,0:T(4,128)} %delays_ref.3, bf16[32,8,2048]{2,1,0:T(8,128)(2,1)} %window_ref.3), custom_call_target="tpu_custom_call" | custom-call | tf_op jit(solution)/shard_map/pallas_call | solution.py:34
  11.4 18.3 %collective-permute-done.refs_0_ = bf16[128,2048]{1,0:T(8,128)(2,1)} collective-permute-done((bf16[128,2048]{1,0:T(8,128)(2,1)}, bf16[128,2048]{1,0:T(8,128)(2,1)}, u32[]{:S(2)}, u32[]{:S(2)}) %collective-permute-start) | collective-permute-done | bytes 524320 | tf_op jit(solution)/shard_map/ppermute | solution.py:17
  29.7 0.0 collective-permute-start.5
  29.7 1.7 %collective-permute-start.4 = (bf16[128,2048]{1,0:T(8,128)(2,1)}, bf16[128,2048]{1,0:T(8,128)(2,1)}, u32[]{:S(2)}, u32[]{:S(2)}) collective-permute-start(bf16[128,2048]{1,0:T(8,128)(2,1)} %collective-permute-done.refs_0_), channel_id=1, source_target_pairs={{0,2},{1,3},{2,0},{3,1},{4,6},{5,7},{6,4},{7,5},{8,10},{9,11},{10,... | collective-permute-start | bytes 1572872 | tf_op jit(solution)/shard_map/ppermute | solution.py:17
  31.4 0.9 collective-permute-done.1.refs_4_
  32.3 1.5 %collective-permute-start.7 = (bf16[128,2048]{1,0:T(8,128)(2,1)}, bf16[128,2048]{1,0:T(8,128)(2,1)}, u32[]{:S(2)}, u32[]{:S(2)}) collective-permute-start(bf16[128,2048]{1,0:T(8,128)(2,1)} %collective-permute-done.1.refs_4_), channel_id=1, source_target_pairs={{0,2},{1,3},{2,0},{3,1},{4,6},{5,7},{6,4},{7,5},{8,10},{9,11},{10,... | collective-permute-start | bytes 1572872 | tf_op jit(solution)/shard_map/ppermute | solution.py:17
  33.8 0.4 collective-permute-start.2
  34.2 2.6 %collective-permute-start.12 = (bf16[128,2048]{1,0:T(8,128)(2,1)}, bf16[128,2048]{1,0:T(8,128)(2,1)S(1)}, u32[]{:S(2)}, u32[]{:S(2)}) collective-permute-start(bf16[128,2048]{1,0:T(8,128)(2,1)} %get-tuple-element.20), channel_id=1, source_target_pairs={{0,8},{4,12},{8,0},{12,4},{1,9},{5,13},{9,1},{13,5},{2,10},{6,14},... | collective-permute-start | bytes 1572872 | tf_op jit(solution)/shard_map/ppermute | solution.py:17
  36.8 0.0 collective-permute-done.5.refs_2_
  36.8 0.0 copy-start.13
  36.8 0.0 collective-permute-start.8
  36.8 8.0 %collective-permute-done.4.refs_1_ = bf16[128,2048]{1,0:T(8,128)(2,1)} collective-permute-done((bf16[128,2048]{1,0:T(8,128)(2,1)}, bf16[128,2048]{1,0:T(8,128)(2,1)}, u32[]{:S(2)}, u32[]{:S(2)}) %collective-permute-start.4) | collective-permute-done | bytes 524320 | tf_op jit(solution)/shard_map/ppermute | solution.py:17
  44.8 0.0 collective-permute-start.6
  44.8 10.8 %collective-permute-done.7.refs_5_ = bf16[128,2048]{1,0:T(8,128)(2,1)} collective-permute-done((bf16[128,2048]{1,0:T(8,128)(2,1)}, bf16[128,2048]{1,0:T(8,128)(2,1)}, u32[]{:S(2)}, u32[]{:S(2)}) %collective-permute-start.7) | collective-permute-done | bytes 524320 | tf_op jit(solution)/shard_map/ppermute | solution.py:17
  55.6 0.0 collective-permute-start.9
  55.6 0.6 collective-permute-done.2.refs_0_
  56.2 0.0 copy-start.7
  56.2 2.2 %collective-permute-start.3 = (bf16[128,2048]{1,0:T(8,128)(2,1)S(1)}, bf16[128,2048]{1,0:T(8,128)(2,1)}, u32[]{:S(2)}, u32[]{:S(2)}) collective-permute-start(bf16[128,2048]{1,0:T(8,128)(2,1)S(1)} %collective-permute-done.2.refs_0_), channel_id=1, source_target_pairs={{0,2},{1,3},{2,0},{3,1},{4,6},{5,7},{6,4},{7,5},{8,10},{9,11},{10,... | collective-permute-start | bytes 1572872 | tf_op jit(solution)/shard_map/ppermute | solution.py:17
  58.4 0.3 collective-permute-done.12.refs_4_
  58.8 0.0 copy-done.13
  58.8 0.0 copy-start.8
  58.8 0.9 %collective-permute-start.13 = (bf16[128,2048]{1,0:T(8,128)(2,1)S(1)}, bf16[128,2048]{1,0:T(8,128)(2,1)}, u32[]{:S(2)}, u32[]{:S(2)}) collective-permute-start(bf16[128,2048]{1,0:T(8,128)(2,1)S(1)} %collective-permute-done.12.refs_4_), channel_id=1, source_target_pairs={{0,2},{1,3},{2,0},{3,1},{4,6},{5,7},{6,4},{7,5},{8,10},{9,11},{10,... | collective-permute-start | bytes 1572872 | tf_op jit(solution)/shard_map/ppermute | solution.py:17
  59.7 1.4 %copy.15.bi_ref = s32[4,1,16,4]{3,2,1,0:T(8,128)} copy(s32[4,1,16,4]{2,3,1,0:T(4,128)} %param.20) | data formatting | bytes 2048 | tf_op args[9]
  61.1 0.0 collective-permute-done.8.refs_6_
  61.1 0.0 collective-permute-done.6.refs_3_
  61.1 0.0 collective-permute-done.9.refs_7_
  61.1 6.6 %shard_map.132.refs_9_ = f32[16,8,2048]{2,1,0:T(8,128)} custom-call(s32[4,1,16,4]{3,2,1,0:T(8,128)} %copy.15.bi_ref, bf16[128,2048]{1,0:T(8,128)(2,1)} %collective-permute-done.refs_0_, bf16[128,2048]{1,0:T(8,128)(2,1)} %collective-permute-done.4.refs_1_, bf16[128,2048]{1,0:T(8,128)(2,1)} %copy-done.13, bf16[128,2048]{1,0:T(8,128)(2,1)} %collective-permute-done.6.refs_3_, ...), custom_call_target="tpu_custom_call" | custom-call | tf_op jit(solution)/shard_map/pallas_call | solution.py:176
  67.7 3.6 %collective-permute-done.3.refs_1_ = bf16[128,2048]{1,0:T(8,128)(2,1)} collective-permute-done((bf16[128,2048]{1,0:T(8,128)(2,1)S(1)}, bf16[128,2048]{1,0:T(8,128)(2,1)}, u32[]{:S(2)}, u32[]{:S(2)}) %collective-permute-start.3) | collective-permute-done | bytes 524320 | tf_op jit(solution)/shard_map/ppermute | solution.py:17
  71.3 0.0 collective-permute-start.10
  71.3 0.5 collective-permute-start.11
  71.8 9.5 %collective-permute-done.13.refs_5_ = bf16[128,2048]{1,0:T(8,128)(2,1)} collective-permute-done((bf16[128,2048]{1,0:T(8,128)(2,1)S(1)}, bf16[128,2048]{1,0:T(8,128)(2,1)}, u32[]{:S(2)}, u32[]{:S(2)}) %collective-permute-start.13) | collective-permute-done | bytes 524320 | tf_op jit(solution)/shard_map/ppermute | solution.py:17
  81.3 0.0 collective-permute-start.14
  81.3 0.5 collective-permute-start.15
  81.8 0.0 collective-permute-done.10.refs_2_
  81.8 0.0 copy-start.9
  81.8 0.0 collective-permute-done.11.refs_3_
  81.8 0.0 copy-start.10
  81.8 2.1 %collective-permute-done.14.refs_6_ = bf16[128,2048]{1,0:T(8,128)(2,1)S(1)} collective-permute-done((bf16[128,2048]{1,0:T(8,128)(2,1)S(1)}, bf16[128,2048]{1,0:T(8,128)(2,1)S(1)}, u32[]{:S(2)}, u32[]{:S(2)}) %collective-permute-start.14) | collective-permute-done | bytes 524320 | tf_op jit(solution)/shard_map/ppermute | solution.py:17
  83.9 0.0 copy-done.9
  83.9 0.0 copy-start.11
  83.9 0.2 collective-permute-done.15.refs_7_
  84.2 0.0 copy-done.10
  84.2 0.6 copy-done.11
  84.8 0.2 copy-done.12
  85.0 0.0 copy-done.7
  85.0 0.0 copy-done.8
  85.0 0.0 copy-done.6
  85.0 0.0 copy-done.5
  85.0 0.0 copy-done.4
  85.0 0.0 copy-done.3
  85.0 0.0 copy-done.2
  85.0 0.0 copy-done.1
  85.0 0.0 copy-done
  85.1 7.0 %shard_map.133 = (bf16[16,8,2048]{2,1,0:T(8,128)(2,1)}, f32[8,2048]{1,0:T(8,128)}, f32[8,2048]{1,0:T(8,128)}) custom-call(s32[4,1,16,4]{3,2,1,0:T(8,128)} %copy.15.bi_ref, bf16[128,2048]{1,0:T(8,128)(2,1)} %copy-done.7, bf16[128,2048]{1,0:T(8,128)(2,1)} %collective-permute-done.3.refs_1_, bf16[128,2048]{1,0:T(8,128)(2,1)} %copy-done.9, ...), custom_call_target="tpu_custom_call" | custom-call | tf_op jit(solution)/shard_map/pallas_call | solution.py:176
  (1 shorter events, 0.0 us)
Async XLA Ops:
  0.6 84.4 %copy-start.6 = (f32[2048]{0:T(1024)S(1)}, f32[2048]{0:T(1024)}, u32[]{:S(2)}) copy-start(f32[2048]{0:T(1024)} %param.18) | copy-start | bytes 24580
  0.6 84.4 %copy-start.5 = (f32[2048]{0:T(1024)S(1)}, f32[2048]{0:T(1024)}, u32[]{:S(2)}) copy-start(f32[2048]{0:T(1024)} %param.17) | copy-start | bytes 24580
  0.7 84.4 %copy-start.4 = (f32[2048]{0:T(1024)S(1)}, f32[2048]{0:T(1024)}, u32[]{:S(2)}) copy-start(f32[2048]{0:T(1024)} %param.16) | copy-start | bytes 24580
  0.7 84.4 %copy-start.3 = (f32[8,2048]{1,0:T(8,128)S(1)}, f32[8,2048]{1,0:T(8,128)}, u32[]{:S(2)}) copy-start(f32[8,2048]{1,0:T(8,128)} %refs_13_.1) | copy-start | bytes 196612
  0.7 84.4 %copy-start.2 = (f32[8,2048]{1,0:T(8,128)S(1)}, f32[8,2048]{1,0:T(8,128)}, u32[]{:S(2)}) copy-start(f32[8,2048]{1,0:T(8,128)} %refs_12_.1) | copy-start | bytes 196612
  0.7 84.4 %copy-start.1 = (f32[16,8,2048]{2,1,0:T(8,128)S(1)}, f32[16,8,2048]{2,1,0:T(8,128)}, u32[]{:S(2)}) copy-start(f32[16,8,2048]{2,1,0:T(8,128)} %refs_11_.1) | copy-start | bytes 3145732
  0.7 84.4 %copy-start = (f32[16,8,2048]{2,1,0:T(8,128)S(1)}, f32[16,8,2048]{2,1,0:T(8,128)}, u32[]{:S(2)}) copy-start(f32[16,8,2048]{2,1,0:T(8,128)} %refs_10_.1) | copy-start | bytes 3145732
  3.4 26.4 %collective-permute-start = (bf16[128,2048]{1,0:T(8,128)(2,1)}, bf16[128,2048]{1,0:T(8,128)(2,1)}, u32[]{:S(2)}, u32[]{:S(2)}) collective-permute-start(bf16[128,2048]{1,0:T(8,128)(2,1)} %get-tuple-element.15), channel_id=1, source_target_pairs={{0,4},{4,0},{8,12},{12,8},{1,5},{5,1},{9,13},{13,9},{2,6},{6,2},{1... | collective-permute-start | bytes 1572872 | tf_op jit(solution)/shard_map/ppermute | solution.py:17
  6.4 25.9 %collective-permute-start.1 = (bf16[128,2048]{1,0:T(8,128)(2,1)}, bf16[128,2048]{1,0:T(8,128)(2,1)}, u32[]{:S(2)}, u32[]{:S(2)}) collective-permute-start(bf16[128,2048]{1,0:T(8,128)(2,1)} %get-tuple-element.16), channel_id=1, source_target_pairs={{0,8},{4,12},{8,0},{12,4},{1,9},{5,13},{9,1},{13,5},{2,10},{6,14},... | collective-permute-start | bytes 1572872 | tf_op jit(solution)/shard_map/ppermute | solution.py:17
  29.7 7.1 %collective-permute-start.5 = (bf16[128,2048]{1,0:T(8,128)(2,1)}, bf16[128,2048]{1,0:T(8,128)(2,1)S(1)}, u32[]{:S(2)}, u32[]{:S(2)}) collective-permute-start(bf16[128,2048]{1,0:T(8,128)(2,1)} %collective-permute-done.refs_0_), channel_id=1, source_target_pairs={{0,1},{1,0},{2,3},{3,2},{4,5},{5,4},{6,7},{7,6},{8,9},{9,8},{10,11... | collective-permute-start | bytes 1572872 | tf_op jit(solution)/shard_map/ppermute | solution.py:17
  29.7 15.0 %collective-permute-start.4 = (bf16[128,2048]{1,0:T(8,128)(2,1)}, bf16[128,2048]{1,0:T(8,128)(2,1)}, u32[]{:S(2)}, u32[]{:S(2)}) collective-permute-start(bf16[128,2048]{1,0:T(8,128)(2,1)} %collective-permute-done.refs_0_), channel_id=1, source_target_pairs={{0,2},{1,3},{2,0},{3,1},{4,6},{5,7},{6,4},{7,5},{8,10},{9,11},{10,... | collective-permute-start | bytes 1572872 | tf_op jit(solution)/shard_map/ppermute | solution.py:17
  32.3 23.4 %collective-permute-start.7 = (bf16[128,2048]{1,0:T(8,128)(2,1)}, bf16[128,2048]{1,0:T(8,128)(2,1)}, u32[]{:S(2)}, u32[]{:S(2)}) collective-permute-start(bf16[128,2048]{1,0:T(8,128)(2,1)} %collective-permute-done.1.refs_4_), channel_id=1, source_target_pairs={{0,2},{1,3},{2,0},{3,1},{4,6},{5,7},{6,4},{7,5},{8,10},{9,11},{10,... | collective-permute-start | bytes 1572872 | tf_op jit(solution)/shard_map/ppermute | solution.py:17
  33.8 22.5 %collective-permute-start.2 = (bf16[128,2048]{1,0:T(8,128)(2,1)}, bf16[128,2048]{1,0:T(8,128)(2,1)S(1)}, u32[]{:S(2)}, u32[]{:S(2)}) collective-permute-start(bf16[128,2048]{1,0:T(8,128)(2,1)} %get-tuple-element.17), channel_id=1, source_target_pairs={{0,4},{4,0},{8,12},{12,8},{1,5},{5,1},{9,13},{13,9},{2,6},{6,2},{1... | collective-permute-start | bytes 1572872 | tf_op jit(solution)/shard_map/ppermute | solution.py:17
  34.2 24.6 %collective-permute-start.12 = (bf16[128,2048]{1,0:T(8,128)(2,1)}, bf16[128,2048]{1,0:T(8,128)(2,1)S(1)}, u32[]{:S(2)}, u32[]{:S(2)}) collective-permute-start(bf16[128,2048]{1,0:T(8,128)(2,1)} %get-tuple-element.20), channel_id=1, source_target_pairs={{0,8},{4,12},{8,0},{12,4},{1,9},{5,13},{9,1},{13,5},{2,10},{6,14},... | collective-permute-start | bytes 1572872 | tf_op jit(solution)/shard_map/ppermute | solution.py:17
  36.8 22.0 %copy-start.13 = (bf16[128,2048]{1,0:T(8,128)(2,1)}, bf16[128,2048]{1,0:T(8,128)(2,1)S(1)}, u32[]{:S(2)}) copy-start(bf16[128,2048]{1,0:T(8,128)(2,1)S(1)} %collective-permute-done.5.refs_2_) | copy-start | bytes 1572868
  36.8 24.3 %collective-permute-start.8 = (bf16[128,2048]{1,0:T(8,128)(2,1)}, bf16[128,2048]{1,0:T(8,128)(2,1)}, u32[]{:S(2)}, u32[]{:S(2)}) collective-permute-start(bf16[128,2048]{1,0:T(8,128)(2,1)} %collective-permute-done.1.refs_4_), channel_id=1, source_target_pairs={{0,1},{1,0},{2,3},{3,2},{4,5},{5,4},{6,7},{7,6},{8,9},{9,8},{10,11... | collective-permute-start | bytes 1572872 | tf_op jit(solution)/shard_map/ppermute | solution.py:17
  44.8 16.3 %collective-permute-start.6 = (bf16[128,2048]{1,0:T(8,128)(2,1)}, bf16[128,2048]{1,0:T(8,128)(2,1)}, u32[]{:S(2)}, u32[]{:S(2)}) collective-permute-start(bf16[128,2048]{1,0:T(8,128)(2,1)} %collective-permute-done.4.refs_1_), channel_id=1, source_target_pairs={{0,1},{1,0},{2,3},{3,2},{4,5},{5,4},{6,7},{7,6},{8,9},{9,8},{10,11... | collective-permute-start | bytes 1572872 | tf_op jit(solution)/shard_map/ppermute | solution.py:17
  55.6 5.5 %collective-permute-start.9 = (bf16[128,2048]{1,0:T(8,128)(2,1)}, bf16[128,2048]{1,0:T(8,128)(2,1)}, u32[]{:S(2)}, u32[]{:S(2)}) collective-permute-start(bf16[128,2048]{1,0:T(8,128)(2,1)} %collective-permute-done.7.refs_5_), channel_id=1, source_target_pairs={{0,1},{1,0},{2,3},{3,2},{4,5},{5,4},{6,7},{7,6},{8,9},{9,8},{10,11... | collective-permute-start | bytes 1572872 | tf_op jit(solution)/shard_map/ppermute | solution.py:17
  56.2 28.8 %copy-start.7 = (bf16[128,2048]{1,0:T(8,128)(2,1)}, bf16[128,2048]{1,0:T(8,128)(2,1)S(1)}, u32[]{:S(2)}) copy-start(bf16[128,2048]{1,0:T(8,128)(2,1)S(1)} %collective-permute-done.2.refs_0_) | copy-start | bytes 1572868
  56.2 15.1 %collective-permute-start.3 = (bf16[128,2048]{1,0:T(8,128)(2,1)S(1)}, bf16[128,2048]{1,0:T(8,128)(2,1)}, u32[]{:S(2)}, u32[]{:S(2)}) collective-permute-start(bf16[128,2048]{1,0:T(8,128)(2,1)S(1)} %collective-permute-done.2.refs_0_), channel_id=1, source_target_pairs={{0,2},{1,3},{2,0},{3,1},{4,6},{5,7},{6,4},{7,5},{8,10},{9,11},{10,... | collective-permute-start | bytes 1572872 | tf_op jit(solution)/shard_map/ppermute | solution.py:17
  58.8 26.2 %copy-start.8 = (bf16[128,2048]{1,0:T(8,128)(2,1)}, bf16[128,2048]{1,0:T(8,128)(2,1)S(1)}, u32[]{:S(2)}) copy-start(bf16[128,2048]{1,0:T(8,128)(2,1)S(1)} %collective-permute-done.12.refs_4_) | copy-start | bytes 1572868
  58.8 22.5 %collective-permute-start.13 = (bf16[128,2048]{1,0:T(8,128)(2,1)S(1)}, bf16[128,2048]{1,0:T(8,128)(2,1)}, u32[]{:S(2)}, u32[]{:S(2)}) collective-permute-start(bf16[128,2048]{1,0:T(8,128)(2,1)S(1)} %collective-permute-done.12.refs_4_), channel_id=1, source_target_pairs={{0,2},{1,3},{2,0},{3,1},{4,6},{5,7},{6,4},{7,5},{8,10},{9,11},{10,... | collective-permute-start | bytes 1572872 | tf_op jit(solution)/shard_map/ppermute | solution.py:17
  71.3 10.5 %collective-permute-start.10 = (bf16[128,2048]{1,0:T(8,128)(2,1)S(1)}, bf16[128,2048]{1,0:T(8,128)(2,1)S(1)}, u32[]{:S(2)}, u32[]{:S(2)}) collective-permute-start(bf16[128,2048]{1,0:T(8,128)(2,1)S(1)} %collective-permute-done.2.refs_0_), channel_id=1, source_target_pairs={{0,1},{1,0},{2,3},{3,2},{4,5},{5,4},{6,7},{7,6},{8,9},{9,8},{10,11... | collective-permute-start | bytes 1572872 | tf_op jit(solution)/shard_map/ppermute | solution.py:17
  71.3 10.5 %collective-permute-start.11 = (bf16[128,2048]{1,0:T(8,128)(2,1)}, bf16[128,2048]{1,0:T(8,128)(2,1)S(1)}, u32[]{:S(2)}, u32[]{:S(2)}) collective-permute-start(bf16[128,2048]{1,0:T(8,128)(2,1)} %collective-permute-done.3.refs_1_), channel_id=1, source_target_pairs={{0,1},{1,0},{2,3},{3,2},{4,5},{5,4},{6,7},{7,6},{8,9},{9,8},{10,11... | collective-permute-start | bytes 1572872 | tf_op jit(solution)/shard_map/ppermute | solution.py:17
  81.3 2.6 %collective-permute-start.14 = (bf16[128,2048]{1,0:T(8,128)(2,1)S(1)}, bf16[128,2048]{1,0:T(8,128)(2,1)S(1)}, u32[]{:S(2)}, u32[]{:S(2)}) collective-permute-start(bf16[128,2048]{1,0:T(8,128)(2,1)S(1)} %collective-permute-done.12.refs_4_), channel_id=1, source_target_pairs={{0,1},{1,0},{2,3},{3,2},{4,5},{5,4},{6,7},{7,6},{8,9},{9,8},{10,11... | collective-permute-start | bytes 1572872 | tf_op jit(solution)/shard_map/ppermute | solution.py:17
  81.3 2.9 %collective-permute-start.15 = (bf16[128,2048]{1,0:T(8,128)(2,1)}, bf16[128,2048]{1,0:T(8,128)(2,1)S(1)}, u32[]{:S(2)}, u32[]{:S(2)}) collective-permute-start(bf16[128,2048]{1,0:T(8,128)(2,1)} %collective-permute-done.13.refs_5_), channel_id=1, source_target_pairs={{0,1},{1,0},{2,3},{3,2},{4,5},{5,4},{6,7},{7,6},{8,9},{9,8},{10,11... | collective-permute-start | bytes 1572872 | tf_op jit(solution)/shard_map/ppermute | solution.py:17
  81.8 2.1 %copy-start.9 = (bf16[128,2048]{1,0:T(8,128)(2,1)}, bf16[128,2048]{1,0:T(8,128)(2,1)S(1)}, u32[]{:S(2)}) copy-start(bf16[128,2048]{1,0:T(8,128)(2,1)S(1)} %collective-permute-done.10.refs_2_) | copy-start | bytes 1572868
  81.8 2.4 %copy-start.10 = (bf16[128,2048]{1,0:T(8,128)(2,1)}, bf16[128,2048]{1,0:T(8,128)(2,1)S(1)}, u32[]{:S(2)}) copy-start(bf16[128,2048]{1,0:T(8,128)(2,1)S(1)} %collective-permute-done.11.refs_3_) | copy-start | bytes 1572868
  83.9 0.8 copy-start.11
  84.2 0.8 copy-start.12

commit v17 on v11

--- a/solution.py
+++ b/solution.py
@@ -201,7 +201,7 @@
     levels = lax.axis_size("area").bit_length() - 1
     nbits = lax.axis_size("neuron").bit_length() - 1
     n_pos = 1 << nbits
-    stages = [list(range(f, min(f + 2, rounds))) for f in range(0, rounds, 2)]
+    stages = [[0]] + [list(range(f, min(f + 2, rounds))) for f in range(1, rounds, 2)]
     arrived = []
     gate = None
     for stage in stages:

time: 92.5 us -> 94.2 us (1.018)
  Pallas kernels: 18.7 us -> 24.6 us
  waiting for transfers between devices: 54.4 us -> 49.1 us
  local copies, waits for them, and re-layouts: 2.25 us -> 6.26 us
  starting transfers between devices: 16 us -> 12.9 us
    ppermute x16, waiting for transfers between devices: 54.4 us -> 49.1 us  [swap(): return lax.ppermute(value, axis, pairs)]
    pallas_call x2 -> x3, Pallas kernels: 13.6 us -> 17.8 us  [stage_contrib(): pl.pallas_call(kernel, in_specs=[SMEM] + specs, out_specs=out_specs, scra...]
    unnamed x29 -> x37, local copies, waits for them, and re-layouts: 2.25 us -> 6.26 us
    ppermute x16, starting transfers between devices: 16 us -> 12.9 us  [swap(): return lax.ppermute(value, axis, pairs)]
    pallas_call x2 -> x3, Pallas kernels: 5.12 us -> 6.78 us  [send_slices(): pl.pallas_call(kernel, in_specs=[SMEM, VMEM], out_specs=[VMEM] * len(roun...]
  transfers between devices with their start and end apart: 16 -> 16, of which waited for: 10 -> 10; matrix products, arithmetic and copies ran while one was open for 2% -> 2% of each run, Pallas kernels for 10% -> 18%
where the time goes in v17:
time: 94.2 us; the launch traced here: 93.7 us
  waiting for transfers between devices  49.1 us (52%)
  Pallas kernels  24.6 us (26%)
  starting transfers between devices  12.9 us (14%)
  local copies, waits for them, and re-layouts  6.26 us (7%)
    ppermute x16, waiting for transfers between devices, swap(): return lax.ppermute(value, axis, pairs)  49.1 us
    pallas_call x3, Pallas kernels, stage_contrib(): pl.pallas_call(kernel, in_specs=[SMEM] + specs, out_specs=out_specs, scra...  17.8 us
    ppermute x16, starting transfers between devices, swap(): return lax.ppermute(value, axis, pairs)  12.9 us
    pallas_call x3, Pallas kernels, send_slices(): pl.pallas_call(kernel, in_specs=[SMEM, VMEM], out_specs=[VMEM] * len(roun...  6.78 us
    unnamed x37, local copies, waits for them, and re-layouts  6.26 us
  transfers between devices with their start and end apart: 16, of which 10 were waited for; matrix products, arithmetic and copies ran while one was open for 2% of the time, Pallas kernels for 18%

profile of v17, /device:TPU:0, one launch (start us, length us, event | category | flops | bytes accessed | tf_op | source)
XLA Modules:
  0.0 93.7 jit_solution(17397991462528857989)
XLA Ops:
  0.6 2.2 %shard_map.132 = bf16[128,2048]{1,0:T(8,128)(2,1)} custom-call(s32[4,4]{1,0:T(4,128)} %delays_ref.5, bf16[32,8,2048]{2,1,0:T(8,128)(2,1)} %window_ref.5), custom_call_target="tpu_custom_call" | custom-call | tf_op jit(solution)/shard_map/pallas_call | solution.py:34
  2.8 3.0 %collective-permute-start = (bf16[128,2048]{1,0:T(8,128)(2,1)}, bf16[128,2048]{1,0:T(8,128)(2,1)S(1)}, u32[]{:S(2)}, u32[]{:S(2)}) collective-permute-start(bf16[128,2048]{1,0:T(8,128)(2,1)} %shard_map.132), channel_id=1, source_target_pairs={{0,4},{4,0},{8,12},{12,8},{1,5},{5,1},{9,13},{13,9},{2,6},{6,2},{1... | collective-permute-start | bytes 1572872 | tf_op jit(solution)/shard_map/ppermute | solution.py:17
  5.8 2.5 %shard_map.131 = (bf16[128,2048]{1,0:T(8,128)(2,1)}, bf16[128,2048]{1,0:T(8,128)(2,1)}) custom-call(s32[4,4]{1,0:T(4,128)} %delays_ref.5, bf16[32,8,2048]{2,1,0:T(8,128)(2,1)} %window_ref.5), custom_call_target="tpu_custom_call" | custom-call | tf_op jit(solution)/shard_map/pallas_call | solution.py:34
  8.3 9.7 %collective-permute-done.refs_0_ = bf16[128,2048]{1,0:T(8,128)(2,1)S(1)} collective-permute-done((bf16[128,2048]{1,0:T(8,128)(2,1)}, bf16[128,2048]{1,0:T(8,128)(2,1)S(1)}, u32[]{:S(2)}, u32[]{:S(2)}) %collective-permute-start) | collective-permute-done | bytes 524320 | tf_op jit(solution)/shard_map/ppermute | solution.py:17
  18.0 1.7 %collective-permute-start.6 = (bf16[128,2048]{1,0:T(8,128)(2,1)S(1)}, bf16[128,2048]{1,0:T(8,128)(2,1)S(1)}, u32[]{:S(2)}, u32[]{:S(2)}) collective-permute-start(bf16[128,2048]{1,0:T(8,128)(2,1)S(1)} %collective-permute-done.refs_0_), channel_id=1, source_target_pairs={{0,2},{1,3},{2,0},{3,1},{4,6},{5,7},{6,4},{7,5},{8,10},{9,11},{10,... | collective-permute-start | bytes 1572872 | tf_op jit(solution)/shard_map/ppermute | solution.py:17
  19.6 1.6 %collective-permute-start.2 = (bf16[128,2048]{1,0:T(8,128)(2,1)}, bf16[128,2048]{1,0:T(8,128)(2,1)S(1)}, u32[]{:S(2)}, u32[]{:S(2)}) collective-permute-start(bf16[128,2048]{1,0:T(8,128)(2,1)} %get-tuple-element.17), channel_id=1, source_target_pairs={{0,4},{4,0},{8,12},{12,8},{1,5},{5,1},{9,13},{13,9},{2,6},{6,2},{1... | collective-permute-start | bytes 1572872 | tf_op jit(solution)/shard_map/ppermute | solution.py:17
  21.2 2.6 %collective-permute-start.1 = (bf16[128,2048]{1,0:T(8,128)(2,1)}, bf16[128,2048]{1,0:T(8,128)(2,1)S(1)}, u32[]{:S(2)}, u32[]{:S(2)}) collective-permute-start(bf16[128,2048]{1,0:T(8,128)(2,1)} %get-tuple-element.16), channel_id=1, source_target_pairs={{0,8},{4,12},{8,0},{12,4},{1,9},{5,13},{9,1},{13,5},{2,10},{6,14},... | collective-permute-start | bytes 1572872 | tf_op jit(solution)/shard_map/ppermute | solution.py:17
  23.8 0.0 collective-permute-start.7
  23.8 7.3 %collective-permute-done.6.refs_1_ = bf16[128,2048]{1,0:T(8,128)(2,1)S(1)} collective-permute-done((bf16[128,2048]{1,0:T(8,128)(2,1)S(1)}, bf16[128,2048]{1,0:T(8,128)(2,1)S(1)}, u32[]{:S(2)}, u32[]{:S(2)}) %collective-permute-start.6) | collective-permute-done | bytes 524320 | tf_op jit(solution)/shard_map/ppermute | solution.py:17
  31.1 0.0 collective-permute-start.8
  31.1 12.4 %collective-permute-done.2.refs_4_ = bf16[128,2048]{1,0:T(8,128)(2,1)S(1)} collective-permute-done((bf16[128,2048]{1,0:T(8,128)(2,1)}, bf16[128,2048]{1,0:T(8,128)(2,1)S(1)}, u32[]{:S(2)}, u32[]{:S(2)}) %collective-permute-start.2) | collective-permute-done | bytes 524320 | tf_op jit(solution)/shard_map/ppermute | solution.py:17
  43.5 0.7 collective-permute-start.11
  44.1 1.7 %collective-permute-done.1.refs_0_ = bf16[128,2048]{1,0:T(8,128)(2,1)S(1)} collective-permute-done((bf16[128,2048]{1,0:T(8,128)(2,1)}, bf16[128,2048]{1,0:T(8,128)(2,1)S(1)}, u32[]{:S(2)}, u32[]{:S(2)}) %collective-permute-start.1) | collective-permute-done | bytes 524320 | tf_op jit(solution)/shard_map/ppermute | solution.py:17
  45.8 0.5 collective-permute-start.5
  46.3 2.2 %shard_map.130 = bf16[128,2048]{1,0:T(8,128)(2,1)} custom-call(s32[4,4]{1,0:T(4,128)} %delays_ref.5, bf16[32,8,2048]{2,1,0:T(8,128)(2,1)} %window_ref.5), custom_call_target="tpu_custom_call" | custom-call | tf_op jit(solution)/shard_map/pallas_call | solution.py:34
  48.5 0.3 collective-permute-start.3
  48.8 1.4 %copy.16.bi_ref = s32[4,1,16,4]{3,2,1,0:T(8,128)} copy(s32[4,1,16,4]{2,3,1,0:T(4,128)} %param.20) | data formatting | bytes 2048 | tf_op args[9]
  50.3 0.0 collective-permute-done.7.refs_2_
  50.3 0.0 collective-permute-done.8.refs_3_
  50.3 0.0 copy-done.9
  50.3 0.0 copy-done.10
  50.3 0.8 copy-done.12
  51.1 0.8 copy-done.14
  51.9 5.3 %shard_map.133.refs_9_ = f32[16,8,2048]{2,1,0:T(8,128)} custom-call(s32[4,1,16,4]{3,2,1,0:T(8,128)} %copy.16.bi_ref, bf16[128,2048]{1,0:T(8,128)(2,1)} %copy-done.9, bf16[128,2048]{1,0:T(8,128)(2,1)} %copy-done.10, bf16[128,2048]{1,0:T(8,128)(2,1)} %copy-done.12, bf16[128,2048]{1,0:T(8,128)(2,1)} %copy-done.14, bf16[4,1,16,4,128,128]{5,4,3,2,1,0:T(8,128)(2,1)} %refs_4_.3), custom_call_target="tpu_custom_call" | custom-call | tf_op jit(solution)/shard_map/pallas_call | solution.py:184
  57.1 0.0 copy-start
  57.2 0.0 copy-start.1
  57.2 0.0 copy-start.2
  57.2 0.0 copy-start.3
  57.2 0.0 copy-start.4
  57.2 0.0 copy-start.5
  57.2 0.0 copy-start.6
  57.2 1.2 %collective-permute-done.11.refs_5_ = bf16[128,2048]{1,0:T(8,128)(2,1)} collective-permute-done((bf16[128,2048]{1,0:T(8,128)(2,1)S(1)}, bf16[128,2048]{1,0:T(8,128)(2,1)}, u32[]{:S(2)}, u32[]{:S(2)}) %collective-permute-start.11) | collective-permute-done | bytes 524320 | tf_op jit(solution)/shard_map/ppermute | solution.py:17
  58.4 0.0 collective-permute-start.12
  58.4 0.5 collective-permute-start.13
  58.9 7.5 %collective-permute-done.5.refs_1_ = bf16[128,2048]{1,0:T(8,128)(2,1)} collective-permute-done((bf16[128,2048]{1,0:T(8,128)(2,1)S(1)}, bf16[128,2048]{1,0:T(8,128)(2,1)}, u32[]{:S(2)}, u32[]{:S(2)}) %collective-permute-start.5) | collective-permute-done | bytes 524320 | tf_op jit(solution)/shard_map/ppermute | solution.py:17
  66.4 0.0 collective-permute-start.10
  66.4 0.5 collective-permute-start.9
  66.9 4.2 %collective-permute-done.3.refs_0_ = bf16[128,2048]{1,0:T(8,128)(2,1)} collective-permute-done((bf16[128,2048]{1,0:T(8,128)(2,1)}, bf16[128,2048]{1,0:T(8,128)(2,1)}, u32[]{:S(2)}, u32[]{:S(2)}) %collective-permute-start.3) | collective-permute-done | bytes 524320 | tf_op jit(solution)/shard_map/ppermute | solution.py:17
  71.1 1.0 %collective-permute-start.4 = (bf16[128,2048]{1,0:T(8,128)(2,1)}, bf16[128,2048]{1,0:T(8,128)(2,1)}, u32[]{:S(2)}, u32[]{:S(2)}) collective-permute-start(bf16[128,2048]{1,0:T(8,128)(2,1)} %collective-permute-done.3.refs_0_), channel_id=1, source_target_pairs={{0,2},{1,3},{2,0},{3,1},{4,6},{5,7},{6,4},{7,5},{8,10},{9,11},{10,... | collective-permute-start | bytes 1572872 | tf_op jit(solution)/shard_map/ppermute | solution.py:17
  72.1 0.0 collective-permute-done.12.refs_6_
  72.1 0.8 copy-done.11
  72.9 0.0 collective-permute-done.13.refs_7_
  72.9 0.8 copy-done.13
  73.8 0.0 collective-permute-done.10.refs_3_
  73.8 0.8 copy-done.15
  74.5 0.0 collective-permute-done.9.refs_2_
  74.6 0.0 copy-done.7
  74.6 0.0 copy-done.8
  74.6 6.9 %shard_map.134.refs_5_ = f32[16,8,2048]{2,1,0:T(8,128)} custom-call(s32[4,1,16,4]{3,2,1,0:T(8,128)} %copy.16.bi_ref, bf16[128,2048]{1,0:T(8,128)(2,1)} %copy-done.8, bf16[128,2048]{1,0:T(8,128)(2,1)} %collective-permute-done.5.refs_1_, bf16[128,2048]{1,0:T(8,128)(2,1)} %collective-permute-done.9.refs_2_, bf16[128,2048]{1,0:T(8,128)(2,1)} %copy-done.15, ...), custom_call_target="tpu_custom_call" | custom-call | tf_op jit(solution)/shard_map/pallas_call | solution.py:184
  81.5 2.8 %collective-permute-done.4.refs_1_ = bf16[128,2048]{1,0:T(8,128)(2,1)} collective-permute-done((bf16[128,2048]{1,0:T(8,128)(2,1)}, bf16[128,2048]{1,0:T(8,128)(2,1)}, u32[]{:S(2)}, u32[]{:S(2)}) %collective-permute-start.4) | collective-permute-done | bytes 524320 | tf_op jit(solution)/shard_map/ppermute | solution.py:17
  84.3 0.0 collective-permute-start.14
  84.3 0.5 collective-permute-start.15
  84.8 1.6 %collective-permute-done.14.refs_2_ = bf16[128,2048]{1,0:T(8,128)(2,1)S(1)} collective-permute-done((bf16[128,2048]{1,0:T(8,128)(2,1)}, bf16[128,2048]{1,0:T(8,128)(2,1)S(1)}, u32[]{:S(2)}, u32[]{:S(2)}) %collective-permute-start.14) | collective-permute-done | bytes 524320 | tf_op jit(solution)/shard_map/ppermute | solution.py:17
  86.4 0.7 collective-permute-done.15.refs_3_
  87.2 0.0 copy-done.16
  87.2 0.8 copy-done.17
  87.9 0.0 copy-done
  88.0 0.0 copy-done.1
  88.0 0.0 copy-done.2
  88.0 0.0 copy-done.3
  88.0 0.0 copy-done.4
  88.0 0.0 copy-done.5
  88.0 0.0 copy-done.6
  88.0 5.7 %shard_map.135 = (bf16[16,8,2048]{2,1,0:T(8,128)(2,1)}, f32[8,2048]{1,0:T(8,128)}, f32[8,2048]{1,0:T(8,128)}) custom-call(s32[4,1,16,4]{3,2,1,0:T(8,128)} %copy.16.bi_ref, bf16[128,2048]{1,0:T(8,128)(2,1)} %collective-permute-done.3.refs_0_, bf16[128,2048]{1,0:T(8,128)(2,1)} %collective-permute-done.4.refs_1_, bf16[128,2048]{1,0:T(8,128)(2,1)} %copy-done.16, ...), custom_call_target="tpu_custom_call" | custom-call | tf_op jit(solution)/shard_map/pallas_call | solution.py:184
  (11 shorter events, 0.0 us)
Async XLA Ops:
  2.8 15.2 %collective-permute-start = (bf16[128,2048]{1,0:T(8,128)(2,1)}, bf16[128,2048]{1,0:T(8,128)(2,1)S(1)}, u32[]{:S(2)}, u32[]{:S(2)}) collective-permute-start(bf16[128,2048]{1,0:T(8,128)(2,1)} %shard_map.132), channel_id=1, source_target_pairs={{0,4},{4,0},{8,12},{12,8},{1,5},{5,1},{9,13},{13,9},{2,6},{6,2},{1... | collective-permute-start | bytes 1572872 | tf_op jit(solution)/shard_map/ppermute | solution.py:17
  18.0 32.3 %copy-start.9 = (bf16[128,2048]{1,0:T(8,128)(2,1)}, bf16[128,2048]{1,0:T(8,128)(2,1)S(1)}, u32[]{:S(2)}) copy-start(bf16[128,2048]{1,0:T(8,128)(2,1)S(1)} %collective-permute-done.refs_0_) | copy-start | bytes 1572868
  18.0 13.1 %collective-permute-start.6 = (bf16[128,2048]{1,0:T(8,128)(2,1)S(1)}, bf16[128,2048]{1,0:T(8,128)(2,1)S(1)}, u32[]{:S(2)}, u32[]{:S(2)}) collective-permute-start(bf16[128,2048]{1,0:T(8,128)(2,1)S(1)} %collective-permute-done.refs_0_), channel_id=1, source_target_pairs={{0,2},{1,3},{2,0},{3,1},{4,6},{5,7},{6,4},{7,5},{8,10},{9,11},{10,... | collective-permute-start | bytes 1572872 | tf_op jit(solution)/shard_map/ppermute | solution.py:17
  19.6 23.8 %collective-permute-start.2 = (bf16[128,2048]{1,0:T(8,128)(2,1)}, bf16[128,2048]{1,0:T(8,128)(2,1)S(1)}, u32[]{:S(2)}, u32[]{:S(2)}) collective-permute-start(bf16[128,2048]{1,0:T(8,128)(2,1)} %get-tuple-element.17), channel_id=1, source_target_pairs={{0,4},{4,0},{8,12},{12,8},{1,5},{5,1},{9,13},{13,9},{2,6},{6,2},{1... | collective-permute-start | bytes 1572872 | tf_op jit(solution)/shard_map/ppermute | solution.py:17
  21.2 24.6 %collective-permute-start.1 = (bf16[128,2048]{1,0:T(8,128)(2,1)}, bf16[128,2048]{1,0:T(8,128)(2,1)S(1)}, u32[]{:S(2)}, u32[]{:S(2)}) collective-permute-start(bf16[128,2048]{1,0:T(8,128)(2,1)} %get-tuple-element.16), channel_id=1, source_target_pairs={{0,8},{4,12},{8,0},{12,4},{1,9},{5,13},{9,1},{13,5},{2,10},{6,14},... | collective-permute-start | bytes 1572872 | tf_op jit(solution)/shard_map/ppermute | solution.py:17
  23.8 26.5 %collective-permute-start.7 = (bf16[128,2048]{1,0:T(8,128)(2,1)S(1)}, bf16[128,2048]{1,0:T(8,128)(2,1)S(1)}, u32[]{:S(2)}, u32[]{:S(2)}) collective-permute-start(bf16[128,2048]{1,0:T(8,128)(2,1)S(1)} %collective-permute-done.refs_0_), channel_id=1, source_target_pairs={{0,1},{1,0},{2,3},{3,2},{4,5},{5,4},{6,7},{7,6},{8,9},{9,8},{10,11... | collective-permute-start | bytes 1572872 | tf_op jit(solution)/shard_map/ppermute | solution.py:17
  31.1 19.2 %copy-start.10 = (bf16[128,2048]{1,0:T(8,128)(2,1)}, bf16[128,2048]{1,0:T(8,128)(2,1)S(1)}, u32[]{:S(2)}) copy-start(bf16[128,2048]{1,0:T(8,128)(2,1)S(1)} %collective-permute-done.6.refs_1_) | copy-start | bytes 1572868
  31.1 19.2 %collective-permute-start.8 = (bf16[128,2048]{1,0:T(8,128)(2,1)S(1)}, bf16[128,2048]{1,0:T(8,128)(2,1)S(1)}, u32[]{:S(2)}, u32[]{:S(2)}) collective-permute-start(bf16[128,2048]{1,0:T(8,128)(2,1)S(1)} %collective-permute-done.6.refs_1_), channel_id=1, source_target_pairs={{0,1},{1,0},{2,3},{3,2},{4,5},{5,4},{6,7},{7,6},{8,9},{9,8},{10,11... | collective-permute-start | bytes 1572872 | tf_op jit(solution)/shard_map/ppermute | solution.py:17
  43.5 31.1 %copy-start.7 = (bf16[128,2048]{1,0:T(8,128)(2,1)}, bf16[128,2048]{1,0:T(8,128)(2,1)S(1)}, u32[]{:S(2)}) copy-start(bf16[128,2048]{1,0:T(8,128)(2,1)S(1)} %collective-permute-done.2.refs_4_) | copy-start | bytes 1572868
  43.5 15.0 %collective-permute-start.11 = (bf16[128,2048]{1,0:T(8,128)(2,1)S(1)}, bf16[128,2048]{1,0:T(8,128)(2,1)}, u32[]{:S(2)}, u32[]{:S(2)}) collective-permute-start(bf16[128,2048]{1,0:T(8,128)(2,1)S(1)} %collective-permute-done.2.refs_4_), channel_id=1, source_target_pairs={{0,2},{1,3},{2,0},{3,1},{4,6},{5,7},{6,4},{7,5},{8,10},{9,11},{10,... | collective-permute-start | bytes 1572872 | tf_op jit(solution)/shard_map/ppermute | solution.py:17
  45.8 28.7 %copy-start.8 = (bf16[128,2048]{1,0:T(8,128)(2,1)}, bf16[128,2048]{1,0:T(8,128)(2,1)S(1)}, u32[]{:S(2)}) copy-start(bf16[128,2048]{1,0:T(8,128)(2,1)S(1)} %collective-permute-done.1.refs_0_) | copy-start | bytes 1572868
  45.8 20.6 %collective-permute-start.5 = (bf16[128,2048]{1,0:T(8,128)(2,1)S(1)}, bf16[128,2048]{1,0:T(8,128)(2,1)}, u32[]{:S(2)}, u32[]{:S(2)}) collective-permute-start(bf16[128,2048]{1,0:T(8,128)(2,1)S(1)} %collective-permute-done.1.refs_0_), channel_id=1, source_target_pairs={{0,2},{1,3},{2,0},{3,1},{4,6},{5,7},{6,4},{7,5},{8,10},{9,11},{10,... | collective-permute-start | bytes 1572872 | tf_op jit(solution)/shard_map/ppermute | solution.py:17
  48.5 22.6 %collective-permute-start.3 = (bf16[128,2048]{1,0:T(8,128)(2,1)}, bf16[128,2048]{1,0:T(8,128)(2,1)}, u32[]{:S(2)}, u32[]{:S(2)}) collective-permute-start(bf16[128,2048]{1,0:T(8,128)(2,1)} %shard_map.130), channel_id=1, source_target_pairs={{0,8},{4,12},{8,0},{12,4},{1,9},{5,13},{9,1},{13,5},{2,10},{6,14},... | collective-permute-start | bytes 1572872 | tf_op jit(solution)/shard_map/ppermute | solution.py:17
  50.3 0.8 copy-start.12
  51.1 0.8 copy-start.14
  57.1 30.8 %copy-start = (f32[16,8,2048]{2,1,0:T(8,128)S(1)}, f32[16,8,2048]{2,1,0:T(8,128)}, u32[]{:S(2)}) copy-start(f32[16,8,2048]{2,1,0:T(8,128)} %refs_6_.1) | copy-start | bytes 3145732
  57.2 30.8 %copy-start.1 = (f32[16,8,2048]{2,1,0:T(8,128)S(1)}, f32[16,8,2048]{2,1,0:T(8,128)}, u32[]{:S(2)}) copy-start(f32[16,8,2048]{2,1,0:T(8,128)} %refs_7_.1) | copy-start | bytes 3145732
  57.2 30.8 %copy-start.2 = (f32[8,2048]{1,0:T(8,128)S(1)}, f32[8,2048]{1,0:T(8,128)}, u32[]{:S(2)}) copy-start(f32[8,2048]{1,0:T(8,128)} %refs_8_.3) | copy-start | bytes 196612
  57.2 30.8 %copy-start.3 = (f32[8,2048]{1,0:T(8,128)S(1)}, f32[8,2048]{1,0:T(8,128)}, u32[]{:S(2)}) copy-start(f32[8,2048]{1,0:T(8,128)} %refs_9_.1) | copy-start | bytes 196612
  57.2 30.8 %copy-start.4 = (f32[2048]{0:T(1024)S(1)}, f32[2048]{0:T(1024)}, u32[]{:S(2)}) copy-start(f32[2048]{0:T(1024)} %param.16) | copy-start | bytes 24580
  57.2 30.8 %copy-start.5 = (f32[2048]{0:T(1024)S(1)}, f32[2048]{0:T(1024)}, u32[]{:S(2)}) copy-start(f32[2048]{0:T(1024)} %param.17) | copy-start | bytes 24580
  57.2 30.8 %copy-start.6 = (f32[2048]{0:T(1024)S(1)}, f32[2048]{0:T(1024)}, u32[]{:S(2)}) copy-start(f32[2048]{0:T(1024)} %param.18) | copy-start | bytes 24580
  58.4 13.7 %collective-permute-start.12 = (bf16[128,2048]{1,0:T(8,128)(2,1)S(1)}, bf16[128,2048]{1,0:T(8,128)(2,1)S(1)}, u32[]{:S(2)}, u32[]{:S(2)}) collective-permute-start(bf16[128,2048]{1,0:T(8,128)(2,1)S(1)} %collective-permute-done.2.refs_4_), channel_id=1, source_target_pairs={{0,1},{1,0},{2,3},{3,2},{4,5},{5,4},{6,7},{7,6},{8,9},{9,8},{10,11... | collective-permute-start | bytes 1572872 | tf_op jit(solution)/shard_map/ppermute | solution.py:17
  58.4 14.5 %collective-permute-start.13 = (bf16[128,2048]{1,0:T(8,128)(2,1)}, bf16[128,2048]{1,0:T(8,128)(2,1)S(1)}, u32[]{:S(2)}, u32[]{:S(2)}) collective-permute-start(bf16[128,2048]{1,0:T(8,128)(2,1)} %collective-permute-done.11.refs_5_), channel_id=1, source_target_pairs={{0,1},{1,0},{2,3},{3,2},{4,5},{5,4},{6,7},{7,6},{8,9},{9,8},{10,11... | collective-permute-start | bytes 1572872 | tf_op jit(solution)/shard_map/ppermute | solution.py:17
  66.4 7.4 %collective-permute-start.10 = (bf16[128,2048]{1,0:T(8,128)(2,1)}, bf16[128,2048]{1,0:T(8,128)(2,1)S(1)}, u32[]{:S(2)}, u32[]{:S(2)}) collective-permute-start(bf16[128,2048]{1,0:T(8,128)(2,1)} %collective-permute-done.5.refs_1_), channel_id=1, source_target_pairs={{0,1},{1,0},{2,3},{3,2},{4,5},{5,4},{6,7},{7,6},{8,9},{9,8},{10,11... | collective-permute-start | bytes 1572872 | tf_op jit(solution)/shard_map/ppermute | solution.py:17
  66.4 8.2 %collective-permute-start.9 = (bf16[128,2048]{1,0:T(8,128)(2,1)S(1)}, bf16[128,2048]{1,0:T(8,128)(2,1)}, u32[]{:S(2)}, u32[]{:S(2)}) collective-permute-start(bf16[128,2048]{1,0:T(8,128)(2,1)S(1)} %collective-permute-done.1.refs_0_), channel_id=1, source_target_pairs={{0,1},{1,0},{2,3},{3,2},{4,5},{5,4},{6,7},{7,6},{8,9},{9,8},{10,11... | collective-permute-start | bytes 1572872 | tf_op jit(solution)/shard_map/ppermute | solution.py:17
  71.1 13.1 %collective-permute-start.4 = (bf16[128,2048]{1,0:T(8,128)(2,1)}, bf16[128,2048]{1,0:T(8,128)(2,1)}, u32[]{:S(2)}, u32[]{:S(2)}) collective-permute-start(bf16[128,2048]{1,0:T(8,128)(2,1)} %collective-permute-done.3.refs_0_), channel_id=1, source_target_pairs={{0,2},{1,3},{2,0},{3,1},{4,6},{5,7},{6,4},{7,5},{8,10},{9,11},{10,... | collective-permute-start | bytes 1572872 | tf_op jit(solution)/shard_map/ppermute | solution.py:17
  72.1 0.8 copy-start.11
  72.9 0.8 copy-start.13
  73.8 0.8 copy-start.15
  84.3 2.1 %collective-permute-start.14 = (bf16[128,2048]{1,0:T(8,128)(2,1)}, bf16[128,2048]{1,0:T(8,128)(2,1)S(1)}, u32[]{:S(2)}, u32[]{:S(2)}) collective-permute-start(bf16[128,2048]{1,0:T(8,128)(2,1)} %collective-permute-done.3.refs_0_), channel_id=1, source_target_pairs={{0,1},{1,0},{2,3},{3,2},{4,5},{5,4},{6,7},{7,6},{8,9},{9,8},{10,11... | collective-permute-start | bytes 1572872 | tf_op jit(solution)/shard_map/ppermute | solution.py:17
  84.3 2.9 %collective-permute-start.15 = (bf16[128,2048]{1,0:T(8,128)(2,1)}, bf16[128,2048]{1,0:T(8,128)(2,1)S(1)}, u32[]{:S(2)}, u32[]{:S(2)}) collective-permute-start(bf16[128,2048]{1,0:T(8,128)(2,1)} %collective-permute-done.4.refs_1_), channel_id=1, source_target_pairs={{0,1},{1,0},{2,3},{3,2},{4,5},{5,4},{6,7},{7,6},{8,9},{9,8},{10,11... | collective-permute-start | bytes 1572872 | tf_op jit(solution)/shard_map/ppermute | solution.py:17
  86.4 0.8 copy-start.16
  87.1 0.8 copy-start.17

commit v18 on v14

--- a/solution.py
+++ b/solution.py
@@ -201,11 +201,13 @@
     levels = lax.axis_size("area").bit_length() - 1
     nbits = lax.axis_size("neuron").bit_length() - 1
     n_pos = 1 << nbits
-    stages = [list(range(f, min(f + 2, rounds))) for f in range(0, rounds, 2)]
+    if rounds == 4 and levels == 2:
+        stages = [[1], [0, 3], [2]]
+    else:
+        stages = [list(range(f, min(f + 2, rounds))) for f in range(0, rounds, 2)]
     arrived = {}
     gate = None
     for stage in stages:
-        stage = sorted(stage, key=lambda rnd: -(rnd % levels))
         pieces = send_slices(window, delays, stage, levels, steps)
         if gate is not None:
             pieces, _ = lax.optimization_barrier((pieces, gate))

time: 93.7 us -> 105 us (1.12)
  Pallas kernels: 18.7 us -> 24.6 us
  local copies, waits for them, and re-layouts: 2.25 us -> 6.26 us
  waiting for transfers between devices: 55.9 us -> 58.1 us
  starting transfers between devices: 15.7 us -> 14.2 us
    pallas_call x2 -> x3, Pallas kernels: 13.6 us -> 17.9 us  [stage_contrib(): pl.pallas_call(kernel, in_specs=[SMEM] + specs, out_specs=out_specs, scra...]
    unnamed x29 -> x37, local copies, waits for them, and re-layouts: 2.25 us -> 6.26 us
    ppermute x16, waiting for transfers between devices: 55.9 us -> 58.1 us  [swap(): return lax.ppermute(value, axis, pairs)]
    pallas_call x2 -> x3, Pallas kernels: 5.12 us -> 6.78 us  [send_slices(): pl.pallas_call(kernel, in_specs=[SMEM, VMEM], out_specs=[VMEM] * len(roun...]
    ppermute x16, starting transfers between devices: 15.7 us -> 14.2 us  [swap(): return lax.ppermute(value, axis, pairs)]
  transfers between devices with their start and end apart: 16 -> 16, of which waited for: 9 -> 8; matrix products, arithmetic and copies ran while one was open for 1% -> 1% of each run, Pallas kernels for 10% -> 16%
where the time goes in v18:
time: 105 us; the launch traced here: 104 us
  waiting for transfers between devices  58.1 us (55%)
  Pallas kernels  24.6 us (23%)
  starting transfers between devices  14.2 us (14%)
  local copies, waits for them, and re-layouts  6.26 us (6%)
    ppermute x16, waiting for transfers between devices, swap(): return lax.ppermute(value, axis, pairs)  58.1 us
    pallas_call x3, Pallas kernels, stage_contrib(): pl.pallas_call(kernel, in_specs=[SMEM] + specs, out_specs=out_specs, scra...  17.9 us
    ppermute x16, starting transfers between devices, swap(): return lax.ppermute(value, axis, pairs)  14.2 us
    pallas_call x3, Pallas kernels, send_slices(): pl.pallas_call(kernel, in_specs=[SMEM, VMEM], out_specs=[VMEM] * len(roun...  6.78 us
    unnamed x37, local copies, waits for them, and re-layouts  6.26 us
  transfers between devices with their start and end apart: 16, of which 8 were waited for; matrix products, arithmetic and copies ran while one was open for 1% of the time, Pallas kernels for 16%

profile of v18, /device:TPU:0, one launch (start us, length us, event | category | flops | bytes accessed | tf_op | source)
XLA Modules:
  0.0 104.0 jit_solution(3332344434224929851)
XLA Ops:
  0.6 2.2 %shard_map.132 = bf16[128,2048]{1,0:T(8,128)(2,1)} custom-call(s32[4,4]{1,0:T(4,128)} %delays_ref.5, bf16[32,8,2048]{2,1,0:T(8,128)(2,1)} %window_ref.5), custom_call_target="tpu_custom_call" | custom-call | tf_op jit(solution)/shard_map/pallas_call | solution.py:34
  2.8 4.0 %collective-permute-start = (bf16[128,2048]{1,0:T(8,128)(2,1)}, bf16[128,2048]{1,0:T(8,128)(2,1)S(1)}, u32[]{:S(2)}, u32[]{:S(2)}) collective-permute-start(bf16[128,2048]{1,0:T(8,128)(2,1)} %shard_map.132), channel_id=1, source_target_pairs={{0,8},{4,12},{8,0},{12,4},{1,9},{5,13},{9,1},{13,5},{2,10},{6,14},... | collective-permute-start | bytes 1572872 | tf_op jit(solution)/shard_map/ppermute | solution.py:17
  6.8 2.4 %shard_map.131 = (bf16[128,2048]{1,0:T(8,128)(2,1)}, bf16[128,2048]{1,0:T(8,128)(2,1)}) custom-call(s32[4,4]{1,0:T(4,128)} %delays_ref.5, bf16[32,8,2048]{2,1,0:T(8,128)(2,1)} %window_ref.5), custom_call_target="tpu_custom_call" | custom-call | tf_op jit(solution)/shard_map/pallas_call | solution.py:34
  9.3 20.9 %collective-permute-done.refs_0_ = bf16[128,2048]{1,0:T(8,128)(2,1)S(1)} collective-permute-done((bf16[128,2048]{1,0:T(8,128)(2,1)}, bf16[128,2048]{1,0:T(8,128)(2,1)S(1)}, u32[]{:S(2)}, u32[]{:S(2)}) %collective-permute-start) | collective-permute-done | bytes 524320 | tf_op jit(solution)/shard_map/ppermute | solution.py:17
  30.2 1.5 %collective-permute-start.6 = (bf16[128,2048]{1,0:T(8,128)(2,1)S(1)}, bf16[128,2048]{1,0:T(8,128)(2,1)S(1)}, u32[]{:S(2)}, u32[]{:S(2)}) collective-permute-start(bf16[128,2048]{1,0:T(8,128)(2,1)S(1)} %collective-permute-done.refs_0_), channel_id=1, source_target_pairs={{0,2},{1,3},{2,0},{3,1},{4,6},{5,7},{6,4},{7,5},{8,10},{9,11},{10,... | collective-permute-start | bytes 1572872 | tf_op jit(solution)/shard_map/ppermute | solution.py:17
  31.7 0.0 collective-permute-start.2
  31.8 4.0 %collective-permute-start.1 = (bf16[128,2048]{1,0:T(8,128)(2,1)}, bf16[128,2048]{1,0:T(8,128)(2,1)S(1)}, u32[]{:S(2)}, u32[]{:S(2)}) collective-permute-start(bf16[128,2048]{1,0:T(8,128)(2,1)} %get-tuple-element.16), channel_id=1, source_target_pairs={{0,4},{4,0},{8,12},{12,8},{1,5},{5,1},{9,13},{13,9},{2,6},{6,2},{1... | collective-permute-start | bytes 1572872 | tf_op jit(solution)/shard_map/ppermute | solution.py:17
  35.8 0.0 collective-permute-start.7
  35.8 7.5 %collective-permute-done.6.refs_1_ = bf16[128,2048]{1,0:T(8,128)(2,1)S(1)} collective-permute-done((bf16[128,2048]{1,0:T(8,128)(2,1)S(1)}, bf16[128,2048]{1,0:T(8,128)(2,1)S(1)}, u32[]{:S(2)}, u32[]{:S(2)}) %collective-permute-start.6) | collective-permute-done | bytes 524320 | tf_op jit(solution)/shard_map/ppermute | solution.py:17
  43.3 0.0 collective-permute-start.8
  43.3 13.4 %collective-permute-done.2.refs_4_ = bf16[128,2048]{1,0:T(8,128)(2,1)S(1)} collective-permute-done((bf16[128,2048]{1,0:T(8,128)(2,1)}, bf16[128,2048]{1,0:T(8,128)(2,1)S(1)}, u32[]{:S(2)}, u32[]{:S(2)}) %collective-permute-start.2) | collective-permute-done | bytes 524320 | tf_op jit(solution)/shard_map/ppermute | solution.py:17
  56.7 0.8 collective-permute-start.11
  57.5 0.0 collective-permute-done.1.refs_0_
  57.5 1.3 %collective-permute-start.5 = (bf16[128,2048]{1,0:T(8,128)(2,1)S(1)}, bf16[128,2048]{1,0:T(8,128)(2,1)}, u32[]{:S(2)}, u32[]{:S(2)}) collective-permute-start(bf16[128,2048]{1,0:T(8,128)(2,1)S(1)} %collective-permute-done.1.refs_0_), channel_id=1, source_target_pairs={{0,2},{1,3},{2,0},{3,1},{4,6},{5,7},{6,4},{7,5},{8,10},{9,11},{10,... | collective-permute-start | bytes 1572872 | tf_op jit(solution)/shard_map/ppermute | solution.py:17
  58.8 2.2 %shard_map.130 = bf16[128,2048]{1,0:T(8,128)(2,1)} custom-call(s32[4,4]{1,0:T(4,128)} %delays_ref.5, bf16[32,8,2048]{2,1,0:T(8,128)(2,1)} %window_ref.5), custom_call_target="tpu_custom_call" | custom-call | tf_op jit(solution)/shard_map/pallas_call | solution.py:34
  60.9 0.0 collective-permute-start.3
  60.9 1.4 %copy.16.bi_ref = s32[4,1,16,4]{3,2,1,0:T(8,128)} copy(s32[4,1,16,4]{2,3,1,0:T(4,128)} %param.20) | data formatting | bytes 2048 | tf_op args[9]
  62.3 0.0 collective-permute-done.7.refs_2_
  62.3 0.0 collective-permute-done.8.refs_3_
  62.4 0.0 copy-done.9
  62.4 0.0 copy-done.10
  62.4 0.8 copy-done.12
  63.2 0.8 copy-done.14
  64.0 5.3 %shard_map.133.refs_9_ = f32[16,8,2048]{2,1,0:T(8,128)} custom-call(s32[4,1,16,4]{3,2,1,0:T(8,128)} %copy.16.bi_ref, bf16[128,2048]{1,0:T(8,128)(2,1)} %copy-done.9, bf16[128,2048]{1,0:T(8,128)(2,1)} %copy-done.10, bf16[128,2048]{1,0:T(8,128)(2,1)} %copy-done.12, bf16[128,2048]{1,0:T(8,128)(2,1)} %copy-done.14, bf16[4,1,16,4,128,128]{5,4,3,2,1,0:T(8,128)(2,1)} %refs_4_.3), custom_call_target="tpu_custom_call" | custom-call | tf_op jit(solution)/shard_map/pallas_call | solution.py:184
  69.2 0.0 copy-start
  69.3 0.0 copy-start.1
  69.3 0.0 copy-start.2
  69.3 0.0 copy-start.3
  69.3 0.0 copy-start.4
  69.3 0.0 copy-start.5
  69.3 0.0 copy-start.6
  69.3 2.4 %collective-permute-done.11.refs_5_ = bf16[128,2048]{1,0:T(8,128)(2,1)} collective-permute-done((bf16[128,2048]{1,0:T(8,128)(2,1)S(1)}, bf16[128,2048]{1,0:T(8,128)(2,1)}, u32[]{:S(2)}, u32[]{:S(2)}) %collective-permute-start.11) | collective-permute-done | bytes 524320 | tf_op jit(solution)/shard_map/ppermute | solution.py:17
  71.7 0.0 collective-permute-start.12
  71.7 0.5 collective-permute-start.13
  72.2 7.7 %collective-permute-done.5.refs_1_ = bf16[128,2048]{1,0:T(8,128)(2,1)} collective-permute-done((bf16[128,2048]{1,0:T(8,128)(2,1)S(1)}, bf16[128,2048]{1,0:T(8,128)(2,1)}, u32[]{:S(2)}, u32[]{:S(2)}) %collective-permute-start.5) | collective-permute-done | bytes 524320 | tf_op jit(solution)/shard_map/ppermute | solution.py:17
  79.9 0.0 collective-permute-start.10
  79.9 0.5 collective-permute-start.9
  80.4 0.0 collective-permute-done.3.refs_0_
  80.4 1.0 collective-permute-start.4
  81.5 0.0 collective-permute-done.12.refs_6_
  81.5 0.8 copy-done.11
  82.3 0.0 collective-permute-done.13.refs_7_
  82.3 0.8 copy-done.13
  83.1 0.0 collective-permute-done.10.refs_3_
  83.1 0.8 copy-done.15
  83.9 0.0 collective-permute-done.9.refs_2_
  83.9 0.0 copy-done.7
  83.9 0.0 copy-done.8
  83.9 6.9 %shard_map.134.refs_5_ = f32[16,8,2048]{2,1,0:T(8,128)} custom-call(s32[4,1,16,4]{3,2,1,0:T(8,128)} %copy.16.bi_ref, bf16[128,2048]{1,0:T(8,128)(2,1)} %copy-done.8, bf16[128,2048]{1,0:T(8,128)(2,1)} %collective-permute-done.5.refs_1_, bf16[128,2048]{1,0:T(8,128)(2,1)} %collective-permute-done.9.refs_2_, bf16[128,2048]{1,0:T(8,128)(2,1)} %copy-done.15, ...), custom_call_target="tpu_custom_call" | custom-call | tf_op jit(solution)/shard_map/pallas_call | solution.py:184
  90.8 3.8 %collective-permute-done.4.refs_1_ = bf16[128,2048]{1,0:T(8,128)(2,1)} collective-permute-done((bf16[128,2048]{1,0:T(8,128)(2,1)}, bf16[128,2048]{1,0:T(8,128)(2,1)}, u32[]{:S(2)}, u32[]{:S(2)}) %collective-permute-start.4) | collective-permute-done | bytes 524320 | tf_op jit(solution)/shard_map/ppermute | solution.py:17
  94.6 0.0 collective-permute-start.14
  94.6 0.5 collective-permute-start.15
  95.1 1.6 %collective-permute-done.14.refs_2_ = bf16[128,2048]{1,0:T(8,128)(2,1)S(1)} collective-permute-done((bf16[128,2048]{1,0:T(8,128)(2,1)}, bf16[128,2048]{1,0:T(8,128)(2,1)S(1)}, u32[]{:S(2)}, u32[]{:S(2)}) %collective-permute-start.14) | collective-permute-done | bytes 524320 | tf_op jit(solution)/shard_map/ppermute | solution.py:17
  96.7 0.7 collective-permute-done.15.refs_3_
  97.5 0.0 copy-done.16
  97.5 0.8 copy-done.17
  98.2 0.0 copy-done
  98.3 0.0 copy-done.1
  98.3 0.0 copy-done.2
  98.3 0.0 copy-done.3
  98.3 0.0 copy-done.4
  98.3 0.0 copy-done.5
  98.3 0.0 copy-done.6
  98.3 5.7 %shard_map.135 = (bf16[16,8,2048]{2,1,0:T(8,128)(2,1)}, f32[8,2048]{1,0:T(8,128)}, f32[8,2048]{1,0:T(8,128)}) custom-call(s32[4,1,16,4]{3,2,1,0:T(8,128)} %copy.16.bi_ref, bf16[128,2048]{1,0:T(8,128)(2,1)} %collective-permute-done.3.refs_0_, bf16[128,2048]{1,0:T(8,128)(2,1)} %collective-permute-done.4.refs_1_, bf16[128,2048]{1,0:T(8,128)(2,1)} %copy-done.16, ...), custom_call_target="tpu_custom_call" | custom-call | tf_op jit(solution)/shard_map/pallas_call | solution.py:184
  (11 shorter events, 0.0 us)
Async XLA Ops:
  2.8 27.4 %collective-permute-start = (bf16[128,2048]{1,0:T(8,128)(2,1)}, bf16[128,2048]{1,0:T(8,128)(2,1)S(1)}, u32[]{:S(2)}, u32[]{:S(2)}) collective-permute-start(bf16[128,2048]{1,0:T(8,128)(2,1)} %shard_map.132), channel_id=1, source_target_pairs={{0,8},{4,12},{8,0},{12,4},{1,9},{5,13},{9,1},{13,5},{2,10},{6,14},... | collective-permute-start | bytes 1572872 | tf_op jit(solution)/shard_map/ppermute | solution.py:17
  30.2 32.2 %copy-start.9 = (bf16[128,2048]{1,0:T(8,128)(2,1)}, bf16[128,2048]{1,0:T(8,128)(2,1)S(1)}, u32[]{:S(2)}) copy-start(bf16[128,2048]{1,0:T(8,128)(2,1)S(1)} %collective-permute-done.refs_0_) | copy-start | bytes 1572868
  30.2 13.1 %collective-permute-start.6 = (bf16[128,2048]{1,0:T(8,128)(2,1)S(1)}, bf16[128,2048]{1,0:T(8,128)(2,1)S(1)}, u32[]{:S(2)}, u32[]{:S(2)}) collective-permute-start(bf16[128,2048]{1,0:T(8,128)(2,1)S(1)} %collective-permute-done.refs_0_), channel_id=1, source_target_pairs={{0,2},{1,3},{2,0},{3,1},{4,6},{5,7},{6,4},{7,5},{8,10},{9,11},{10,... | collective-permute-start | bytes 1572872 | tf_op jit(solution)/shard_map/ppermute | solution.py:17
  31.7 25.0 %collective-permute-start.2 = (bf16[128,2048]{1,0:T(8,128)(2,1)}, bf16[128,2048]{1,0:T(8,128)(2,1)S(1)}, u32[]{:S(2)}, u32[]{:S(2)}) collective-permute-start(bf16[128,2048]{1,0:T(8,128)(2,1)} %get-tuple-element.17), channel_id=1, source_target_pairs={{0,8},{4,12},{8,0},{12,4},{1,9},{5,13},{9,1},{13,5},{2,10},{6,14},... | collective-permute-start | bytes 1572872 | tf_op jit(solution)/shard_map/ppermute | solution.py:17
  31.8 25.8 %collective-permute-start.1 = (bf16[128,2048]{1,0:T(8,128)(2,1)}, bf16[128,2048]{1,0:T(8,128)(2,1)S(1)}, u32[]{:S(2)}, u32[]{:S(2)}) collective-permute-start(bf16[128,2048]{1,0:T(8,128)(2,1)} %get-tuple-element.16), channel_id=1, source_target_pairs={{0,4},{4,0},{8,12},{12,8},{1,5},{5,1},{9,13},{13,9},{2,6},{6,2},{1... | collective-permute-start | bytes 1572872 | tf_op jit(solution)/shard_map/ppermute | solution.py:17
  35.8 26.5 %collective-permute-start.7 = (bf16[128,2048]{1,0:T(8,128)(2,1)S(1)}, bf16[128,2048]{1,0:T(8,128)(2,1)S(1)}, u32[]{:S(2)}, u32[]{:S(2)}) collective-permute-start(bf16[128,2048]{1,0:T(8,128)(2,1)S(1)} %collective-permute-done.refs_0_), channel_id=1, source_target_pairs={{0,1},{1,0},{2,3},{3,2},{4,5},{5,4},{6,7},{7,6},{8,9},{9,8},{10,11... | collective-permute-start | bytes 1572872 | tf_op jit(solution)/shard_map/ppermute | solution.py:17
  43.3 19.1 %copy-start.10 = (bf16[128,2048]{1,0:T(8,128)(2,1)}, bf16[128,2048]{1,0:T(8,128)(2,1)S(1)}, u32[]{:S(2)}) copy-start(bf16[128,2048]{1,0:T(8,128)(2,1)S(1)} %collective-permute-done.6.refs_1_) | copy-start | bytes 1572868
  43.3 19.0 %collective-permute-start.8 = (bf16[128,2048]{1,0:T(8,128)(2,1)S(1)}, bf16[128,2048]{1,0:T(8,128)(2,1)S(1)}, u32[]{:S(2)}, u32[]{:S(2)}) collective-permute-start(bf16[128,2048]{1,0:T(8,128)(2,1)S(1)} %collective-permute-done.6.refs_1_), channel_id=1, source_target_pairs={{0,1},{1,0},{2,3},{3,2},{4,5},{5,4},{6,7},{7,6},{8,9},{9,8},{10,11... | collective-permute-start | bytes 1572872 | tf_op jit(solution)/shard_map/ppermute | solution.py:17
  56.7 27.1 %copy-start.7 = (bf16[128,2048]{1,0:T(8,128)(2,1)}, bf16[128,2048]{1,0:T(8,128)(2,1)S(1)}, u32[]{:S(2)}) copy-start(bf16[128,2048]{1,0:T(8,128)(2,1)S(1)} %collective-permute-done.2.refs_4_) | copy-start | bytes 1572868
  56.7 15.0 %collective-permute-start.11 = (bf16[128,2048]{1,0:T(8,128)(2,1)S(1)}, bf16[128,2048]{1,0:T(8,128)(2,1)}, u32[]{:S(2)}, u32[]{:S(2)}) collective-permute-start(bf16[128,2048]{1,0:T(8,128)(2,1)S(1)} %collective-permute-done.2.refs_4_), channel_id=1, source_target_pairs={{0,2},{1,3},{2,0},{3,1},{4,6},{5,7},{6,4},{7,5},{8,10},{9,11},{10,... | collective-permute-start | bytes 1572872 | tf_op jit(solution)/shard_map/ppermute | solution.py:17
  57.5 26.4 %copy-start.8 = (bf16[128,2048]{1,0:T(8,128)(2,1)}, bf16[128,2048]{1,0:T(8,128)(2,1)S(1)}, u32[]{:S(2)}) copy-start(bf16[128,2048]{1,0:T(8,128)(2,1)S(1)} %collective-permute-done.1.refs_0_) | copy-start | bytes 1572868
  57.5 22.4 %collective-permute-start.5 = (bf16[128,2048]{1,0:T(8,128)(2,1)S(1)}, bf16[128,2048]{1,0:T(8,128)(2,1)}, u32[]{:S(2)}, u32[]{:S(2)}) collective-permute-start(bf16[128,2048]{1,0:T(8,128)(2,1)S(1)} %collective-permute-done.1.refs_0_), channel_id=1, source_target_pairs={{0,2},{1,3},{2,0},{3,1},{4,6},{5,7},{6,4},{7,5},{8,10},{9,11},{10,... | collective-permute-start | bytes 1572872 | tf_op jit(solution)/shard_map/ppermute | solution.py:17
  60.9 19.5 %collective-permute-start.3 = (bf16[128,2048]{1,0:T(8,128)(2,1)}, bf16[128,2048]{1,0:T(8,128)(2,1)}, u32[]{:S(2)}, u32[]{:S(2)}) collective-permute-start(bf16[128,2048]{1,0:T(8,128)(2,1)} %shard_map.130), channel_id=1, source_target_pairs={{0,4},{4,0},{8,12},{12,8},{1,5},{5,1},{9,13},{13,9},{2,6},{6,2},{1... | collective-permute-start | bytes 1572872 | tf_op jit(solution)/shard_map/ppermute | solution.py:17
  62.3 0.8 copy-start.12
  63.2 0.8 copy-start.14
  69.2 29.0 %copy-start = (f32[16,8,2048]{2,1,0:T(8,128)S(1)}, f32[16,8,2048]{2,1,0:T(8,128)}, u32[]{:S(2)}) copy-start(f32[16,8,2048]{2,1,0:T(8,128)} %refs_6_.1) | copy-start | bytes 3145732
  69.3 29.0 %copy-start.1 = (f32[16,8,2048]{2,1,0:T(8,128)S(1)}, f32[16,8,2048]{2,1,0:T(8,128)}, u32[]{:S(2)}) copy-start(f32[16,8,2048]{2,1,0:T(8,128)} %refs_7_.1) | copy-start | bytes 3145732
  69.3 29.0 %copy-start.2 = (f32[8,2048]{1,0:T(8,128)S(1)}, f32[8,2048]{1,0:T(8,128)}, u32[]{:S(2)}) copy-start(f32[8,2048]{1,0:T(8,128)} %refs_8_.3) | copy-start | bytes 196612
  69.3 29.0 %copy-start.3 = (f32[8,2048]{1,0:T(8,128)S(1)}, f32[8,2048]{1,0:T(8,128)}, u32[]{:S(2)}) copy-start(f32[8,2048]{1,0:T(8,128)} %refs_9_.1) | copy-start | bytes 196612
  69.3 29.0 %copy-start.4 = (f32[2048]{0:T(1024)S(1)}, f32[2048]{0:T(1024)}, u32[]{:S(2)}) copy-start(f32[2048]{0:T(1024)} %param.16) | copy-start | bytes 24580
  69.3 29.0 %copy-start.5 = (f32[2048]{0:T(1024)S(1)}, f32[2048]{0:T(1024)}, u32[]{:S(2)}) copy-start(f32[2048]{0:T(1024)} %param.17) | copy-start | bytes 24580
  69.3 29.0 %copy-start.6 = (f32[2048]{0:T(1024)S(1)}, f32[2048]{0:T(1024)}, u32[]{:S(2)}) copy-start(f32[2048]{0:T(1024)} %param.18) | copy-start | bytes 24580
  71.7 9.8 %collective-permute-start.12 = (bf16[128,2048]{1,0:T(8,128)(2,1)S(1)}, bf16[128,2048]{1,0:T(8,128)(2,1)S(1)}, u32[]{:S(2)}, u32[]{:S(2)}) collective-permute-start(bf16[128,2048]{1,0:T(8,128)(2,1)S(1)} %collective-permute-done.2.refs_4_), channel_id=1, source_target_pairs={{0,1},{1,0},{2,3},{3,2},{4,5},{5,4},{6,7},{7,6},{8,9},{9,8},{10,11... | collective-permute-start | bytes 1572872 | tf_op jit(solution)/shard_map/ppermute | solution.py:17
  71.7 10.6 %collective-permute-start.13 = (bf16[128,2048]{1,0:T(8,128)(2,1)}, bf16[128,2048]{1,0:T(8,128)(2,1)S(1)}, u32[]{:S(2)}, u32[]{:S(2)}) collective-permute-start(bf16[128,2048]{1,0:T(8,128)(2,1)} %collective-permute-done.11.refs_5_), channel_id=1, source_target_pairs={{0,1},{1,0},{2,3},{3,2},{4,5},{5,4},{6,7},{7,6},{8,9},{9,8},{10,11... | collective-permute-start | bytes 1572872 | tf_op jit(solution)/shard_map/ppermute | solution.py:17
  79.9 3.2 %collective-permute-start.10 = (bf16[128,2048]{1,0:T(8,128)(2,1)}, bf16[128,2048]{1,0:T(8,128)(2,1)S(1)}, u32[]{:S(2)}, u32[]{:S(2)}) collective-permute-start(bf16[128,2048]{1,0:T(8,128)(2,1)} %collective-permute-done.5.refs_1_), channel_id=1, source_target_pairs={{0,1},{1,0},{2,3},{3,2},{4,5},{5,4},{6,7},{7,6},{8,9},{9,8},{10,11... | collective-permute-start | bytes 1572872 | tf_op jit(solution)/shard_map/ppermute | solution.py:17
  79.9 4.0 %collective-permute-start.9 = (bf16[128,2048]{1,0:T(8,128)(2,1)S(1)}, bf16[128,2048]{1,0:T(8,128)(2,1)}, u32[]{:S(2)}, u32[]{:S(2)}) collective-permute-start(bf16[128,2048]{1,0:T(8,128)(2,1)S(1)} %collective-permute-done.1.refs_0_), channel_id=1, source_target_pairs={{0,1},{1,0},{2,3},{3,2},{4,5},{5,4},{6,7},{7,6},{8,9},{9,8},{10,11... | collective-permute-start | bytes 1572872 | tf_op jit(solution)/shard_map/ppermute | solution.py:17
  80.4 14.1 %collective-permute-start.4 = (bf16[128,2048]{1,0:T(8,128)(2,1)}, bf16[128,2048]{1,0:T(8,128)(2,1)}, u32[]{:S(2)}, u32[]{:S(2)}) collective-permute-start(bf16[128,2048]{1,0:T(8,128)(2,1)} %collective-permute-done.3.refs_0_), channel_id=1, source_target_pairs={{0,2},{1,3},{2,0},{3,1},{4,6},{5,7},{6,4},{7,5},{8,10},{9,11},{10,... | collective-permute-start | bytes 1572872 | tf_op jit(solution)/shard_map/ppermute | solution.py:17
  81.5 0.8 copy-start.11
  82.3 0.8 copy-start.13
  83.1 0.8 copy-start.15
  94.6 2.1 %collective-permute-start.14 = (bf16[128,2048]{1,0:T(8,128)(2,1)}, bf16[128,2048]{1,0:T(8,128)(2,1)S(1)}, u32[]{:S(2)}, u32[]{:S(2)}) collective-permute-start(bf16[128,2048]{1,0:T(8,128)(2,1)} %collective-permute-done.3.refs_0_), channel_id=1, source_target_pairs={{0,1},{1,0},{2,3},{3,2},{4,5},{5,4},{6,7},{7,6},{8,9},{9,8},{10,11... | collective-permute-start | bytes 1572872 | tf_op jit(solution)/shard_map/ppermute | solution.py:17
  94.6 2.9 %collective-permute-start.15 = (bf16[128,2048]{1,0:T(8,128)(2,1)}, bf16[128,2048]{1,0:T(8,128)(2,1)S(1)}, u32[]{:S(2)}, u32[]{:S(2)}) collective-permute-start(bf16[128,2048]{1,0:T(8,128)(2,1)} %collective-permute-done.4.refs_1_), channel_id=1, source_target_pairs={{0,1},{1,0},{2,3},{3,2},{4,5},{5,4},{6,7},{7,6},{8,9},{9,8},{10,11... | collective-permute-start | bytes 1572872 | tf_op jit(solution)/shard_map/ppermute | solution.py:17
  96.7 0.8 copy-start.16
  97.5 0.8 copy-start.17

commit v19 on v11

--- a/solution.py
+++ b/solution.py
@@ -177,7 +177,7 @@
         stage_kernel, n_pieces=len(pieces), stage=tuple(stage), n_pos=n_pos,
         final=final, has_rec=has_rec,
     )
-    pinned = [final and i > len(pieces) + has_rec for i in range(len(operands))]
+    pinned = [final and i > len(pieces) for i in range(len(operands))]
     specs = [VMEM if p else ANY for p in pinned]
     operands = [pltpu.with_memory_space_constraint(x, pltpu.VMEM) if p else x
                 for x, p in zip(operands, pinned)]

time: 92.5 us -> 93.4 us (level)
  local copies, waits for them, and re-layouts: 2.25 us -> 3.45 us
    unnamed x29 -> x31, local copies, waits for them, and re-layouts: 2.25 us -> 3.45 us
where the time goes in v19:
time: 93.4 us; the launch traced here: 93 us
  waiting for transfers between devices  54.4 us (58%)
  Pallas kernels  18.4 us (20%)
  starting transfers between devices  16 us (17%)
  local copies, waits for them, and re-layouts  3.45 us (4%)
    ppermute x16, waiting for transfers between devices, swap(): return lax.ppermute(value, axis, pairs)  54.4 us
    ppermute x16, starting transfers between devices, swap(): return lax.ppermute(value, axis, pairs)  16 us
    pallas_call x2, Pallas kernels, stage_contrib(): pl.pallas_call(kernel, in_specs=[SMEM] + specs, out_specs=out_specs, scra...  13.3 us
    pallas_call x2, Pallas kernels, send_slices(): pl.pallas_call(kernel, in_specs=[SMEM, VMEM], out_specs=[VMEM] * len(roun...  5.11 us
    unnamed x31, local copies, waits for them, and re-layouts  3.45 us
  transfers between devices with their start and end apart: 16, of which 10 were waited for; matrix products, arithmetic and copies ran while one was open for 2% of the time, Pallas kernels for 10%

profile of v19, /device:TPU:0, one launch (start us, length us, event | category | flops | bytes accessed | tf_op | source)
XLA Modules:
  0.0 93.0 jit_solution(11369719072284636866)
XLA Ops:
  0.6 0.0 copy-start.7
  0.6 0.0 copy-start.6
  0.7 0.0 copy-start.5
  0.7 0.0 copy-start.4
  0.7 0.0 copy-start.3
  0.7 0.0 copy-start.2
  0.7 0.0 copy-start.1
  0.7 2.6 %shard_map.131 = (bf16[128,2048]{1,0:T(8,128)(2,1)}, bf16[128,2048]{1,0:T(8,128)(2,1)}) custom-call(s32[4,4]{1,0:T(4,128)} %delays_ref.3, bf16[32,8,2048]{2,1,0:T(8,128)(2,1)} %window_ref.3), custom_call_target="tpu_custom_call" | custom-call | tf_op jit(solution)/shard_map/pallas_call | solution.py:34
  3.4 3.0 %collective-permute-start = (bf16[128,2048]{1,0:T(8,128)(2,1)}, bf16[128,2048]{1,0:T(8,128)(2,1)}, u32[]{:S(2)}, u32[]{:S(2)}) collective-permute-start(bf16[128,2048]{1,0:T(8,128)(2,1)} %get-tuple-element.15), channel_id=1, source_target_pairs={{0,4},{4,0},{8,12},{12,8},{1,5},{5,1},{9,13},{13,9},{2,6},{6,2},{1... | collective-permute-start | bytes 1572872 | tf_op jit(solution)/shard_map/ppermute | solution.py:17
  6.4 2.6 %collective-permute-start.1 = (bf16[128,2048]{1,0:T(8,128)(2,1)}, bf16[128,2048]{1,0:T(8,128)(2,1)}, u32[]{:S(2)}, u32[]{:S(2)}) collective-permute-start(bf16[128,2048]{1,0:T(8,128)(2,1)} %get-tuple-element.16), channel_id=1, source_target_pairs={{0,8},{4,12},{8,0},{12,4},{1,9},{5,13},{9,1},{13,5},{2,10},{6,14},... | collective-permute-start | bytes 1572872 | tf_op jit(solution)/shard_map/ppermute | solution.py:17
  9.0 2.5 %shard_map.130 = (bf16[128,2048]{1,0:T(8,128)(2,1)}, bf16[128,2048]{1,0:T(8,128)(2,1)}) custom-call(s32[4,4]{1,0:T(4,128)} %delays_ref.3, bf16[32,8,2048]{2,1,0:T(8,128)(2,1)} %window_ref.3), custom_call_target="tpu_custom_call" | custom-call | tf_op jit(solution)/shard_map/pallas_call | solution.py:34
  11.4 18.3 %collective-permute-done.refs_0_ = bf16[128,2048]{1,0:T(8,128)(2,1)} collective-permute-done((bf16[128,2048]{1,0:T(8,128)(2,1)}, bf16[128,2048]{1,0:T(8,128)(2,1)}, u32[]{:S(2)}, u32[]{:S(2)}) %collective-permute-start) | collective-permute-done | bytes 524320 | tf_op jit(solution)/shard_map/ppermute | solution.py:17
  29.7 0.0 collective-permute-start.5
  29.7 1.7 %collective-permute-start.4 = (bf16[128,2048]{1,0:T(8,128)(2,1)}, bf16[128,2048]{1,0:T(8,128)(2,1)}, u32[]{:S(2)}, u32[]{:S(2)}) collective-permute-start(bf16[128,2048]{1,0:T(8,128)(2,1)} %collective-permute-done.refs_0_), channel_id=1, source_target_pairs={{0,2},{1,3},{2,0},{3,1},{4,6},{5,7},{6,4},{7,5},{8,10},{9,11},{10,... | collective-permute-start | bytes 1572872 | tf_op jit(solution)/shard_map/ppermute | solution.py:17
  31.4 0.9 collective-permute-done.1.refs_4_
  32.3 1.5 %collective-permute-start.7 = (bf16[128,2048]{1,0:T(8,128)(2,1)}, bf16[128,2048]{1,0:T(8,128)(2,1)}, u32[]{:S(2)}, u32[]{:S(2)}) collective-permute-start(bf16[128,2048]{1,0:T(8,128)(2,1)} %collective-permute-done.1.refs_4_), channel_id=1, source_target_pairs={{0,2},{1,3},{2,0},{3,1},{4,6},{5,7},{6,4},{7,5},{8,10},{9,11},{10,... | collective-permute-start | bytes 1572872 | tf_op jit(solution)/shard_map/ppermute | solution.py:17
  33.7 0.4 collective-permute-start.2
  34.2 2.6 %collective-permute-start.12 = (bf16[128,2048]{1,0:T(8,128)(2,1)}, bf16[128,2048]{1,0:T(8,128)(2,1)S(1)}, u32[]{:S(2)}, u32[]{:S(2)}) collective-permute-start(bf16[128,2048]{1,0:T(8,128)(2,1)} %get-tuple-element.20), channel_id=1, source_target_pairs={{0,8},{4,12},{8,0},{12,4},{1,9},{5,13},{9,1},{13,5},{2,10},{6,14},... | collective-permute-start | bytes 1572872 | tf_op jit(solution)/shard_map/ppermute | solution.py:17
  36.8 0.0 collective-permute-done.5.refs_2_
  36.8 0.0 copy-start.14
  36.8 0.0 collective-permute-start.8
  36.8 8.0 %collective-permute-done.4.refs_1_ = bf16[128,2048]{1,0:T(8,128)(2,1)} collective-permute-done((bf16[128,2048]{1,0:T(8,128)(2,1)}, bf16[128,2048]{1,0:T(8,128)(2,1)}, u32[]{:S(2)}, u32[]{:S(2)}) %collective-permute-start.4) | collective-permute-done | bytes 524320 | tf_op jit(solution)/shard_map/ppermute | solution.py:17
  44.8 0.0 collective-permute-start.6
  44.8 10.8 %collective-permute-done.7.refs_5_ = bf16[128,2048]{1,0:T(8,128)(2,1)} collective-permute-done((bf16[128,2048]{1,0:T(8,128)(2,1)}, bf16[128,2048]{1,0:T(8,128)(2,1)}, u32[]{:S(2)}, u32[]{:S(2)}) %collective-permute-start.7) | collective-permute-done | bytes 524320 | tf_op jit(solution)/shard_map/ppermute | solution.py:17
  55.6 0.0 collective-permute-start.9
  55.6 0.6 collective-permute-done.2.refs_0_
  56.2 0.0 copy-start.8
  56.2 2.2 %collective-permute-start.3 = (bf16[128,2048]{1,0:T(8,128)(2,1)S(1)}, bf16[128,2048]{1,0:T(8,128)(2,1)}, u32[]{:S(2)}, u32[]{:S(2)}) collective-permute-start(bf16[128,2048]{1,0:T(8,128)(2,1)S(1)} %collective-permute-done.2.refs_0_), channel_id=1, source_target_pairs={{0,2},{1,3},{2,0},{3,1},{4,6},{5,7},{6,4},{7,5},{8,10},{9,11},{10,... | collective-permute-start | bytes 1572872 | tf_op jit(solution)/shard_map/ppermute | solution.py:17
  58.4 0.3 collective-permute-done.12.refs_4_
  58.8 0.0 copy-done.14
  58.8 0.0 copy-start.9
  58.8 0.9 %collective-permute-start.13 = (bf16[128,2048]{1,0:T(8,128)(2,1)S(1)}, bf16[128,2048]{1,0:T(8,128)(2,1)}, u32[]{:S(2)}, u32[]{:S(2)}) collective-permute-start(bf16[128,2048]{1,0:T(8,128)(2,1)S(1)} %collective-permute-done.12.refs_4_), channel_id=1, source_target_pairs={{0,2},{1,3},{2,0},{3,1},{4,6},{5,7},{6,4},{7,5},{8,10},{9,11},{10,... | collective-permute-start | bytes 1572872 | tf_op jit(solution)/shard_map/ppermute | solution.py:17
  59.7 1.4 %copy.15.bi_ref = s32[4,1,16,4]{3,2,1,0:T(8,128)} copy(s32[4,1,16,4]{2,3,1,0:T(4,128)} %param.20) | data formatting | bytes 2048 | tf_op args[9]
  61.1 0.0 collective-permute-done.8.refs_6_
  61.1 0.0 collective-permute-done.6.refs_3_
  61.1 0.0 collective-permute-done.9.refs_7_
  61.1 6.6 %shard_map.132.refs_9_ = f32[16,8,2048]{2,1,0:T(8,128)} custom-call(s32[4,1,16,4]{3,2,1,0:T(8,128)} %copy.15.bi_ref, bf16[128,2048]{1,0:T(8,128)(2,1)} %collective-permute-done.refs_0_, bf16[128,2048]{1,0:T(8,128)(2,1)} %collective-permute-done.4.refs_1_, bf16[128,2048]{1,0:T(8,128)(2,1)} %copy-done.14, bf16[128,2048]{1,0:T(8,128)(2,1)} %collective-permute-done.6.refs_3_, ...), custom_call_target="tpu_custom_call" | custom-call | tf_op jit(solution)/shard_map/pallas_call | solution.py:184
  67.7 3.6 %collective-permute-done.3.refs_1_ = bf16[128,2048]{1,0:T(8,128)(2,1)} collective-permute-done((bf16[128,2048]{1,0:T(8,128)(2,1)S(1)}, bf16[128,2048]{1,0:T(8,128)(2,1)}, u32[]{:S(2)}, u32[]{:S(2)}) %collective-permute-start.3) | collective-permute-done | bytes 524320 | tf_op jit(solution)/shard_map/ppermute | solution.py:17
  71.3 0.0 collective-permute-start.10
  71.3 0.5 collective-permute-start.11
  71.8 9.5 %collective-permute-done.13.refs_5_ = bf16[128,2048]{1,0:T(8,128)(2,1)} collective-permute-done((bf16[128,2048]{1,0:T(8,128)(2,1)S(1)}, bf16[128,2048]{1,0:T(8,128)(2,1)}, u32[]{:S(2)}, u32[]{:S(2)}) %collective-permute-start.13) | collective-permute-done | bytes 524320 | tf_op jit(solution)/shard_map/ppermute | solution.py:17
  81.3 0.0 collective-permute-start.14
  81.3 0.5 collective-permute-start.15
  81.8 0.0 collective-permute-done.10.refs_2_
  81.8 0.0 collective-permute-done.11.refs_3_
  81.8 0.0 copy-start.11
  81.8 2.1 %collective-permute-done.14.refs_6_ = bf16[128,2048]{1,0:T(8,128)(2,1)S(1)} collective-permute-done((bf16[128,2048]{1,0:T(8,128)(2,1)S(1)}, bf16[128,2048]{1,0:T(8,128)(2,1)S(1)}, u32[]{:S(2)}, u32[]{:S(2)}) %collective-permute-start.14) | collective-permute-done | bytes 524320 | tf_op jit(solution)/shard_map/ppermute | solution.py:17
  83.9 0.2 collective-permute-done.15.refs_7_
  84.2 0.0 copy-done.8
  84.2 0.0 copy-done.9
  84.2 0.0 copy-done.10
  84.2 0.0 copy-done.11
  84.2 0.5 copy-done.12
  84.7 0.2 copy-done.13
  85.0 0.0 copy-done.7
  85.0 0.0 copy-done.6
  85.0 0.0 copy-done.5
  85.0 0.0 copy-done.4
  85.0 0.0 copy-done.3
  85.0 0.0 copy-done.2
  85.0 0.0 copy-done.1
  85.0 0.0 copy-start
  85.0 1.2 %copy-done = f32[16,8,2048]{2,1,0:T(8,128)S(1)} copy-done((f32[16,8,2048]{2,1,0:T(8,128)S(1)}, f32[16,8,2048]{2,1,0:T(8,128)}, u32[]{:S(2)}) %copy-start) | copy-done | bytes 1048600
  86.3 6.8 %shard_map.133 = (bf16[16,8,2048]{2,1,0:T(8,128)(2,1)}, f32[8,2048]{1,0:T(8,128)}, f32[8,2048]{1,0:T(8,128)}) custom-call(s32[4,1,16,4]{3,2,1,0:T(8,128)} %copy.15.bi_ref, bf16[128,2048]{1,0:T(8,128)(2,1)} %copy-done.8, bf16[128,2048]{1,0:T(8,128)(2,1)} %collective-permute-done.3.refs_1_, bf16[128,2048]{1,0:T(8,128)(2,1)} %copy-done.10, ...), custom_call_target="tpu_custom_call" | custom-call | tf_op jit(solution)/shard_map/pallas_call | solution.py:184
  (3 shorter events, 0.0 us)
Async XLA Ops:
  0.6 84.4 %copy-start.7 = (f32[2048]{0:T(1024)S(1)}, f32[2048]{0:T(1024)}, u32[]{:S(2)}) copy-start(f32[2048]{0:T(1024)} %param.18) | copy-start | bytes 24580
  0.6 84.3 %copy-start.6 = (f32[2048]{0:T(1024)S(1)}, f32[2048]{0:T(1024)}, u32[]{:S(2)}) copy-start(f32[2048]{0:T(1024)} %param.17) | copy-start | bytes 24580
  0.7 84.3 %copy-start.5 = (f32[2048]{0:T(1024)S(1)}, f32[2048]{0:T(1024)}, u32[]{:S(2)}) copy-start(f32[2048]{0:T(1024)} %param.16) | copy-start | bytes 24580
  0.7 84.3 %copy-start.4 = (f32[8,2048]{1,0:T(8,128)S(1)}, f32[8,2048]{1,0:T(8,128)}, u32[]{:S(2)}) copy-start(f32[8,2048]{1,0:T(8,128)} %refs_13_.1) | copy-start | bytes 196612
  0.7 84.3 %copy-start.3 = (f32[8,2048]{1,0:T(8,128)S(1)}, f32[8,2048]{1,0:T(8,128)}, u32[]{:S(2)}) copy-start(f32[8,2048]{1,0:T(8,128)} %refs_12_.1) | copy-start | bytes 196612
  0.7 84.3 %copy-start.2 = (f32[16,8,2048]{2,1,0:T(8,128)S(1)}, f32[16,8,2048]{2,1,0:T(8,128)}, u32[]{:S(2)}) copy-start(f32[16,8,2048]{2,1,0:T(8,128)} %refs_11_.1) | copy-start | bytes 3145732
  0.7 84.3 %copy-start.1 = (f32[16,8,2048]{2,1,0:T(8,128)S(1)}, f32[16,8,2048]{2,1,0:T(8,128)}, u32[]{:S(2)}) copy-start(f32[16,8,2048]{2,1,0:T(8,128)} %refs_10_.1) | copy-start | bytes 3145732
  3.4 26.4 %collective-permute-start = (bf16[128,2048]{1,0:T(8,128)(2,1)}, bf16[128,2048]{1,0:T(8,128)(2,1)}, u32[]{:S(2)}, u32[]{:S(2)}) collective-permute-start(bf16[128,2048]{1,0:T(8,128)(2,1)} %get-tuple-element.15), channel_id=1, source_target_pairs={{0,4},{4,0},{8,12},{12,8},{1,5},{5,1},{9,13},{13,9},{2,6},{6,2},{1... | collective-permute-start | bytes 1572872 | tf_op jit(solution)/shard_map/ppermute | solution.py:17
  6.4 25.9 %collective-permute-start.1 = (bf16[128,2048]{1,0:T(8,128)(2,1)}, bf16[128,2048]{1,0:T(8,128)(2,1)}, u32[]{:S(2)}, u32[]{:S(2)}) collective-permute-start(bf16[128,2048]{1,0:T(8,128)(2,1)} %get-tuple-element.16), channel_id=1, source_target_pairs={{0,8},{4,12},{8,0},{12,4},{1,9},{5,13},{9,1},{13,5},{2,10},{6,14},... | collective-permute-start | bytes 1572872 | tf_op jit(solution)/shard_map/ppermute | solution.py:17
  29.7 7.1 %collective-permute-start.5 = (bf16[128,2048]{1,0:T(8,128)(2,1)}, bf16[128,2048]{1,0:T(8,128)(2,1)S(1)}, u32[]{:S(2)}, u32[]{:S(2)}) collective-permute-start(bf16[128,2048]{1,0:T(8,128)(2,1)} %collective-permute-done.refs_0_), channel_id=1, source_target_pairs={{0,1},{1,0},{2,3},{3,2},{4,5},{5,4},{6,7},{7,6},{8,9},{9,8},{10,11... | collective-permute-start | bytes 1572872 | tf_op jit(solution)/shard_map/ppermute | solution.py:17
  29.7 15.0 %collective-permute-start.4 = (bf16[128,2048]{1,0:T(8,128)(2,1)}, bf16[128,2048]{1,0:T(8,128)(2,1)}, u32[]{:S(2)}, u32[]{:S(2)}) collective-permute-start(bf16[128,2048]{1,0:T(8,128)(2,1)} %collective-permute-done.refs_0_), channel_id=1, source_target_pairs={{0,2},{1,3},{2,0},{3,1},{4,6},{5,7},{6,4},{7,5},{8,10},{9,11},{10,... | collective-permute-start | bytes 1572872 | tf_op jit(solution)/shard_map/ppermute | solution.py:17
  32.3 23.4 %collective-permute-start.7 = (bf16[128,2048]{1,0:T(8,128)(2,1)}, bf16[128,2048]{1,0:T(8,128)(2,1)}, u32[]{:S(2)}, u32[]{:S(2)}) collective-permute-start(bf16[128,2048]{1,0:T(8,128)(2,1)} %collective-permute-done.1.refs_4_), channel_id=1, source_target_pairs={{0,2},{1,3},{2,0},{3,1},{4,6},{5,7},{6,4},{7,5},{8,10},{9,11},{10,... | collective-permute-start | bytes 1572872 | tf_op jit(solution)/shard_map/ppermute | solution.py:17
  33.7 22.5 %collective-permute-start.2 = (bf16[128,2048]{1,0:T(8,128)(2,1)}, bf16[128,2048]{1,0:T(8,128)(2,1)S(1)}, u32[]{:S(2)}, u32[]{:S(2)}) collective-permute-start(bf16[128,2048]{1,0:T(8,128)(2,1)} %get-tuple-element.17), channel_id=1, source_target_pairs={{0,4},{4,0},{8,12},{12,8},{1,5},{5,1},{9,13},{13,9},{2,6},{6,2},{1... | collective-permute-start | bytes 1572872 | tf_op jit(solution)/shard_map/ppermute | solution.py:17
  34.2 24.6 %collective-permute-start.12 = (bf16[128,2048]{1,0:T(8,128)(2,1)}, bf16[128,2048]{1,0:T(8,128)(2,1)S(1)}, u32[]{:S(2)}, u32[]{:S(2)}) collective-permute-start(bf16[128,2048]{1,0:T(8,128)(2,1)} %get-tuple-element.20), channel_id=1, source_target_pairs={{0,8},{4,12},{8,0},{12,4},{1,9},{5,13},{9,1},{13,5},{2,10},{6,14},... | collective-permute-start | bytes 1572872 | tf_op jit(solution)/shard_map/ppermute | solution.py:17
  36.8 22.0 %copy-start.14 = (bf16[128,2048]{1,0:T(8,128)(2,1)}, bf16[128,2048]{1,0:T(8,128)(2,1)S(1)}, u32[]{:S(2)}) copy-start(bf16[128,2048]{1,0:T(8,128)(2,1)S(1)} %collective-permute-done.5.refs_2_) | copy-start | bytes 1572868
  36.8 24.3 %collective-permute-start.8 = (bf16[128,2048]{1,0:T(8,128)(2,1)}, bf16[128,2048]{1,0:T(8,128)(2,1)}, u32[]{:S(2)}, u32[]{:S(2)}) collective-permute-start(bf16[128,2048]{1,0:T(8,128)(2,1)} %collective-permute-done.1.refs_4_), channel_id=1, source_target_pairs={{0,1},{1,0},{2,3},{3,2},{4,5},{5,4},{6,7},{7,6},{8,9},{9,8},{10,11... | collective-permute-start | bytes 1572872 | tf_op jit(solution)/shard_map/ppermute | solution.py:17
  44.8 16.4 %collective-permute-start.6 = (bf16[128,2048]{1,0:T(8,128)(2,1)}, bf16[128,2048]{1,0:T(8,128)(2,1)}, u32[]{:S(2)}, u32[]{:S(2)}) collective-permute-start(bf16[128,2048]{1,0:T(8,128)(2,1)} %collective-permute-done.4.refs_1_), channel_id=1, source_target_pairs={{0,1},{1,0},{2,3},{3,2},{4,5},{5,4},{6,7},{7,6},{8,9},{9,8},{10,11... | collective-permute-start | bytes 1572872 | tf_op jit(solution)/shard_map/ppermute | solution.py:17
  55.6 5.5 %collective-permute-start.9 = (bf16[128,2048]{1,0:T(8,128)(2,1)}, bf16[128,2048]{1,0:T(8,128)(2,1)}, u32[]{:S(2)}, u32[]{:S(2)}) collective-permute-start(bf16[128,2048]{1,0:T(8,128)(2,1)} %collective-permute-done.7.refs_5_), channel_id=1, source_target_pairs={{0,1},{1,0},{2,3},{3,2},{4,5},{5,4},{6,7},{7,6},{8,9},{9,8},{10,11... | collective-permute-start | bytes 1572872 | tf_op jit(solution)/shard_map/ppermute | solution.py:17
  56.2 28.0 %copy-start.8 = (bf16[128,2048]{1,0:T(8,128)(2,1)}, bf16[128,2048]{1,0:T(8,128)(2,1)S(1)}, u32[]{:S(2)}) copy-start(bf16[128,2048]{1,0:T(8,128)(2,1)S(1)} %collective-permute-done.2.refs_0_) | copy-start | bytes 1572868
  56.2 15.1 %collective-permute-start.3 = (bf16[128,2048]{1,0:T(8,128)(2,1)S(1)}, bf16[128,2048]{1,0:T(8,128)(2,1)}, u32[]{:S(2)}, u32[]{:S(2)}) collective-permute-start(bf16[128,2048]{1,0:T(8,128)(2,1)S(1)} %collective-permute-done.2.refs_0_), channel_id=1, source_target_pairs={{0,2},{1,3},{2,0},{3,1},{4,6},{5,7},{6,4},{7,5},{8,10},{9,11},{10,... | collective-permute-start | bytes 1572872 | tf_op jit(solution)/shard_map/ppermute | solution.py:17
  58.8 25.4 %copy-start.9 = (bf16[128,2048]{1,0:T(8,128)(2,1)}, bf16[128,2048]{1,0:T(8,128)(2,1)S(1)}, u32[]{:S(2)}) copy-start(bf16[128,2048]{1,0:T(8,128)(2,1)S(1)} %collective-permute-done.12.refs_4_) | copy-start | bytes 1572868
  58.8 22.5 %collective-permute-start.13 = (bf16[128,2048]{1,0:T(8,128)(2,1)S(1)}, bf16[128,2048]{1,0:T(8,128)(2,1)}, u32[]{:S(2)}, u32[]{:S(2)}) collective-permute-start(bf16[128,2048]{1,0:T(8,128)(2,1)S(1)} %collective-permute-done.12.refs_4_), channel_id=1, source_target_pairs={{0,2},{1,3},{2,0},{3,1},{4,6},{5,7},{6,4},{7,5},{8,10},{9,11},{10,... | collective-permute-start | bytes 1572872 | tf_op jit(solution)/shard_map/ppermute | solution.py:17
  71.3 10.5 %collective-permute-start.10 = (bf16[128,2048]{1,0:T(8,128)(2,1)S(1)}, bf16[128,2048]{1,0:T(8,128)(2,1)S(1)}, u32[]{:S(2)}, u32[]{:S(2)}) collective-permute-start(bf16[128,2048]{1,0:T(8,128)(2,1)S(1)} %collective-permute-done.2.refs_0_), channel_id=1, source_target_pairs={{0,1},{1,0},{2,3},{3,2},{4,5},{5,4},{6,7},{7,6},{8,9},{9,8},{10,11... | collective-permute-start | bytes 1572872 | tf_op jit(solution)/shard_map/ppermute | solution.py:17
  71.3 10.5 %collective-permute-start.11 = (bf16[128,2048]{1,0:T(8,128)(2,1)}, bf16[128,2048]{1,0:T(8,128)(2,1)S(1)}, u32[]{:S(2)}, u32[]{:S(2)}) collective-permute-start(bf16[128,2048]{1,0:T(8,128)(2,1)} %collective-permute-done.3.refs_1_), channel_id=1, source_target_pairs={{0,1},{1,0},{2,3},{3,2},{4,5},{5,4},{6,7},{7,6},{8,9},{9,8},{10,11... | collective-permute-start | bytes 1572872 | tf_op jit(solution)/shard_map/ppermute | solution.py:17
  81.3 2.6 %collective-permute-start.14 = (bf16[128,2048]{1,0:T(8,128)(2,1)S(1)}, bf16[128,2048]{1,0:T(8,128)(2,1)S(1)}, u32[]{:S(2)}, u32[]{:S(2)}) collective-permute-start(bf16[128,2048]{1,0:T(8,128)(2,1)S(1)} %collective-permute-done.12.refs_4_), channel_id=1, source_target_pairs={{0,1},{1,0},{2,3},{3,2},{4,5},{5,4},{6,7},{7,6},{8,9},{9,8},{10,11... | collective-permute-start | bytes 1572872 | tf_op jit(solution)/shard_map/ppermute | solution.py:17
  81.3 2.9 %collective-permute-start.15 = (bf16[128,2048]{1,0:T(8,128)(2,1)}, bf16[128,2048]{1,0:T(8,128)(2,1)S(1)}, u32[]{:S(2)}, u32[]{:S(2)}) collective-permute-start(bf16[128,2048]{1,0:T(8,128)(2,1)} %collective-permute-done.13.refs_5_), channel_id=1, source_target_pairs={{0,1},{1,0},{2,3},{3,2},{4,5},{5,4},{6,7},{7,6},{8,9},{9,8},{10,11... | collective-permute-start | bytes 1572872 | tf_op jit(solution)/shard_map/ppermute | solution.py:17
  81.8 2.4 %copy-start.10 = (bf16[128,2048]{1,0:T(8,128)(2,1)}, bf16[128,2048]{1,0:T(8,128)(2,1)S(1)}, u32[]{:S(2)}) copy-start(bf16[128,2048]{1,0:T(8,128)(2,1)S(1)} %collective-permute-done.10.refs_2_) | copy-start | bytes 1572868
  81.8 2.4 %copy-start.11 = (bf16[128,2048]{1,0:T(8,128)(2,1)}, bf16[128,2048]{1,0:T(8,128)(2,1)S(1)}, u32[]{:S(2)}) copy-start(bf16[128,2048]{1,0:T(8,128)(2,1)S(1)} %collective-permute-done.11.refs_3_) | copy-start | bytes 1572868
  83.9 0.8 copy-start.12
  84.2 0.8 copy-start.13
  85.0 1.2 %copy-start = (f32[16,8,2048]{2,1,0:T(8,128)S(1)}, f32[16,8,2048]{2,1,0:T(8,128)}, u32[]{:S(2)}) copy-start(f32[16,8,2048]{2,1,0:T(8,128)} %shard_map.132.refs_9_) | copy-start | bytes 3145732
